TPU v7x, 32 devices: a whole 2x2x4 slice. The times are simulated.
32 devices in a mesh: blk: 8 (over z, core), mesh: 4 (over y, x).
Axes of the slice: x: 2, y: 2, z: 4, core: 2. Of those that a mesh axis runs over, the one named last changes fastest.
Arguments:
- flow_field: float32 [8, 5, 96, 1024], P('blk', None, None, 'mesh'), may hold values from -6 to 6
- lower_row_history: float32 [8, 64, 5, 1024], P('blk', None, None, 'mesh'), may hold values from -6 to 6
- upper_row_history: float32 [8, 64, 5, 1024], P('blk', None, None, 'mesh'), may hold values from -6 to 6
- lower_lag_slot: int32 [8], replicated, may hold values from 0 to 63
- upper_lag_slot: int32 [8], replicated, may hold values from 0 to 63
- axial_jacobian: float32 [5, 5], replicated, may hold values from -2.5 to 2.5
- pitch_jacobian: float32 [5, 5], replicated, may hold values from -2.5 to 2.5
- mode_shape: float32 [4, 96, 1024], P(None, None, 'mesh'), may hold values from -16 to 16
- stiffness: float32 [8, 4], P('blk'), may hold values from 0.5 to 4
- displacement: float32 [8, 4], P('blk'), may hold values from -4 to 4
- velocity: float32 [8, 4], P('blk'), may hold values from -4 to 4
Outputs:
- new_flow: float32 [8, 5, 96, 1024], P('blk', None, None, 'mesh')
- new_displacement: float32 [8, 4], P('blk')
- new_velocity: float32 [8, 4], P('blk')
All inputs are finite; a program needn't handle non-finite values.
Results may differ from a plain program's by a relative error of at most 0.0003.
Values sent between devices are 32-bit elements; how exact they have to be, the bound alone decides.
No kernel may reach another device: no remote copies, remote signals or barrier semaphores. Data moves between devices by JAX's collectives and lax.ppermute only.
A program may use at most 64 MiB of HBM per device.

v0:
```python
import math

import jax
import jax.numpy as jnp
from jax import lax
from jax.sharding import PartitionSpec as P

STEP_COUNT = 2


PRECISE = lax.Precision.HIGHEST
TIME_STEP = 0.4
DIFFUSION = 0.1
COUPLING = 0.3
DAMPING = 0.1


def shifted(value, axis, by):
    peers = lax.axis_size(axis)
    return lax.ppermute(value, axis, [(i, (i + by) % peers) for i in range(peers)])


def padded(value, sides, width):
    for axis, dim in sides:
        peers, length = (lax.axis_size(axis), value.shape[dim])
        up = [(i, (i + 1) % peers) for i in range(peers - 1)]
        down = [(j, i) for i, j in up]
        last = lax.slice_in_dim(value, length - width, length, axis=dim)
        initial = lax.slice_in_dim(value, 0, width, axis=dim)
        before = lax.ppermute(last, axis, up)
        after = lax.ppermute(initial, axis, down)
        value = jnp.concatenate([before, value, after], axis=dim)
    return value


def rates_from(
    flow_state,
    padded_axial,
    modal_velocity,
    lower_ghost,
    upper_ghost,
    axial_jacobian,
    pitch_jacobian,
    mode_shape,
):
    padded_pitch = jnp.concatenate(
        [lower_ghost[:, None, :], flow_state, upper_ghost[:, None, :]], axis=1
    )
    grad_axial = 0.5 * (padded_axial[:, :, 2:] - padded_axial[:, :, :-2])
    grad_pitch = 0.5 * (padded_pitch[:, 2:, :] - padded_pitch[:, :-2, :])
    laplacian = (
        padded_axial[:, :, 2:]
        + padded_axial[:, :, :-2]
        + padded_pitch[:, 2:, :]
        + padded_pitch[:, :-2, :]
        - 4.0 * flow_state
    )
    flux = jnp.einsum("ij,jpx->ipx", axial_jacobian, grad_axial, precision=PRECISE)
    flux = flux + jnp.einsum("ij,jpx->ipx", pitch_jacobian, grad_pitch, precision=PRECISE)
    push = COUPLING * jnp.einsum("m,mpx->px", modal_velocity, mode_shape, precision=PRECISE)
    rate = DIFFUSION * laplacian - flux
    rate = rate.at[1].add(push)
    partial_value = jnp.einsum("mpx,px->m", mode_shape, flow_state[4], precision=PRECISE)
    return (rate, partial_value)


def on_device(
    flow_field,
    lower_row_history,
    upper_row_history,
    lower_lag_slot,
    upper_lag_slot,
    axial_jacobian,
    pitch_jacobian,
    mode_shape,
    stiffness,
    displacement,
    velocity,
):
    flow_state = flow_field[0]
    pitch_cells = flow_state.shape[1]
    axial_cells = flow_state.shape[2]
    force_scale = 1.0 / math.sqrt(pitch_cells * axial_cells * lax.axis_size("mesh"))
    position = lax.axis_index("blk")
    slot_count = lower_row_history.shape[1]
    own_low = lax.dynamic_index_in_dim(lower_lag_slot, position, 0, keepdims=False)
    own_high = lax.dynamic_index_in_dim(upper_lag_slot, position, 0, keepdims=False)
    blade_stiffness = stiffness[0]
    modal_disp = displacement[0]
    modal_velocity = velocity[0]
    store_below = shifted(upper_row_history[0], "blk", 1)
    store_above = shifted(lower_row_history[0], "blk", -1)
    for advance_once in range(STEP_COUNT):
        lower_ghost = lax.dynamic_index_in_dim(
            store_below, (own_low + advance_once) % slot_count, 0, keepdims=False
        )
        upper_ghost = lax.dynamic_index_in_dim(
            store_above, (own_high + advance_once) % slot_count, 0, keepdims=False
        )

        def evaluate(state_now, disp_now, velocity_now):
            padded_axial = padded(state_now, (("mesh", 2),), 1)
            rate, partial_value = rates_from(
                state_now,
                padded_axial,
                velocity_now,
                lower_ghost,
                upper_ghost,
                axial_jacobian,
                pitch_jacobian,
                mode_shape,
            )
            total = lax.psum(partial_value, "mesh")
            accel = total * force_scale - blade_stiffness * disp_now - DAMPING * velocity_now
            return (rate, velocity_now, accel)

        first_rate, first_disp, first_accel = evaluate(flow_state, modal_disp, modal_velocity)
        mid_state = flow_state + TIME_STEP * first_rate
        mid_disp = modal_disp + TIME_STEP * first_disp
        mid_velocity = modal_velocity + TIME_STEP * first_accel
        second_rate, second_disp, second_accel = evaluate(mid_state, mid_disp, mid_velocity)
        flow_state = flow_state + 0.5 * TIME_STEP * (first_rate + second_rate)
        modal_disp = modal_disp + 0.5 * TIME_STEP * (first_disp + second_disp)
        modal_velocity = modal_velocity + 0.5 * TIME_STEP * (first_accel + second_accel)
    return (flow_state[None], modal_disp[None], modal_velocity[None])


def solution(mesh):
    return jax.shard_map(
        on_device,
        mesh=mesh,
        in_specs=(
            P("blk", None, None, "mesh"),
            P("blk", None, None, "mesh"),
            P("blk", None, None, "mesh"),
            P(),
            P(),
            P(),
            P(),
            P(None, None, "mesh"),
            P("blk", None),
            P("blk", None),
            P("blk", None),
        ),
        out_specs=(P("blk", None, None, "mesh"), P("blk", None), P("blk", None)),
        check_vma=False,
    )
```

profile of v0, /device:TPU:0, one launch (start us, length us, event | category | flops | bytes accessed | tf_op | source)
XLA Modules:
  0.0 90.3 jit_solution(17063163354739248446)
XLA Ops:
  0.6 0.0 copy-start
  0.7 1.3 %fusion.64 = (f32[5,96,1]{2,1,0:T(8,128)S(1)}, f32[5,96,1]{2,1,0:T(8,128)S(1)}) fusion(f32[5,96,256]{2,1,0:T(8,128)} %bitcast.194), kind=kLoop, calls=%fused_computation.131 | loop fusion | bytes 7680 | tf_op jit(solution)/shard_map/slice | solution.py:28
  1.9 1.3 %collective-permute-start = (f32[5,96,1]{2,1,0:T(8,128)S(1)}, f32[5,96,1]{2,1,0:T(8,128)S(1)}, u32[]{:S(2)}, u32[]{:S(2)}) collective-permute-start(f32[5,96,1]{2,1,0:T(8,128)S(1)} %get-tuple-element.75), channel_id=1, source_target_pairs={{1,0},{2,1},{3,2},{5,4},{6,5},{7,6},{9,8},{10,9},{11,10},{13,12},{... | collective-permute-start | bytes 5768 | tf_op jit(solution)/shard_map/ppermute | solution.py:31
  3.2 5.5 %collective-permute-start.1 = (f32[5,96,1]{2,1,0:T(8,128)S(1)}, f32[5,96,1]{2,1,0:T(8,128)S(1)}, u32[]{:S(2)}, u32[]{:S(2)}) collective-permute-start(f32[5,96,1]{2,1,0:T(8,128)S(1)} %get-tuple-element.74), channel_id=1, source_target_pairs={{0,1},{1,2},{2,3},{4,5},{5,6},{6,7},{8,9},{9,10},{10,11},{12,13},{... | collective-permute-start | bytes 5768 | tf_op jit(solution)/shard_map/ppermute | solution.py:30
  8.7 0.1 collective-permute-start.3
  8.8 3.5 %collective-permute-start.2 = (f32[64,5,256]{2,0,1:T(8,128)}, f32[64,5,256]{2,0,1:T(8,128)S(1)}, u32[]{:S(2)}, u32[]{:S(2)}) collective-permute-start(f32[64,5,256]{2,0,1:T(8,128)} %bitcast.198), channel_id=1, source_target_pairs={{0,28},{4,0},{8,4},{12,8},{16,12},{20,16},{24,20},{28,24},{1,29},{... | collective-permute-start | bytes 983048 | tf_op jit(solution)/shard_map/ppermute | solution.py:20
  12.3 0.7 copy-done.7
  13.0 0.6 dynamic_slice.22
  16.2 0.0 copy-start.8
  16.2 0.6 copy-done.8
  16.8 0.6 dynamic_slice.20
  20.1 0.0 copy-start.5
  20.1 1.8 %convolution_bitcast_fusion.3 = f32[4]{0:T(128)S(1)} fusion(f32[96,256,1]{1,0,2:T(8,128)S(1)} %slice_bitcast_fusion.3, f32[4,96,256]{2,1,0:T(8,128)S(1)} %copy-done.2), kind=kOutput, calls=%fused_computation.3 | convolution fusion | flops 1179648 | bytes 491536 | tf_op jit(solution)/shard_map/mpx,px->m/dot_general | solution.py:63
  22.0 1.0 %fusion.34 = f32[1,96,256]{2,0,1:T(1,128)S(1)} fusion(f32[4,96,256]{2,1,0:T(8,128)S(1)} %copy-done.2, f32[1,4]{1,0:T(1,128)S(1)} %copy-done.5), kind=kOutput, calls=%fused_computation.86 | convolution fusion | flops 1179648 | bytes 491536 | tf_op jit(solution)/shard_map/m,mpx->px/dot_general | solution.py:60
  22.9 0.0 collective-permute-done.3
  23.0 0.0 collective-permute-done.2
  23.0 0.0 collective-permute-done.1
  23.0 0.4 subtract_multiply_fusion.7
  23.5 0.0 copy-start.3
  23.5 1.0 %fusion.12 = f32[96,256,5]{1,2,0:T(8,128)S(1)} fusion(f32[5,96,256]{2,1,0:T(8,128)S(1)} %get-tuple-element.73, f32[5,5]{1,0:T(8,128)S(1)} %copy-done), kind=kOutput, calls=%fused_computation.16 | convolution fusion | flops 7372800 | bytes 983140 | tf_op jit(solution)/shard_map/ij,jpx->ipx/dot_general | solution.py:59
  24.6 1.0 %fusion.14 = f32[96,256,5]{1,2,0:T(8,128)S(1)} fusion(f32[5,96,256]{2,1,0:T(8,128)S(1)} %get-tuple-element.72, f32[5,5]{1,0:T(8,128)S(1)} %copy-done.3), kind=kOutput, calls=%fused_computation.18 | convolution fusion | flops 7372800 | bytes 983140 | tf_op jit(solution)/shard_map/ij,jpx->ipx/dot_general | solution.py:58
  25.6 0.6 bitcast_subtract_fusion.3
  26.3 0.1 multiply_add_fusion.2
  26.3 0.1 fusion.63
  26.5 1.3 %collective-permute-start.4 = (f32[5,96,1]{2,1,0:T(8,128)S(1)}, f32[5,96,1]{2,1,0:T(8,128)S(1)}, u32[]{:S(2)}, u32[]{:S(2)}) collective-permute-start(f32[5,96,1]{2,1,0:T(8,128)S(1)} %get-tuple-element.71), channel_id=1, source_target_pairs={{1,0},{2,1},{3,2},{5,4},{6,5},{7,6},{9,8},{10,9},{11,10},{13,12},{... | collective-permute-start | bytes 5768 | tf_op jit(solution)/shard_map/ppermute | solution.py:31
  27.8 2.0 %convolution_bitcast_fusion.2 = f32[4]{0:T(128)S(1)} fusion(f32[96,256,1]{1,0,2:T(8,128)S(1)} %slice_bitcast_fusion.2, f32[4,96,256]{2,1,0:T(8,128)S(1)} %copy-done.2), kind=kOutput, calls=%fused_computation.2 | convolution fusion | flops 1179648 | bytes 491536 | tf_op jit(solution)/shard_map/mpx,px->m/dot_general | solution.py:63
  29.8 5.5 %collective-permute-start.5 = (f32[5,96,1]{2,1,0:T(8,128)S(1)}, f32[5,96,1]{2,1,0:T(8,128)S(1)}, u32[]{:S(2)}, u32[]{:S(2)}) collective-permute-start(f32[5,96,1]{2,1,0:T(8,128)S(1)} %get-tuple-element.70), channel_id=1, source_target_pairs={{0,1},{1,2},{2,3},{4,5},{5,6},{6,7},{8,9},{9,10},{10,11},{12,13},{... | collective-permute-start | bytes 5768 | tf_op jit(solution)/shard_map/ppermute | solution.py:30
  35.2 10.6 %all-reduce.1 = (f32[4]{0:T(128)S(1)}, f32[4]{0:T(128)S(1)}) all-reduce(f32[4]{0:T(128)S(1)} %convolution_bitcast_fusion.3, f32[4]{0:T(128)S(1)} %convolution_bitcast_fusion.2), channel_id=1, replica_groups=mesh['blk'=8,'mesh'=4] {'mesh'}, use_global_device_ids=true, to_apply=%region_0.1 | all-reduce | flops 8 | bytes 64 | tf_op jit(solution)/shard_map/psum | solution.py:113
  45.8 0.7 copy-done.4
  46.4 0.0 copy-done.6
  46.4 1.0 %fusion.31 = f32[1,96,256]{2,0,1:T(1,128)S(1)} fusion(f32[4,96,256]{2,1,0:T(8,128)S(1)} %copy-done.2, f32[1,4]{1,0:T(1,128)S(1)} %copy-done.5, f32[1,4]{1,0:T(1,128)S(1)} %copy-done.6, f32[1,4]{1,0:T(1,128)S(1)} %copy-done.4, f32[4]{0:T(128)S(1)} %get-tuple-element.56), kind=kOutput, calls=%fused_computation.83 | convolution fusion | flops 1179676 | bytes 491584 | tf_op jit(solution)/shard_map/m,mpx->px/dot_general | solution.py:60
  47.4 1.0 %fusion.28 = f32[1,96,256]{2,0,1:T(1,128)S(1)} fusion(f32[4,96,256]{2,1,0:T(8,128)S(1)} %copy-done.2, f32[4]{0:T(128)S(1)} %bitcast_add_fusion.2), kind=kOutput, calls=%fused_computation.80 | convolution fusion | flops 1179648 | bytes 491536 | tf_op jit(solution)/shard_map/m,mpx->px/dot_general | solution.py:60
  48.4 0.0 collective-permute-done.5
  48.4 0.4 subtract_multiply_fusion.5
  48.9 1.0 %fusion.8 = f32[96,256,5]{1,2,0:T(8,128)S(1)} fusion(f32[5,96,256]{2,1,0:T(8,128)S(1)} %get-tuple-element.69, f32[5,5]{1,0:T(8,128)S(1)} %copy-done), kind=kOutput, calls=%fused_computation.12 | convolution fusion | flops 7372800 | bytes 983140 | tf_op jit(solution)/shard_map/ij,jpx->ipx/dot_general | solution.py:59
  49.9 1.0 %fusion.10 = f32[96,256,5]{1,2,0:T(8,128)S(1)} fusion(f32[5,96,256]{2,1,0:T(8,128)S(1)} %get-tuple-element.68, f32[5,5]{1,0:T(8,128)S(1)} %copy-done.3), kind=kOutput, calls=%fused_computation.14 | convolution fusion | flops 7372800 | bytes 983140 | tf_op jit(solution)/shard_map/ij,jpx->ipx/dot_general | solution.py:58
  51.0 0.6 bitcast_subtract_fusion.2
  51.6 0.1 multiply_add_fusion.1
  51.7 0.1 fusion.62
  51.9 1.3 %collective-permute-start.6 = (f32[5,96,1]{2,1,0:T(8,128)S(1)}, f32[5,96,1]{2,1,0:T(8,128)S(1)}, u32[]{:S(2)}, u32[]{:S(2)}) collective-permute-start(f32[5,96,1]{2,1,0:T(8,128)S(1)} %get-tuple-element.67), channel_id=1, source_target_pairs={{1,0},{2,1},{3,2},{5,4},{6,5},{7,6},{9,8},{10,9},{11,10},{13,12},{... | collective-permute-start | bytes 5768 | tf_op jit(solution)/shard_map/ppermute | solution.py:31
  53.2 4.6 %collective-permute-start.7 = (f32[5,96,1]{2,1,0:T(8,128)S(1)}, f32[5,96,1]{2,1,0:T(8,128)S(1)}, u32[]{:S(2)}, u32[]{:S(2)}) collective-permute-start(f32[5,96,1]{2,1,0:T(8,128)S(1)} %get-tuple-element.66), channel_id=1, source_target_pairs={{0,1},{1,2},{2,3},{4,5},{5,6},{6,7},{8,9},{9,10},{10,11},{12,13},{... | collective-permute-start | bytes 5768 | tf_op jit(solution)/shard_map/ppermute | solution.py:30
  57.7 2.0 %convolution_bitcast_fusion.1 = f32[4]{0:T(128)S(1)} fusion(f32[96,256,1]{1,0,2:T(8,128)S(1)} %slice_bitcast_fusion.1, f32[4,96,256]{2,1,0:T(8,128)S(1)} %copy-done.2), kind=kOutput, calls=%fused_computation.1 | convolution fusion | flops 1179648 | bytes 491536 | tf_op jit(solution)/shard_map/mpx,px->m/dot_general | solution.py:63
  59.7 1.8 %collective-permute-done.6 = f32[5,96,1]{2,1,0:T(8,128)S(1)} collective-permute-done((f32[5,96,1]{2,1,0:T(8,128)S(1)}, f32[5,96,1]{2,1,0:T(8,128)S(1)}, u32[]{:S(2)}, u32[]{:S(2)}) %collective-permute-start.6) | collective-permute-done | bytes 1952 | tf_op jit(solution)/shard_map/ppermute | solution.py:31
  61.5 0.0 collective-permute-done.7
  61.5 0.4 subtract_multiply_fusion.3
  62.0 1.0 %fusion.4 = f32[96,256,5]{1,2,0:T(8,128)S(1)} fusion(f32[5,96,256]{2,1,0:T(8,128)S(1)} %get-tuple-element.65, f32[5,5]{1,0:T(8,128)S(1)} %copy-done), kind=kOutput, calls=%fused_computation.8 | convolution fusion | flops 7372800 | bytes 983140 | tf_op jit(solution)/shard_map/ij,jpx->ipx/dot_general | solution.py:59
  63.0 1.0 %fusion.6 = f32[96,256,5]{1,2,0:T(8,128)S(1)} fusion(f32[5,96,256]{2,1,0:T(8,128)S(1)} %get-tuple-element.64, f32[5,5]{1,0:T(8,128)S(1)} %copy-done.3), kind=kOutput, calls=%fused_computation.10 | convolution fusion | flops 7372800 | bytes 983140 | tf_op jit(solution)/shard_map/ij,jpx->ipx/dot_general | solution.py:58
  64.1 0.6 bitcast_subtract_fusion.1
  64.7 0.1 multiply_add_fusion
  64.8 0.1 fusion.61
  64.9 1.3 %collective-permute-start.8 = (f32[5,96,1]{2,1,0:T(8,128)S(1)}, f32[5,96,1]{2,1,0:T(8,128)S(1)}, u32[]{:S(2)}, u32[]{:S(2)}) collective-permute-start(f32[5,96,1]{2,1,0:T(8,128)S(1)} %get-tuple-element.63), channel_id=1, source_target_pairs={{1,0},{2,1},{3,2},{5,4},{6,5},{7,6},{9,8},{10,9},{11,10},{13,12},{... | collective-permute-start | bytes 5768 | tf_op jit(solution)/shard_map/ppermute | solution.py:31
  66.2 2.0 %convolution_bitcast_fusion = f32[4]{0:T(128)S(1)} fusion(f32[96,256,1]{1,0,2:T(8,128)S(1)} %slice_bitcast_fusion, f32[4,96,256]{2,1,0:T(8,128)S(1)} %copy-done.2), kind=kOutput, calls=%fused_computation | convolution fusion | flops 1179648 | bytes 491536 | tf_op jit(solution)/shard_map/mpx,px->m/dot_general | solution.py:63
  68.2 4.9 %collective-permute-start.9 = (f32[5,96,1]{2,1,0:T(8,128)S(1)}, f32[5,96,1]{2,1,0:T(8,128)S(1)}, u32[]{:S(2)}, u32[]{:S(2)}) collective-permute-start(f32[5,96,1]{2,1,0:T(8,128)S(1)} %get-tuple-element.62), channel_id=1, source_target_pairs={{0,1},{1,2},{2,3},{4,5},{5,6},{6,7},{8,9},{9,10},{10,11},{12,13},{... | collective-permute-start | bytes 5768 | tf_op jit(solution)/shard_map/ppermute | solution.py:30
  73.2 11.0 %all-reduce = (f32[4]{0:T(128)S(1)}, f32[4]{0:T(128)S(1)}) all-reduce(f32[4]{0:T(128)S(1)} %convolution_bitcast_fusion.1, f32[4]{0:T(128)S(1)} %convolution_bitcast_fusion), channel_id=1, replica_groups=mesh['blk'=8,'mesh'=4] {'mesh'}, use_global_device_ids=true, to_apply=%region_2.3 | all-reduce | flops 8 | bytes 64 | tf_op jit(solution)/shard_map/psum | solution.py:113
  84.2 0.5 add_bitcast_fusion.1
  84.7 1.0 %fusion.25 = f32[1,96,256]{2,0,1:T(1,128)S(1)} fusion(f32[4,96,256]{2,1,0:T(8,128)S(1)} %copy-done.2, f32[4]{0:T(128)S(1)} %bitcast_add_fusion.2, f32[4]{0:T(128)S(1)} %get-tuple-element.59, f32[1,4]{1,0:T(1,128)S(1)} %copy-done.4, f32[4]{0:T(128)S(1)} %get-tuple-element.54), kind=kOutput, calls=%fused_computation.77 | convolution fusion | flops 1179676 | bytes 491584 | tf_op jit(solution)/shard_map/m,mpx->px/dot_general | solution.py:60
  85.7 0.5 add_bitcast_fusion.2
  86.2 0.0 collective-permute-done.8
  86.2 0.0 collective-permute-done.9
  86.2 0.4 subtract_multiply_fusion.1
  86.6 1.0 %fusion = f32[96,256,5]{1,2,0:T(8,128)S(1)} fusion(f32[5,96,256]{2,1,0:T(8,128)S(1)} %get-tuple-element.61, f32[5,5]{1,0:T(8,128)S(1)} %copy-done), kind=kOutput, calls=%fused_computation.4 | convolution fusion | flops 7372800 | bytes 983140 | tf_op jit(solution)/shard_map/ij,jpx->ipx/dot_general | solution.py:59
  87.7 1.0 %fusion.2 = f32[96,256,5]{1,2,0:T(8,128)S(1)} fusion(f32[5,96,256]{2,1,0:T(8,128)S(1)} %get-tuple-element.60, f32[5,5]{1,0:T(8,128)S(1)} %copy-done.3), kind=kOutput, calls=%fused_computation.6 | convolution fusion | flops 7372800 | bytes 983140 | tf_op jit(solution)/shard_map/ij,jpx->ipx/dot_general | solution.py:58
  88.7 0.6 bitcast_subtract_fusion
  89.4 0.9 add_bitcast_fusion
  (23 shorter events, 0.2 us)
Async XLA Ops:
  0.6 22.8 %copy-start = (f32[5,5]{1,0:T(8,128)S(1)}, f32[5,5]{1,0:T(8,128)}, u32[]{:S(2)}) copy-start(f32[5,5]{1,0:T(8,128)} %param.25) | copy-start | bytes 304
  0.6 19.4 %copy-start.1 = (f32[1,5,96,256]{3,2,1,0:T(8,128)S(1)}, f32[1,5,96,256]{3,2,1,0:T(8,128)}, u32[]{:S(2)}) copy-start(f32[1,5,96,256]{3,2,1,0:T(8,128)} %param.19) | copy-start | bytes 1474564
  0.7 19.4 %copy-start.2 = (f32[4,96,256]{2,1,0:T(8,128)S(1)}, f32[4,96,256]{2,1,0:T(8,128)}, u32[]{:S(2)}) copy-start(f32[4,96,256]{2,1,0:T(8,128)} %param.26) | copy-start | bytes 1179652
  1.9 21.1 %collective-permute-start = (f32[5,96,1]{2,1,0:T(8,128)S(1)}, f32[5,96,1]{2,1,0:T(8,128)S(1)}, u32[]{:S(2)}, u32[]{:S(2)}) collective-permute-start(f32[5,96,1]{2,1,0:T(8,128)S(1)} %get-tuple-element.75), channel_id=1, source_target_pairs={{1,0},{2,1},{3,2},{5,4},{6,5},{7,6},{9,8},{10,9},{11,10},{13,12},{... | collective-permute-start | bytes 5768 | tf_op jit(solution)/shard_map/ppermute | solution.py:31
  3.2 19.8 %collective-permute-start.1 = (f32[5,96,1]{2,1,0:T(8,128)S(1)}, f32[5,96,1]{2,1,0:T(8,128)S(1)}, u32[]{:S(2)}, u32[]{:S(2)}) collective-permute-start(f32[5,96,1]{2,1,0:T(8,128)S(1)} %get-tuple-element.74), channel_id=1, source_target_pairs={{0,1},{1,2},{2,3},{4,5},{5,6},{6,7},{8,9},{9,10},{10,11},{12,13},{... | collective-permute-start | bytes 5768 | tf_op jit(solution)/shard_map/ppermute | solution.py:30
  8.7 14.2 %collective-permute-start.3 = (f32[64,5,256]{2,0,1:T(8,128)}, f32[64,5,256]{2,0,1:T(8,128)S(1)}, u32[]{:S(2)}, u32[]{:S(2)}) collective-permute-start(f32[64,5,256]{2,0,1:T(8,128)} %bitcast.197), channel_id=1, source_target_pairs={{0,4},{4,8},{8,12},{12,16},{16,20},{20,24},{24,28},{28,0},{1,5},{5... | collective-permute-start | bytes 983048 | tf_op jit(solution)/shard_map/ppermute | solution.py:20
  8.8 14.2 %collective-permute-start.2 = (f32[64,5,256]{2,0,1:T(8,128)}, f32[64,5,256]{2,0,1:T(8,128)S(1)}, u32[]{:S(2)}, u32[]{:S(2)}) collective-permute-start(f32[64,5,256]{2,0,1:T(8,128)} %bitcast.198), channel_id=1, source_target_pairs={{0,28},{4,0},{8,4},{12,8},{16,12},{20,16},{24,20},{28,24},{1,29},{... | collective-permute-start | bytes 983048 | tf_op jit(solution)/shard_map/ppermute | solution.py:20
  12.3 0.7 copy-start.7
  16.2 0.7 copy-start.8
  20.1 1.8 %copy-start.5 = (f32[1,4]{1,0:T(1,128)S(1)}, f32[1,4]{1,0:T(1,128)}, u32[]{:S(2)}) copy-start(f32[1,4]{1,0:T(1,128)} %param.29) | copy-start | bytes 52
  23.5 1.1 %copy-start.3 = (f32[5,5]{1,0:T(8,128)S(1)}, f32[5,5]{1,0:T(8,128)}, u32[]{:S(2)}) copy-start(f32[5,5]{1,0:T(8,128)} %param.24) | copy-start | bytes 304
  26.5 21.9 %collective-permute-start.4 = (f32[5,96,1]{2,1,0:T(8,128)S(1)}, f32[5,96,1]{2,1,0:T(8,128)S(1)}, u32[]{:S(2)}, u32[]{:S(2)}) collective-permute-start(f32[5,96,1]{2,1,0:T(8,128)S(1)} %get-tuple-element.71), channel_id=1, source_target_pairs={{1,0},{2,1},{3,2},{5,4},{6,5},{7,6},{9,8},{10,9},{11,10},{13,12},{... | collective-permute-start | bytes 5768 | tf_op jit(solution)/shard_map/ppermute | solution.py:31
  29.8 18.7 %collective-permute-start.5 = (f32[5,96,1]{2,1,0:T(8,128)S(1)}, f32[5,96,1]{2,1,0:T(8,128)S(1)}, u32[]{:S(2)}, u32[]{:S(2)}) collective-permute-start(f32[5,96,1]{2,1,0:T(8,128)S(1)} %get-tuple-element.70), channel_id=1, source_target_pairs={{0,1},{1,2},{2,3},{4,5},{5,6},{6,7},{8,9},{9,10},{10,11},{12,13},{... | collective-permute-start | bytes 5768 | tf_op jit(solution)/shard_map/ppermute | solution.py:30
  45.8 0.7 copy-start.4
  45.8 0.7 copy-start.6
  51.9 9.7 %collective-permute-start.6 = (f32[5,96,1]{2,1,0:T(8,128)S(1)}, f32[5,96,1]{2,1,0:T(8,128)S(1)}, u32[]{:S(2)}, u32[]{:S(2)}) collective-permute-start(f32[5,96,1]{2,1,0:T(8,128)S(1)} %get-tuple-element.67), channel_id=1, source_target_pairs={{1,0},{2,1},{3,2},{5,4},{6,5},{7,6},{9,8},{10,9},{11,10},{13,12},{... | collective-permute-start | bytes 5768 | tf_op jit(solution)/shard_map/ppermute | solution.py:31
  53.2 8.4 %collective-permute-start.7 = (f32[5,96,1]{2,1,0:T(8,128)S(1)}, f32[5,96,1]{2,1,0:T(8,128)S(1)}, u32[]{:S(2)}, u32[]{:S(2)}) collective-permute-start(f32[5,96,1]{2,1,0:T(8,128)S(1)} %get-tuple-element.66), channel_id=1, source_target_pairs={{0,1},{1,2},{2,3},{4,5},{5,6},{6,7},{8,9},{9,10},{10,11},{12,13},{... | collective-permute-start | bytes 5768 | tf_op jit(solution)/shard_map/ppermute | solution.py:30
  64.9 21.2 %collective-permute-start.8 = (f32[5,96,1]{2,1,0:T(8,128)S(1)}, f32[5,96,1]{2,1,0:T(8,128)S(1)}, u32[]{:S(2)}, u32[]{:S(2)}) collective-permute-start(f32[5,96,1]{2,1,0:T(8,128)S(1)} %get-tuple-element.63), channel_id=1, source_target_pairs={{1,0},{2,1},{3,2},{5,4},{6,5},{7,6},{9,8},{10,9},{11,10},{13,12},{... | collective-permute-start | bytes 5768 | tf_op jit(solution)/shard_map/ppermute | solution.py:31
  68.2 18.0 %collective-permute-start.9 = (f32[5,96,1]{2,1,0:T(8,128)S(1)}, f32[5,96,1]{2,1,0:T(8,128)S(1)}, u32[]{:S(2)}, u32[]{:S(2)}) collective-permute-start(f32[5,96,1]{2,1,0:T(8,128)S(1)} %get-tuple-element.62), channel_id=1, source_target_pairs={{0,1},{1,2},{2,3},{4,5},{5,6},{6,7},{8,9},{9,10},{10,11},{12,13},{... | collective-permute-start | bytes 5768 | tf_op jit(solution)/shard_map/ppermute | solution.py:30
where the time goes:
time: 90.7 us; the launch traced here: 90.3 us
  starting transfers between devices  29.2 us (32%)
  blocking collectives  21.5 us (24%)
  matrix products  20 us (22%)
  other arithmetic  6.47 us (7%)
  between operations  6.36 us (7%)
  local copies, waits for them, and re-layouts  4.88 us (5%)
  waiting for transfers between devices  1.83 us (2%)
    psum x2, blocking collectives, evaluate(): total = lax.psum(partial_value, 'mesh')  21.5 us
    ppermute x4, starting transfers between devices, padded(): before = lax.ppermute(last, axis, up)  20.4 us
    dot_general x4, matrix products, rates_from(): jnp.einsum('mpx,px->m', mode_shape, flow_state[4], precision=PRECISE)  7.76 us
    ppermute x4, starting transfers between devices, padded(): after = lax.ppermute(initial, axis, down)  5.17 us
    dot_general x4, matrix products, rates_from(): jnp.einsum('ij,jpx->ipx', axial_jacobian, grad_axial, precision=PRECISE)  4.19 us
    dot_general x4, matrix products, rates_from(): jnp.einsum('ij,jpx->ipx', pitch_jacobian, grad_pitch, precision=PRECISE)  4.19 us
    dot_general x4, matrix products, rates_from(): jnp.einsum('m,mpx->px', modal_velocity, mode_shape, precision=PRECISE)  3.86 us
    ppermute x2, starting transfers between devices, shifted(): lax.ppermute(value, axis, [(i, (i + by) % peers) for i in range(peers)])  3.59 us
  transfers between devices with their start and end apart: 10, of which 1 were waited for; matrix products, arithmetic and copies ran while one was open for 15% of the time, Pallas kernels for 0%

commit v1 on v0

v1 whole, which is shorter than its diff:
```python
import math

import jax
import jax.numpy as jnp
from jax import lax
from jax.sharding import PartitionSpec as P

STEP_COUNT = 2


PRECISE = lax.Precision.HIGHEST
TIME_STEP = 0.4
DIFFUSION = 0.1
COUPLING = 0.3
DAMPING = 0.1


def shifted(value, axis, by):
    peers = lax.axis_size(axis)
    return lax.ppermute(value, axis, [(i, (i + by) % peers) for i in range(peers)])


def halo(value):
    peers = lax.axis_size("mesh")
    up = [(i, i + 1) for i in range(peers - 1)]
    down = [(i + 1, i) for i in range(peers - 1)]
    before = lax.ppermute(value[..., -1:], "mesh", up)
    after = lax.ppermute(value[..., :1], "mesh", down)
    return before, after


def axial_pad(value, before, after):
    return jnp.concatenate([before, value, after], axis=-1)


def pitch_pad(value, lower, upper):
    return jnp.concatenate([lower[:, None, :], value, upper[:, None, :]], axis=1)


def flow_rate(state, before, after, lower_ghost, upper_ghost, axial_jacobian, pitch_jacobian):
    padded_axial = axial_pad(state, before, after)
    padded_pitch = pitch_pad(state, lower_ghost, upper_ghost)
    grad_axial = 0.5 * (padded_axial[:, :, 2:] - padded_axial[:, :, :-2])
    grad_pitch = 0.5 * (padded_pitch[:, 2:, :] - padded_pitch[:, :-2, :])
    laplacian = (
        padded_axial[:, :, 2:]
        + padded_axial[:, :, :-2]
        + padded_pitch[:, 2:, :]
        + padded_pitch[:, :-2, :]
        - 4.0 * state
    )
    flux = jnp.einsum("ij,jpx->ipx", axial_jacobian, grad_axial, precision=PRECISE)
    flux = flux + jnp.einsum("ij,jpx->ipx", pitch_jacobian, grad_pitch, precision=PRECISE)
    return DIFFUSION * laplacian - flux


def single_field_grads(field, before, after):
    padded_axial = jnp.concatenate([before, field, after], axis=-1)
    zero_row = jnp.zeros_like(field[..., :1, :])
    padded_pitch = jnp.concatenate([zero_row, field, zero_row], axis=-2)
    grad_axial = 0.5 * (padded_axial[..., 2:] - padded_axial[..., :-2])
    grad_pitch = 0.5 * (padded_pitch[..., 2:, :] - padded_pitch[..., :-2, :])
    laplacian = (
        padded_axial[..., 2:]
        + padded_axial[..., :-2]
        + padded_pitch[..., 2:, :]
        + padded_pitch[..., :-2, :]
        - 4.0 * field
    )
    return grad_axial, grad_pitch, laplacian


def modal_field(weights, mode_shape):
    return jnp.einsum("m,mpx->px", weights, mode_shape, precision=PRECISE)


def projection(mode_shape, field):
    return jnp.einsum("mpx,px->m", mode_shape, field, precision=PRECISE)


def add_field_one(rate, extra):
    return rate.at[1].add(extra)


def on_device(
    flow_field,
    lower_row_history,
    upper_row_history,
    lower_lag_slot,
    upper_lag_slot,
    axial_jacobian,
    pitch_jacobian,
    mode_shape,
    stiffness,
    displacement,
    velocity,
):
    h = TIME_STEP
    state0 = flow_field[0]
    fields = state0.shape[0]
    pitch_cells = state0.shape[1]
    axial_cells = state0.shape[2]
    modes = mode_shape.shape[0]
    force_scale = 1.0 / math.sqrt(pitch_cells * axial_cells * lax.axis_size("mesh"))
    passages = lax.axis_size("blk")
    position = lax.axis_index("blk")
    slot_count = lower_row_history.shape[1]
    blade_stiffness = stiffness[0]
    disp0 = displacement[0]
    vel0 = velocity[0]

    after_me = (position + 1) % passages
    before_me = (position + passages - 1) % passages
    slot_next = lax.dynamic_index_in_dim(lower_lag_slot, after_me, 0, keepdims=False)
    slot_prev = lax.dynamic_index_in_dim(upper_lag_slot, before_me, 0, keepdims=False)
    rows_up = jnp.stack(
        [
            lax.dynamic_index_in_dim(
                upper_row_history[0], (slot_next + s) % slot_count, 0, keepdims=False
            )
            for s in range(STEP_COUNT)
        ]
    )
    rows_down = jnp.stack(
        [
            lax.dynamic_index_in_dim(
                lower_row_history[0], (slot_prev + s) % slot_count, 0, keepdims=False
            )
            for s in range(STEP_COUNT)
        ]
    )
    lower_ghosts = shifted(rows_up, "blk", 1)
    upper_ghosts = shifted(rows_down, "blk", -1)

    both_before, both_after = halo(jnp.concatenate([state0, mode_shape], axis=0))
    state0_before, mode_before = both_before[:fields], both_before[fields:]
    state0_after, mode_after = both_after[:fields], both_after[fields:]

    ax_col = axial_jacobian[:, 1]
    pt_col = pitch_jacobian[:, 1]

    def zero_ghost_rate_one(weights):
        field = modal_field(weights, mode_shape)
        f_before = modal_field(weights, mode_before)
        f_after = modal_field(weights, mode_after)
        ga, gp, lap = single_field_grads(field, f_before, f_after)
        rate = -(ax_col[:, None, None] * ga[None] + pt_col[:, None, None] * gp[None])
        return add_field_one(rate, DIFFUSION * lap)

    ms_ga, ms_gp, _ = single_field_grads(mode_shape, mode_before, mode_after)
    grad_a_sum = jnp.einsum("mpx,npx->mn", mode_shape, ms_ga, precision=PRECISE)
    grad_p_sum = jnp.einsum("mpx,npx->mn", mode_shape, ms_gp, precision=PRECISE)
    coupling_sum = -(axial_jacobian[4, 1] * grad_a_sum + pitch_jacobian[4, 1] * grad_p_sum)

    gl1, gu1 = lower_ghosts[0], upper_ghosts[0]
    gl2, gu2 = lower_ghosts[1], upper_ghosts[1]
    push0 = COUPLING * modal_field(vel0, mode_shape)
    rate1 = add_field_one(
        flow_rate(state0, state0_before, state0_after, gl1, gu1, axial_jacobian, pitch_jacobian),
        push0,
    )
    mid1 = state0 + h * rate1
    m_before, m_after = halo(mid1)
    rate1b = add_field_one(
        flow_rate(mid1, m_before, m_after, gl1, gu1, axial_jacobian, pitch_jacobian), push0
    )
    base1 = state0 + 0.5 * h * (rate1 + rate1b)
    b_before, b_after = halo(base1)
    rate2_base = flow_rate(base1, b_before, b_after, gl2, gu2, axial_jacobian, pitch_jacobian)

    partials = jnp.concatenate(
        [
            projection(mode_shape, state0[4]),
            projection(mode_shape, mid1[4]),
            projection(mode_shape, base1[4]),
            projection(mode_shape, rate2_base[4]),
            coupling_sum.reshape(-1),
        ]
    )
    totals = lax.psum(partials, "mesh")
    force0 = force_scale * totals[0:modes]
    force1 = force_scale * totals[modes : 2 * modes]
    force2 = force_scale * totals[2 * modes : 3 * modes]
    force3 = force_scale * totals[3 * modes : 4 * modes]
    couple = force_scale * totals[4 * modes :].reshape(modes, modes)

    acc1 = force0 - blade_stiffness * disp0 - DAMPING * vel0
    disp1m = disp0 + h * vel0
    vel1m = vel0 + h * acc1
    acc1m = force1 - blade_stiffness * disp1m - DAMPING * vel1m
    disp1 = disp0 + 0.5 * h * (vel0 + vel1m)
    vel1 = vel0 + 0.5 * h * (acc1 + acc1m)

    acc2 = force2 - blade_stiffness * disp1 - DAMPING * vel1
    disp2m = disp1 + h * vel1
    vel2m = vel1 + h * acc2
    force2m = force2 + h * force3 + h * (0.5 * h * h * COUPLING) * (couple @ acc1)
    acc2m = force2m - blade_stiffness * disp2m - DAMPING * vel2m
    disp2 = disp1 + 0.5 * h * (vel1 + vel2m)
    vel2 = vel1 + 0.5 * h * (acc2 + acc2m)

    corr = 0.5 * h * h * COUPLING
    state1 = add_field_one(base1, corr * modal_field(acc1, mode_shape))
    rate2 = rate2_base + corr * zero_ghost_rate_one(acc1)
    rate2 = add_field_one(rate2, COUPLING * modal_field(vel1, mode_shape))
    mid2 = state1 + h * rate2
    m2_before, m2_after = halo(mid2)
    rate2b = add_field_one(
        flow_rate(mid2, m2_before, m2_after, gl2, gu2, axial_jacobian, pitch_jacobian),
        COUPLING * modal_field(vel2m, mode_shape),
    )
    state2 = state1 + 0.5 * h * (rate2 + rate2b)
    return (state2[None], disp2[None], vel2[None])


def solution(mesh):
    return jax.shard_map(
        on_device,
        mesh=mesh,
        in_specs=(
            P("blk", None, None, "mesh"),
            P("blk", None, None, "mesh"),
            P("blk", None, None, "mesh"),
            P(),
            P(),
            P(),
            P(),
            P(None, None, "mesh"),
            P("blk", None),
            P("blk", None),
            P("blk", None),
        ),
        out_specs=(P("blk", None, None, "mesh"), P("blk", None), P("blk", None)),
        check_vma=False,
    )
```

time: 90.7 us -> 112 us (1.23)
  waiting for transfers between devices: 1.83 us -> 31.8 us
  blocking collectives: 21.5 us -> 8.38 us
  starting transfers between devices: 29.2 us -> 22.1 us
  matrix products: 20 us -> 26.6 us
  local copies, waits for them, and re-layouts: 4.88 us -> 7.32 us
  other arithmetic: 6.47 us -> 8.4 us
    ppermute x8, waiting for transfers between devices: 1.82 us -> 31.8 us  [the longest x4 27.3 us: halo(): after = lax.ppermute(value[..., :1], 'mesh', down)]
    psum x2 -> x1, blocking collectives: 21.5 us -> 8.38 us  [on_device(): totals = lax.psum(partials, 'mesh')]
    ppermute x8, starting transfers between devices: 25.6 us -> 17.5 us  [the longest x4 12.2 us: halo(): before = lax.ppermute(value[..., -1:], 'mesh', up)]
    dot_general x16 -> x21, matrix products: 20 us -> 26.6 us  [the longest x4 7.66 us: projection(): return jnp.einsum('mpx,px->m', mode_shape, field, precision=PRECISE)]
    dynamic_slice x2 -> x4, local copies, waits for them, and re-layouts: 1.16 us -> 2.9 us  [the longest x1 0.87 us: on_device(): lax.dynamic_index_in_dim(upper_row_history[0], (slot_next + s) % slot_cou...]
    concatenate x0 -> x1, other arithmetic: none -> 1.51 us  [on_device(): jnp.concatenate([state0, mode_shape], axis=0)]
    mul x4 -> x7, other arithmetic: 1.72 us -> 2.3 us  [the longest x4 1.74 us: flow_rate(): grad_axial = 0.5 * (padded_axial[:, :, 2:] - padded_axial[:, :, :-2])]
  transfers between devices with their start and end apart: 10 -> 10, of which waited for: 1 -> 8; matrix products, arithmetic and copies ran while one was open for 15% -> 16% of each run, Pallas kernels for 0% -> 0%
where the time goes in v1:
time: 112 us; the launch traced here: 111 us
  waiting for transfers between devices  31.8 us (28%)
  matrix products  26.6 us (24%)
  starting transfers between devices  22.1 us (20%)
  other arithmetic  8.4 us (8%)
  blocking collectives  8.38 us (7%)
  local copies, waits for them, and re-layouts  7.32 us (7%)
  between operations  6.37 us (6%)
    ppermute x4, waiting for transfers between devices, halo(): after = lax.ppermute(value[..., :1], 'mesh', down)  27.3 us
    ppermute x4, starting transfers between devices, halo(): before = lax.ppermute(value[..., -1:], 'mesh', up)  12.2 us
    psum x1, blocking collectives, on_device(): totals = lax.psum(partials, 'mesh')  8.38 us
    dot_general x4, matrix products, projection(): return jnp.einsum('mpx,px->m', mode_shape, field, precision=PRECISE)  7.66 us
    ppermute x4, starting transfers between devices, halo(): after = lax.ppermute(value[..., :1], 'mesh', down)  5.35 us
    ppermute x2, starting transfers between devices, shifted(): lax.ppermute(value, axis, [(i, (i + by) % peers) for i in range(peers)])  4.57 us
    ppermute x4, waiting for transfers between devices, halo(): before = lax.ppermute(value[..., -1:], 'mesh', up)  4.47 us
    dot_general x6, matrix products, modal_field(): return jnp.einsum('m,mpx->px', weights, mode_shape, precision=PRECISE)  4.38 us
  transfers between devices with their start and end apart: 10, of which 8 were waited for; matrix products, arithmetic and copies ran while one was open for 16% of the time, Pallas kernels for 0%

profile of v1, /device:TPU:0, one launch (start us, length us, event | category | flops | bytes accessed | tf_op | source)
XLA Modules:
  0.0 111.0 jit_solution(107647380731222191)
XLA Ops:
  0.7 0.6 copy-done.7
  1.3 0.6 dynamic_slice.33
  4.5 0.9 dynamic-slice_bitcast_fusion.1
  5.4 0.5 collective-permute-start.3
  5.9 0.7 copy-done.8
  6.6 0.6 dynamic_slice.28
  9.8 0.9 dynamic-slice_bitcast_fusion.3
  10.7 4.1 %collective-permute-start.2 = (f32[2,5,256]{2,0,1:T(2,128)S(1)}, f32[2,5,256]{2,0,1:T(2,128)S(1)}, u32[]{:S(2)}, u32[]{:S(2)}) collective-permute-start(f32[2,5,256]{2,0,1:T(2,128)S(1)} %pad_maximum_fusion.21), channel_id=1, source_target_pairs={{0,28},{4,0},{8,4},{12,8},{16,12},{20,16},{24,20},{28,24},{1,29},{... | collective-permute-start | bytes 30728 | tf_op jit(solution)/shard_map/ppermute | solution.py:20
  14.7 1.5 %pad_maximum_fusion.16 = (f32[9,96,1]{2,1,0:T(8,128)S(1)}, f32[9,96,1]{2,1,0:T(8,128)S(1)}) fusion(f32[4,96,256]{2,1,0:T(8,128)} %param.30, f32[5,96,256]{2,1,0:T(8,128)} %bitcast.249), kind=kLoop, calls=%fused_computation.79 | loop fusion | flops 1728 | bytes 891648 | tf_op jit(solution)/shard_map/concatenate | solution.py:135
  16.2 3.9 %collective-permute-start.1 = (f32[9,96,1]{2,1,0:T(8,128)S(1)}, f32[9,96,1]{2,1,0:T(8,128)S(1)}, u32[]{:S(2)}, u32[]{:S(2)}) collective-permute-start(f32[9,96,1]{2,1,0:T(8,128)S(1)} %get-tuple-element.85), channel_id=1, source_target_pairs={{0,1},{1,2},{2,3},{4,5},{5,6},{6,7},{8,9},{9,10},{10,11},{12,13},{... | collective-permute-start | bytes 10376 | tf_op jit(solution)/shard_map/ppermute | solution.py:27
  20.2 1.3 %collective-permute-start = (f32[9,96,1]{2,1,0:T(8,128)S(1)}, f32[9,96,1]{2,1,0:T(8,128)S(1)}, u32[]{:S(2)}, u32[]{:S(2)}) collective-permute-start(f32[9,96,1]{2,1,0:T(8,128)S(1)} %get-tuple-element.86), channel_id=1, source_target_pairs={{1,0},{2,1},{3,2},{5,4},{6,5},{7,6},{9,8},{10,9},{11,10},{13,12},{... | collective-permute-start | bytes 10376 | tf_op jit(solution)/shard_map/ppermute | solution.py:28
  21.6 1.0 fusion.54
  22.5 1.8 %convolution_bitcast_fusion.8 = f32[4]{0:T(128)S(1)} fusion(f32[96,256,1]{1,0,2:T(8,128)S(1)} %slice_bitcast_fusion.3, f32[4,96,256]{2,1,0:T(8,128)S(1)} %copy-done), kind=kOutput, calls=%fused_computation.13 | convolution fusion | flops 1179648 | bytes 491536 | tf_op jit(solution)/shard_map/mpx,px->m/dot_general | solution.py:78
  24.4 0.2 slice_reduce_fusion
  24.6 0.6 slice.380
  25.2 0.6 slice.375
  25.8 2.0 %collective-permute-done.1 = f32[9,96,1]{2,1,0:T(8,128)S(1)} collective-permute-done((f32[9,96,1]{2,1,0:T(8,128)S(1)}, f32[9,96,1]{2,1,0:T(8,128)S(1)}, u32[]{:S(2)}, u32[]{:S(2)}) %collective-permute-start.1) | collective-permute-done | bytes 3488 | tf_op jit(solution)/shard_map/ppermute | solution.py:27
  28.0 11.3 %collective-permute-done = f32[9,96,1]{2,1,0:T(8,128)S(1)} collective-permute-done((f32[9,96,1]{2,1,0:T(8,128)S(1)}, f32[9,96,1]{2,1,0:T(8,128)S(1)}, u32[]{:S(2)}, u32[]{:S(2)}) %collective-permute-start) | collective-permute-done | bytes 3488 | tf_op jit(solution)/shard_map/ppermute | solution.py:28
  39.2 0.1 slice_reduce_fusion.3
  39.4 0.3 fusion.31
  39.7 2.8 %fusion.4 = f32[4,4]{1,0:T(4,128)S(1)} fusion(f32[4,96,256]{2,1,0:T(8,128)S(1)} %get-tuple-element.106, f32[]{:T(128)} %bitcast.32, f32[4,96,256]{2,1,0:T(8,128)S(1)} %copy-done), kind=kOutput, calls=%fused_computation.8 | convolution fusion | flops 4718608 | bytes 786500 | tf_op jit(solution)/shard_map/mpx,npx->mn/dot_general | solution.py:151
  42.5 2.8 %fusion.3 = f32[4,4]{0,1:T(4,128)S(1)} fusion(f32[4,4]{1,0:T(4,128)S(1)} %fusion.4, f32[4,96,256]{2,1,0:T(8,128)S(1)} %get-tuple-element.105, f32[]{:T(128)} %bitcast.34, f32[4,96,256]{2,1,0:T(8,128)S(1)} %copy-done), kind=kOutput, calls=%fused_computation.6 | convolution fusion | flops 4718640 | bytes 786564 | tf_op jit(solution)/shard_map/mpx,npx->mn/dot_general | solution.py:152
  45.6 0.4 subtract_multiply_fusion.7
  46.0 1.0 fusion.27
  47.1 1.0 fusion.25
  48.1 0.6 bitcast_subtract_fusion.3
  49.0 3.4 %collective-permute-start.5 = (f32[5,96,1]{2,1,0:T(8,128)S(1)}, f32[5,96,1]{2,1,0:T(8,128)S(1)}, u32[]{:S(2)}, u32[]{:S(2)}) collective-permute-start(f32[5,96,1]{2,1,0:T(8,128)S(1)} %get-tuple-element.97), channel_id=1, source_target_pairs={{0,1},{1,2},{2,3},{4,5},{5,6},{6,7},{8,9},{9,10},{10,11},{12,13},{... | collective-permute-start | bytes 5768 | tf_op jit(solution)/shard_map/ppermute | solution.py:27
  52.4 1.5 %collective-permute-start.4 = (f32[5,96,1]{2,1,0:T(8,128)S(1)}, f32[5,96,1]{2,1,0:T(8,128)S(1)}, u32[]{:S(2)}, u32[]{:S(2)}) collective-permute-start(f32[5,96,1]{2,1,0:T(8,128)S(1)} %get-tuple-element.98), channel_id=1, source_target_pairs={{1,0},{2,1},{3,2},{5,4},{6,5},{7,6},{9,8},{10,9},{11,10},{13,12},{... | collective-permute-start | bytes 5768 | tf_op jit(solution)/shard_map/ppermute | solution.py:28
  53.9 1.9 %convolution_bitcast_fusion.7 = f32[4]{0:T(128)S(1)} fusion(f32[96,256,1]{1,0,2:T(8,128)S(1)} %slice_bitcast_fusion.2, f32[4,96,256]{2,1,0:T(8,128)S(1)} %copy-done), kind=kOutput, calls=%fused_computation.12 | convolution fusion | flops 1179648 | bytes 491536 | tf_op jit(solution)/shard_map/mpx,px->m/dot_general | solution.py:78
  55.8 0.3 collective-permute-done.5
  56.1 5.6 %collective-permute-done.4 = f32[5,96,1]{2,1,0:T(8,128)S(1)} collective-permute-done((f32[5,96,1]{2,1,0:T(8,128)S(1)}, f32[5,96,1]{2,1,0:T(8,128)S(1)}, u32[]{:S(2)}, u32[]{:S(2)}) %collective-permute-start.4) | collective-permute-done | bytes 1952 | tf_op jit(solution)/shard_map/ppermute | solution.py:28
  61.7 0.4 subtract_multiply_fusion.5
  62.1 1.0 fusion.23
  63.2 1.0 fusion.21
  64.2 0.6 bitcast_subtract_fusion.2
  65.1 1.7 %collective-permute-start.7 = (f32[5,96,1]{2,1,0:T(8,128)S(1)}, f32[5,96,1]{2,1,0:T(8,128)S(1)}, u32[]{:S(2)}, u32[]{:S(2)}) collective-permute-start(f32[5,96,1]{2,1,0:T(8,128)S(1)} %get-tuple-element.93), channel_id=1, source_target_pairs={{0,1},{1,2},{2,3},{4,5},{5,6},{6,7},{8,9},{9,10},{10,11},{12,13},{... | collective-permute-start | bytes 5768 | tf_op jit(solution)/shard_map/ppermute | solution.py:27
  66.8 1.3 %collective-permute-start.6 = (f32[5,96,1]{2,1,0:T(8,128)S(1)}, f32[5,96,1]{2,1,0:T(8,128)S(1)}, u32[]{:S(2)}, u32[]{:S(2)}) collective-permute-start(f32[5,96,1]{2,1,0:T(8,128)S(1)} %get-tuple-element.94), channel_id=1, source_target_pairs={{1,0},{2,1},{3,2},{5,4},{6,5},{7,6},{9,8},{10,9},{11,10},{13,12},{... | collective-permute-start | bytes 5768 | tf_op jit(solution)/shard_map/ppermute | solution.py:28
  68.1 1.9 %convolution_bitcast_fusion.6 = f32[4]{0:T(128)S(1)} fusion(f32[96,256,1]{1,0,2:T(8,128)S(1)} %slice_bitcast_fusion.1, f32[4,96,256]{2,1,0:T(8,128)S(1)} %copy-done), kind=kOutput, calls=%fused_computation.11 | convolution fusion | flops 1179648 | bytes 491536 | tf_op jit(solution)/shard_map/mpx,px->m/dot_general | solution.py:78
  70.0 0.4 collective-permute-done.7
  70.4 5.6 %collective-permute-done.6 = f32[5,96,1]{2,1,0:T(8,128)S(1)} collective-permute-done((f32[5,96,1]{2,1,0:T(8,128)S(1)}, f32[5,96,1]{2,1,0:T(8,128)S(1)}, u32[]{:S(2)}, u32[]{:S(2)}) %collective-permute-start.6) | collective-permute-done | bytes 1952 | tf_op jit(solution)/shard_map/ppermute | solution.py:28
  76.0 0.4 subtract_multiply_fusion.3
  76.5 1.0 fusion.19
  77.5 1.0 fusion.17
  78.6 0.6 bitcast_subtract_fusion.1
  79.2 1.9 %convolution_bitcast_fusion.5 = f32[4]{0:T(128)S(1)} fusion(f32[96,256,1]{1,0,2:T(8,128)S(1)} %slice_bitcast_fusion, f32[4,96,256]{2,1,0:T(8,128)S(1)} %copy-done), kind=kOutput, calls=%fused_computation.10 | convolution fusion | flops 1179648 | bytes 491536 | tf_op jit(solution)/shard_map/mpx,px->m/dot_general | solution.py:78
  81.2 8.4 %psum.7 = f32[32]{0:T(128)S(1)} all-reduce(f32[32]{0:T(128)S(1)} %concatenate.119), channel_id=1, replica_groups=mesh['blk'=8,'mesh'=4] {'mesh'}, use_global_device_ids=true, to_apply=%region_0.1 | all-reduce | flops 32 | bytes 256 | tf_op jit(solution)/shard_map/psum | solution.py:180
  89.7 0.6 copy-done.5
  90.3 0.6 add_bitcast_fusion.1
  90.9 1.0 fusion.63
  91.9 0.3 convolution_bitcast_fusion
  92.2 0.3 convolution_bitcast_fusion.1
  92.5 1.0 fusion.58
  93.4 1.0 fusion.56
  94.7 0.1 fusion.38
  95.2 3.2 %collective-permute-start.9 = (f32[5,96,1]{2,1,0:T(8,128)S(1)}, f32[5,96,1]{2,1,0:T(8,128)S(1)}, u32[]{:S(2)}, u32[]{:S(2)}) collective-permute-start(f32[5,96,1]{2,1,0:T(8,128)S(1)} %get-tuple-element.89), channel_id=1, source_target_pairs={{0,1},{1,2},{2,3},{4,5},{5,6},{6,7},{8,9},{9,10},{10,11},{12,13},{... | collective-permute-start | bytes 5768 | tf_op jit(solution)/shard_map/ppermute | solution.py:27
  98.3 1.3 %collective-permute-start.8 = (f32[5,96,1]{2,1,0:T(8,128)S(1)}, f32[5,96,1]{2,1,0:T(8,128)S(1)}, u32[]{:S(2)}, u32[]{:S(2)}) collective-permute-start(f32[5,96,1]{2,1,0:T(8,128)S(1)} %get-tuple-element.90), channel_id=1, source_target_pairs={{1,0},{2,1},{3,2},{5,4},{6,5},{7,6},{9,8},{10,9},{11,10},{13,12},{... | collective-permute-start | bytes 5768 | tf_op jit(solution)/shard_map/ppermute | solution.py:28
  99.6 0.6 fusion.12
  100.3 1.7 %collective-permute-done.9 = f32[5,96,1]{2,1,0:T(8,128)S(1)} collective-permute-done((f32[5,96,1]{2,1,0:T(8,128)S(1)}, f32[5,96,1]{2,1,0:T(8,128)S(1)}, u32[]{:S(2)}, u32[]{:S(2)}) %collective-permute-start.9) | collective-permute-done | bytes 1952 | tf_op jit(solution)/shard_map/ppermute | solution.py:27
  102.0 4.9 %collective-permute-done.8 = f32[5,96,1]{2,1,0:T(8,128)S(1)} collective-permute-done((f32[5,96,1]{2,1,0:T(8,128)S(1)}, f32[5,96,1]{2,1,0:T(8,128)S(1)}, u32[]{:S(2)}, u32[]{:S(2)}) %collective-permute-start.8) | collective-permute-done | bytes 1952 | tf_op jit(solution)/shard_map/ppermute | solution.py:28
  106.9 0.4 subtract_multiply_fusion.1
  107.4 1.0 fusion.15
  108.4 1.0 fusion.13
  109.5 0.6 bitcast_subtract_fusion
  110.1 0.9 add_bitcast_fusion
  (47 shorter events, 1.9 us)
Async XLA Ops:
  0.6 0.7 copy-start.7
  5.4 40.1 %collective-permute-start.3 = (f32[2,5,256]{2,0,1:T(2,128)S(1)}, f32[2,5,256]{2,0,1:T(2,128)S(1)}, u32[]{:S(2)}, u32[]{:S(2)}) collective-permute-start(f32[2,5,256]{2,0,1:T(2,128)S(1)} %pad_maximum_fusion.22), channel_id=1, source_target_pairs={{0,4},{4,8},{8,12},{12,16},{16,20},{20,24},{24,28},{28,0},{1,5},{5... | collective-permute-start | bytes 30728 | tf_op jit(solution)/shard_map/ppermute | solution.py:20
  5.9 0.7 copy-start.8
  10.7 34.9 %collective-permute-start.2 = (f32[2,5,256]{2,0,1:T(2,128)S(1)}, f32[2,5,256]{2,0,1:T(2,128)S(1)}, u32[]{:S(2)}, u32[]{:S(2)}) collective-permute-start(f32[2,5,256]{2,0,1:T(2,128)S(1)} %pad_maximum_fusion.21), channel_id=1, source_target_pairs={{0,28},{4,0},{8,4},{12,8},{16,12},{20,16},{24,20},{28,24},{1,29},{... | collective-permute-start | bytes 30728 | tf_op jit(solution)/shard_map/ppermute | solution.py:20
  14.7 6.8 %copy-start.1 = (f32[1,5,96,256]{3,2,1,0:T(8,128)S(1)}, f32[1,5,96,256]{3,2,1,0:T(8,128)}, u32[]{:S(2)}) copy-start(f32[1,5,96,256]{3,2,1,0:T(8,128)} %param.23) | copy-start | bytes 1474564
  14.7 6.8 %copy-start = (f32[4,96,256]{2,1,0:T(8,128)S(1)}, f32[4,96,256]{2,1,0:T(8,128)}, u32[]{:S(2)}) copy-start(f32[4,96,256]{2,1,0:T(8,128)} %param.30) | copy-start | bytes 1179652
  16.2 11.6 %collective-permute-start.1 = (f32[9,96,1]{2,1,0:T(8,128)S(1)}, f32[9,96,1]{2,1,0:T(8,128)S(1)}, u32[]{:S(2)}, u32[]{:S(2)}) collective-permute-start(f32[9,96,1]{2,1,0:T(8,128)S(1)} %get-tuple-element.85), channel_id=1, source_target_pairs={{0,1},{1,2},{2,3},{4,5},{5,6},{6,7},{8,9},{9,10},{10,11},{12,13},{... | collective-permute-start | bytes 10376 | tf_op jit(solution)/shard_map/ppermute | solution.py:27
  20.2 1.4 %copy-start.4 = (f32[1,4]{1,0:T(1,128)S(1)}, f32[1,4]{1,0:T(1,128)}, u32[]{:S(2)}) copy-start(f32[1,4]{1,0:T(1,128)} %param.33) | copy-start | bytes 52
  20.2 19.0 %collective-permute-start = (f32[9,96,1]{2,1,0:T(8,128)S(1)}, f32[9,96,1]{2,1,0:T(8,128)S(1)}, u32[]{:S(2)}, u32[]{:S(2)}) collective-permute-start(f32[9,96,1]{2,1,0:T(8,128)S(1)} %get-tuple-element.86), channel_id=1, source_target_pairs={{1,0},{2,1},{3,2},{5,4},{6,5},{7,6},{9,8},{10,9},{11,10},{13,12},{... | collective-permute-start | bytes 10376 | tf_op jit(solution)/shard_map/ppermute | solution.py:28
  22.5 1.9 %copy-start.2 = (f32[5,5]{1,0:T(8,128)S(1)}, f32[5,5]{1,0:T(8,128)}, u32[]{:S(2)}) copy-start(f32[5,5]{1,0:T(8,128)} %param.28) | copy-start | bytes 304
  22.5 1.8 %copy-start.3 = (f32[5,5]{1,0:T(8,128)S(1)}, f32[5,5]{1,0:T(8,128)}, u32[]{:S(2)}) copy-start(f32[5,5]{1,0:T(8,128)} %param.29) | copy-start | bytes 304
  49.0 7.1 %collective-permute-start.5 = (f32[5,96,1]{2,1,0:T(8,128)S(1)}, f32[5,96,1]{2,1,0:T(8,128)S(1)}, u32[]{:S(2)}, u32[]{:S(2)}) collective-permute-start(f32[5,96,1]{2,1,0:T(8,128)S(1)} %get-tuple-element.97), channel_id=1, source_target_pairs={{0,1},{1,2},{2,3},{4,5},{5,6},{6,7},{8,9},{9,10},{10,11},{12,13},{... | collective-permute-start | bytes 5768 | tf_op jit(solution)/shard_map/ppermute | solution.py:27
  52.4 9.3 %collective-permute-start.4 = (f32[5,96,1]{2,1,0:T(8,128)S(1)}, f32[5,96,1]{2,1,0:T(8,128)S(1)}, u32[]{:S(2)}, u32[]{:S(2)}) collective-permute-start(f32[5,96,1]{2,1,0:T(8,128)S(1)} %get-tuple-element.98), channel_id=1, source_target_pairs={{1,0},{2,1},{3,2},{5,4},{6,5},{7,6},{9,8},{10,9},{11,10},{13,12},{... | collective-permute-start | bytes 5768 | tf_op jit(solution)/shard_map/ppermute | solution.py:28
  65.1 5.3 %collective-permute-start.7 = (f32[5,96,1]{2,1,0:T(8,128)S(1)}, f32[5,96,1]{2,1,0:T(8,128)S(1)}, u32[]{:S(2)}, u32[]{:S(2)}) collective-permute-start(f32[5,96,1]{2,1,0:T(8,128)S(1)} %get-tuple-element.93), channel_id=1, source_target_pairs={{0,1},{1,2},{2,3},{4,5},{5,6},{6,7},{8,9},{9,10},{10,11},{12,13},{... | collective-permute-start | bytes 5768 | tf_op jit(solution)/shard_map/ppermute | solution.py:27
  66.8 9.3 %collective-permute-start.6 = (f32[5,96,1]{2,1,0:T(8,128)S(1)}, f32[5,96,1]{2,1,0:T(8,128)S(1)}, u32[]{:S(2)}, u32[]{:S(2)}) collective-permute-start(f32[5,96,1]{2,1,0:T(8,128)S(1)} %get-tuple-element.94), channel_id=1, source_target_pairs={{1,0},{2,1},{3,2},{5,4},{6,5},{7,6},{9,8},{10,9},{11,10},{13,12},{... | collective-permute-start | bytes 5768 | tf_op jit(solution)/shard_map/ppermute | solution.py:28
  89.7 0.7 copy-start.5
  89.7 0.7 copy-start.6
  95.2 6.9 %collective-permute-start.9 = (f32[5,96,1]{2,1,0:T(8,128)S(1)}, f32[5,96,1]{2,1,0:T(8,128)S(1)}, u32[]{:S(2)}, u32[]{:S(2)}) collective-permute-start(f32[5,96,1]{2,1,0:T(8,128)S(1)} %get-tuple-element.89), channel_id=1, source_target_pairs={{0,1},{1,2},{2,3},{4,5},{5,6},{6,7},{8,9},{9,10},{10,11},{12,13},{... | collective-permute-start | bytes 5768 | tf_op jit(solution)/shard_map/ppermute | solution.py:27
  98.3 8.6 %collective-permute-start.8 = (f32[5,96,1]{2,1,0:T(8,128)S(1)}, f32[5,96,1]{2,1,0:T(8,128)S(1)}, u32[]{:S(2)}, u32[]{:S(2)}) collective-permute-start(f32[5,96,1]{2,1,0:T(8,128)S(1)} %get-tuple-element.90), channel_id=1, source_target_pairs={{1,0},{2,1},{3,2},{5,4},{6,5},{7,6},{9,8},{10,9},{11,10},{13,12},{... | collective-permute-start | bytes 5768 | tf_op jit(solution)/shard_map/ppermute | solution.py:28

commit v2 on v1

--- a/solution.py
+++ b/solution.py
@@ -22,11 +22,36 @@
 
 def halo(value):
     peers = lax.axis_size("mesh")
-    up = [(i, i + 1) for i in range(peers - 1)]
-    down = [(i + 1, i) for i in range(peers - 1)]
-    before = lax.ppermute(value[..., -1:], "mesh", up)
-    after = lax.ppermute(value[..., :1], "mesh", down)
+    me = lax.axis_index("mesh")
+    before = shifted(value[..., -1:], "mesh", 1)
+    after = shifted(value[..., :1], "mesh", -1)
+    before = jnp.where(me > 0, before, jnp.zeros_like(before))
+    after = jnp.where(me < peers - 1, after, jnp.zeros_like(after))
     return before, after
+
+
+def mesh_sum(value):
+    peers = lax.axis_size("mesh")
+    if peers & (peers - 1):
+        return lax.psum(value, "mesh")
+    step = 1
+    while step < peers:
+        value = value + lax.ppermute(value, "mesh", [(i, i ^ step) for i in range(peers)])
+        step *= 2
+    return value
+
+
+def pick_rows(table, index, count):
+    slots = table.shape[0]
+    wanted = (index + jnp.arange(count, dtype=jnp.int32)) % slots
+    hit = wanted[:, None] == jnp.arange(slots, dtype=jnp.int32)[None, :]
+    hit = hit.reshape(hit.shape + (1,) * (table.ndim - 1))
+    return jnp.sum(jnp.where(hit, table[None], jnp.zeros_like(table[None])), axis=1)
+
+
+def pick_entry(values, index):
+    hit = jnp.arange(values.shape[0], dtype=jnp.int32) == index
+    return jnp.sum(jnp.where(hit, values, jnp.zeros_like(values)))
 
 
 def axial_pad(value, before, after):
@@ -104,31 +129,16 @@
     force_scale = 1.0 / math.sqrt(pitch_cells * axial_cells * lax.axis_size("mesh"))
     passages = lax.axis_size("blk")
     position = lax.axis_index("blk")
-    slot_count = lower_row_history.shape[1]
     blade_stiffness = stiffness[0]
     disp0 = displacement[0]
     vel0 = velocity[0]
 
     after_me = (position + 1) % passages
     before_me = (position + passages - 1) % passages
-    slot_next = lax.dynamic_index_in_dim(lower_lag_slot, after_me, 0, keepdims=False)
-    slot_prev = lax.dynamic_index_in_dim(upper_lag_slot, before_me, 0, keepdims=False)
-    rows_up = jnp.stack(
-        [
-            lax.dynamic_index_in_dim(
-                upper_row_history[0], (slot_next + s) % slot_count, 0, keepdims=False
-            )
-            for s in range(STEP_COUNT)
-        ]
-    )
-    rows_down = jnp.stack(
-        [
-            lax.dynamic_index_in_dim(
-                lower_row_history[0], (slot_prev + s) % slot_count, 0, keepdims=False
-            )
-            for s in range(STEP_COUNT)
-        ]
-    )
+    slot_next = pick_entry(lower_lag_slot, after_me)
+    slot_prev = pick_entry(upper_lag_slot, before_me)
+    rows_up = pick_rows(upper_row_history[0], slot_next, STEP_COUNT)
+    rows_down = pick_rows(lower_row_history[0], slot_prev, STEP_COUNT)
     lower_ghosts = shifted(rows_up, "blk", 1)
     upper_ghosts = shifted(rows_down, "blk", -1)
 
@@ -148,9 +158,8 @@
         return add_field_one(rate, DIFFUSION * lap)
 
     ms_ga, ms_gp, _ = single_field_grads(mode_shape, mode_before, mode_after)
-    grad_a_sum = jnp.einsum("mpx,npx->mn", mode_shape, ms_ga, precision=PRECISE)
-    grad_p_sum = jnp.einsum("mpx,npx->mn", mode_shape, ms_gp, precision=PRECISE)
-    coupling_sum = -(axial_jacobian[4, 1] * grad_a_sum + pitch_jacobian[4, 1] * grad_p_sum)
+    ms_rate4 = -(axial_jacobian[4, 1] * ms_ga + pitch_jacobian[4, 1] * ms_gp)
+    coupling_sum = jnp.einsum("mpx,npx->mn", mode_shape, ms_rate4, precision=PRECISE)
 
     gl1, gu1 = lower_ghosts[0], upper_ghosts[0]
     gl2, gu2 = lower_ghosts[1], upper_ghosts[1]
@@ -177,7 +186,7 @@
             coupling_sum.reshape(-1),
         ]
     )
-    totals = lax.psum(partials, "mesh")
+    totals = mesh_sum(partials)
     force0 = force_scale * totals[0:modes]
     force1 = force_scale * totals[modes : 2 * modes]
     force2 = force_scale * totals[2 * modes : 3 * modes]
@@ -194,7 +203,7 @@
     acc2 = force2 - blade_stiffness * disp1 - DAMPING * vel1
     disp2m = disp1 + h * vel1
     vel2m = vel1 + h * acc2
-    force2m = force2 + h * force3 + h * (0.5 * h * h * COUPLING) * (couple @ acc1)
+    force2m = force2 + h * force3 + h * (0.5 * h * h * COUPLING) * jnp.dot(couple, acc1, precision=PRECISE)
     acc2m = force2m - blade_stiffness * disp2m - DAMPING * vel2m
     disp2 = disp1 + 0.5 * h * (vel1 + vel2m)
     vel2 = vel1 + 0.5 * h * (acc2 + acc2m)

time: 112 us -> 97.3 us (0.87)
  blocking collectives: 8.38 us -> 0 us
  other arithmetic: 8.4 us -> 13.6 us
  between operations: 6.37 us -> 2.38 us
  local copies, waits for them, and re-layouts: 7.32 us -> 3.79 us
  starting transfers between devices: 22.1 us -> 18.6 us
  matrix products: 26.6 us -> 23.2 us
  waiting for transfers between devices: 31.8 us -> 34.6 us
    ppermute x2 -> x10, waiting for transfers between devices: 0.01 us -> 29.6 us  [shifted(): lax.ppermute(value, axis, [(i, (i + by) % peers) for i in range(peers)])]
    ppermute x8 -> x2, waiting for transfers between devices: 31.8 us -> 5.01 us  [mesh_sum(): lax.ppermute(value, 'mesh', [(i, i ^ step) for i in range(peers)])]
    ppermute x8 -> x2, starting transfers between devices: 17.5 us -> 1.88 us  [mesh_sum(): lax.ppermute(value, 'mesh', [(i, i ^ step) for i in range(peers)])]
    ppermute x2 -> x10, starting transfers between devices: 4.57 us -> 16.8 us  [shifted(): lax.ppermute(value, axis, [(i, (i + by) % peers) for i in range(peers)])]
    psum x1 -> x0, blocking collectives: 8.38 us -> none  [on_device(): totals = lax.psum(partials, 'mesh')]
    reduce_sum x0 -> x4, other arithmetic: none -> 3.88 us  [the longest x2 2.65 us: pick_entry(): return jnp.sum(jnp.where(hit, values, jnp.zeros_like(values)))]
    dot_general x3 -> x2, matrix products: 6.15 us -> 2.76 us  [the longest x1 2.1 us: on_device(): jnp.einsum('mpx,npx->mn', mode_shape, ms_rate4, precision=PRECISE)]
    dynamic_slice x4 -> x0, local copies, waits for them, and re-layouts: 2.9 us -> none  [the longest x1 0.87 us: on_device(): lax.dynamic_index_in_dim(upper_row_history[0], (slot_next + s) % slot_cou...]
  transfers between devices with their start and end apart: 10 -> 12, of which waited for: 8 -> 10; matrix products, arithmetic and copies ran while one was open for 16% -> 14% of each run, Pallas kernels for 0% -> 0%
where the time goes in v2:
time: 97.3 us; the launch traced here: 96.2 us
  waiting for transfers between devices  34.6 us (36%)
  matrix products  23.2 us (24%)
  starting transfers between devices  18.6 us (19%)
  other arithmetic  13.6 us (14%)
  local copies, waits for them, and re-layouts  3.79 us (4%)
  between operations  2.38 us (2%)
    ppermute x10, waiting for transfers between devices, shifted(): lax.ppermute(value, axis, [(i, (i + by) % peers) for i in range(peers)])  29.6 us
    ppermute x10, starting transfers between devices, shifted(): lax.ppermute(value, axis, [(i, (i + by) % peers) for i in range(peers)])  16.8 us
    dot_general x4, matrix products, projection(): return jnp.einsum('mpx,px->m', mode_shape, field, precision=PRECISE)  7.67 us
    ppermute x2, waiting for transfers between devices, mesh_sum(): lax.ppermute(value, 'mesh', [(i, i ^ step) for i in range(peers)])  5.01 us
    dot_general x6, matrix products, modal_field(): return jnp.einsum('m,mpx->px', weights, mode_shape, precision=PRECISE)  4.38 us
    dot_general x4, matrix products, flow_rate(): jnp.einsum('ij,jpx->ipx', axial_jacobian, grad_axial, precision=PRECISE)  4.19 us
    dot_general x4, matrix products, flow_rate(): jnp.einsum('ij,jpx->ipx', pitch_jacobian, grad_pitch, precision=PRECISE)  4.19 us
    reduce_sum x2, other arithmetic, pick_entry(): return jnp.sum(jnp.where(hit, values, jnp.zeros_like(values)))  2.65 us
  transfers between devices with their start and end apart: 12, of which 10 were waited for; matrix products, arithmetic and copies ran while one was open for 14% of the time, Pallas kernels for 0%

profile of v2, /device:TPU:0, one launch (start us, length us, event | category | flops | bytes accessed | tf_op | source)
XLA Modules:
  0.0 96.2 jit_solution(10216919449694216256)
XLA Ops:
  0.7 1.4 %fusion.56 = s32[]{:T(128)} fusion(s32[8]{0:T(128)} %param.27, s32[]{:T(128)S(6)} %select_n.91), kind=kLoop, calls=%fused_computation.155 | loop fusion | flops 23 | bytes 40 | tf_op jit(solution)/shard_map/reduce_sum | solution.py:54
  2.0 1.3 %fusion.57 = s32[]{:T(128)} fusion(s32[8]{0:T(128)} %param.26, s32[]{:T(128)S(6)} %select_n.95), kind=kLoop, calls=%fused_computation.156 | loop fusion | flops 23 | bytes 40 | tf_op jit(solution)/shard_map/reduce_sum | solution.py:54
  3.3 1.3 %and_select_fusion = (s32[2]{0:T(128)S(1)}, s32[2]{0:T(128)S(1)}) fusion(s32[]{:T(128)} %fusion.57, s32[]{:T(128)} %fusion.56), kind=kLoop, calls=%fused_computation.149 | loop fusion | flops 48 | bytes 24 | tf_op jit(solution)/shard_map/jit(remainder)/select_n | solution.py:46
  4.7 1.1 %select_reduce_fusion = f32[2,5,256]{2,1,0:T(8,128)S(1)} fusion(f32[64,5,256]{2,0,1:T(8,128)} %bitcast.219, pred[2,64]{1,0:T(4,128)(4,1)S(1)} %iota_compare_fusion), kind=kLoop, calls=%fused_computation.35 | loop fusion | flops 325120 | bytes 338048 | tf_op jit(solution)/shard_map/reduce_sum | solution.py:49
  5.8 0.5 collective-permute-start.3
  6.6 4.1 %collective-permute-start.2 = (f32[2,5,256]{2,0,1:T(2,128)S(1)}, f32[2,5,256]{2,0,1:T(2,128)S(1)}, u32[]{:S(2)}, u32[]{:S(2)}) collective-permute-start(f32[2,5,256]{2,0,1:T(2,128)S(1)} %copy.137), channel_id=1, source_target_pairs={{0,28},{4,0},{8,4},{12,8},{16,12},{20,16},{24,20},{28,24},{1,29},{... | collective-permute-start | bytes 30728 | tf_op jit(solution)/shard_map/ppermute | solution.py:20
  10.7 1.3 %pad_maximum_fusion.16 = (f32[9,96,1]{2,1,0:T(8,128)S(1)}, f32[9,96,1]{2,1,0:T(8,128)S(1)}) fusion(f32[4,96,256]{2,1,0:T(8,128)S(1)} %copy-done, f32[5,96,256]{2,1,0:T(8,128)} %bitcast.216), kind=kLoop, calls=%fused_computation.68 | loop fusion | flops 1728 | bytes 891648 | tf_op jit(solution)/shard_map/concatenate | solution.py:145
  12.0 2.0 %collective-permute-start.1 = (f32[9,96,1]{2,1,0:T(8,128)S(1)}, f32[9,96,1]{2,1,0:T(8,128)S(1)}, u32[]{:S(2)}, u32[]{:S(2)}) collective-permute-start(f32[9,96,1]{2,1,0:T(8,128)S(1)} %get-tuple-element.88), channel_id=1, source_target_pairs={{0,1},{1,2},{2,3},{3,0},{4,5},{5,6},{6,7},{7,4},{8,9},{9,10},{10,1... | collective-permute-start | bytes 10376 | tf_op jit(solution)/shard_map/ppermute | solution.py:20
  14.0 1.0 %collective-permute-start = (f32[9,96,1]{2,1,0:T(8,128)S(1)}, f32[9,96,1]{2,1,0:T(8,128)S(1)}, u32[]{:S(2)}, u32[]{:S(2)}) collective-permute-start(f32[9,96,1]{2,1,0:T(8,128)S(1)} %get-tuple-element.89), channel_id=1, source_target_pairs={{0,3},{1,0},{2,1},{3,2},{4,7},{5,4},{6,5},{7,6},{8,11},{9,8},{10,9... | collective-permute-start | bytes 10376 | tf_op jit(solution)/shard_map/ppermute | solution.py:20
  15.1 1.0 fusion.45
  16.0 1.8 %convolution_bitcast_fusion.7 = f32[4]{0:T(128)S(1)} fusion(f32[96,256,1]{1,0,2:T(8,128)S(1)} %slice_bitcast_fusion.3, f32[4,96,256]{2,1,0:T(8,128)S(1)} %copy-done), kind=kOutput, calls=%fused_computation.7 | convolution fusion | flops 1179648 | bytes 491536 | tf_op jit(solution)/shard_map/mpx,px->m/dot_general | solution.py:103
  17.9 0.7 copy-done.4
  18.6 0.6 slice.382
  19.1 0.6 slice.379
  21.0 5.0 %collective-permute-done.1 = f32[9,96,1]{2,1,0:T(8,128)S(1)} collective-permute-done((f32[9,96,1]{2,1,0:T(8,128)S(1)}, f32[9,96,1]{2,1,0:T(8,128)S(1)}, u32[]{:S(2)}, u32[]{:S(2)}) %collective-permute-start.1) | collective-permute-done | bytes 3488 | tf_op jit(solution)/shard_map/ppermute | solution.py:20
  26.1 0.1 slice_reduce_fusion.2
  26.2 7.0 %collective-permute-done = f32[9,96,1]{2,1,0:T(8,128)S(1)} collective-permute-done((f32[9,96,1]{2,1,0:T(8,128)S(1)}, f32[9,96,1]{2,1,0:T(8,128)S(1)}, u32[]{:S(2)}, u32[]{:S(2)}) %collective-permute-start) | collective-permute-done | bytes 3488 | tf_op jit(solution)/shard_map/ppermute | solution.py:20
  33.4 0.3 fusion.21
  33.7 2.1 %convolution_bitcast_fusion.2 = f32[4,4]{0,1:T(4,128)S(1)} fusion(f32[4,96,256]{2,1,0:T(8,128)S(1)} %fusion.21, f32[4,96,256]{2,1,0:T(8,128)S(1)} %copy-done), kind=kOutput, calls=%fused_computation.2 | convolution fusion | flops 4718592 | bytes 786496 | tf_op jit(solution)/shard_map/mpx,npx->mn/dot_general | solution.py:162
  36.1 0.4 subtract_multiply_fusion.7
  36.5 1.0 %fusion.15 = f32[96,256,5]{1,2,0:T(8,128)S(1)} fusion(f32[5,96,256]{2,1,0:T(8,128)S(1)} %get-tuple-element.102, f32[5,5]{1,0:T(8,128)S(1)} %copy-done.3), kind=kOutput, calls=%fused_computation.25 | convolution fusion | flops 7372800 | bytes 983140 | tf_op jit(solution)/shard_map/ij,jpx->ipx/dot_general | solution.py:77
  37.6 1.0 %fusion.13 = f32[96,256,5]{1,2,0:T(8,128)S(1)} fusion(f32[5,96,256]{2,1,0:T(8,128)S(1)} %get-tuple-element.103, f32[5,5]{1,0:T(8,128)S(1)} %copy-done.4), kind=kOutput, calls=%fused_computation.23 | convolution fusion | flops 7372800 | bytes 983140 | tf_op jit(solution)/shard_map/ij,jpx->ipx/dot_general | solution.py:78
  38.6 0.6 bitcast_subtract_fusion.3
  39.5 1.5 %collective-permute-start.5 = (f32[5,96,1]{2,1,0:T(8,128)S(1)}, f32[5,96,1]{2,1,0:T(8,128)S(1)}, u32[]{:S(2)}, u32[]{:S(2)}) collective-permute-start(f32[5,96,1]{2,1,0:T(8,128)S(1)} %get-tuple-element.100), channel_id=1, source_target_pairs={{0,1},{1,2},{2,3},{3,0},{4,5},{5,6},{6,7},{7,4},{8,9},{9,10},{10,1... | collective-permute-start | bytes 5768 | tf_op jit(solution)/shard_map/ppermute | solution.py:20
  41.0 1.9 %convolution_bitcast_fusion.6 = f32[4]{0:T(128)S(1)} fusion(f32[96,256,1]{1,0,2:T(8,128)S(1)} %slice_bitcast_fusion.2, f32[4,96,256]{2,1,0:T(8,128)S(1)} %copy-done), kind=kOutput, calls=%fused_computation.6 | convolution fusion | flops 1179648 | bytes 491536 | tf_op jit(solution)/shard_map/mpx,px->m/dot_general | solution.py:103
  43.0 1.6 %collective-permute-start.4 = (f32[5,96,1]{2,1,0:T(8,128)S(1)}, f32[5,96,1]{2,1,0:T(8,128)S(1)}, u32[]{:S(2)}, u32[]{:S(2)}) collective-permute-start(f32[5,96,1]{2,1,0:T(8,128)S(1)} %get-tuple-element.101), channel_id=1, source_target_pairs={{0,3},{1,0},{2,1},{3,2},{4,7},{5,4},{6,5},{7,6},{8,11},{9,8},{10,9... | collective-permute-start | bytes 5768 | tf_op jit(solution)/shard_map/ppermute | solution.py:20
  44.6 3.6 %collective-permute-done.5 = f32[5,96,1]{2,1,0:T(8,128)S(1)} collective-permute-done((f32[5,96,1]{2,1,0:T(8,128)S(1)}, f32[5,96,1]{2,1,0:T(8,128)S(1)}, u32[]{:S(2)}, u32[]{:S(2)}) %collective-permute-start.5) | collective-permute-done | bytes 1952 | tf_op jit(solution)/shard_map/ppermute | solution.py:20
  48.2 2.4 %collective-permute-done.4 = f32[5,96,1]{2,1,0:T(8,128)S(1)} collective-permute-done((f32[5,96,1]{2,1,0:T(8,128)S(1)}, f32[5,96,1]{2,1,0:T(8,128)S(1)}, u32[]{:S(2)}, u32[]{:S(2)}) %collective-permute-start.4) | collective-permute-done | bytes 1952 | tf_op jit(solution)/shard_map/ppermute | solution.py:20
  50.6 0.4 subtract_multiply_fusion.5
  51.1 1.0 %fusion.11 = f32[96,256,5]{1,2,0:T(8,128)S(1)} fusion(f32[5,96,256]{2,1,0:T(8,128)S(1)} %get-tuple-element.98, f32[5,5]{1,0:T(8,128)S(1)} %copy-done.3), kind=kOutput, calls=%fused_computation.21 | convolution fusion | flops 7372800 | bytes 983140 | tf_op jit(solution)/shard_map/ij,jpx->ipx/dot_general | solution.py:77
  52.1 1.0 %fusion.9 = f32[96,256,5]{1,2,0:T(8,128)S(1)} fusion(f32[5,96,256]{2,1,0:T(8,128)S(1)} %get-tuple-element.99, f32[5,5]{1,0:T(8,128)S(1)} %copy-done.4), kind=kOutput, calls=%fused_computation.19 | convolution fusion | flops 7372800 | bytes 983140 | tf_op jit(solution)/shard_map/ij,jpx->ipx/dot_general | solution.py:78
  53.2 0.6 bitcast_subtract_fusion.2
  54.0 1.9 %collective-permute-start.7 = (f32[5,96,1]{2,1,0:T(8,128)S(1)}, f32[5,96,1]{2,1,0:T(8,128)S(1)}, u32[]{:S(2)}, u32[]{:S(2)}) collective-permute-start(f32[5,96,1]{2,1,0:T(8,128)S(1)} %get-tuple-element.96), channel_id=1, source_target_pairs={{0,1},{1,2},{2,3},{3,0},{4,5},{5,6},{6,7},{7,4},{8,9},{9,10},{10,1... | collective-permute-start | bytes 5768 | tf_op jit(solution)/shard_map/ppermute | solution.py:20
  55.9 1.9 %convolution_bitcast_fusion.5 = f32[4]{0:T(128)S(1)} fusion(f32[96,256,1]{1,0,2:T(8,128)S(1)} %slice_bitcast_fusion.1, f32[4,96,256]{2,1,0:T(8,128)S(1)} %copy-done), kind=kOutput, calls=%fused_computation.5 | convolution fusion | flops 1179648 | bytes 491536 | tf_op jit(solution)/shard_map/mpx,px->m/dot_general | solution.py:103
  57.9 1.1 %collective-permute-start.6 = (f32[5,96,1]{2,1,0:T(8,128)S(1)}, f32[5,96,1]{2,1,0:T(8,128)S(1)}, u32[]{:S(2)}, u32[]{:S(2)}) collective-permute-start(f32[5,96,1]{2,1,0:T(8,128)S(1)} %get-tuple-element.97), channel_id=1, source_target_pairs={{0,3},{1,0},{2,1},{3,2},{4,7},{5,4},{6,5},{7,6},{8,11},{9,8},{10,9... | collective-permute-start | bytes 5768 | tf_op jit(solution)/shard_map/ppermute | solution.py:20
  59.0 3.8 %collective-permute-done.7 = f32[5,96,1]{2,1,0:T(8,128)S(1)} collective-permute-done((f32[5,96,1]{2,1,0:T(8,128)S(1)}, f32[5,96,1]{2,1,0:T(8,128)S(1)}, u32[]{:S(2)}, u32[]{:S(2)}) %collective-permute-start.7) | collective-permute-done | bytes 1952 | tf_op jit(solution)/shard_map/ppermute | solution.py:20
  62.8 2.5 %collective-permute-done.6 = f32[5,96,1]{2,1,0:T(8,128)S(1)} collective-permute-done((f32[5,96,1]{2,1,0:T(8,128)S(1)}, f32[5,96,1]{2,1,0:T(8,128)S(1)}, u32[]{:S(2)}, u32[]{:S(2)}) %collective-permute-start.6) | collective-permute-done | bytes 1952 | tf_op jit(solution)/shard_map/ppermute | solution.py:20
  65.3 0.4 subtract_multiply_fusion.3
  65.8 1.0 %fusion.7 = f32[96,256,5]{1,2,0:T(8,128)S(1)} fusion(f32[5,96,256]{2,1,0:T(8,128)S(1)} %get-tuple-element.94, f32[5,5]{1,0:T(8,128)S(1)} %copy-done.3), kind=kOutput, calls=%fused_computation.17 | convolution fusion | flops 7372800 | bytes 983140 | tf_op jit(solution)/shard_map/ij,jpx->ipx/dot_general | solution.py:77
  66.8 1.0 %fusion.5 = f32[96,256,5]{1,2,0:T(8,128)S(1)} fusion(f32[5,96,256]{2,1,0:T(8,128)S(1)} %get-tuple-element.95, f32[5,5]{1,0:T(8,128)S(1)} %copy-done.4), kind=kOutput, calls=%fused_computation.15 | convolution fusion | flops 7372800 | bytes 983140 | tf_op jit(solution)/shard_map/ij,jpx->ipx/dot_general | solution.py:78
  67.9 0.6 bitcast_subtract_fusion.1
  68.5 1.9 %convolution_bitcast_fusion.4 = f32[4]{0:T(128)S(1)} fusion(f32[96,256,1]{1,0,2:T(8,128)S(1)} %slice_bitcast_fusion, f32[4,96,256]{2,1,0:T(8,128)S(1)} %copy-done), kind=kOutput, calls=%fused_computation.4 | convolution fusion | flops 1179648 | bytes 491536 | tf_op jit(solution)/shard_map/mpx,px->m/dot_general | solution.py:103
  70.5 1.2 %collective-permute-start.8 = (f32[32]{0:T(128)S(1)}, f32[32]{0:T(128)S(1)}, u32[]{:S(2)}, u32[]{:S(2)}) collective-permute-start(f32[32]{0:T(128)S(1)} %concatenate.119), channel_id=1, source_target_pairs={{0,1},{1,0},{2,3},{3,2},{4,5},{5,4},{6,7},{7,6},{8,9},{9,8},{10,11... | collective-permute-start | bytes 392 | tf_op jit(solution)/shard_map/ppermute | solution.py:39
  71.7 2.3 %collective-permute-done.8 = f32[32]{0:T(128)S(1)} collective-permute-done((f32[32]{0:T(128)S(1)}, f32[32]{0:T(128)S(1)}, u32[]{:S(2)}, u32[]{:S(2)}) %collective-permute-start.8) | collective-permute-done | bytes 160 | tf_op jit(solution)/shard_map/ppermute | solution.py:39
  74.1 0.7 collective-permute-start.9
  74.7 0.2 slice_reduce_fusion
  74.9 2.7 %collective-permute-done.9 = f32[32]{0:T(128)S(1)} collective-permute-done((f32[32]{0:T(128)S(1)}, f32[32]{0:T(128)S(1)}, u32[]{:S(2)}, u32[]{:S(2)}) %collective-permute-start.9) | collective-permute-done | bytes 160 | tf_op jit(solution)/shard_map/ppermute | solution.py:39
  77.8 0.6 copy-done.6
  78.3 0.6 add_bitcast_fusion.2
  78.9 1.0 fusion.39
  79.9 0.3 convolution_bitcast_fusion
  80.2 0.3 convolution_bitcast_fusion.1
  80.5 1.0 fusion.37
  81.4 1.0 %fusion.35 = f32[1,96,256]{2,0,1:T(1,128)S(1)} fusion(f32[4,96,256]{2,1,0:T(8,128)S(1)} %copy-done, f32[4]{0:T(128)S(1)} %get-tuple-element.86, f32[4]{0:T(128)S(1)} %get-tuple-element.85, f32[1,4]{1,0:T(1,128)S(1)} %copy-done.6, f32[32]{0:T(128)S(1)} %add.277), kind=kOutput, calls=%fused_computation.118 | convolution fusion | flops 1179676 | bytes 491696 | tf_op jit(solution)/shard_map/m,mpx->px/dot_general | solution.py:99
  83.2 1.2 %collective-permute-start.11 = (f32[5,96,1]{2,1,0:T(8,128)S(1)}, f32[5,96,1]{2,1,0:T(8,128)S(1)}, u32[]{:S(2)}, u32[]{:S(2)}) collective-permute-start(f32[5,96,1]{2,1,0:T(8,128)S(1)} %get-tuple-element.92), channel_id=1, source_target_pairs={{0,1},{1,2},{2,3},{3,0},{4,5},{5,6},{6,7},{7,4},{8,9},{9,10},{10,1... | collective-permute-start | bytes 5768 | tf_op jit(solution)/shard_map/ppermute | solution.py:20
  84.4 0.7 add_bitcast_fusion.1
  85.1 1.7 %collective-permute-start.10 = (f32[5,96,1]{2,1,0:T(8,128)S(1)}, f32[5,96,1]{2,1,0:T(8,128)S(1)}, u32[]{:S(2)}, u32[]{:S(2)}) collective-permute-start(f32[5,96,1]{2,1,0:T(8,128)S(1)} %get-tuple-element.93), channel_id=1, source_target_pairs={{0,3},{1,0},{2,1},{3,2},{4,7},{5,4},{6,5},{7,6},{8,11},{9,8},{10,9... | collective-permute-start | bytes 5768 | tf_op jit(solution)/shard_map/ppermute | solution.py:20
  86.8 3.5 %collective-permute-done.11 = f32[5,96,1]{2,1,0:T(8,128)S(1)} collective-permute-done((f32[5,96,1]{2,1,0:T(8,128)S(1)}, f32[5,96,1]{2,1,0:T(8,128)S(1)}, u32[]{:S(2)}, u32[]{:S(2)}) %collective-permute-start.11) | collective-permute-done | bytes 1952 | tf_op jit(solution)/shard_map/ppermute | solution.py:20
  90.3 1.8 %collective-permute-done.10 = f32[5,96,1]{2,1,0:T(8,128)S(1)} collective-permute-done((f32[5,96,1]{2,1,0:T(8,128)S(1)}, f32[5,96,1]{2,1,0:T(8,128)S(1)}, u32[]{:S(2)}, u32[]{:S(2)}) %collective-permute-start.10) | collective-permute-done | bytes 1952 | tf_op jit(solution)/shard_map/ppermute | solution.py:20
  92.2 0.4 subtract_multiply_fusion.1
  92.6 1.0 %fusion.3 = f32[96,256,5]{1,2,0:T(8,128)S(1)} fusion(f32[5,96,256]{2,1,0:T(8,128)S(1)} %get-tuple-element.90, f32[5,5]{1,0:T(8,128)S(1)} %copy-done.3), kind=kOutput, calls=%fused_computation.13 | convolution fusion | flops 7372800 | bytes 983140 | tf_op jit(solution)/shard_map/ij,jpx->ipx/dot_general | solution.py:77
  93.7 1.0 %fusion.1 = f32[96,256,5]{1,2,0:T(8,128)S(1)} fusion(f32[5,96,256]{2,1,0:T(8,128)S(1)} %get-tuple-element.91, f32[5,5]{1,0:T(8,128)S(1)} %copy-done.4), kind=kOutput, calls=%fused_computation.11 | convolution fusion | flops 7372800 | bytes 983140 | tf_op jit(solution)/shard_map/ij,jpx->ipx/dot_general | solution.py:78
  94.7 0.6 bitcast_subtract_fusion
  95.3 0.9 add_bitcast_fusion
  (60 shorter events, 2.5 us)
Async XLA Ops:
  0.6 5.8 %copy-start.2 = (f32[1,64,5,256]{3,1,2,0:T(8,128)S(1)}, f32[1,64,5,256]{3,1,2,0:T(8,128)}, u32[]{:S(2)}) copy-start(f32[1,64,5,256]{3,1,2,0:T(8,128)} %param.24) | copy-start | bytes 983044
  0.7 10.0 %copy-start = (f32[4,96,256]{2,1,0:T(8,128)S(1)}, f32[4,96,256]{2,1,0:T(8,128)}, u32[]{:S(2)}) copy-start(f32[4,96,256]{2,1,0:T(8,128)} %param.30) | copy-start | bytes 1179652
  5.8 30.2 %collective-permute-start.3 = (f32[2,5,256]{2,0,1:T(2,128)S(1)}, f32[2,5,256]{2,0,1:T(2,128)S(1)}, u32[]{:S(2)}, u32[]{:S(2)}) collective-permute-start(f32[2,5,256]{2,0,1:T(2,128)S(1)} %copy.138), channel_id=1, source_target_pairs={{0,4},{4,8},{8,12},{12,16},{16,20},{20,24},{24,28},{28,0},{1,5},{5... | collective-permute-start | bytes 30728 | tf_op jit(solution)/shard_map/ppermute | solution.py:20
  6.6 29.5 %collective-permute-start.2 = (f32[2,5,256]{2,0,1:T(2,128)S(1)}, f32[2,5,256]{2,0,1:T(2,128)S(1)}, u32[]{:S(2)}, u32[]{:S(2)}) collective-permute-start(f32[2,5,256]{2,0,1:T(2,128)S(1)} %copy.137), channel_id=1, source_target_pairs={{0,28},{4,0},{8,4},{12,8},{16,12},{20,16},{24,20},{28,24},{1,29},{... | collective-permute-start | bytes 30728 | tf_op jit(solution)/shard_map/ppermute | solution.py:20
  10.7 4.4 %copy-start.1 = (f32[1,5,96,256]{3,2,1,0:T(8,128)S(1)}, f32[1,5,96,256]{3,2,1,0:T(8,128)}, u32[]{:S(2)}) copy-start(f32[1,5,96,256]{3,2,1,0:T(8,128)} %param.23) | copy-start | bytes 1474564
  12.0 14.1 %collective-permute-start.1 = (f32[9,96,1]{2,1,0:T(8,128)S(1)}, f32[9,96,1]{2,1,0:T(8,128)S(1)}, u32[]{:S(2)}, u32[]{:S(2)}) collective-permute-start(f32[9,96,1]{2,1,0:T(8,128)S(1)} %get-tuple-element.88), channel_id=1, source_target_pairs={{0,1},{1,2},{2,3},{3,0},{4,5},{5,6},{6,7},{7,4},{8,9},{9,10},{10,1... | collective-permute-start | bytes 10376 | tf_op jit(solution)/shard_map/ppermute | solution.py:20
  14.0 1.0 %copy-start.5 = (f32[1,4]{1,0:T(1,128)S(1)}, f32[1,4]{1,0:T(1,128)}, u32[]{:S(2)}) copy-start(f32[1,4]{1,0:T(1,128)} %param.33) | copy-start | bytes 52
  14.0 19.2 %collective-permute-start = (f32[9,96,1]{2,1,0:T(8,128)S(1)}, f32[9,96,1]{2,1,0:T(8,128)S(1)}, u32[]{:S(2)}, u32[]{:S(2)}) collective-permute-start(f32[9,96,1]{2,1,0:T(8,128)S(1)} %get-tuple-element.89), channel_id=1, source_target_pairs={{0,3},{1,0},{2,1},{3,2},{4,7},{5,4},{6,5},{7,6},{8,11},{9,8},{10,9... | collective-permute-start | bytes 10376 | tf_op jit(solution)/shard_map/ppermute | solution.py:20
  17.9 0.7 copy-start.4
  17.9 1.3 %copy-start.3 = (f32[5,5]{1,0:T(8,128)S(1)}, f32[5,5]{1,0:T(8,128)}, u32[]{:S(2)}) copy-start(f32[5,5]{1,0:T(8,128)} %param.28) | copy-start | bytes 304
  39.5 8.7 %collective-permute-start.5 = (f32[5,96,1]{2,1,0:T(8,128)S(1)}, f32[5,96,1]{2,1,0:T(8,128)S(1)}, u32[]{:S(2)}, u32[]{:S(2)}) collective-permute-start(f32[5,96,1]{2,1,0:T(8,128)S(1)} %get-tuple-element.100), channel_id=1, source_target_pairs={{0,1},{1,2},{2,3},{3,0},{4,5},{5,6},{6,7},{7,4},{8,9},{9,10},{10,1... | collective-permute-start | bytes 5768 | tf_op jit(solution)/shard_map/ppermute | solution.py:20
  43.0 7.6 %collective-permute-start.4 = (f32[5,96,1]{2,1,0:T(8,128)S(1)}, f32[5,96,1]{2,1,0:T(8,128)S(1)}, u32[]{:S(2)}, u32[]{:S(2)}) collective-permute-start(f32[5,96,1]{2,1,0:T(8,128)S(1)} %get-tuple-element.101), channel_id=1, source_target_pairs={{0,3},{1,0},{2,1},{3,2},{4,7},{5,4},{6,5},{7,6},{8,11},{9,8},{10,9... | collective-permute-start | bytes 5768 | tf_op jit(solution)/shard_map/ppermute | solution.py:20
  54.0 8.7 %collective-permute-start.7 = (f32[5,96,1]{2,1,0:T(8,128)S(1)}, f32[5,96,1]{2,1,0:T(8,128)S(1)}, u32[]{:S(2)}, u32[]{:S(2)}) collective-permute-start(f32[5,96,1]{2,1,0:T(8,128)S(1)} %get-tuple-element.96), channel_id=1, source_target_pairs={{0,1},{1,2},{2,3},{3,0},{4,5},{5,6},{6,7},{7,4},{8,9},{9,10},{10,1... | collective-permute-start | bytes 5768 | tf_op jit(solution)/shard_map/ppermute | solution.py:20
  57.9 7.4 %collective-permute-start.6 = (f32[5,96,1]{2,1,0:T(8,128)S(1)}, f32[5,96,1]{2,1,0:T(8,128)S(1)}, u32[]{:S(2)}, u32[]{:S(2)}) collective-permute-start(f32[5,96,1]{2,1,0:T(8,128)S(1)} %get-tuple-element.97), channel_id=1, source_target_pairs={{0,3},{1,0},{2,1},{3,2},{4,7},{5,4},{6,5},{7,6},{8,11},{9,8},{10,9... | collective-permute-start | bytes 5768 | tf_op jit(solution)/shard_map/ppermute | solution.py:20
  70.5 3.6 %collective-permute-start.8 = (f32[32]{0:T(128)S(1)}, f32[32]{0:T(128)S(1)}, u32[]{:S(2)}, u32[]{:S(2)}) collective-permute-start(f32[32]{0:T(128)S(1)} %concatenate.119), channel_id=1, source_target_pairs={{0,1},{1,0},{2,3},{3,2},{4,5},{5,4},{6,7},{7,6},{8,9},{9,8},{10,11... | collective-permute-start | bytes 392 | tf_op jit(solution)/shard_map/ppermute | solution.py:39
  74.1 3.5 %collective-permute-start.9 = (f32[32]{0:T(128)S(1)}, f32[32]{0:T(128)S(1)}, u32[]{:S(2)}, u32[]{:S(2)}) collective-permute-start(f32[32]{0:T(128)S(1)} %add.276), channel_id=1, source_target_pairs={{0,2},{1,3},{2,0},{3,1},{4,6},{5,7},{6,4},{7,5},{8,10},{9,11},{10,... | collective-permute-start | bytes 392 | tf_op jit(solution)/shard_map/ppermute | solution.py:39
  77.7 0.7 copy-start.6
  77.7 0.7 copy-start.7
  83.2 7.1 %collective-permute-start.11 = (f32[5,96,1]{2,1,0:T(8,128)S(1)}, f32[5,96,1]{2,1,0:T(8,128)S(1)}, u32[]{:S(2)}, u32[]{:S(2)}) collective-permute-start(f32[5,96,1]{2,1,0:T(8,128)S(1)} %get-tuple-element.92), channel_id=1, source_target_pairs={{0,1},{1,2},{2,3},{3,0},{4,5},{5,6},{6,7},{7,4},{8,9},{9,10},{10,1... | collective-permute-start | bytes 5768 | tf_op jit(solution)/shard_map/ppermute | solution.py:20
  85.1 7.1 %collective-permute-start.10 = (f32[5,96,1]{2,1,0:T(8,128)S(1)}, f32[5,96,1]{2,1,0:T(8,128)S(1)}, u32[]{:S(2)}, u32[]{:S(2)}) collective-permute-start(f32[5,96,1]{2,1,0:T(8,128)S(1)} %get-tuple-element.93), channel_id=1, source_target_pairs={{0,3},{1,0},{2,1},{3,2},{4,7},{5,4},{6,5},{7,6},{8,11},{9,8},{10,9... | collective-permute-start | bytes 5768 | tf_op jit(solution)/shard_map/ppermute | solution.py:20

commit v3 on v2

--- a/solution.py
+++ b/solution.py
@@ -43,10 +43,12 @@
 
 def pick_rows(table, index, count):
     slots = table.shape[0]
-    wanted = (index + jnp.arange(count, dtype=jnp.int32)) % slots
-    hit = wanted[:, None] == jnp.arange(slots, dtype=jnp.int32)[None, :]
-    hit = hit.reshape(hit.shape + (1,) * (table.ndim - 1))
-    return jnp.sum(jnp.where(hit, table[None], jnp.zeros_like(table[None])), axis=1)
+    slot = jnp.arange(slots, dtype=jnp.int32).reshape((slots,) + (1,) * (table.ndim - 1))
+    rows = []
+    for s in range(count):
+        hit = slot == (index + s) % slots
+        rows.append(jnp.sum(jnp.where(hit, table, jnp.zeros_like(table)), axis=0))
+    return jnp.stack(rows)
 
 
 def pick_entry(values, index):
@@ -105,6 +107,38 @@
 
 def add_field_one(rate, extra):
     return rate.at[1].add(extra)
+
+
+def rate_field4(state, lower_ghost, upper_ghost, axial_jacobian, pitch_jacobian):
+    zero_col = jnp.zeros_like(state[..., :1])
+    padded_axial = jnp.concatenate([zero_col, state, zero_col], axis=-1)
+    padded_pitch = pitch_pad(state, lower_ghost, upper_ghost)
+    grad_axial = 0.5 * (padded_axial[:, :, 2:] - padded_axial[:, :, :-2])
+    grad_pitch = 0.5 * (padded_pitch[:, 2:, :] - padded_pitch[:, :-2, :])
+    laplacian = (
+        padded_axial[4, :, 2:]
+        + padded_axial[4, :, :-2]
+        + padded_pitch[4, 2:, :]
+        + padded_pitch[4, :-2, :]
+        - 4.0 * state[4]
+    )
+    flux = jnp.einsum("j,jpx->px", axial_jacobian[4], grad_axial, precision=PRECISE)
+    flux = flux + jnp.einsum("j,jpx->px", pitch_jacobian[4], grad_pitch, precision=PRECISE)
+    return DIFFUSION * laplacian - flux
+
+
+def pack(parts, width):
+    flat = [part.reshape(-1, width) for part in parts]
+    return jnp.concatenate(flat, axis=0)
+
+
+def unpack(buffer, shapes):
+    out, offset = [], 0
+    for shape in shapes:
+        count = math.prod(shape[:-1])
+        out.append(buffer[offset : offset + count].reshape(shape))
+        offset += count
+    return out
 
 
 def on_device(
@@ -122,11 +156,11 @@
 ):
     h = TIME_STEP
     state0 = flow_field[0]
-    fields = state0.shape[0]
-    pitch_cells = state0.shape[1]
-    axial_cells = state0.shape[2]
+    fields, pitch_cells, axial_cells = state0.shape
     modes = mode_shape.shape[0]
-    force_scale = 1.0 / math.sqrt(pitch_cells * axial_cells * lax.axis_size("mesh"))
+    mesh_peers = lax.axis_size("mesh")
+    me = lax.axis_index("mesh")
+    force_scale = 1.0 / math.sqrt(pitch_cells * axial_cells * mesh_peers)
     passages = lax.axis_size("blk")
     position = lax.axis_index("blk")
     blade_stiffness = stiffness[0]
@@ -142,47 +176,51 @@
     lower_ghosts = shifted(rows_up, "blk", 1)
     upper_ghosts = shifted(rows_down, "blk", -1)
 
-    both_before, both_after = halo(jnp.concatenate([state0, mode_shape], axis=0))
-    state0_before, mode_before = both_before[:fields], both_before[fields:]
-    state0_after, mode_after = both_after[:fields], both_after[fields:]
-
-    ax_col = axial_jacobian[:, 1]
-    pt_col = pitch_jacobian[:, 1]
-
-    def zero_ghost_rate_one(weights):
-        field = modal_field(weights, mode_shape)
-        f_before = modal_field(weights, mode_before)
-        f_after = modal_field(weights, mode_after)
-        ga, gp, lap = single_field_grads(field, f_before, f_after)
-        rate = -(ax_col[:, None, None] * ga[None] + pt_col[:, None, None] * gp[None])
-        return add_field_one(rate, DIFFUSION * lap)
-
-    ms_ga, ms_gp, _ = single_field_grads(mode_shape, mode_before, mode_after)
+    reach = 2 * STEP_COUNT
+    own = [state0, mode_shape, lower_ghosts, upper_ghosts]
+    shapes = [part.shape[:-1] + (reach,) for part in own]
+    from_left = shifted(pack([part[..., -reach:] for part in own], reach), "mesh", 1)
+    from_right = shifted(pack([part[..., :reach] for part in own], reach), "mesh", -1)
+    from_left = jnp.where(me > 0, from_left, jnp.zeros_like(from_left))
+    from_right = jnp.where(me < mesh_peers - 1, from_right, jnp.zeros_like(from_right))
+    wide = [
+        jnp.concatenate([left, part, right], axis=-1)
+        for left, part, right in zip(unpack(from_left, shapes), own, unpack(from_right, shapes))
+    ]
+    state0_w, mode_w, lower_w, upper_w = wide
+    width = axial_cells + 2 * reach
+    column = jnp.arange(width, dtype=jnp.int32)
+    inside = ((column >= reach) | (me > 0)) & ((column < axial_cells + reach) | (me < mesh_peers - 1))
+    inside = inside.astype(state0.dtype)
+    owned = ((column >= reach) & (column < axial_cells + reach)).astype(state0.dtype)
+    mode_owned = mode_w * owned
+
+    def rate(state, lower_ghost, upper_ghost, weights):
+        no_col = jnp.zeros_like(state[..., :1])
+        flow = flow_rate(
+            state, no_col, no_col, lower_ghost, upper_ghost, axial_jacobian, pitch_jacobian
+        )
+        return add_field_one(flow, COUPLING * modal_field(weights, mode_w)) * inside
+
+    no_mode_col = jnp.zeros_like(mode_w[..., :1])
+    ms_ga, ms_gp, _ = single_field_grads(mode_w, no_mode_col, no_mode_col)
     ms_rate4 = -(axial_jacobian[4, 1] * ms_ga + pitch_jacobian[4, 1] * ms_gp)
-    coupling_sum = jnp.einsum("mpx,npx->mn", mode_shape, ms_rate4, precision=PRECISE)
-
-    gl1, gu1 = lower_ghosts[0], upper_ghosts[0]
-    gl2, gu2 = lower_ghosts[1], upper_ghosts[1]
-    push0 = COUPLING * modal_field(vel0, mode_shape)
-    rate1 = add_field_one(
-        flow_rate(state0, state0_before, state0_after, gl1, gu1, axial_jacobian, pitch_jacobian),
-        push0,
-    )
-    mid1 = state0 + h * rate1
-    m_before, m_after = halo(mid1)
-    rate1b = add_field_one(
-        flow_rate(mid1, m_before, m_after, gl1, gu1, axial_jacobian, pitch_jacobian), push0
-    )
-    base1 = state0 + 0.5 * h * (rate1 + rate1b)
-    b_before, b_after = halo(base1)
-    rate2_base = flow_rate(base1, b_before, b_after, gl2, gu2, axial_jacobian, pitch_jacobian)
+    coupling_sum = jnp.einsum("mpx,npx->mn", mode_owned, ms_rate4, precision=PRECISE)
+
+    gl1, gu1 = lower_w[0], upper_w[0]
+    gl2, gu2 = lower_w[1], upper_w[1]
+    rate1 = rate(state0_w, gl1, gu1, vel0)
+    mid1 = state0_w + h * rate1
+    rate1b = rate(mid1, gl1, gu1, vel0)
+    base1 = state0_w + 0.5 * h * (rate1 + rate1b)
+    rate2_base4 = rate_field4(base1, gl2, gu2, axial_jacobian, pitch_jacobian)
 
     partials = jnp.concatenate(
         [
-            projection(mode_shape, state0[4]),
-            projection(mode_shape, mid1[4]),
-            projection(mode_shape, base1[4]),
-            projection(mode_shape, rate2_base[4]),
+            projection(mode_owned, state0_w[4]),
+            projection(mode_owned, mid1[4]),
+            projection(mode_owned, base1[4]),
+            projection(mode_owned, rate2_base4),
             coupling_sum.reshape(-1),
         ]
     )
@@ -203,22 +241,18 @@
     acc2 = force2 - blade_stiffness * disp1 - DAMPING * vel1
     disp2m = disp1 + h * vel1
     vel2m = vel1 + h * acc2
-    force2m = force2 + h * force3 + h * (0.5 * h * h * COUPLING) * jnp.dot(couple, acc1, precision=PRECISE)
+    corr = 0.5 * h * h * COUPLING
+    force2m = force2 + h * force3 + h * corr * jnp.dot(couple, acc1, precision=PRECISE)
     acc2m = force2m - blade_stiffness * disp2m - DAMPING * vel2m
     disp2 = disp1 + 0.5 * h * (vel1 + vel2m)
     vel2 = vel1 + 0.5 * h * (acc2 + acc2m)
 
-    corr = 0.5 * h * h * COUPLING
-    state1 = add_field_one(base1, corr * modal_field(acc1, mode_shape))
-    rate2 = rate2_base + corr * zero_ghost_rate_one(acc1)
-    rate2 = add_field_one(rate2, COUPLING * modal_field(vel1, mode_shape))
+    state1 = add_field_one(base1, corr * modal_field(acc1, mode_w))
+    rate2 = rate(state1, gl2, gu2, vel1)
     mid2 = state1 + h * rate2
-    m2_before, m2_after = halo(mid2)
-    rate2b = add_field_one(
-        flow_rate(mid2, m2_before, m2_after, gl2, gu2, axial_jacobian, pitch_jacobian),
-        COUPLING * modal_field(vel2m, mode_shape),
-    )
+    rate2b = rate(mid2, gl2, gu2, vel2m)
     state2 = state1 + 0.5 * h * (rate2 + rate2b)
+    state2 = state2[..., reach : reach + axial_cells]
     return (state2[None], disp2[None], vel2[None])
 
 

time: 97.3 us -> 89.5 us (0.920)
  waiting for transfers between devices: 34.6 us -> 6.44 us
  local copies, waits for them, and re-layouts: 3.79 us -> 13.2 us
  matrix products: 23.2 us -> 30.8 us
  starting transfers between devices: 18.6 us -> 11.1 us
  other arithmetic: 13.6 us -> 19.7 us
  between operations: 2.38 us -> 7.84 us
    ppermute x10 -> x4, waiting for transfers between devices: 29.6 us -> 2.6 us  [shifted(): lax.ppermute(value, axis, [(i, (i + by) % peers) for i in range(peers)])]
    ppermute x10 -> x4, starting transfers between devices: 16.8 us -> 7.56 us  [shifted(): lax.ppermute(value, axis, [(i, (i + by) % peers) for i in range(peers)])]
    sub x4, other arithmetic: 2.27 us -> 5.8 us  [flow_rate(): return DIFFUSION * laplacian - flux]
    dot_general x4, matrix products: 7.67 us -> 11 us  [projection(): return jnp.einsum('mpx,px->m', mode_shape, field, precision=PRECISE)]
    dot_general x4, matrix products: 4.19 us -> 6.53 us  [flow_rate(): jnp.einsum('ij,jpx->ipx', pitch_jacobian, grad_pitch, precision=PRECISE)]
    reshape x0 -> x22, local copies, waits for them, and re-layouts: none -> 1.88 us  [the longest x14 1.18 us: unpack(): out.append(buffer[offset:offset + count].reshape(shape))]
    slice x8 -> x23, local copies, waits for them, and re-layouts: 0.91 us -> 2.72 us  [the longest x1 0.99 us: on_device(): state0_w[4]]
    ppermute x2, starting transfers between devices: 1.88 us -> 3.56 us  [mesh_sum(): lax.ppermute(value, 'mesh', [(i, i ^ step) for i in range(peers)])]
  transfers between devices with their start and end apart: 12 -> 6, of which waited for: 10 -> 4; matrix products, arithmetic and copies ran while one was open for 14% -> 4% of each run, Pallas kernels for 0% -> 0%
where the time goes in v3:
time: 89.5 us; the launch traced here: 89.1 us
  matrix products  30.8 us (34%)
  other arithmetic  19.7 us (22%)
  local copies, waits for them, and re-layouts  13.2 us (15%)
  starting transfers between devices  11.1 us (12%)
  between operations  7.84 us (9%)
  waiting for transfers between devices  6.44 us (7%)
    dot_general x4, matrix products, projection(): return jnp.einsum('mpx,px->m', mode_shape, field, precision=PRECISE)  11 us
    ppermute x4, starting transfers between devices, shifted(): lax.ppermute(value, axis, [(i, (i + by) % peers) for i in range(peers)])  7.56 us
    dot_general x4, matrix products, flow_rate(): jnp.einsum('ij,jpx->ipx', pitch_jacobian, grad_pitch, precision=PRECISE)  6.53 us
    sub x4, other arithmetic, flow_rate(): return DIFFUSION * laplacian - flux  5.8 us
    dot_general x4, matrix products, flow_rate(): jnp.einsum('ij,jpx->ipx', axial_jacobian, grad_axial, precision=PRECISE)  5.69 us
    ppermute x2, waiting for transfers between devices, mesh_sum(): lax.ppermute(value, 'mesh', [(i, i ^ step) for i in range(peers)])  3.83 us
    dot_general x1, matrix products, on_device(): jnp.einsum('mpx,npx->mn', mode_owned, ms_rate4, precision=PRECISE)  3.8 us
    ppermute x2, starting transfers between devices, mesh_sum(): lax.ppermute(value, 'mesh', [(i, i ^ step) for i in range(peers)])  3.56 us
  transfers between devices with their start and end apart: 6, of which 4 were waited for; matrix products, arithmetic and copies ran while one was open for 4% of the time, Pallas kernels for 0%

profile of v3, /device:TPU:0, one launch (start us, length us, event | category | flops | bytes accessed | tf_op | source)
XLA Modules:
  0.0 89.1 jit_solution(8231627217244190154)
XLA Ops:
  0.7 1.4 %fusion.65 = (s32[]{:T(128)}, s32[]{:T(128)}) fusion(s32[8]{0:T(128)} %param.24, s32[]{:T(128)S(6)} %select_n.62, s32[8]{0:T(128)} %param.25, s32[]{:T(128)S(6)} %select_n.68), kind=kLoop, calls=%fused_computation.166 | loop fusion | flops 46 | bytes 80 | tf_op jit(solution)/shard_map/reduce_sum | solution.py:56
  4.7 1.1 %fusion.35 = (f32[5,256]{1,0:T(8,128)S(1)}, f32[5,256]{1,0:T(8,128)S(1)}) fusion(f32[1,64,5,256]{3,1,2,0:T(8,128)} %param.23, pred[64]{0:T(512)(128)(4,1)S(1)} %iota_compare_fusion.5, pred[64]{0:T(512)(128)(4,1)S(1)} %iota_compare_fusion.4), kind=kLoop, calls=%fused_computation.113 | loop fusion | flops 325120 | bytes 338048 | tf_op jit(solution)/shard_map/reduce_sum | solution.py:50
  5.9 0.5 collective-permute-start
  9.0 1.1 %fusion.33 = (f32[5,256]{1,0:T(8,128)S(1)}, f32[5,256]{1,0:T(8,128)S(1)}) fusion(f32[1,64,5,256]{3,1,2,0:T(8,128)} %param.22, pred[64]{0:T(512)(128)(4,1)S(1)} %iota_compare_fusion.3, pred[64]{0:T(512)(128)(4,1)S(1)} %iota_compare_fusion.2), kind=kLoop, calls=%fused_computation.109 | loop fusion | flops 325120 | bytes 338048 | tf_op jit(solution)/shard_map/reduce_sum | solution.py:50
  10.2 4.1 %collective-permute-start.1 = (f32[2,5,256]{2,0,1:T(2,128)S(1)}, f32[2,5,256]{2,0,1:T(2,128)S(1)}, u32[]{:S(2)}, u32[]{:S(2)}) collective-permute-start(f32[2,5,256]{2,0,1:T(2,128)S(1)} %pad_maximum_fusion.31), channel_id=1, source_target_pairs={{0,28},{4,0},{8,4},{12,8},{16,12},{20,16},{24,20},{28,24},{1,29},{... | collective-permute-start | bytes 30728 | tf_op jit(solution)/shard_map/ppermute | solution.py:20
  14.3 0.2 copy.220
  15.1 0.6 slice.392
  15.7 0.6 slice.395
  18.2 2.0 %collective-permute-start.2 = (f32[884,4]{0,1:T(4,128)S(1)}, f32[884,4]{0,1:T(4,128)S(1)}, u32[]{:S(2)}, u32[]{:S(2)}) collective-permute-start(f32[884,4]{0,1:T(4,128)S(1)} %pad_maximum_fusion.28), channel_id=1, source_target_pairs={{0,1},{1,2},{2,3},{3,0},{4,5},{5,6},{6,7},{7,4},{8,9},{9,10},{10,1... | collective-permute-start | bytes 42440 | tf_op jit(solution)/shard_map/ppermute | solution.py:20
  20.6 1.0 %collective-permute-start.3 = (f32[884,4]{0,1:T(4,128)S(1)}, f32[884,4]{0,1:T(4,128)S(1)}, u32[]{:S(2)}, u32[]{:S(2)}) collective-permute-start(f32[884,4]{0,1:T(4,128)S(1)} %pad_maximum_fusion.29), channel_id=1, source_target_pairs={{0,3},{1,0},{2,1},{3,2},{4,7},{5,4},{6,5},{7,6},{8,11},{9,8},{10,9... | collective-permute-start | bytes 42440 | tf_op jit(solution)/shard_map/ppermute | solution.py:20
  21.6 1.2 %collective-permute-done.2 = f32[884,4]{0,1:T(4,128)S(1)} collective-permute-done((f32[884,4]{0,1:T(4,128)S(1)}, f32[884,4]{0,1:T(4,128)S(1)}, u32[]{:S(2)}, u32[]{:S(2)}) %collective-permute-start.2) | collective-permute-done | bytes 14176 | tf_op jit(solution)/shard_map/ppermute | solution.py:20
  23.0 1.4 %collective-permute-done.3 = f32[884,4]{0,1:T(4,128)S(1)} collective-permute-done((f32[884,4]{0,1:T(4,128)S(1)}, f32[884,4]{0,1:T(4,128)S(1)}, u32[]{:S(2)}, u32[]{:S(2)}) %collective-permute-start.3) | collective-permute-done | bytes 14176 | tf_op jit(solution)/shard_map/ppermute | solution.py:20
  24.5 0.1 copy.300
  24.6 0.1 copy.301
  24.8 1.1 %broadcast_multiply_fusion.1 = (f32[4,96,264]{2,1,0:T(8,128)}, f32[4,96,264]{2,1,0:T(8,128)S(1)}) fusion(f32[264]{0:T(512)S(1)} %fusion.62, f32[4,96,4]{2,1,0:T(8,128)S(1)} %bitcast.228, f32[4,96,256]{2,1,0:T(8,128)S(1)} %copy-done.1, f32[4,96,4]{2,1,0:T(8,128)S(1)} %bitcast.226), kind=kLoop, calls=%fused_computation.115 | loop fusion | flops 304128 | bytes 1217568 | tf_op jit(solution)/shard_map/mul | solution.py:196
  25.9 1.6 %fusion.30 = (f32[4,96,264]{2,1,0:T(8,128)}, f32[96,264]{1,0:T(8,128)S(1)}) fusion(f32[4,96,264]{2,1,0:T(8,128)S(1)} %get-tuple-element.90, f32[4,96,4]{2,1,0:T(8,128)S(1)} %bitcast.229, f32[4,96,256]{2,1,0:T(8,128)S(1)} %copy-done.1, f32[4,96,4]{2,1,0:T(8,128)S(1)} %bitcast.227, f32[4,96,1]{2,1,0:T(8,128)S(1)} %broadcast_in_dim.45, f32[]{:T(128)} %bitcast.38, ...), kind=kLoop, calls=%fused_computation.92 | loop fusion | flops 1393920 | bytes 1319448 | tf_op jit(solution)/shard_map/neg | solution.py:207
  28.1 0.3 copy.237
  28.8 0.3 copy.240
  29.3 0.7 subtract_multiply_fusion.8
  30.0 1.1 %fusion.17 = f32[96,264,5]{0,2,1:T(8,128)S(1)} fusion(f32[5,96,264]{1,2,0:T(8,128)S(1)} %get-tuple-element.102, f32[5,5]{1,0:T(8,128)S(1)} %copy-done.11), kind=kOutput, calls=%fused_computation.23 | convolution fusion | flops 7603200 | bytes 1013860 | tf_op jit(solution)/shard_map/ij,jpx->ipx/dot_general | solution.py:80
  31.2 1.1 %fusion.19 = f32[96,264,5]{0,2,1:T(8,128)S(1)} fusion(f32[5,96,264]{1,2,0:T(8,128)S(1)} %get-tuple-element.101, f32[5,5]{1,0:T(8,128)S(1)} %copy-done.12), kind=kOutput, calls=%fused_computation.25 | convolution fusion | flops 7603200 | bytes 1013860 | tf_op jit(solution)/shard_map/ij,jpx->ipx/dot_general | solution.py:79
  32.3 0.8 bitcast_subtract_fusion.3
  33.1 0.2 multiply_add_fusion.2
  33.3 0.7 subtract_multiply_fusion.6
  34.0 1.1 %fusion.13 = f32[96,264,5]{0,2,1:T(8,128)S(1)} fusion(f32[5,96,264]{1,2,0:T(8,128)S(1)} %get-tuple-element.100, f32[5,5]{1,0:T(8,128)S(1)} %copy-done.11), kind=kOutput, calls=%fused_computation.19 | convolution fusion | flops 7603200 | bytes 1013860 | tf_op jit(solution)/shard_map/ij,jpx->ipx/dot_general | solution.py:80
  35.1 1.1 %fusion.15 = f32[96,264,5]{0,2,1:T(8,128)S(1)} fusion(f32[5,96,264]{1,2,0:T(8,128)S(1)} %get-tuple-element.99, f32[5,5]{1,0:T(8,128)S(1)} %copy-done.12), kind=kOutput, calls=%fused_computation.21 | convolution fusion | flops 7603200 | bytes 1013860 | tf_op jit(solution)/shard_map/ij,jpx->ipx/dot_general | solution.py:79
  36.3 0.9 bitcast_subtract_fusion.2
  37.2 1.2 %pad_maximum_fusion.18 = (f32[5,96,264]{1,2,0:T(8,128)}, f32[5,96,264]{1,2,0:T(8,128)S(1)}) fusion(f32[5,96,4]{1,2,0:T(4,128)S(1)} %copy.230, f32[5,96,256]{1,2,0:T(8,128)S(1)} %bitcast.224, f32[5,96,4]{1,2,0:T(4,128)S(1)} %copy.229, f32[5,96,264]{1,2,0:T(8,128)S(1)} %fusion.49, f32[5,96,264]{1,2,0:T(8,128)S(1)} %fusion.50, f32[264]{0:T(512)S(1)} %fusion.64), kind=kLoop, calls=%fused_computation.55 | loop fusion | flops 887040 | bytes 2535456 | tf_op jit(solution)/shard_map/concatenate | solution.py:187
  38.3 0.3 copy.253
  38.6 0.3 copy.254
  38.9 0.7 slice.433
  39.6 0.7 fusion.22
  40.2 1.1 %fusion.3 = f32[1,96,264]{1,0,2:T(1,128)S(1)} fusion(f32[5,96,264]{1,2,0:T(8,128)S(1)} %get-tuple-element.96, f32[5,5]{1,0:T(8,128)S(1)} %copy-done.12), kind=kOutput, calls=%fused_computation.9 | convolution fusion | flops 1520640 | bytes 777728 | tf_op jit(solution)/shard_map/j,jpx->px/dot_general | solution.py:125
  41.4 2.0 %fusion.1 = f32[1,96,264]{1,0,2:T(1,128)} fusion(f32[5,96,264]{1,2,0:T(8,128)S(1)} %get-tuple-element.95, f32[5,5]{1,0:T(8,128)S(1)} %copy-done.11), kind=kOutput, calls=%fused_computation.7 | convolution fusion | flops 1520640 | bytes 777728 | tf_op jit(solution)/shard_map/j,jpx->px/dot_general | solution.py:126
  43.3 1.4 %copy.259 = f32[4,96,264]{1,0,2:T(4,128)S(1)} copy(f32[4,96,264]{2,1,0:T(8,128)} %get-tuple-element.89) | data formatting | bytes 811008 | tf_op jit(solution)/shard_map/mul | solution.py:196
  44.8 0.2 fusion.43
  44.9 2.5 %convolution_bitcast_fusion.2 = f32[4]{0:T(128)S(1)} fusion(f32[4,96,264]{1,0,2:T(4,128)S(1)} %copy.259, f32[96,264,1]{0,2,1:T(1,128)S(1)} %bitcast.234), kind=kOutput, calls=%fused_computation.2 | convolution fusion | flops 1216512 | bytes 506896 | tf_op jit(solution)/shard_map/mpx,px->m/dot_general | solution.py:105
  47.5 2.5 %convolution_bitcast_fusion.3 = f32[4]{0:T(128)S(1)} fusion(f32[4,96,264]{1,0,2:T(4,128)S(1)} %copy.259, f32[96,264,1]{0,2,1:T(1,128)S(1)} %bitcast.235), kind=kOutput, calls=%fused_computation.3 | convolution fusion | flops 1216512 | bytes 506896 | tf_op jit(solution)/shard_map/mpx,px->m/dot_general | solution.py:105
  49.9 1.0 %slice.431 = f32[1,96,264]{1,2,0:T(8,128)S(1)} slice(f32[5,96,264]{1,2,0:T(8,128)} %get-tuple-element.97), slice={[4:5], [0:96], [0:264]} | slice | bytes 202752 | tf_op jit(solution)/shard_map/slice | solution.py:220
  50.9 3.5 %convolution_bitcast_fusion.5 = f32[4]{0:T(128)S(1)} fusion(f32[4,96,264]{1,0,2:T(4,128)} %copy-done.3, f32[96,264,1]{0,2,1:T(1,128)S(1)} %bitcast.236), kind=kOutput, calls=%fused_computation.5 | convolution fusion | flops 1216512 | bytes 506896 | tf_op jit(solution)/shard_map/mpx,px->m/dot_general | solution.py:105
  54.5 2.5 %convolution_bitcast_fusion.4 = f32[4]{0:T(128)S(1)} fusion(f32[4,96,264]{1,0,2:T(4,128)S(1)} %copy-done.4, f32[96,264,1]{0,2,1:T(1,128)S(1)} %bitcast.225), kind=kOutput, calls=%fused_computation.4 | convolution fusion | flops 1216512 | bytes 506896 | tf_op jit(solution)/shard_map/mpx,px->m/dot_general | solution.py:105
  57.0 1.1 %copy.260 = f32[4,96,264]{1,0,2:T(4,128)} copy(f32[4,96,264]{2,1,0:T(8,128)S(1)} %copy-done.2) | data formatting | bytes 811008 | tf_op jit(solution)/shard_map/neg | solution.py:207
  58.1 3.8 %convolution_bitcast_fusion = f32[4,4]{1,0:T(4,128)S(1)} fusion(f32[4,96,264]{1,0,2:T(4,128)} %copy-done.3, f32[4,96,264]{1,0,2:T(4,128)} %copy.260), kind=kOutput, calls=%fused_computation | convolution fusion | flops 4866048 | bytes 811072 | tf_op jit(solution)/shard_map/mpx,npx->mn/dot_general | solution.py:208
  62.0 2.4 %collective-permute-start.4 = (f32[32]{0:T(128)S(1)}, f32[32]{0:T(128)S(1)}, u32[]{:S(2)}, u32[]{:S(2)}) collective-permute-start(f32[32]{0:T(128)S(1)} %concatenate.143), channel_id=1, source_target_pairs={{0,1},{1,0},{2,3},{3,2},{4,5},{5,4},{6,7},{7,6},{8,9},{9,8},{10,11... | collective-permute-start | bytes 392 | tf_op jit(solution)/shard_map/ppermute | solution.py:39
  64.5 1.5 %collective-permute-done.4 = f32[32]{0:T(128)S(1)} collective-permute-done((f32[32]{0:T(128)S(1)}, f32[32]{0:T(128)S(1)}, u32[]{:S(2)}, u32[]{:S(2)}) %collective-permute-start.4) | collective-permute-done | bytes 160 | tf_op jit(solution)/shard_map/ppermute | solution.py:39
  66.0 1.2 %collective-permute-start.5 = (f32[32]{0:T(128)S(1)}, f32[32]{0:T(128)S(1)}, u32[]{:S(2)}, u32[]{:S(2)}) collective-permute-start(f32[32]{0:T(128)S(1)} %add.263), channel_id=1, source_target_pairs={{0,2},{1,3},{2,0},{3,1},{4,6},{5,7},{6,4},{7,5},{8,10},{9,11},{10,... | collective-permute-start | bytes 392 | tf_op jit(solution)/shard_map/ppermute | solution.py:39
  67.2 2.3 %collective-permute-done.5 = f32[32]{0:T(128)S(1)} collective-permute-done((f32[32]{0:T(128)S(1)}, f32[32]{0:T(128)S(1)}, u32[]{:S(2)}, u32[]{:S(2)}) %collective-permute-start.5) | collective-permute-done | bytes 160 | tf_op jit(solution)/shard_map/ppermute | solution.py:39
  69.6 0.7 mul.286
  70.3 0.6 add_bitcast_fusion.1
  70.9 0.9 multiply_reduce_fusion
  71.9 0.7 subtract_multiply_fusion.3
  72.6 1.3 %fusion.11 = f32[96,264,5]{0,2,1:T(8,128)S(1)} fusion(f32[5,96,264]{1,2,0:T(8,128)S(1)} %get-tuple-element.93, f32[5,5]{1,0:T(8,128)S(1)} %copy-done.12), kind=kOutput, calls=%fused_computation.17 | convolution fusion | flops 7603200 | bytes 1013860 | tf_op jit(solution)/shard_map/ij,jpx->ipx/dot_general | solution.py:79
  74.0 2.1 %fusion.9 = f32[96,264,5]{0,2,1:T(8,128)} fusion(f32[5,96,264]{1,2,0:T(8,128)S(1)} %get-tuple-element.94, f32[5,5]{1,0:T(8,128)S(1)} %copy-done.11), kind=kOutput, calls=%fused_computation.15 | convolution fusion | flops 7603200 | bytes 1013860 | tf_op jit(solution)/shard_map/ij,jpx->ipx/dot_general | solution.py:80
  76.1 0.8 copy.293
  76.9 1.9 %bitcast_subtract_fusion.1 = f32[5,96,264]{1,2,0:T(8,128)S(1)} fusion(f32[96,264,5]{0,2,1:T(8,128)} %fusion.9, f32[96,264,5]{0,2,1:T(8,128)S(1)} %fusion.11, f32[5,96,264]{1,2,0:T(8,128)S(1)} %fusion.48, f32[5,1,264]{1,2,0:T(8,128)S(1)} %copy.253, f32[5,1,264]{1,2,0:T(8,128)S(1)} %copy.254), kind=kLoop, calls=%fused_computation.61 | loop fusion | flops 1267200 | bytes 2038080 | tf_op jit(solution)/shard_map/sub | solution.py:81
  78.8 0.2 multiply_add_fusion
  79.0 0.7 subtract_multiply_fusion.1
  79.7 2.1 %fusion.5 = f32[96,264,5]{0,2,1:T(8,128)} fusion(f32[5,96,264]{1,2,0:T(8,128)S(1)} %get-tuple-element.92, f32[5,5]{1,0:T(8,128)S(1)} %copy-done.11), kind=kOutput, calls=%fused_computation.11 | convolution fusion | flops 7603200 | bytes 1013860 | tf_op jit(solution)/shard_map/ij,jpx->ipx/dot_general | solution.py:80
  81.9 2.1 %fusion.7 = f32[96,264,5]{0,2,1:T(8,128)} fusion(f32[5,96,264]{1,2,0:T(8,128)S(1)} %get-tuple-element.91, f32[5,5]{1,0:T(8,128)S(1)} %copy-done.12), kind=kOutput, calls=%fused_computation.13 | convolution fusion | flops 7603200 | bytes 1013860 | tf_op jit(solution)/shard_map/ij,jpx->ipx/dot_general | solution.py:79
  84.0 0.8 copy.297
  84.7 2.2 %bitcast_subtract_fusion = f32[5,96,264]{1,2,0:T(8,128)S(1)} fusion(f32[96,264,5]{0,2,1:T(8,128)} %fusion.5, f32[96,264,5]{0,2,1:T(8,128)} %fusion.7, f32[5,96,264]{1,2,0:T(8,128)S(1)} %get-tuple-element.87, f32[5,1,264]{1,2,0:T(8,128)S(1)} %copy.253, f32[5,1,264]{1,2,0:T(8,128)S(1)} %copy.254), kind=kLoop, calls=%fused_computation.60 | loop fusion | flops 1267200 | bytes 2038080 | tf_op jit(solution)/shard_map/sub | solution.py:81
  87.0 0.3 fusion.25
  87.4 1.0 %copy.273 = f32[1,5,96,256]{3,2,1,0:T(8,128)} copy(f32[1,5,96,256]{2,3,1,0:T(8,128)S(1)} %fusion.25) | data formatting | bytes 983040
  88.4 0.7 add_bitcast_fusion
  (123 shorter events, 3.9 us)
Async XLA Ops:
  0.6 13.6 %copy-start.9 = (f32[1,5,96,256]{3,2,1,0:T(8,128)S(1)}, f32[1,5,96,256]{3,2,1,0:T(8,128)}, u32[]{:S(2)}) copy-start(f32[1,5,96,256]{3,2,1,0:T(8,128)} %param.21) | copy-start | bytes 1474564
  0.6 13.9 %copy-start.1 = (f32[4,96,256]{2,1,0:T(8,128)S(1)}, f32[4,96,256]{2,1,0:T(8,128)}, u32[]{:S(2)}) copy-start(f32[4,96,256]{2,1,0:T(8,128)} %param.28) | copy-start | bytes 1179652
  5.9 11.7 %collective-permute-start = (f32[2,5,256]{2,0,1:T(2,128)S(1)}, f32[2,5,256]{2,0,1:T(2,128)S(1)}, u32[]{:S(2)}, u32[]{:S(2)}) collective-permute-start(f32[2,5,256]{2,0,1:T(2,128)S(1)} %pad_maximum_fusion.30), channel_id=1, source_target_pairs={{0,4},{4,8},{8,12},{12,16},{16,20},{20,24},{24,28},{28,0},{1,5},{5... | collective-permute-start | bytes 30728 | tf_op jit(solution)/shard_map/ppermute | solution.py:20
  10.2 7.7 %collective-permute-start.1 = (f32[2,5,256]{2,0,1:T(2,128)S(1)}, f32[2,5,256]{2,0,1:T(2,128)S(1)}, u32[]{:S(2)}, u32[]{:S(2)}) collective-permute-start(f32[2,5,256]{2,0,1:T(2,128)S(1)} %pad_maximum_fusion.31), channel_id=1, source_target_pairs={{0,28},{4,0},{8,4},{12,8},{16,12},{20,16},{24,20},{28,24},{1,29},{... | collective-permute-start | bytes 30728 | tf_op jit(solution)/shard_map/ppermute | solution.py:20
  14.3 0.8 copy-start.12
  14.3 1.4 %copy-start.11 = (f32[5,5]{1,0:T(8,128)S(1)}, f32[5,5]{1,0:T(8,128)}, u32[]{:S(2)}) copy-start(f32[5,5]{1,0:T(8,128)} %param.27) | copy-start | bytes 304
  18.2 4.6 %collective-permute-start.2 = (f32[884,4]{0,1:T(4,128)S(1)}, f32[884,4]{0,1:T(4,128)S(1)}, u32[]{:S(2)}, u32[]{:S(2)}) collective-permute-start(f32[884,4]{0,1:T(4,128)S(1)} %pad_maximum_fusion.28), channel_id=1, source_target_pairs={{0,1},{1,2},{2,3},{3,0},{4,5},{5,6},{6,7},{7,4},{8,9},{9,10},{10,1... | collective-permute-start | bytes 42440 | tf_op jit(solution)/shard_map/ppermute | solution.py:20
  20.6 3.7 %collective-permute-start.3 = (f32[884,4]{0,1:T(4,128)S(1)}, f32[884,4]{0,1:T(4,128)S(1)}, u32[]{:S(2)}, u32[]{:S(2)}) collective-permute-start(f32[884,4]{0,1:T(4,128)S(1)} %pad_maximum_fusion.29), channel_id=1, source_target_pairs={{0,3},{1,0},{2,1},{3,2},{4,7},{5,4},{6,5},{7,6},{8,11},{9,8},{10,9... | collective-permute-start | bytes 42440 | tf_op jit(solution)/shard_map/ppermute | solution.py:20
  22.8 3.1 %copy-start.13 = (f32[884,4]{0,1:T(4,128)}, f32[884,4]{0,1:T(4,128)S(1)}, u32[]{:S(2)}) copy-start(f32[884,4]{0,1:T(4,128)S(1)} %broadcast_select_fusion.1) | copy-start | bytes 42436
  24.3 1.5 %copy-start.14 = (f32[884,4]{0,1:T(4,128)}, f32[884,4]{0,1:T(4,128)S(1)}, u32[]{:S(2)}) copy-start(f32[884,4]{0,1:T(4,128)S(1)} %broadcast_select_fusion) | copy-start | bytes 42436
  24.8 1.1 %copy-start.15 = (f32[1,4]{1,0:T(1,128)S(1)}, f32[1,4]{1,0:T(1,128)}, u32[]{:S(2)}) copy-start(f32[1,4]{1,0:T(1,128)} %param.31) | copy-start | bytes 52
  27.5 1.6 %slice-start.1 = ((f32[884,4]{0,1:T(4,128)}), f32[480,4]{0,1:T(4,128)S(1)}, s32[]{:S(2)}) async-start(f32[884,4]{0,1:T(4,128)} %copy-done.13), calls=%async_computation.1 | async-start | bytes 16384 | tf_op jit(solution)/shard_map/slice | solution.py:139
  27.5 1.7 %slice-start.2 = ((f32[884,4]{0,1:T(4,128)}), f32[480,4]{0,1:T(4,128)S(1)}, s32[]{:S(2)}) async-start(f32[884,4]{0,1:T(4,128)} %copy-done.14), calls=%async_computation.2 | async-start | bytes 16384 | tf_op jit(solution)/shard_map/slice | solution.py:139
  33.3 3.0 %copy-start = (f32[5,96,264]{1,2,0:T(8,128)}, f32[5,96,264]{1,2,0:T(8,128)S(1)}, u32[]{:S(2)}) copy-start(f32[5,96,264]{1,2,0:T(8,128)S(1)} %multiply_add_fusion.2) | copy-start | bytes 1520644
  43.3 1.4 %copy-start.6 = (f32[1,96,264]{1,0,2:T(1,128)S(1)}, f32[1,96,264]{1,0,2:T(1,128)}, u32[]{:S(2)}) copy-start(f32[1,96,264]{1,0,2:T(1,128)} %fusion.1) | copy-start | bytes 304132
  44.7 2.7 %copy-start.3 = (f32[4,96,264]{1,0,2:T(4,128)}, f32[4,96,264]{1,0,2:T(4,128)S(1)}, u32[]{:S(2)}) copy-start(f32[4,96,264]{1,0,2:T(4,128)S(1)} %copy.259) | copy-start | bytes 1216516
  44.7 2.7 %copy-start.10 = (f32[1,96,264]{1,2,0:T(8,128)S(1)}, f32[1,96,264]{1,2,0:T(8,128)}, u32[]{:S(2)}) copy-start(f32[1,96,264]{1,2,0:T(8,128)} %slice.433) | copy-start | bytes 304132
  47.4 7.1 %slice-start = ((f32[5,96,264]{1,2,0:T(8,128)}), f32[1,96,264]{1,2,0:T(8,128)S(1)}, s32[]{:S(2)}) async-start(f32[5,96,264]{1,2,0:T(8,128)} %copy-done), calls=%async_computation | async-start | bytes 270336 | tf_op jit(solution)/shard_map/slice | solution.py:221
  49.9 4.6 %copy-start.4 = (f32[4,96,264]{1,0,2:T(4,128)S(1)}, f32[4,96,264]{1,0,2:T(4,128)}, u32[]{:S(2)}) copy-start(f32[4,96,264]{1,0,2:T(4,128)} %copy-done.3) | copy-start | bytes 1216516
  50.9 6.1 %copy-start.2 = (f32[4,96,264]{2,1,0:T(8,128)S(1)}, f32[4,96,264]{2,1,0:T(8,128)}, u32[]{:S(2)}) copy-start(f32[4,96,264]{2,1,0:T(8,128)} %get-tuple-element.105) | copy-start | bytes 1216516
  57.0 13.3 %copy-start.19 = (f32[1,4]{1,0:T(1,128)S(1)}, f32[1,4]{1,0:T(1,128)}, u32[]{:S(2)}) copy-start(f32[1,4]{1,0:T(1,128)} %param.30) | copy-start | bytes 52
  57.0 13.3 %copy-start.20 = (f32[1,4]{1,0:T(1,128)S(1)}, f32[1,4]{1,0:T(1,128)}, u32[]{:S(2)}) copy-start(f32[1,4]{1,0:T(1,128)} %param.29) | copy-start | bytes 52
  62.0 3.9 %collective-permute-start.4 = (f32[32]{0:T(128)S(1)}, f32[32]{0:T(128)S(1)}, u32[]{:S(2)}, u32[]{:S(2)}) collective-permute-start(f32[32]{0:T(128)S(1)} %concatenate.143), channel_id=1, source_target_pairs={{0,1},{1,0},{2,3},{3,2},{4,5},{5,4},{6,7},{7,6},{8,9},{9,8},{10,11... | collective-permute-start | bytes 392 | tf_op jit(solution)/shard_map/ppermute | solution.py:39
  66.0 3.5 %collective-permute-start.5 = (f32[32]{0:T(128)S(1)}, f32[32]{0:T(128)S(1)}, u32[]{:S(2)}, u32[]{:S(2)}) collective-permute-start(f32[32]{0:T(128)S(1)} %add.263), channel_id=1, source_target_pairs={{0,2},{1,3},{2,0},{3,1},{4,6},{5,7},{6,4},{7,5},{8,10},{9,11},{10,... | collective-permute-start | bytes 392 | tf_op jit(solution)/shard_map/ppermute | solution.py:39
  70.9 1.7 %copy-start.16 = (f32[4]{0:T(128)}, f32[4]{0:T(128)S(1)}, u32[]{:S(2)}) copy-start(f32[4]{0:T(128)S(1)} %get-tuple-element.86) | copy-start | bytes 52
  73.9 2.2 %copy-start.5 = (f32[96,264]{1,0:T(8,128)S(1)}, f32[96,264]{1,0:T(8,128)}, u32[]{:S(2)}) copy-start(f32[96,264]{1,0:T(8,128)} %get-tuple-element.76) | copy-start | bytes 304132
  76.9 1.9 %copy-start.8 = (f32[96,264]{0,1:T(8,128)S(1)}, f32[96,264]{0,1:T(8,128)}, u32[]{:S(2)}) copy-start(f32[96,264]{0,1:T(8,128)} %copy.293) | copy-start | bytes 304132
  84.7 2.2 %copy-start.7 = (f32[96,264]{0,1:T(8,128)S(1)}, f32[96,264]{0,1:T(8,128)}, u32[]{:S(2)}) copy-start(f32[96,264]{0,1:T(8,128)} %copy.297) | copy-start | bytes 304132
  87.4 1.1 %copy-start.17 = (f32[4]{0:T(128)S(1)}, f32[4]{0:T(128)}, u32[]{:S(2)}) copy-start(f32[4]{0:T(128)} %copy-done.16) | copy-start | bytes 52
  87.4 1.0 %copy-start.18 = (f32[4,4]{1,0:T(4,128)S(1)}, f32[4,4]{1,0:T(4,128)}, u32[]{:S(2)}) copy-start(f32[4,4]{1,0:T(4,128)} %mul.286) | copy-start | bytes 196
  87.4 1.0 %copy-start.21 = (f32[1,4]{1,0:T(1,128)S(1)}, f32[1,4]{1,0:T(1,128)}, u32[]{:S(2)}) copy-start(f32[1,4]{1,0:T(1,128)} %param.29) | copy-start | bytes 52
  87.4 1.0 %copy-start.22 = (f32[4]{0:T(128)S(1)}, f32[4]{0:T(128)}, u32[]{:S(2)}) copy-start(f32[4]{0:T(128)} %get-tuple-element.84) | copy-start | bytes 52

commit v4 on v3

--- a/solution.py
+++ b/solution.py
@@ -3,6 +3,8 @@
 import jax
 import jax.numpy as jnp
 from jax import lax
+from jax.experimental import pallas as pl
+from jax.experimental.pallas import tpu as pltpu
 from jax.sharding import PartitionSpec as P
 
 STEP_COUNT = 2
@@ -139,6 +141,141 @@
         out.append(buffer[offset : offset + count].reshape(shape))
         offset += count
     return out
+
+
+LANES = 128
+
+
+def lane_roll(x, shift):
+    return pltpu.roll(x, shift % x.shape[-1], x.ndim - 1)
+
+
+def row_roll(x, shift):
+    return pltpu.roll(x, shift % x.shape[0], 0)
+
+
+def kernel_rate(state, lower, upper, jac, push, inside, fields_out):
+    ax, pt = jac
+    rows = state[0].shape[0]
+    row = lax.broadcasted_iota(jnp.int32, state[0].shape, 0)
+    grads_a, grads_p, laps = [], [], []
+    for j, s in enumerate(state):
+        east = lane_roll(s, -1)
+        west = lane_roll(s, 1)
+        north = jnp.where(row == rows - 1, upper[j], row_roll(s, -1))
+        south = jnp.where(row == 0, lower[j], row_roll(s, 1))
+        grads_a.append(0.5 * (east - west))
+        grads_p.append(0.5 * (north - south))
+        laps.append(east + west + north + south - 4.0 * s)
+    out = []
+    for i in fields_out:
+        r = DIFFUSION * laps[i]
+        for j in range(len(state)):
+            r = r - ax[i][j] * grads_a[j] - pt[i][j] * grads_p[j]
+        if i == 1 and push is not None:
+            r = r + push
+        out.append(r * inside)
+    return out
+
+
+def read_jacobians(sc_ref, fields):
+    ax = [[sc_ref[i * fields + j] for j in range(fields)] for i in range(fields)]
+    pt = [[sc_ref[fields * fields + i * fields + j] for j in range(fields)] for i in range(fields)]
+    return ax, pt
+
+
+def lane_fold(x):
+    x = jnp.sum(x, axis=0, keepdims=True)
+    total = x[:, :LANES]
+    for t in range(1, x.shape[1] // LANES):
+        total = total + x[:, t * LANES : (t + 1) * LANES]
+    return total
+
+
+def first_kernel(sc_ref, u_ref, ms_ref, gl_ref, gu_ref, inside_ref, owned_ref, a_ref, part_ref):
+    h = TIME_STEP
+    fields = u_ref.shape[0]
+    modes = ms_ref.shape[0]
+    jac = read_jacobians(sc_ref, fields)
+    base = 2 * fields * fields
+    vel = [sc_ref[base + m] for m in range(modes)]
+    inside = inside_ref[...]
+    owned = owned_ref[...]
+    ms = [ms_ref[m] for m in range(modes)]
+    push = vel[0] * ms[0]
+    for m in range(1, modes):
+        push = push + vel[m] * ms[m]
+    push = COUPLING * push
+    gl1 = [gl_ref[0, j : j + 1, :] for j in range(fields)]
+    gu1 = [gu_ref[0, j : j + 1, :] for j in range(fields)]
+    gl2 = [gl_ref[1, j : j + 1, :] for j in range(fields)]
+    gu2 = [gu_ref[1, j : j + 1, :] for j in range(fields)]
+    every = list(range(fields))
+    u0 = [u_ref[j] for j in range(fields)]
+    k1 = kernel_rate(u0, gl1, gu1, jac, push, inside, every)
+    mid = [u0[j] + h * k1[j] for j in every]
+    k2 = kernel_rate(mid, gl1, gu1, jac, push, inside, every)
+    a = [u0[j] + 0.5 * h * (k1[j] + k2[j]) for j in every]
+    for j in every:
+        a_ref[j] = a[j]
+    (ra4,) = kernel_rate(a, gl2, gu2, jac, None, inside, [4])
+    weighted = [ms[m] * owned for m in range(modes)]
+    k = 0
+    for field in (u0[4], mid[4], a[4], ra4):
+        for m in range(modes):
+            part_ref[k : k + 1, :] = lane_fold(weighted[m] * field)
+            k += 1
+    ax41, pt41 = jac[0][4][1], jac[1][4][1]
+    rows = ms[0].shape[0]
+    row = lax.broadcasted_iota(jnp.int32, ms[0].shape, 0)
+    for n in range(modes):
+        s = ms[n]
+        ga = 0.5 * (lane_roll(s, -1) - lane_roll(s, 1))
+        north = jnp.where(row == rows - 1, 0.0, row_roll(s, -1))
+        south = jnp.where(row == 0, 0.0, row_roll(s, 1))
+        gp = 0.5 * (north - south)
+        t = -(ax41 * ga + pt41 * gp)
+        for m in range(modes):
+            part_ref[k + m * modes + n : k + m * modes + n + 1, :] = lane_fold(weighted[m] * t)
+
+
+def second_kernel(sc_ref, a_ref, ms_ref, gl_ref, gu_ref, inside_ref, out_ref):
+    h = TIME_STEP
+    fields = a_ref.shape[0]
+    modes = ms_ref.shape[0]
+    reach = 2 * STEP_COUNT
+    jac = read_jacobians(sc_ref, fields)
+    base = 2 * fields * fields
+    coef = [[sc_ref[base + w * modes + m] for m in range(modes)] for w in range(3)]
+    inside = inside_ref[...]
+    ms = [ms_ref[m] for m in range(modes)]
+
+    def combine(weights):
+        total = weights[0] * ms[0]
+        for m in range(1, modes):
+            total = total + weights[m] * ms[m]
+        return total
+
+    gl2 = [gl_ref[1, j : j + 1, :] for j in range(fields)]
+    gu2 = [gu_ref[1, j : j + 1, :] for j in range(fields)]
+    every = list(range(fields))
+    s1 = [a_ref[j] for j in every]
+    s1[1] = s1[1] + combine(coef[0])
+    k1 = kernel_rate(s1, gl2, gu2, jac, COUPLING * combine(coef[1]), inside, every)
+    mid = [s1[j] + h * k1[j] for j in every]
+    k2 = kernel_rate(mid, gl2, gu2, jac, COUPLING * combine(coef[2]), inside, every)
+    width = out_ref.shape[-1]
+    for j in every:
+        s2 = s1[j] + 0.5 * h * (k1[j] + k2[j])
+        out_ref[j] = lane_roll(s2, -reach)[:, :width]
+
+
+def vmem_spec():
+    return pl.BlockSpec(memory_space=pltpu.VMEM)
+
+
+def smem_spec():
+    return pl.BlockSpec(memory_space=pltpu.SMEM)
 
 
 def on_device(
@@ -183,48 +320,37 @@
     from_right = shifted(pack([part[..., :reach] for part in own], reach), "mesh", -1)
     from_left = jnp.where(me > 0, from_left, jnp.zeros_like(from_left))
     from_right = jnp.where(me < mesh_peers - 1, from_right, jnp.zeros_like(from_right))
+    def widen(left, part, right):
+        spare = lanes_wide - axial_cells - 2 * reach
+        tail = jnp.zeros(part.shape[:-1] + (spare,), part.dtype)
+        return jnp.concatenate([left, part, right, tail], axis=-1)
+
+    lanes_wide = -(-(axial_cells + 2 * reach) // LANES) * LANES
     wide = [
-        jnp.concatenate([left, part, right], axis=-1)
+        widen(left, part, right)
         for left, part, right in zip(unpack(from_left, shapes), own, unpack(from_right, shapes))
     ]
     state0_w, mode_w, lower_w, upper_w = wide
-    width = axial_cells + 2 * reach
-    column = jnp.arange(width, dtype=jnp.int32)
-    inside = ((column >= reach) | (me > 0)) & ((column < axial_cells + reach) | (me < mesh_peers - 1))
-    inside = inside.astype(state0.dtype)
+    column = jnp.arange(lanes_wide, dtype=jnp.int32)[None, :]
+    inside = (
+        ((column >= reach) | (me > 0))
+        & ((column < axial_cells + reach) | (me < mesh_peers - 1))
+        & (column < axial_cells + 2 * reach)
+    ).astype(state0.dtype)
     owned = ((column >= reach) & (column < axial_cells + reach)).astype(state0.dtype)
-    mode_owned = mode_w * owned
-
-    def rate(state, lower_ghost, upper_ghost, weights):
-        no_col = jnp.zeros_like(state[..., :1])
-        flow = flow_rate(
-            state, no_col, no_col, lower_ghost, upper_ghost, axial_jacobian, pitch_jacobian
-        )
-        return add_field_one(flow, COUPLING * modal_field(weights, mode_w)) * inside
-
-    no_mode_col = jnp.zeros_like(mode_w[..., :1])
-    ms_ga, ms_gp, _ = single_field_grads(mode_w, no_mode_col, no_mode_col)
-    ms_rate4 = -(axial_jacobian[4, 1] * ms_ga + pitch_jacobian[4, 1] * ms_gp)
-    coupling_sum = jnp.einsum("mpx,npx->mn", mode_owned, ms_rate4, precision=PRECISE)
-
-    gl1, gu1 = lower_w[0], upper_w[0]
-    gl2, gu2 = lower_w[1], upper_w[1]
-    rate1 = rate(state0_w, gl1, gu1, vel0)
-    mid1 = state0_w + h * rate1
-    rate1b = rate(mid1, gl1, gu1, vel0)
-    base1 = state0_w + 0.5 * h * (rate1 + rate1b)
-    rate2_base4 = rate_field4(base1, gl2, gu2, axial_jacobian, pitch_jacobian)
-
-    partials = jnp.concatenate(
-        [
-            projection(mode_owned, state0_w[4]),
-            projection(mode_owned, mid1[4]),
-            projection(mode_owned, base1[4]),
-            projection(mode_owned, rate2_base4),
-            coupling_sum.reshape(-1),
-        ]
-    )
-    totals = mesh_sum(partials)
+
+    jac_flat = jnp.concatenate([axial_jacobian.reshape(-1), pitch_jacobian.reshape(-1)])
+    base1, part_lanes = pl.pallas_call(
+        first_kernel,
+        out_shape=(
+            jax.ShapeDtypeStruct(state0_w.shape, state0.dtype),
+            jax.ShapeDtypeStruct((4 * modes + modes * modes, LANES), state0.dtype),
+        ),
+        in_specs=[smem_spec()] + [vmem_spec()] * 6,
+        out_specs=(vmem_spec(), vmem_spec()),
+    )(jnp.concatenate([jac_flat, vel0]), state0_w, mode_w, lower_w, upper_w, inside, owned)
+
+    totals = mesh_sum(jnp.sum(part_lanes, axis=1))
     force0 = force_scale * totals[0:modes]
     force1 = force_scale * totals[modes : 2 * modes]
     force2 = force_scale * totals[2 * modes : 3 * modes]
@@ -247,12 +373,12 @@
     disp2 = disp1 + 0.5 * h * (vel1 + vel2m)
     vel2 = vel1 + 0.5 * h * (acc2 + acc2m)
 
-    state1 = add_field_one(base1, corr * modal_field(acc1, mode_w))
-    rate2 = rate(state1, gl2, gu2, vel1)
-    mid2 = state1 + h * rate2
-    rate2b = rate(mid2, gl2, gu2, vel2m)
-    state2 = state1 + 0.5 * h * (rate2 + rate2b)
-    state2 = state2[..., reach : reach + axial_cells]
+    state2 = pl.pallas_call(
+        second_kernel,
+        out_shape=jax.ShapeDtypeStruct(state0.shape, state0.dtype),
+        in_specs=[smem_spec()] + [vmem_spec()] * 5,
+        out_specs=vmem_spec(),
+    )(jnp.concatenate([jac_flat, corr * acc1, vel1, vel2m]), base1, mode_w, lower_w, upper_w, inside)
     return (state2[None], disp2[None], vel2[None])
 
 

time: 89.5 us -> 52.4 us (0.59)
  matrix products: 30.8 us -> 0.65 us
  other arithmetic: 19.7 us -> 9.17 us
  Pallas kernels: 0 us -> 9.94 us
  local copies, waits for them, and re-layouts: 13.2 us -> 7.41 us
  waiting for transfers between devices: 6.44 us -> 10.6 us
  starting transfers between devices: 11.1 us -> 8.13 us
  between operations: 7.84 us -> 6.07 us
    dot_general x15 -> x0, matrix products: 30.1 us -> none  [the longest x4 11 us: projection(): return jnp.einsum('mpx,px->m', mode_shape, field, precision=PRECISE)]
    pallas_call x0 -> x2, Pallas kernels: none -> 9.94 us  [the longest x1 5.47 us: on_device(): pl.pallas_call(first_kernel, out_shape=(jax.ShapeDtypeStruct(state0_w.sha...]
    sub x5 -> x0, other arithmetic: 5.98 us -> none  [the longest x4 5.8 us: flow_rate(): return DIFFUSION * laplacian - flux]
    mul x6 -> x1, other arithmetic: 4.56 us -> 0.01 us  [on_device(): corr * acc1]
    ppermute x2, starting transfers between devices: 3.56 us -> 0.57 us  [mesh_sum(): lax.ppermute(value, 'mesh', [(i, i ^ step) for i in range(peers)])]
    slice x7 -> x0, local copies, waits for them, and re-layouts: 2.94 us -> none  [the longest x2 1.19 us: on_device(): ms_rate4 = -(axial_jacobian[4, 1] * ms_ga + pitch_jacobian[4, 1] * ms_gp)]
    ppermute x2, waiting for transfers between devices: 3.83 us -> 6.56 us  [mesh_sum(): lax.ppermute(value, 'mesh', [(i, i ^ step) for i in range(peers)])]
    concatenate x3 -> x4, other arithmetic: 1.34 us -> 3.61 us  [the longest x3 3.02 us: widen(): return jnp.concatenate([left, part, right, tail], axis=-1)]
  transfers between devices with their start and end apart: 6 -> 6, of which waited for: 4 -> 4; matrix products, arithmetic and copies ran while one was open for 4% -> 7% of each run, Pallas kernels for 0% -> 0%
where the time goes in v4:
time: 52.4 us; the launch traced here: 51.9 us
  waiting for transfers between devices  10.6 us (20%)
  Pallas kernels  9.94 us (19%)
  other arithmetic  9.17 us (18%)
  starting transfers between devices  8.13 us (16%)
  local copies, waits for them, and re-layouts  7.41 us (14%)
  between operations  6.07 us (12%)
  matrix products  0.65 us (1%)
    ppermute x4, starting transfers between devices, shifted(): lax.ppermute(value, axis, [(i, (i + by) % peers) for i in range(peers)])  7.56 us
    ppermute x2, waiting for transfers between devices, mesh_sum(): lax.ppermute(value, 'mesh', [(i, i ^ step) for i in range(peers)])  6.56 us
    pallas_call x1, Pallas kernels, on_device(): pl.pallas_call(first_kernel, out_shape=(jax.ShapeDtypeStruct(state0_w.sha...  5.47 us
    pallas_call x1, Pallas kernels, on_device(): pl.pallas_call(second_kernel, out_shape=jax.ShapeDtypeStruct(state0.shape...  4.47 us
    ppermute x4, waiting for transfers between devices, shifted(): lax.ppermute(value, axis, [(i, (i + by) % peers) for i in range(peers)])  4.01 us
    concatenate x3, other arithmetic, widen(): return jnp.concatenate([left, part, right, tail], axis=-1)  3.02 us
    unnamed x22, local copies, waits for them, and re-layouts  2.18 us
    reduce_sum x2, other arithmetic, pick_entry(): return jnp.sum(jnp.where(hit, values, jnp.zeros_like(values)))  1.97 us
  transfers between devices with their start and end apart: 6, of which 4 were waited for; matrix products, arithmetic and copies ran while one was open for 7% of the time, Pallas kernels for 0%

profile of v4, /device:TPU:0, one launch (start us, length us, event | category | flops | bytes accessed | tf_op | source)
XLA Modules:
  0.0 51.9 jit_solution(16647906339044970621)
XLA Ops:
  0.7 1.3 %fusion.5 = s32[]{:T(128)} fusion(s32[8]{0:T(128)} %param.14, s32[]{:T(128)S(6)} %select_n.62), kind=kLoop, calls=%fused_computation.24 | loop fusion | flops 23 | bytes 40 | tf_op jit(solution)/shard_map/reduce_sum | solution.py:58
  4.6 1.2 %fusion.3 = (f32[5,256]{1,0:T(8,128)S(1)}, f32[5,256]{1,0:T(8,128)S(1)}) fusion(f32[1,64,5,256]{3,1,2,0:T(8,128)} %param.13, pred[64]{0:T(512)(128)(4,1)S(1)} %get-tuple-element.33, pred[64]{0:T(512)(128)(4,1)S(1)} %get-tuple-element.32), kind=kLoop, calls=%fused_computation.10 | loop fusion | flops 325120 | bytes 338048 | tf_op jit(solution)/shard_map/reduce_sum | solution.py:52
  5.8 0.5 collective-permute-start
  6.3 0.6 %fusion.6 = s32[]{:T(128)} fusion(s32[8]{0:T(128)S(1)} %copy-done.10, s32[]{:T(128)S(6)} %select_n.68), kind=kLoop, calls=%fused_computation.25 | loop fusion | flops 23 | bytes 40 | tf_op jit(solution)/shard_map/reduce_sum | solution.py:58
  9.6 0.1 fusion.1
  9.8 4.1 %collective-permute-start.1 = (f32[2,5,256]{2,1,0:T(8,128)S(1)}, f32[2,5,256]{2,1,0:T(8,128)S(1)}, u32[]{:S(2)}, u32[]{:S(2)}) collective-permute-start(f32[2,5,256]{2,1,0:T(8,128)S(1)} %pad_maximum_fusion.1), channel_id=1, source_target_pairs={{0,28},{4,0},{8,4},{12,8},{16,12},{20,16},{24,20},{28,24},{1,29},{... | collective-permute-start | bytes 30728 | tf_op jit(solution)/shard_map/ppermute | solution.py:22
  13.9 0.1 reshape.145
  14.0 0.1 reshape.146
  14.1 0.1 fusion.22
  14.2 0.1 fusion.21
  14.3 0.6 %and_convert_fusion = (f32[1,384]{1,0:T(1,128)}, f32[1,384]{1,0:T(1,128)}) fusion(pred[]{:T(512)S(6)} %lt.68, pred[]{:T(512)S(6)} %gt.4), kind=kLoop, calls=%fused_computation.20 | loop fusion | flops 3840 | bytes 3074 | tf_op jit(solution)/shard_map/convert_element_type | solution.py:340
  14.9 0.7 %copy-done.7 = f32[1,4]{1,0:T(1,128)S(1)} copy-done((f32[1,4]{1,0:T(1,128)S(1)}, f32[1,4]{1,0:T(1,128)}, u32[]{:S(2)}) %copy-start.7) | copy-done | bytes 40
  15.6 0.6 %pad_maximum_fusion.4.sc_ref = f32[54]{0:T(128)} fusion(f32[4]{0:T(128)S(1)} %bitcast.127, f32[25]{0:T(128)S(1)} %reshape.146, f32[25]{0:T(128)S(1)} %reshape.145), kind=kLoop, calls=%fused_computation.26 | loop fusion | flops 108 | bytes 432 | tf_op jit(solution)/shard_map/concatenate | solution.py:351
  16.2 0.1 copy.17
  16.3 0.1 copy.22
  16.4 0.1 copy.16
  16.5 0.1 copy.21
  16.6 0.1 pad.15.clone
  16.8 0.1 copy.14
  16.9 0.1 reshape.149
  17.0 0.1 copy.19
  17.1 0.1 reshape.154
  17.2 0.1 fusion.24
  17.2 0.1 copy.15
  17.3 0.1 reshape.150
  17.4 0.1 copy.20
  17.5 0.1 reshape.155
  17.6 0.1 pad_maximum_fusion.3
  17.7 2.9 %collective-permute-start.3 = (f32[884,4]{0,1:T(4,128)S(1)}, f32[884,4]{0,1:T(4,128)S(1)}, u32[]{:S(2)}, u32[]{:S(2)}) collective-permute-start(f32[884,4]{0,1:T(4,128)S(1)} %pad_maximum_fusion.3), channel_id=1, source_target_pairs={{0,3},{1,0},{2,1},{3,2},{4,7},{5,4},{6,5},{7,6},{8,11},{9,8},{10,9... | collective-permute-start | bytes 42440 | tf_op jit(solution)/shard_map/ppermute | solution.py:22
  20.6 0.1 pad_maximum_fusion.2
  20.7 1.3 %collective-permute-done.3 = f32[884,4]{0,1:T(4,128)S(1)} collective-permute-done((f32[884,4]{0,1:T(4,128)S(1)}, f32[884,4]{0,1:T(4,128)S(1)}, u32[]{:S(2)}, u32[]{:S(2)}) %collective-permute-start.3) | collective-permute-done | bytes 14176 | tf_op jit(solution)/shard_map/ppermute | solution.py:22
  22.0 0.1 fusion.26
  22.2 0.5 copy-done.3
  22.6 2.7 %collective-permute-done.2 = f32[884,4]{0,1:T(4,128)S(1)} collective-permute-done((f32[884,4]{0,1:T(4,128)S(1)}, f32[884,4]{0,1:T(4,128)S(1)}, u32[]{:S(2)}, u32[]{:S(2)}) %collective-permute-start.2) | collective-permute-done | bytes 14176 | tf_op jit(solution)/shard_map/ppermute | solution.py:22
  25.5 0.4 copy-done.4
  25.9 0.1 reshape.162
  26.0 0.1 copy.29
  26.1 0.1 reshape.160
  26.2 0.1 copy.27
  26.3 0.1 reshape.161
  26.4 0.1 copy.28
  26.5 0.1 reshape.159
  26.5 0.1 copy.26
  26.6 0.1 copy.24
  26.8 0.1 copy.25
  26.9 0.5 %slice-done.1 = f32[480,4]{0,1:T(4,128)S(1)} async-done(((f32[884,4]{0,1:T(4,128)}), f32[480,4]{0,1:T(4,128)S(1)}, s32[]{:S(2)}) %slice-start.1) | async-done | bytes 7704 | tf_op jit(solution)/shard_map/slice | solution.py:141
  27.5 0.1 copy.18
  27.6 0.6 %slice-done = f32[480,4]{0,1:T(4,128)S(1)} async-done(((f32[884,4]{0,1:T(4,128)}), f32[480,4]{0,1:T(4,128)S(1)}, s32[]{:S(2)}) %slice-start) | async-done | bytes 7704 | tf_op jit(solution)/shard_map/slice | solution.py:141
  28.2 0.1 copy.23
  28.3 1.1 %maximum_maximum_fusion.1.ms_ref = f32[4,96,384]{2,1,0:T(8,128)} fusion(f32[4,96,4]{2,1,0:T(8,128)S(1)} %bitcast.121, f32[4,96,256]{2,1,0:T(8,128)S(1)} %copy-done.1, f32[4,96,4]{2,1,0:T(8,128)S(1)} %bitcast.120, f32[384]{0:T(512)S(1)} %pad.15.clone), kind=kLoop, calls=%fused_computation.3 | loop fusion | flops 442368 | bytes 996864 | tf_op jit(solution)/shard_map/concatenate | solution.py:326
  29.4 1.2 %maximum_maximum_fusion.u_ref = f32[5,96,384]{2,1,0:T(8,128)} fusion(f32[5,96,4]{2,1,0:T(8,128)S(1)} %bitcast.115, f32[5,96,256]{2,1,0:T(8,128)S(1)} %bitcast.113, f32[5,96,4]{2,1,0:T(8,128)S(1)} %bitcast.114, f32[384]{0:T(512)S(1)} %pad.15.clone), kind=kLoop, calls=%fused_computation.2 | loop fusion | flops 552960 | bytes 1245696 | tf_op jit(solution)/shard_map/concatenate | solution.py:326
  30.6 0.7 %maximum_maximum_fusion.3 = (f32[2,5,384]{2,1,0:T(8,128)}, f32[2,5,384]{2,1,0:T(8,128)}) fusion(f32[2,5,4]{2,1,0:T(8,128)S(1)} %copy.29, f32[2,5,256]{2,1,0:T(8,128)S(1)} %collective-permute-done.1, f32[2,5,4]{2,1,0:T(8,128)S(1)} %copy.28, f32[384]{0:T(512)S(1)} %pad.15.clone, f32[2,5,4]{2,1,0:T(8,128)S(1)} %copy.27, ...), kind=kLoop, calls=%fused_computation.13 | loop fusion | flops 23040 | bytes 53376 | tf_op jit(solution)/shard_map/concatenate | solution.py:326
  31.4 5.5 %shard_map.130 = (f32[5,96,384]{2,1,0:T(8,128)}, f32[32,128]{1,0:T(8,128)}) custom-call(f32[54]{0:T(128)} %pad_maximum_fusion.4.sc_ref, f32[5,96,384]{2,1,0:T(8,128)} %maximum_maximum_fusion.u_ref, f32[4,96,384]{2,1,0:T(8,128)} %maximum_maximum_fusion.1.ms_ref, f32[2,5,384]{2,1,0:T(8,128)} %get-tuple-element.29.gl_ref, ...), custom_call_target="tpu_custom_call" | custom-call | tf_op jit(solution)/shard_map/pallas_call | solution.py:343
  36.8 0.8 %reduce_sum.69 = f32[32]{0:T(128)S(1)} reduce(f32[32,128]{1,0:T(8,128)} %get-tuple-element.5, f32[]{:T(128)} %constant.72.clone.1), dimensions={1}, to_apply=%region_6.7 | reduce | flops 4064 | bytes 16516 | tf_op jit(solution)/shard_map/reduce_sum | solution.py:353
  37.7 3.5 %collective-permute-done.4 = f32[32]{0:T(128)S(1)} collective-permute-done((f32[32]{0:T(128)S(1)}, f32[32]{0:T(128)S(1)}, u32[]{:S(2)}, u32[]{:S(2)}) %collective-permute-start.4) | collective-permute-done | bytes 160 | tf_op jit(solution)/shard_map/ppermute | solution.py:41
  41.3 0.5 collective-permute-start.5
  41.8 3.0 %collective-permute-done.5 = f32[32]{0:T(128)S(1)} collective-permute-done((f32[32]{0:T(128)S(1)}, f32[32]{0:T(128)S(1)}, u32[]{:S(2)}, u32[]{:S(2)}) %collective-permute-start.5) | collective-permute-done | bytes 160 | tf_op jit(solution)/shard_map/ppermute | solution.py:41
  44.8 0.1 slice_multiply_fusion
  44.9 0.1 mul.94
  45.0 0.6 %copy-done.8 = f32[1,4]{1,0:T(1,128)S(1)} copy-done((f32[1,4]{1,0:T(1,128)S(1)}, f32[1,4]{1,0:T(1,128)}, u32[]{:S(2)}) %copy-start.8) | copy-done | bytes 40
  45.6 0.6 %add_bitcast_fusion.1 = (f32[1,4]{1,0:T(1,128)}, f32[4]{0:T(128)S(1)}, f32[4]{0:T(128)S(1)}, f32[4]{0:T(128)S(1)}, f32[4]{0:T(128)S(1)}) fusion(f32[1,4]{1,0:T(1,128)S(1)} %copy-done.9, f32[32]{0:T(128)S(1)} %add.90, f32[1,4]{1,0:T(1,128)S(1)} %copy-done.7, f32[1,4]{1,0:T(1,128)S(1)} %copy-done.8), kind=kLoop, calls=%fused_computation.45 | loop fusion | flops 120 | bytes 176 | tf_op jit(solution)/shard_map/broadcast_in_dim | solution.py:382
  46.2 0.7 %concatenate.34.sc_ref = f32[62]{0:T(128)} concatenate(f32[25]{0:T(128)S(1)} %reshape.145, f32[25]{0:T(128)S(1)} %reshape.146, f32[4]{0:T(128)S(1)} %broadcast_multiply_fusion, f32[4]{0:T(128)S(1)} %get-tuple-element.14, f32[4]{0:T(128)S(1)} %get-tuple-element.12), dimensions={0} | concatenate | bytes 496 | tf_op jit(solution)/shard_map/concatenate | solution.py:381
  46.8 0.7 %add_bitcast_fusion = f32[1,4]{1,0:T(1,128)} fusion(f32[4]{0:T(128)S(1)} %get-tuple-element.14, f32[4]{0:T(128)S(1)} %get-tuple-element.12, f32[4]{0:T(128)S(1)} %get-tuple-element.13, f32[1,4]{1,0:T(1,128)S(1)} %copy-done.9, f32[32]{0:T(128)S(1)} %add.90, f32[4,4]{1,0:T(4,128)S(1)} %mul.94, f32[4]{0:T(128)S(1)} %get-tuple-element.15), kind=kOutput, calls=%fused_computation.43 | convolution fusion | flops 264 | bytes 192 | tf_op jit(solution)/shard_map/dot_general | solution.py:371
  47.5 4.5 %shard_map.131 = f32[5,96,256]{2,1,0:T(8,128)} custom-call(f32[62]{0:T(128)} %concatenate.34.sc_ref, f32[5,96,384]{2,1,0:T(8,128)} %get-tuple-element.6.a_ref, f32[4,96,384]{2,1,0:T(8,128)} %maximum_maximum_fusion.1.ms_ref, f32[2,5,384]{2,1,0:T(8,128)} %get-tuple-element.29.gl_ref, f32[2,5,384]{2,1,0:T(8,128)} %get-tuple-element.28.gu_ref, ...), custom_call_target="tpu_custom_call" | custom-call | tf_op jit(solution)/shard_map/pallas_call | solution.py:376
  (38 shorter events, 0.5 us)
Async XLA Ops:
  0.6 9.0 %copy-start.2 = (f32[1,64,5,256]{3,1,2,0:T(8,128)S(1)}, f32[1,64,5,256]{3,1,2,0:T(8,128)}, u32[]{:S(2)}) copy-start(f32[1,64,5,256]{3,1,2,0:T(8,128)} %param.12) | copy-start | bytes 983044
  4.6 1.7 %copy-start.10 = (s32[8]{0:T(128)S(1)}, s32[8]{0:T(128)}, u32[]{:S(2)}) copy-start(s32[8]{0:T(128)} %param.15) | copy-start | bytes 100
  4.6 9.4 %copy-start.1 = (f32[4,96,256]{2,1,0:T(8,128)S(1)}, f32[4,96,256]{2,1,0:T(8,128)}, u32[]{:S(2)}) copy-start(f32[4,96,256]{2,1,0:T(8,128)} %param.18) | copy-start | bytes 1179652
  5.8 10.9 %collective-permute-start = (f32[2,5,256]{2,1,0:T(8,128)S(1)}, f32[2,5,256]{2,1,0:T(8,128)S(1)}, u32[]{:S(2)}, u32[]{:S(2)}) collective-permute-start(f32[2,5,256]{2,1,0:T(8,128)S(1)} %pad_maximum_fusion), channel_id=1, source_target_pairs={{0,4},{4,8},{8,12},{12,16},{16,20},{20,24},{24,28},{28,0},{1,5},{5... | collective-permute-start | bytes 30728 | tf_op jit(solution)/shard_map/ppermute | solution.py:22
  9.6 4.3 %copy-start.5 = (f32[5,5]{1,0:T(8,128)S(1)}, f32[5,5]{1,0:T(8,128)}, u32[]{:S(2)}) copy-start(f32[5,5]{1,0:T(8,128)} %param.16) | copy-start | bytes 304
  9.6 4.4 %copy-start.6 = (f32[5,5]{1,0:T(8,128)S(1)}, f32[5,5]{1,0:T(8,128)}, u32[]{:S(2)}) copy-start(f32[5,5]{1,0:T(8,128)} %param.17) | copy-start | bytes 304
  9.8 4.4 %copy-start = (f32[1,5,96,256]{3,2,1,0:T(8,128)S(1)}, f32[1,5,96,256]{3,2,1,0:T(8,128)}, u32[]{:S(2)}) copy-start(f32[1,5,96,256]{3,2,1,0:T(8,128)} %param.11) | copy-start | bytes 1474564
  9.8 7.4 %collective-permute-start.1 = (f32[2,5,256]{2,1,0:T(8,128)S(1)}, f32[2,5,256]{2,1,0:T(8,128)S(1)}, u32[]{:S(2)}, u32[]{:S(2)}) collective-permute-start(f32[2,5,256]{2,1,0:T(8,128)S(1)} %pad_maximum_fusion.1), channel_id=1, source_target_pairs={{0,28},{4,0},{8,4},{12,8},{16,12},{20,16},{24,20},{28,24},{1,29},{... | collective-permute-start | bytes 30728 | tf_op jit(solution)/shard_map/ppermute | solution.py:22
  14.9 0.7 %copy-start.7 = (f32[1,4]{1,0:T(1,128)S(1)}, f32[1,4]{1,0:T(1,128)}, u32[]{:S(2)}) copy-start(f32[1,4]{1,0:T(1,128)} %param.21) | copy-start | bytes 52
  17.7 4.4 %collective-permute-start.3 = (f32[884,4]{0,1:T(4,128)S(1)}, f32[884,4]{0,1:T(4,128)S(1)}, u32[]{:S(2)}, u32[]{:S(2)}) collective-permute-start(f32[884,4]{0,1:T(4,128)S(1)} %pad_maximum_fusion.3), channel_id=1, source_target_pairs={{0,3},{1,0},{2,1},{3,2},{4,7},{5,4},{6,5},{7,6},{8,11},{9,8},{10,9... | collective-permute-start | bytes 42440 | tf_op jit(solution)/shard_map/ppermute | solution.py:22
  20.7 4.6 %collective-permute-start.2 = (f32[884,4]{0,1:T(4,128)S(1)}, f32[884,4]{0,1:T(4,128)S(1)}, u32[]{:S(2)}, u32[]{:S(2)}) collective-permute-start(f32[884,4]{0,1:T(4,128)S(1)} %pad_maximum_fusion.2), channel_id=1, source_target_pairs={{0,1},{1,2},{2,3},{3,0},{4,5},{5,6},{6,7},{7,4},{8,9},{9,10},{10,1... | collective-permute-start | bytes 42440 | tf_op jit(solution)/shard_map/ppermute | solution.py:22
  22.0 0.6 %copy-start.3 = (f32[884,4]{0,1:T(4,128)}, f32[884,4]{0,1:T(4,128)S(1)}, u32[]{:S(2)}) copy-start(f32[884,4]{0,1:T(4,128)S(1)} %broadcast_select_fusion) | copy-start | bytes 42436
  25.3 0.6 %copy-start.4 = (f32[884,4]{0,1:T(4,128)}, f32[884,4]{0,1:T(4,128)S(1)}, u32[]{:S(2)}) copy-start(f32[884,4]{0,1:T(4,128)S(1)} %broadcast_select_fusion.1) | copy-start | bytes 42436
  26.8 0.7 %slice-start.1 = ((f32[884,4]{0,1:T(4,128)}), f32[480,4]{0,1:T(4,128)S(1)}, s32[]{:S(2)}) async-start(f32[884,4]{0,1:T(4,128)} %copy-done.4), calls=%async_computation.1 | async-start | bytes 16384 | tf_op jit(solution)/shard_map/slice | solution.py:141
  27.5 0.7 %slice-start = ((f32[884,4]{0,1:T(4,128)}), f32[480,4]{0,1:T(4,128)S(1)}, s32[]{:S(2)}) async-start(f32[884,4]{0,1:T(4,128)} %copy-done.3), calls=%async_computation | async-start | bytes 16384 | tf_op jit(solution)/shard_map/slice | solution.py:141
  37.7 3.6 %collective-permute-start.4 = (f32[32]{0:T(128)S(1)}, f32[32]{0:T(128)S(1)}, u32[]{:S(2)}, u32[]{:S(2)}) collective-permute-start(f32[32]{0:T(128)S(1)} %reduce_sum.69), channel_id=1, source_target_pairs={{0,1},{1,0},{2,3},{3,2},{4,5},{5,4},{6,7},{7,6},{8,9},{9,8},{10,11... | collective-permute-start | bytes 392 | tf_op jit(solution)/shard_map/ppermute | solution.py:41
  41.3 3.5 %collective-permute-start.5 = (f32[32]{0:T(128)S(1)}, f32[32]{0:T(128)S(1)}, u32[]{:S(2)}, u32[]{:S(2)}) collective-permute-start(f32[32]{0:T(128)S(1)} %add.89), channel_id=1, source_target_pairs={{0,2},{1,3},{2,0},{3,1},{4,6},{5,7},{6,4},{7,5},{8,10},{9,11},{10,... | collective-permute-start | bytes 392 | tf_op jit(solution)/shard_map/ppermute | solution.py:41
  44.9 0.7 %copy-start.8 = (f32[1,4]{1,0:T(1,128)S(1)}, f32[1,4]{1,0:T(1,128)}, u32[]{:S(2)}) copy-start(f32[1,4]{1,0:T(1,128)} %param.20) | copy-start | bytes 52
  44.9 0.7 %copy-start.9 = (f32[1,4]{1,0:T(1,128)S(1)}, f32[1,4]{1,0:T(1,128)}, u32[]{:S(2)}) copy-start(f32[1,4]{1,0:T(1,128)} %param.19) | copy-start | bytes 52

commit v5 on v4

--- a/solution.py
+++ b/solution.py
@@ -1,3 +1,4 @@
+import functools
 import math
 
 import jax
@@ -192,26 +193,72 @@
     return total
 
 
-def first_kernel(sc_ref, u_ref, ms_ref, gl_ref, gu_ref, inside_ref, owned_ref, a_ref, part_ref):
+def pick_kernel(peers, lower_slot_ref, upper_slot_ref, upper_hist_ref, lower_hist_ref, up_ref, down_ref):
+    slots = upper_hist_ref.shape[0]
+    position = lax.axis_index("blk")
+    slot_next = lower_slot_ref[(position + 1) % peers]
+    slot_prev = upper_slot_ref[(position + peers - 1) % peers]
+    for s in range(up_ref.shape[0]):
+        up_ref[s] = upper_hist_ref[(slot_next + s) % slots]
+        down_ref[s] = lower_hist_ref[(slot_prev + s) % slots]
+
+
+def widened(own, left, right):
+    tile = right + lane_roll(left, -2 * STEP_COUNT)
+    return jnp.concatenate([own, tile], axis=-1)
+
+
+def lane_masks(peers, shape, own_width):
+    reach = 2 * STEP_COUNT
+    me = lax.axis_index("mesh")
+    lane = lax.broadcasted_iota(jnp.int32, shape, len(shape) - 1)
+    width = shape[-1]
+    right_ok = (lane >= own_width) & (lane < own_width + reach) & (me < peers - 1)
+    left_ok = (lane >= width - reach) & (me > 0)
+    owned = lane < own_width
+    inside = owned | right_ok | left_ok
+    return inside.astype(jnp.float32), owned.astype(jnp.float32)
+
+
+def assemble(u_ref, ms_ref, glo_ref, gup_ref, left_ref, right_ref, fields, modes, pitch):
+    u = []
+    for j in range(fields):
+        rows = slice(j * pitch, (j + 1) * pitch)
+        u.append(widened(u_ref[j], left_ref[rows, :], right_ref[rows, :]))
+    ms = []
+    for m in range(modes):
+        rows = slice((fields + m) * pitch, (fields + m + 1) * pitch)
+        ms.append(widened(ms_ref[m], left_ref[rows, :], right_ref[rows, :]))
+    base = (fields + modes) * pitch
+    steps = glo_ref.shape[0]
+    ghosts = []
+    for side, ref in enumerate((glo_ref, gup_ref)):
+        per_step = []
+        for s in range(steps):
+            start = base + (side * steps + s) * fields
+            rows = slice(start, start + fields)
+            block = widened(ref[s], left_ref[rows, :], right_ref[rows, :])
+            per_step.append([block[j : j + 1, :] for j in range(fields)])
+        ghosts.append(per_step)
+    return u, ms, ghosts[0], ghosts[1]
+
+
+def first_kernel(peers, sc_ref, u_ref, ms_ref, glo_ref, gup_ref, left_ref, right_ref, a_ref, part_ref):
     h = TIME_STEP
     fields = u_ref.shape[0]
     modes = ms_ref.shape[0]
+    pitch = u_ref.shape[1]
     jac = read_jacobians(sc_ref, fields)
     base = 2 * fields * fields
     vel = [sc_ref[base + m] for m in range(modes)]
-    inside = inside_ref[...]
-    owned = owned_ref[...]
-    ms = [ms_ref[m] for m in range(modes)]
+    u0, ms, gl, gu = assemble(u_ref, ms_ref, glo_ref, gup_ref, left_ref, right_ref, fields, modes, pitch)
+    inside, owned = lane_masks(peers, u0[0].shape, u_ref.shape[-1])
     push = vel[0] * ms[0]
     for m in range(1, modes):
         push = push + vel[m] * ms[m]
     push = COUPLING * push
-    gl1 = [gl_ref[0, j : j + 1, :] for j in range(fields)]
-    gu1 = [gu_ref[0, j : j + 1, :] for j in range(fields)]
-    gl2 = [gl_ref[1, j : j + 1, :] for j in range(fields)]
-    gu2 = [gu_ref[1, j : j + 1, :] for j in range(fields)]
+    gl1, gu1, gl2, gu2 = gl[0], gu[0], gl[1], gu[1]
     every = list(range(fields))
-    u0 = [u_ref[j] for j in range(fields)]
     k1 = kernel_rate(u0, gl1, gu1, jac, push, inside, every)
     mid = [u0[j] + h * k1[j] for j in every]
     k2 = kernel_rate(mid, gl1, gu1, jac, push, inside, every)
@@ -239,16 +286,16 @@
             part_ref[k + m * modes + n : k + m * modes + n + 1, :] = lane_fold(weighted[m] * t)
 
 
-def second_kernel(sc_ref, a_ref, ms_ref, gl_ref, gu_ref, inside_ref, out_ref):
+def second_kernel(peers, sc_ref, a_ref, u_ref, ms_ref, glo_ref, gup_ref, left_ref, right_ref, out_ref):
     h = TIME_STEP
     fields = a_ref.shape[0]
     modes = ms_ref.shape[0]
-    reach = 2 * STEP_COUNT
+    pitch = u_ref.shape[1]
     jac = read_jacobians(sc_ref, fields)
     base = 2 * fields * fields
     coef = [[sc_ref[base + w * modes + m] for m in range(modes)] for w in range(3)]
-    inside = inside_ref[...]
-    ms = [ms_ref[m] for m in range(modes)]
+    _, ms, gl, gu = assemble(u_ref, ms_ref, glo_ref, gup_ref, left_ref, right_ref, fields, modes, pitch)
+    inside, _ = lane_masks(peers, ms[0].shape, u_ref.shape[-1])
 
     def combine(weights):
         total = weights[0] * ms[0]
@@ -256,8 +303,7 @@
             total = total + weights[m] * ms[m]
         return total
 
-    gl2 = [gl_ref[1, j : j + 1, :] for j in range(fields)]
-    gu2 = [gu_ref[1, j : j + 1, :] for j in range(fields)]
+    gl2, gu2 = gl[1], gu[1]
     every = list(range(fields))
     s1 = [a_ref[j] for j in every]
     s1[1] = s1[1] + combine(coef[0])
@@ -267,7 +313,7 @@
     width = out_ref.shape[-1]
     for j in every:
         s2 = s1[j] + 0.5 * h * (k1[j] + k2[j])
-        out_ref[j] = lane_roll(s2, -reach)[:, :width]
+        out_ref[j] = s2[:, :width]
 
 
 def vmem_spec():
@@ -304,12 +350,13 @@
     disp0 = displacement[0]
     vel0 = velocity[0]
 
-    after_me = (position + 1) % passages
-    before_me = (position + passages - 1) % passages
-    slot_next = pick_entry(lower_lag_slot, after_me)
-    slot_prev = pick_entry(upper_lag_slot, before_me)
-    rows_up = pick_rows(upper_row_history[0], slot_next, STEP_COUNT)
-    rows_down = pick_rows(lower_row_history[0], slot_prev, STEP_COUNT)
+    row_shape = jax.ShapeDtypeStruct((STEP_COUNT,) + upper_row_history.shape[2:], state0.dtype)
+    rows_up, rows_down = pl.pallas_call(
+        functools.partial(pick_kernel, passages),
+        out_shape=(row_shape, row_shape),
+        in_specs=[smem_spec(), smem_spec(), vmem_spec(), vmem_spec()],
+        out_specs=(vmem_spec(), vmem_spec()),
+    )(lower_lag_slot, upper_lag_slot, upper_row_history[0], lower_row_history[0])
     lower_ghosts = shifted(rows_up, "blk", 1)
     upper_ghosts = shifted(rows_down, "blk", -1)
 
@@ -320,35 +367,22 @@
     from_right = shifted(pack([part[..., :reach] for part in own], reach), "mesh", -1)
     from_left = jnp.where(me > 0, from_left, jnp.zeros_like(from_left))
     from_right = jnp.where(me < mesh_peers - 1, from_right, jnp.zeros_like(from_right))
-    def widen(left, part, right):
-        spare = lanes_wide - axial_cells - 2 * reach
-        tail = jnp.zeros(part.shape[:-1] + (spare,), part.dtype)
-        return jnp.concatenate([left, part, right, tail], axis=-1)
-
-    lanes_wide = -(-(axial_cells + 2 * reach) // LANES) * LANES
-    wide = [
-        widen(left, part, right)
-        for left, part, right in zip(unpack(from_left, shapes), own, unpack(from_right, shapes))
-    ]
-    state0_w, mode_w, lower_w, upper_w = wide
-    column = jnp.arange(lanes_wide, dtype=jnp.int32)[None, :]
-    inside = (
-        ((column >= reach) | (me > 0))
-        & ((column < axial_cells + reach) | (me < mesh_peers - 1))
-        & (column < axial_cells + 2 * reach)
-    ).astype(state0.dtype)
-    owned = ((column >= reach) & (column < axial_cells + reach)).astype(state0.dtype)
+    pad = [(0, 0), (0, LANES - reach)]
+    from_left = jnp.pad(from_left, pad)
+    from_right = jnp.pad(from_right, pad)
+    lanes_wide = axial_cells + LANES
+    ins = (state0, mode_shape, lower_ghosts, upper_ghosts, from_left, from_right)
 
     jac_flat = jnp.concatenate([axial_jacobian.reshape(-1), pitch_jacobian.reshape(-1)])
     base1, part_lanes = pl.pallas_call(
-        first_kernel,
+        functools.partial(first_kernel, mesh_peers),
         out_shape=(
-            jax.ShapeDtypeStruct(state0_w.shape, state0.dtype),
+            jax.ShapeDtypeStruct((fields, pitch_cells, lanes_wide), state0.dtype),
             jax.ShapeDtypeStruct((4 * modes + modes * modes, LANES), state0.dtype),
         ),
         in_specs=[smem_spec()] + [vmem_spec()] * 6,
         out_specs=(vmem_spec(), vmem_spec()),
-    )(jnp.concatenate([jac_flat, vel0]), state0_w, mode_w, lower_w, upper_w, inside, owned)
+    )(jnp.concatenate([jac_flat, vel0]), *ins)
 
     totals = mesh_sum(jnp.sum(part_lanes, axis=1))
     force0 = force_scale * totals[0:modes]
@@ -374,11 +408,11 @@
     vel2 = vel1 + 0.5 * h * (acc2 + acc2m)
 
     state2 = pl.pallas_call(
-        second_kernel,
+        functools.partial(second_kernel, mesh_peers),
         out_shape=jax.ShapeDtypeStruct(state0.shape, state0.dtype),
-        in_specs=[smem_spec()] + [vmem_spec()] * 5,
+        in_specs=[smem_spec()] + [vmem_spec()] * 7,
         out_specs=vmem_spec(),
-    )(jnp.concatenate([jac_flat, corr * acc1, vel1, vel2m]), base1, mode_w, lower_w, upper_w, inside)
+    )(jnp.concatenate([jac_flat, corr * acc1, vel1, vel2m]), base1, *ins)
     return (state2[None], disp2[None], vel2[None])
 
 

time: 52.4 us -> 57.3 us (1.094)
  waiting for transfers between devices: 10.6 us -> 24.3 us
  other arithmetic: 9.17 us -> 2.23 us
  between operations: 6.07 us -> 0.7 us
  Pallas kernels: 9.94 us -> 12 us
  starting transfers between devices: 8.13 us -> 9.44 us
    ppermute x4, waiting for transfers between devices: 4.01 us -> 19.1 us  [shifted(): lax.ppermute(value, axis, [(i, (i + by) % peers) for i in range(peers)])]
    reduce_sum x4 -> x0, other arithmetic: 3.25 us -> none  [the longest x2 1.97 us: pick_entry(): return jnp.sum(jnp.where(hit, values, jnp.zeros_like(values)))]
    concatenate x3 -> x0, other arithmetic: 3.02 us -> none  [widen(): return jnp.concatenate([left, part, right, tail], axis=-1)]
    slice x18 -> x0, local copies, waits for them, and re-layouts: 2.53 us -> none  [the longest x12 1.94 us: unpack(): out.append(buffer[offset:offset + count].reshape(shape))]
    squeeze x0 -> x1, local copies, waits for them, and re-layouts: none -> 2.47 us  [on_device(): lower_row_history[0]]
    pallas_call x2 -> x3, Pallas kernels: 9.94 us -> 12 us  [the longest x1 5.7 us: on_device(): pl.pallas_call(functools.partial(first_kernel, mesh_peers), out_shape=(ja...]
    pad x0 -> x2, local copies, waits for them, and re-layouts: none -> 1.61 us  [the longest x1 0.82 us: on_device(): from_left = jnp.pad(from_left, pad)]
    ppermute x2, starting transfers between devices: 0.57 us -> 1.87 us  [mesh_sum(): lax.ppermute(value, 'mesh', [(i, i ^ step) for i in range(peers)])]
  transfers between devices with their start and end apart: 6 -> 6, of which waited for: 4 -> 4; matrix products, arithmetic and copies ran while one was open for 7% -> 3% of each run, Pallas kernels for 0% -> 0%
where the time goes in v5:
time: 57.3 us; the launch traced here: 57 us
  waiting for transfers between devices  24.3 us (42%)
  Pallas kernels  12 us (21%)
  starting transfers between devices  9.44 us (16%)
  local copies, waits for them, and re-layouts  7.67 us (13%)
  other arithmetic  2.23 us (4%)
  between operations  0.7 us (1%)
  matrix products  0.65 us (1%)
    ppermute x4, waiting for transfers between devices, shifted(): lax.ppermute(value, axis, [(i, (i + by) % peers) for i in range(peers)])  19.1 us
    ppermute x4, starting transfers between devices, shifted(): lax.ppermute(value, axis, [(i, (i + by) % peers) for i in range(peers)])  7.58 us
    pallas_call x1, Pallas kernels, on_device(): pl.pallas_call(functools.partial(first_kernel, mesh_peers), out_shape=(ja...  5.7 us
    ppermute x2, waiting for transfers between devices, mesh_sum(): lax.ppermute(value, 'mesh', [(i, i ^ step) for i in range(peers)])  5.27 us
    pallas_call x1, Pallas kernels, on_device(): pl.pallas_call(functools.partial(second_kernel, mesh_peers), out_shape=ja...  4.36 us
    squeeze x1, local copies, waits for them, and re-layouts, on_device(): lower_row_history[0]  2.47 us
    unnamed x18, local copies, waits for them, and re-layouts  2.3 us
    pallas_call x1, Pallas kernels, on_device(): pl.pallas_call(functools.partial(pick_kernel, passages), out_shape=(row_s...  1.9 us
  transfers between devices with their start and end apart: 6, of which 4 were waited for; matrix products, arithmetic and copies ran while one was open for 3% of the time, Pallas kernels for 0%

profile of v5, /device:TPU:0, one launch (start us, length us, event | category | flops | bytes accessed | tf_op | source)
XLA Modules:
  0.0 57.0 jit_solution(10744114568942537160)
XLA Ops:
  0.6 2.5 %copy_bitcast_fusion = (f32[64,5,256]{2,1,0:T(8,128)}, f32[64,5,256]{2,1,0:T(8,128)}) fusion(f32[1,64,5,256]{3,1,2,0:T(8,128)} %param.12, f32[1,64,5,256]{3,1,2,0:T(8,128)} %param.13), kind=kLoop, calls=%fused_computation.2 | loop fusion | bytes 1310720 | tf_op jit(solution)/shard_map/squeeze | solution.py:359
  3.1 0.0 copy-start.4
  3.1 0.0 copy-start.5
  3.1 0.0 copy-start.1
  3.1 1.9 %shard_map.130 = (f32[2,5,256]{2,1,0:T(8,128)}, f32[2,5,256]{2,1,0:T(8,128)}) custom-call(s32[8]{0:T(128)} %lower_slot_ref.1, s32[8]{0:T(128)} %upper_slot_ref.1, f32[64,5,256]{2,1,0:T(8,128)} %get-tuple-element.25.upper_hist_ref, f32[64,5,256]{2,1,0:T(8,128)} %get-tuple-element.24.lower_hist_ref), custom_call_target="tpu_custom_call" | custom-call | tf_op jit(solution)/shard_map/pallas_call | solution.py:354
  5.0 0.0 copy-start
  5.0 0.5 collective-permute-start
  5.5 4.1 %collective-permute-start.1 = (f32[2,5,256]{2,1,0:T(8,128)}, f32[2,5,256]{2,1,0:T(8,128)S(1)}, u32[]{:S(2)}, u32[]{:S(2)}) collective-permute-start(f32[2,5,256]{2,1,0:T(8,128)} %get-tuple-element.8), channel_id=1, source_target_pairs={{0,28},{4,0},{8,4},{12,8},{16,12},{20,16},{24,20},{28,24},{1,29},{... | collective-permute-start | bytes 30728 | tf_op jit(solution)/shard_map/ppermute | solution.py:23
  9.6 0.0 copy-done.4
  9.6 0.1 reshape.47
  9.6 0.0 copy-done.5
  9.6 0.1 reshape.48
  9.7 0.0 copy-done.1
  9.7 0.1 fusion.16
  9.8 0.0 copy-done
  9.8 0.1 fusion.15
  10.0 0.0 copy-start.6
  10.0 0.7 %copy-done.6 = f32[1,4]{1,0:T(1,128)S(1)} copy-done((f32[1,4]{1,0:T(1,128)S(1)}, f32[1,4]{1,0:T(1,128)}, u32[]{:S(2)}) %copy-start.6) | copy-done | bytes 40
  10.6 0.6 %pad_maximum_fusion.2.sc_ref = f32[54]{0:T(128)} fusion(f32[4]{0:T(128)S(1)} %bitcast.86, f32[25]{0:T(128)S(1)} %reshape.48, f32[25]{0:T(128)S(1)} %reshape.47), kind=kLoop, calls=%fused_computation.8 | loop fusion | flops 108 | bytes 432 | tf_op jit(solution)/shard_map/concatenate | solution.py:385
  11.2 0.0 collective-permute-done.glo_ref
  11.2 0.0 copy-start.2
  11.2 0.1 fusion.17
  11.3 0.5 copy-done.2
  11.8 0.0 collective-permute-done.1.gup_ref
  11.8 0.0 copy-start.3
  11.8 0.1 fusion.18
  11.9 0.5 copy-done.3
  12.5 2.0 %collective-permute-start.2 = (f32[884,4]{1,0:T(8,128)S(1)}, f32[884,4]{1,0:T(8,128)S(1)}, u32[]{:S(2)}, u32[]{:S(2)}) collective-permute-start(f32[884,4]{1,0:T(8,128)S(1)} %pad_maximum_fusion), channel_id=1, source_target_pairs={{0,1},{1,2},{2,3},{3,0},{4,5},{5,6},{6,7},{7,4},{8,9},{9,10},{10,1... | collective-permute-start | bytes 42440 | tf_op jit(solution)/shard_map/ppermute | solution.py:23
  14.5 1.0 %collective-permute-start.3 = (f32[884,4]{1,0:T(8,128)S(1)}, f32[884,4]{1,0:T(8,128)S(1)}, u32[]{:S(2)}, u32[]{:S(2)}) collective-permute-start(f32[884,4]{1,0:T(8,128)S(1)} %pad_maximum_fusion.1), channel_id=1, source_target_pairs={{0,3},{1,0},{2,1},{3,2},{4,7},{5,4},{6,5},{7,6},{8,11},{9,8},{10,9... | collective-permute-start | bytes 42440 | tf_op jit(solution)/shard_map/ppermute | solution.py:23
  15.5 11.2 %collective-permute-done.2 = f32[884,4]{1,0:T(8,128)S(1)} collective-permute-done((f32[884,4]{1,0:T(8,128)S(1)}, f32[884,4]{1,0:T(8,128)S(1)}, u32[]{:S(2)}, u32[]{:S(2)}) %collective-permute-start.2) | collective-permute-done | bytes 14176 | tf_op jit(solution)/shard_map/ppermute | solution.py:23
  26.8 0.8 %pad.7.left_ref = f32[884,128]{1,0:T(8,128)} pad(f32[884,4]{1,0:T(8,128)S(1)} %broadcast_select_fusion.1, f32[]{:T(128)} %constant.3.clone.1), padding=0_0x0_124 | pad | bytes 466756 | tf_op jit(solution)/shard_map/jit(_pad)/pad | solution.py:371
  27.6 7.8 %collective-permute-done.3 = f32[884,4]{1,0:T(8,128)S(1)} collective-permute-done((f32[884,4]{1,0:T(8,128)S(1)}, f32[884,4]{1,0:T(8,128)S(1)}, u32[]{:S(2)}, u32[]{:S(2)}) %collective-permute-start.3) | collective-permute-done | bytes 14176 | tf_op jit(solution)/shard_map/ppermute | solution.py:23
  35.5 0.8 %pad.8.right_ref = f32[884,128]{1,0:T(8,128)} pad(f32[884,4]{1,0:T(8,128)S(1)} %broadcast_select_fusion, f32[]{:T(128)} %constant.3.clone.1), padding=0_0x0_124 | pad | bytes 466756 | tf_op jit(solution)/shard_map/jit(_pad)/pad | solution.py:372
  36.3 5.7 %shard_map.131 = (f32[5,96,384]{2,1,0:T(8,128)}, f32[32,128]{1,0:T(8,128)}) custom-call(f32[54]{0:T(128)} %pad_maximum_fusion.2.sc_ref, f32[5,96,256]{2,1,0:T(8,128)} %bitcast.78, f32[4,96,256]{2,1,0:T(8,128)} %ms_ref.3, f32[2,5,256]{2,1,0:T(8,128)} %copy-done.2, f32[2,5,256]{2,1,0:T(8,128)} %copy-done.3, f32[884,128]{1,0:T(8,128)} %pad.7.left_ref, ...), custom_call_target="tpu_custom_call" | custom-call | tf_op jit(solution)/shard_map/pallas_call | solution.py:377
  42.0 0.8 %reduce_sum.9 = f32[32]{0:T(128)S(1)} reduce(f32[32,128]{1,0:T(8,128)} %get-tuple-element.9, f32[]{:T(128)} %constant.3.clone.1), dimensions={1}, to_apply=%region_0.1 | reduce | flops 4064 | bytes 16516 | tf_op jit(solution)/shard_map/reduce_sum | solution.py:387
  42.8 1.6 %collective-permute-start.4 = (f32[32]{0:T(128)S(1)}, f32[32]{0:T(128)S(1)}, u32[]{:S(2)}, u32[]{:S(2)}) collective-permute-start(f32[32]{0:T(128)S(1)} %reduce_sum.9), channel_id=1, source_target_pairs={{0,1},{1,0},{2,3},{3,2},{4,5},{5,4},{6,7},{7,6},{8,9},{9,8},{10,11... | collective-permute-start | bytes 392 | tf_op jit(solution)/shard_map/ppermute | solution.py:42
  44.4 2.0 %collective-permute-done.4 = f32[32]{0:T(128)S(1)} collective-permute-done((f32[32]{0:T(128)S(1)}, f32[32]{0:T(128)S(1)}, u32[]{:S(2)}, u32[]{:S(2)}) %collective-permute-start.4) | collective-permute-done | bytes 160 | tf_op jit(solution)/shard_map/ppermute | solution.py:42
  46.4 0.3 collective-permute-start.5
  46.7 3.2 %collective-permute-done.5 = f32[32]{0:T(128)S(1)} collective-permute-done((f32[32]{0:T(128)S(1)}, f32[32]{0:T(128)S(1)}, u32[]{:S(2)}, u32[]{:S(2)}) %collective-permute-start.5) | collective-permute-done | bytes 160 | tf_op jit(solution)/shard_map/ppermute | solution.py:42
  50.0 0.1 slice_multiply_fusion
  50.1 0.0 copy-start.7
  50.1 0.0 copy-start.8
  50.1 0.1 mul.94
  50.1 0.6 copy-done.7
  50.7 0.0 copy-done.8
  50.7 0.6 %add_bitcast_fusion.1 = (f32[1,4]{1,0:T(1,128)}, f32[4]{0:T(128)S(1)}, f32[4]{0:T(128)S(1)}, f32[4]{0:T(128)S(1)}, f32[4]{0:T(128)S(1)}) fusion(f32[1,4]{1,0:T(1,128)S(1)} %copy-done.8, f32[32]{0:T(128)S(1)} %add.53, f32[1,4]{1,0:T(1,128)S(1)} %copy-done.6, f32[1,4]{1,0:T(1,128)S(1)} %copy-done.7), kind=kLoop, calls=%fused_computation.27 | loop fusion | flops 120 | bytes 176 | tf_op jit(solution)/shard_map/broadcast_in_dim | solution.py:416
  51.3 0.7 %concatenate.18.sc_ref = f32[62]{0:T(128)} concatenate(f32[25]{0:T(128)S(1)} %reshape.47, f32[25]{0:T(128)S(1)} %reshape.48, f32[4]{0:T(128)S(1)} %broadcast_multiply_fusion, f32[4]{0:T(128)S(1)} %get-tuple-element.14, f32[4]{0:T(128)S(1)} %get-tuple-element.12), dimensions={0} | concatenate | bytes 496 | tf_op jit(solution)/shard_map/concatenate | solution.py:415
  52.0 0.7 %add_bitcast_fusion = f32[1,4]{1,0:T(1,128)} fusion(f32[4]{0:T(128)S(1)} %get-tuple-element.14, f32[4]{0:T(128)S(1)} %get-tuple-element.12, f32[4]{0:T(128)S(1)} %get-tuple-element.13, f32[1,4]{1,0:T(1,128)S(1)} %copy-done.8, f32[32]{0:T(128)S(1)} %add.53, f32[4,4]{1,0:T(4,128)S(1)} %mul.94, f32[4]{0:T(128)S(1)} %get-tuple-element.15), kind=kOutput, calls=%fused_computation.25 | convolution fusion | flops 264 | bytes 192 | tf_op jit(solution)/shard_map/dot_general | solution.py:405
  52.6 4.4 %shard_map.132 = f32[5,96,256]{2,1,0:T(8,128)} custom-call(f32[62]{0:T(128)} %concatenate.18.sc_ref, f32[5,96,384]{2,1,0:T(8,128)} %get-tuple-element.10.a_ref, f32[5,96,256]{2,1,0:T(8,128)} %bitcast.79, f32[4,96,256]{2,1,0:T(8,128)} %ms_ref.3, f32[2,5,256]{2,1,0:T(8,128)} %copy-done.2, f32[2,5,256]{2,1,0:T(8,128)} %copy-done.3, f32[884,128]{1,0:T(8,128)} %pad.7.left_ref, ...), custom_call_target="tpu_custom_call" | custom-call | tf_op jit(solution)/shard_map/pallas_call | solution.py:410
  (11 shorter events, 0.2 us)
Async XLA Ops:
  3.1 6.5 %copy-start.4 = (f32[5,5]{1,0:T(8,128)S(1)}, f32[5,5]{1,0:T(8,128)}, u32[]{:S(2)}) copy-start(f32[5,5]{1,0:T(8,128)} %param.16) | copy-start | bytes 304
  3.1 6.5 %copy-start.5 = (f32[5,5]{1,0:T(8,128)S(1)}, f32[5,5]{1,0:T(8,128)}, u32[]{:S(2)}) copy-start(f32[5,5]{1,0:T(8,128)} %param.17) | copy-start | bytes 304
  3.1 6.6 %copy-start.1 = (f32[4,96,256]{2,1,0:T(8,128)S(1)}, f32[4,96,256]{2,1,0:T(8,128)}, u32[]{:S(2)}) copy-start(f32[4,96,256]{2,1,0:T(8,128)} %ms_ref.3) | copy-start | bytes 1179652
  5.0 4.8 %copy-start = (f32[1,5,96,256]{3,2,1,0:T(8,128)S(1)}, f32[1,5,96,256]{3,2,1,0:T(8,128)}, u32[]{:S(2)}) copy-start(f32[1,5,96,256]{3,2,1,0:T(8,128)} %param.11) | copy-start | bytes 1474564
  5.0 6.2 %collective-permute-start = (f32[2,5,256]{2,1,0:T(8,128)}, f32[2,5,256]{2,1,0:T(8,128)S(1)}, u32[]{:S(2)}, u32[]{:S(2)}) collective-permute-start(f32[2,5,256]{2,1,0:T(8,128)} %get-tuple-element.7), channel_id=1, source_target_pairs={{0,4},{4,8},{8,12},{12,16},{16,20},{20,24},{24,28},{28,0},{1,5},{5... | collective-permute-start | bytes 30728 | tf_op jit(solution)/shard_map/ppermute | solution.py:23
  5.5 6.4 %collective-permute-start.1 = (f32[2,5,256]{2,1,0:T(8,128)}, f32[2,5,256]{2,1,0:T(8,128)S(1)}, u32[]{:S(2)}, u32[]{:S(2)}) collective-permute-start(f32[2,5,256]{2,1,0:T(8,128)} %get-tuple-element.8), channel_id=1, source_target_pairs={{0,28},{4,0},{8,4},{12,8},{16,12},{20,16},{24,20},{28,24},{1,29},{... | collective-permute-start | bytes 30728 | tf_op jit(solution)/shard_map/ppermute | solution.py:23
  10.0 0.7 %copy-start.6 = (f32[1,4]{1,0:T(1,128)S(1)}, f32[1,4]{1,0:T(1,128)}, u32[]{:S(2)}) copy-start(f32[1,4]{1,0:T(1,128)} %param.21) | copy-start | bytes 52
  11.2 0.6 %copy-start.2 = (f32[2,5,256]{2,1,0:T(8,128)}, f32[2,5,256]{2,1,0:T(8,128)S(1)}, u32[]{:S(2)}) copy-start(f32[2,5,256]{2,1,0:T(8,128)S(1)} %collective-permute-done.glo_ref) | copy-start | bytes 30724
  11.8 0.6 %copy-start.3 = (f32[2,5,256]{2,1,0:T(8,128)}, f32[2,5,256]{2,1,0:T(8,128)S(1)}, u32[]{:S(2)}) copy-start(f32[2,5,256]{2,1,0:T(8,128)S(1)} %collective-permute-done.1.gup_ref) | copy-start | bytes 30724
  12.5 14.3 %collective-permute-start.2 = (f32[884,4]{1,0:T(8,128)S(1)}, f32[884,4]{1,0:T(8,128)S(1)}, u32[]{:S(2)}, u32[]{:S(2)}) collective-permute-start(f32[884,4]{1,0:T(8,128)S(1)} %pad_maximum_fusion), channel_id=1, source_target_pairs={{0,1},{1,2},{2,3},{3,0},{4,5},{5,6},{6,7},{7,4},{8,9},{9,10},{10,1... | collective-permute-start | bytes 42440 | tf_op jit(solution)/shard_map/ppermute | solution.py:23
  14.5 21.0 %collective-permute-start.3 = (f32[884,4]{1,0:T(8,128)S(1)}, f32[884,4]{1,0:T(8,128)S(1)}, u32[]{:S(2)}, u32[]{:S(2)}) collective-permute-start(f32[884,4]{1,0:T(8,128)S(1)} %pad_maximum_fusion.1), channel_id=1, source_target_pairs={{0,3},{1,0},{2,1},{3,2},{4,7},{5,4},{6,5},{7,6},{8,11},{9,8},{10,9... | collective-permute-start | bytes 42440 | tf_op jit(solution)/shard_map/ppermute | solution.py:23
  42.8 3.6 %collective-permute-start.4 = (f32[32]{0:T(128)S(1)}, f32[32]{0:T(128)S(1)}, u32[]{:S(2)}, u32[]{:S(2)}) collective-permute-start(f32[32]{0:T(128)S(1)} %reduce_sum.9), channel_id=1, source_target_pairs={{0,1},{1,0},{2,3},{3,2},{4,5},{5,4},{6,7},{7,6},{8,9},{9,8},{10,11... | collective-permute-start | bytes 392 | tf_op jit(solution)/shard_map/ppermute | solution.py:42
  46.4 3.5 %collective-permute-start.5 = (f32[32]{0:T(128)S(1)}, f32[32]{0:T(128)S(1)}, u32[]{:S(2)}, u32[]{:S(2)}) collective-permute-start(f32[32]{0:T(128)S(1)} %add.52), channel_id=1, source_target_pairs={{0,2},{1,3},{2,0},{3,1},{4,6},{5,7},{6,4},{7,5},{8,10},{9,11},{10,... | collective-permute-start | bytes 392 | tf_op jit(solution)/shard_map/ppermute | solution.py:42
  50.1 0.7 %copy-start.7 = (f32[1,4]{1,0:T(1,128)S(1)}, f32[1,4]{1,0:T(1,128)}, u32[]{:S(2)}) copy-start(f32[1,4]{1,0:T(1,128)} %param.20) | copy-start | bytes 52
  50.1 0.7 %copy-start.8 = (f32[1,4]{1,0:T(1,128)S(1)}, f32[1,4]{1,0:T(1,128)}, u32[]{:S(2)}) copy-start(f32[1,4]{1,0:T(1,128)} %param.19) | copy-start | bytes 52

commit v6 on v5

--- a/solution.py
+++ b/solution.py
@@ -131,8 +131,8 @@
 
 
 def pack(parts, width):
-    flat = [part.reshape(-1, width) for part in parts]
-    return jnp.concatenate(flat, axis=0)
+    flat = [jnp.moveaxis(part, -1, 0).reshape(width, -1) for part in parts]
+    return jnp.concatenate(flat, axis=1)
 
 
 def unpack(buffer, shapes):
@@ -194,13 +194,16 @@
 
 
 def pick_kernel(peers, lower_slot_ref, upper_slot_ref, upper_hist_ref, lower_hist_ref, up_ref, down_ref):
-    slots = upper_hist_ref.shape[0]
+    fields, slots = upper_hist_ref.shape[0], upper_hist_ref.shape[1]
     position = lax.axis_index("blk")
     slot_next = lower_slot_ref[(position + 1) % peers]
     slot_prev = upper_slot_ref[(position + peers - 1) % peers]
     for s in range(up_ref.shape[0]):
-        up_ref[s] = upper_hist_ref[(slot_next + s) % slots]
-        down_ref[s] = lower_hist_ref[(slot_prev + s) % slots]
+        up_at = (slot_next + s) % slots
+        down_at = (slot_prev + s) % slots
+        for f in range(fields):
+            up_ref[s, f : f + 1, :] = upper_hist_ref[f, pl.ds(up_at, 1), :]
+            down_ref[s, f : f + 1, :] = lower_hist_ref[f, pl.ds(down_at, 1), :]
 
 
 def widened(own, left, right):
@@ -356,20 +359,27 @@
         out_shape=(row_shape, row_shape),
         in_specs=[smem_spec(), smem_spec(), vmem_spec(), vmem_spec()],
         out_specs=(vmem_spec(), vmem_spec()),
-    )(lower_lag_slot, upper_lag_slot, upper_row_history[0], lower_row_history[0])
+    )(
+        lower_lag_slot,
+        upper_lag_slot,
+        jnp.transpose(upper_row_history[0], (1, 0, 2)),
+        jnp.transpose(lower_row_history[0], (1, 0, 2)),
+    )
     lower_ghosts = shifted(rows_up, "blk", 1)
     upper_ghosts = shifted(rows_down, "blk", -1)
 
     reach = 2 * STEP_COUNT
     own = [state0, mode_shape, lower_ghosts, upper_ghosts]
     shapes = [part.shape[:-1] + (reach,) for part in own]
-    from_left = shifted(pack([part[..., -reach:] for part in own], reach), "mesh", 1)
-    from_right = shifted(pack([part[..., :reach] for part in own], reach), "mesh", -1)
+    from_left = shifted(pack([part[..., -reach:] for part in own], reach).reshape(-1), "mesh", 1)
+    from_right = shifted(pack([part[..., :reach] for part in own], reach).reshape(-1), "mesh", -1)
+    from_left = from_left.reshape(reach, -1)
+    from_right = from_right.reshape(reach, -1)
     from_left = jnp.where(me > 0, from_left, jnp.zeros_like(from_left))
     from_right = jnp.where(me < mesh_peers - 1, from_right, jnp.zeros_like(from_right))
     pad = [(0, 0), (0, LANES - reach)]
-    from_left = jnp.pad(from_left, pad)
-    from_right = jnp.pad(from_right, pad)
+    from_left = jnp.pad(from_left.T, pad)
+    from_right = jnp.pad(from_right.T, pad)
     lanes_wide = axial_cells + LANES
     ins = (state0, mode_shape, lower_ghosts, upper_ghosts, from_left, from_right)
 

time: 57.3 us -> 42.1 us (0.73)
  waiting for transfers between devices: 24.3 us -> 11.1 us
  starting transfers between devices: 9.44 us -> 8.02 us
    ppermute x4, waiting for transfers between devices: 19.1 us -> 4.55 us  [shifted(): lax.ppermute(value, axis, [(i, (i + by) % peers) for i in range(peers)])]
    squeeze x1 -> x0, local copies, waits for them, and re-layouts: 2.47 us -> none  [on_device(): lower_row_history[0]]
    ppermute x2, starting transfers between devices: 1.87 us -> 0.57 us  [mesh_sum(): lax.ppermute(value, 'mesh', [(i, i ^ step) for i in range(peers)])]
    ppermute x2, waiting for transfers between devices: 5.27 us -> 6.56 us  [mesh_sum(): lax.ppermute(value, 'mesh', [(i, i ^ step) for i in range(peers)])]
    reshape x4 -> x10, local copies, waits for them, and re-layouts: 0.01 us -> 0.96 us  [the longest x8 0.79 us: pack(): flat = [jnp.moveaxis(part, -1, 0).reshape(width, -1) for part in parts]]
    select_n x0 -> x4, local copies, waits for them, and re-layouts: none -> 0.59 us  [the longest x2 0.3 us: on_device(): jnp.where(me < mesh_peers - 1, from_right, jnp.zeros_like(from_right))]
  transfers between devices with their start and end apart: 6 -> 6, of which waited for: 4 -> 4; matrix products, arithmetic and copies ran while one was open for 3% -> 5% of each run, Pallas kernels for 0% -> 0%
where the time goes in v6:
time: 42.1 us; the launch traced here: 41.8 us
  Pallas kernels  11.8 us (28%)
  waiting for transfers between devices  11.1 us (26%)
  starting transfers between devices  8.02 us (19%)
  local copies, waits for them, and re-layouts  7.18 us (17%)
  other arithmetic  2.25 us (5%)
  between operations  0.73 us (2%)
  matrix products  0.65 us (2%)
    ppermute x4, starting transfers between devices, shifted(): lax.ppermute(value, axis, [(i, (i + by) % peers) for i in range(peers)])  7.44 us
    ppermute x2, waiting for transfers between devices, mesh_sum(): lax.ppermute(value, 'mesh', [(i, i ^ step) for i in range(peers)])  6.56 us
    pallas_call x1, Pallas kernels, on_device(): pl.pallas_call(functools.partial(first_kernel, mesh_peers), out_shape=(ja...  5.7 us
    ppermute x4, waiting for transfers between devices, shifted(): lax.ppermute(value, axis, [(i, (i + by) % peers) for i in range(peers)])  4.55 us
    pallas_call x1, Pallas kernels, on_device(): pl.pallas_call(functools.partial(second_kernel, mesh_peers), out_shape=ja...  4.36 us
    unnamed x18, local copies, waits for them, and re-layouts  2.32 us
    pallas_call x1, Pallas kernels, on_device(): pl.pallas_call(functools.partial(pick_kernel, passages), out_shape=(row_s...  1.77 us
  transfers between devices with their start and end apart: 6, of which 4 were waited for; matrix products, arithmetic and copies ran while one was open for 5% of the time, Pallas kernels for 0%

profile of v6, /device:TPU:0, one launch (start us, length us, event | category | flops | bytes accessed | tf_op | source)
XLA Modules:
  0.0 41.8 jit_solution(3463880659699878430)
XLA Ops:
  0.6 0.0 copy-start.1
  0.6 0.0 copy-start.4
  0.7 0.0 copy-start.5
  0.7 1.8 %shard_map.130 = (f32[2,5,256]{2,1,0:T(8,128)}, f32[2,5,256]{2,1,0:T(8,128)}) custom-call(s32[8]{0:T(128)} %lower_slot_ref.1, s32[8]{0:T(128)} %upper_slot_ref.1, f32[5,64,256]{2,1,0:T(8,128)} %bitcast.108, f32[5,64,256]{2,1,0:T(8,128)} %bitcast.109), custom_call_target="tpu_custom_call" | custom-call | tf_op jit(solution)/shard_map/pallas_call | solution.py:357
  2.4 0.0 copy-start
  2.4 0.5 %collective-permute-start = (f32[2,5,256]{2,1,0:T(8,128)}, f32[2,5,256]{2,1,0:T(8,128)S(1)}, u32[]{:S(2)}, u32[]{:S(2)}) collective-permute-start(f32[2,5,256]{2,1,0:T(8,128)} %get-tuple-element.7), channel_id=1, source_target_pairs={{0,4},{4,8},{8,12},{12,16},{16,20},{20,24},{24,28},{28,0},{1,5},{5... | collective-permute-start | bytes 30728 | tf_op jit(solution)/shard_map/ppermute | solution.py:23
  2.9 4.1 %collective-permute-start.1 = (f32[2,5,256]{2,1,0:T(8,128)}, f32[2,5,256]{2,1,0:T(8,128)S(1)}, u32[]{:S(2)}, u32[]{:S(2)}) collective-permute-start(f32[2,5,256]{2,1,0:T(8,128)} %get-tuple-element.8), channel_id=1, source_target_pairs={{0,28},{4,0},{8,4},{12,8},{16,12},{20,16},{24,20},{28,24},{1,29},{... | collective-permute-start | bytes 30728 | tf_op jit(solution)/shard_map/ppermute | solution.py:23
  7.0 0.0 copy-done.4
  7.0 0.1 reshape.61
  7.1 0.0 copy-done.5
  7.1 0.1 reshape.62
  7.1 0.0 copy-done.1
  7.2 0.1 fusion.16
  7.3 0.0 copy-done
  7.3 0.1 fusion.15
  7.4 0.0 copy-start.6
  7.4 0.7 %copy-done.6 = f32[1,4]{1,0:T(1,128)S(1)} copy-done((f32[1,4]{1,0:T(1,128)S(1)}, f32[1,4]{1,0:T(1,128)}, u32[]{:S(2)}) %copy-start.6) | copy-done | bytes 40
  8.1 0.6 %pad_maximum_fusion.2.sc_ref = f32[54]{0:T(128)} fusion(f32[4]{0:T(128)S(1)} %bitcast.110, f32[25]{0:T(128)S(1)} %reshape.62, f32[25]{0:T(128)S(1)} %reshape.61), kind=kLoop, calls=%fused_computation.10 | loop fusion | flops 108 | bytes 432 | tf_op jit(solution)/shard_map/concatenate | solution.py:395
  8.7 0.1 copy.30
  8.7 0.1 copy.25
  8.9 0.1 copy.29
  9.0 0.1 copy.24
  9.1 0.0 collective-permute-done.glo_ref
  9.1 0.1 slice_bitcast_fusion.1
  9.2 0.5 %copy-done.2 = f32[2,5,256]{2,1,0:T(8,128)} copy-done((f32[2,5,256]{2,1,0:T(8,128)}, f32[2,5,256]{2,1,0:T(8,128)S(1)}, u32[]{:S(2)}) %copy-start.2) | copy-done | bytes 10264
  9.7 0.1 copy.27
  9.8 0.1 reshape.70
  9.9 0.1 copy.22
  10.0 0.1 reshape.65
  10.1 0.0 collective-permute-done.1.gup_ref
  10.1 0.1 slice_bitcast_fusion
  10.2 0.5 %copy-done.3 = f32[2,5,256]{2,1,0:T(8,128)} copy-done((f32[2,5,256]{2,1,0:T(8,128)}, f32[2,5,256]{2,1,0:T(8,128)S(1)}, u32[]{:S(2)}) %copy-start.3) | copy-done | bytes 10264
  10.7 0.1 copy.28
  10.8 0.1 reshape.71
  10.9 0.1 copy.23
  11.0 0.1 reshape.66
  11.1 0.1 pad_maximum_fusion.1
  11.1 0.1 reshape.72
  11.2 2.9 %collective-permute-start.3 = (f32[3536]{0:T(1024)S(1)}, f32[3536]{0:T(1024)S(1)}, u32[]{:S(2)}, u32[]{:S(2)}) collective-permute-start(f32[3536]{0:T(1024)S(1)} %reshape.72), channel_id=1, source_target_pairs={{0,3},{1,0},{2,1},{3,2},{4,7},{5,4},{6,5},{7,6},{8,11},{9,8},{10,9... | collective-permute-start | bytes 42440 | tf_op jit(solution)/shard_map/ppermute | solution.py:23
  14.1 0.1 pad_maximum_fusion
  14.2 0.1 reshape.67
  14.3 0.0 collective-permute-start.2
  14.3 1.3 %collective-permute-done.3 = f32[3536]{0:T(1024)S(1)} collective-permute-done((f32[3536]{0:T(1024)S(1)}, f32[3536]{0:T(1024)S(1)}, u32[]{:S(2)}, u32[]{:S(2)}) %collective-permute-start.3) | collective-permute-done | bytes 14176 | tf_op jit(solution)/shard_map/ppermute | solution.py:23
  15.6 0.1 select_n.25
  15.7 3.3 %collective-permute-done.2 = f32[3536]{0:T(1024)S(1)} collective-permute-done((f32[3536]{0:T(1024)S(1)}, f32[3536]{0:T(1024)S(1)}, u32[]{:S(2)}, u32[]{:S(2)}) %collective-permute-start.2) | collective-permute-done | bytes 14176 | tf_op jit(solution)/shard_map/ppermute | solution.py:23
  18.9 0.1 select_n.22
  19.0 0.2 copy.26
  19.2 0.2 copy.31
  19.4 0.8 %pad.7.left_ref = f32[884,128]{1,0:T(8,128)} pad(f32[884,4]{1,0:T(8,128)S(1)} %bitcast.101, f32[]{:T(128)} %constant.3.clone.1), padding=0_0x0_124 | pad | bytes 466756 | tf_op jit(solution)/shard_map/jit(_pad)/pad | solution.py:381
  20.3 0.8 %pad.8.right_ref = f32[884,128]{1,0:T(8,128)} pad(f32[884,4]{1,0:T(8,128)S(1)} %bitcast.102, f32[]{:T(128)} %constant.3.clone.1), padding=0_0x0_124 | pad | bytes 466756 | tf_op jit(solution)/shard_map/jit(_pad)/pad | solution.py:382
  21.1 5.7 %shard_map.131 = (f32[5,96,384]{2,1,0:T(8,128)}, f32[32,128]{1,0:T(8,128)}) custom-call(f32[54]{0:T(128)} %pad_maximum_fusion.2.sc_ref, f32[5,96,256]{2,1,0:T(8,128)} %bitcast.98, f32[4,96,256]{2,1,0:T(8,128)} %ms_ref.3, f32[2,5,256]{2,1,0:T(8,128)} %copy-done.2, f32[2,5,256]{2,1,0:T(8,128)} %copy-done.3, f32[884,128]{1,0:T(8,128)} %pad.7.left_ref, ...), custom_call_target="tpu_custom_call" | custom-call | tf_op jit(solution)/shard_map/pallas_call | solution.py:387
  26.8 0.8 %reduce_sum.9 = f32[32]{0:T(128)S(1)} reduce(f32[32,128]{1,0:T(8,128)} %get-tuple-element.9, f32[]{:T(128)} %constant.3.clone.1), dimensions={1}, to_apply=%region_0.1 | reduce | flops 4064 | bytes 16516 | tf_op jit(solution)/shard_map/reduce_sum | solution.py:397
  27.6 0.1 collective-permute-start.4
  27.7 3.5 %collective-permute-done.4 = f32[32]{0:T(128)S(1)} collective-permute-done((f32[32]{0:T(128)S(1)}, f32[32]{0:T(128)S(1)}, u32[]{:S(2)}, u32[]{:S(2)}) %collective-permute-start.4) | collective-permute-done | bytes 160 | tf_op jit(solution)/shard_map/ppermute | solution.py:42
  31.2 0.5 %collective-permute-start.5 = (f32[32]{0:T(128)S(1)}, f32[32]{0:T(128)S(1)}, u32[]{:S(2)}, u32[]{:S(2)}) collective-permute-start(f32[32]{0:T(128)S(1)} %add.52), channel_id=1, source_target_pairs={{0,2},{1,3},{2,0},{3,1},{4,6},{5,7},{6,4},{7,5},{8,10},{9,11},{10,... | collective-permute-start | bytes 392 | tf_op jit(solution)/shard_map/ppermute | solution.py:42
  31.7 3.0 %collective-permute-done.5 = f32[32]{0:T(128)S(1)} collective-permute-done((f32[32]{0:T(128)S(1)}, f32[32]{0:T(128)S(1)}, u32[]{:S(2)}, u32[]{:S(2)}) %collective-permute-start.5) | collective-permute-done | bytes 160 | tf_op jit(solution)/shard_map/ppermute | solution.py:42
  34.8 0.1 slice_multiply_fusion
  34.8 0.1 mul.94
  34.9 0.6 %copy-done.7 = f32[1,4]{1,0:T(1,128)S(1)} copy-done((f32[1,4]{1,0:T(1,128)S(1)}, f32[1,4]{1,0:T(1,128)}, u32[]{:S(2)}) %copy-start.7) | copy-done | bytes 40
  35.5 0.0 copy-done.8
  35.5 0.6 %add_bitcast_fusion.1 = (f32[1,4]{1,0:T(1,128)}, f32[4]{0:T(128)S(1)}, f32[4]{0:T(128)S(1)}, f32[4]{0:T(128)S(1)}, f32[4]{0:T(128)S(1)}) fusion(f32[1,4]{1,0:T(1,128)S(1)} %copy-done.8, f32[32]{0:T(128)S(1)} %add.53, f32[1,4]{1,0:T(1,128)S(1)} %copy-done.6, f32[1,4]{1,0:T(1,128)S(1)} %copy-done.7), kind=kLoop, calls=%fused_computation.29 | loop fusion | flops 120 | bytes 176 | tf_op jit(solution)/shard_map/broadcast_in_dim | solution.py:426
  36.1 0.7 %concatenate.18.sc_ref = f32[62]{0:T(128)} concatenate(f32[25]{0:T(128)S(1)} %reshape.61, f32[25]{0:T(128)S(1)} %reshape.62, f32[4]{0:T(128)S(1)} %broadcast_multiply_fusion, f32[4]{0:T(128)S(1)} %get-tuple-element.14, f32[4]{0:T(128)S(1)} %get-tuple-element.12), dimensions={0} | concatenate | bytes 496 | tf_op jit(solution)/shard_map/concatenate | solution.py:425
  36.8 0.7 %add_bitcast_fusion = f32[1,4]{1,0:T(1,128)} fusion(f32[4]{0:T(128)S(1)} %get-tuple-element.14, f32[4]{0:T(128)S(1)} %get-tuple-element.12, f32[4]{0:T(128)S(1)} %get-tuple-element.13, f32[1,4]{1,0:T(1,128)S(1)} %copy-done.8, f32[32]{0:T(128)S(1)} %add.53, f32[4,4]{1,0:T(4,128)S(1)} %mul.94, f32[4]{0:T(128)S(1)} %get-tuple-element.15), kind=kOutput, calls=%fused_computation.27 | convolution fusion | flops 264 | bytes 192 | tf_op jit(solution)/shard_map/dot_general | solution.py:415
  37.4 4.4 %shard_map.132 = f32[5,96,256]{2,1,0:T(8,128)} custom-call(f32[62]{0:T(128)} %concatenate.18.sc_ref, f32[5,96,384]{2,1,0:T(8,128)} %get-tuple-element.10.a_ref, f32[5,96,256]{2,1,0:T(8,128)} %bitcast.99, f32[4,96,256]{2,1,0:T(8,128)} %ms_ref.3, f32[2,5,256]{2,1,0:T(8,128)} %copy-done.2, f32[2,5,256]{2,1,0:T(8,128)} %copy-done.3, f32[884,128]{1,0:T(8,128)} %pad.7.left_ref, ...), custom_call_target="tpu_custom_call" | custom-call | tf_op jit(solution)/shard_map/pallas_call | solution.py:420
  (9 shorter events, 0.0 us)
Async XLA Ops:
  0.6 6.5 %copy-start.1 = (f32[4,96,256]{2,1,0:T(8,128)S(1)}, f32[4,96,256]{2,1,0:T(8,128)}, u32[]{:S(2)}) copy-start(f32[4,96,256]{2,1,0:T(8,128)} %ms_ref.3) | copy-start | bytes 1179652
  0.6 6.3 %copy-start.4 = (f32[5,5]{1,0:T(8,128)S(1)}, f32[5,5]{1,0:T(8,128)}, u32[]{:S(2)}) copy-start(f32[5,5]{1,0:T(8,128)} %param.16) | copy-start | bytes 304
  0.7 6.4 %copy-start.5 = (f32[5,5]{1,0:T(8,128)S(1)}, f32[5,5]{1,0:T(8,128)}, u32[]{:S(2)}) copy-start(f32[5,5]{1,0:T(8,128)} %param.17) | copy-start | bytes 304
  2.4 4.8 %copy-start = (f32[1,5,96,256]{3,2,1,0:T(8,128)S(1)}, f32[1,5,96,256]{3,2,1,0:T(8,128)}, u32[]{:S(2)}) copy-start(f32[1,5,96,256]{3,2,1,0:T(8,128)} %param.11) | copy-start | bytes 1474564
  2.4 6.7 %collective-permute-start = (f32[2,5,256]{2,1,0:T(8,128)}, f32[2,5,256]{2,1,0:T(8,128)S(1)}, u32[]{:S(2)}, u32[]{:S(2)}) collective-permute-start(f32[2,5,256]{2,1,0:T(8,128)} %get-tuple-element.7), channel_id=1, source_target_pairs={{0,4},{4,8},{8,12},{12,16},{16,20},{20,24},{24,28},{28,0},{1,5},{5... | collective-permute-start | bytes 30728 | tf_op jit(solution)/shard_map/ppermute | solution.py:23
  2.9 7.2 %collective-permute-start.1 = (f32[2,5,256]{2,1,0:T(8,128)}, f32[2,5,256]{2,1,0:T(8,128)S(1)}, u32[]{:S(2)}, u32[]{:S(2)}) collective-permute-start(f32[2,5,256]{2,1,0:T(8,128)} %get-tuple-element.8), channel_id=1, source_target_pairs={{0,28},{4,0},{8,4},{12,8},{16,12},{20,16},{24,20},{28,24},{1,29},{... | collective-permute-start | bytes 30728 | tf_op jit(solution)/shard_map/ppermute | solution.py:23
  7.4 0.7 %copy-start.6 = (f32[1,4]{1,0:T(1,128)S(1)}, f32[1,4]{1,0:T(1,128)}, u32[]{:S(2)}) copy-start(f32[1,4]{1,0:T(1,128)} %param.21) | copy-start | bytes 52
  9.1 0.6 %copy-start.2 = (f32[2,5,256]{2,1,0:T(8,128)}, f32[2,5,256]{2,1,0:T(8,128)S(1)}, u32[]{:S(2)}) copy-start(f32[2,5,256]{2,1,0:T(8,128)S(1)} %collective-permute-done.glo_ref) | copy-start | bytes 30724
  10.1 0.6 %copy-start.3 = (f32[2,5,256]{2,1,0:T(8,128)}, f32[2,5,256]{2,1,0:T(8,128)S(1)}, u32[]{:S(2)}) copy-start(f32[2,5,256]{2,1,0:T(8,128)S(1)} %collective-permute-done.1.gup_ref) | copy-start | bytes 30724
  11.2 4.3 %collective-permute-start.3 = (f32[3536]{0:T(1024)S(1)}, f32[3536]{0:T(1024)S(1)}, u32[]{:S(2)}, u32[]{:S(2)}) collective-permute-start(f32[3536]{0:T(1024)S(1)} %reshape.72), channel_id=1, source_target_pairs={{0,3},{1,0},{2,1},{3,2},{4,7},{5,4},{6,5},{7,6},{8,11},{9,8},{10,9... | collective-permute-start | bytes 42440 | tf_op jit(solution)/shard_map/ppermute | solution.py:23
  14.3 4.6 %collective-permute-start.2 = (f32[3536]{0:T(1024)S(1)}, f32[3536]{0:T(1024)S(1)}, u32[]{:S(2)}, u32[]{:S(2)}) collective-permute-start(f32[3536]{0:T(1024)S(1)} %reshape.67), channel_id=1, source_target_pairs={{0,1},{1,2},{2,3},{3,0},{4,5},{5,6},{6,7},{7,4},{8,9},{9,10},{10,1... | collective-permute-start | bytes 42440 | tf_op jit(solution)/shard_map/ppermute | solution.py:23
  27.6 3.6 %collective-permute-start.4 = (f32[32]{0:T(128)S(1)}, f32[32]{0:T(128)S(1)}, u32[]{:S(2)}, u32[]{:S(2)}) collective-permute-start(f32[32]{0:T(128)S(1)} %reduce_sum.9), channel_id=1, source_target_pairs={{0,1},{1,0},{2,3},{3,2},{4,5},{5,4},{6,7},{7,6},{8,9},{9,8},{10,11... | collective-permute-start | bytes 392 | tf_op jit(solution)/shard_map/ppermute | solution.py:42
  31.2 3.5 %collective-permute-start.5 = (f32[32]{0:T(128)S(1)}, f32[32]{0:T(128)S(1)}, u32[]{:S(2)}, u32[]{:S(2)}) collective-permute-start(f32[32]{0:T(128)S(1)} %add.52), channel_id=1, source_target_pairs={{0,2},{1,3},{2,0},{3,1},{4,6},{5,7},{6,4},{7,5},{8,10},{9,11},{10,... | collective-permute-start | bytes 392 | tf_op jit(solution)/shard_map/ppermute | solution.py:42
  34.8 0.7 %copy-start.7 = (f32[1,4]{1,0:T(1,128)S(1)}, f32[1,4]{1,0:T(1,128)}, u32[]{:S(2)}) copy-start(f32[1,4]{1,0:T(1,128)} %param.20) | copy-start | bytes 52
  34.8 0.7 %copy-start.8 = (f32[1,4]{1,0:T(1,128)S(1)}, f32[1,4]{1,0:T(1,128)}, u32[]{:S(2)}) copy-start(f32[1,4]{1,0:T(1,128)} %param.19) | copy-start | bytes 52

commit v7 on v6

--- a/solution.py
+++ b/solution.py
@@ -179,9 +179,9 @@
     return out
 
 
-def read_jacobians(sc_ref, fields):
-    ax = [[sc_ref[i * fields + j] for j in range(fields)] for i in range(fields)]
-    pt = [[sc_ref[fields * fields + i * fields + j] for j in range(fields)] for i in range(fields)]
+def read_jacobians(ax_ref, pt_ref, fields):
+    ax = [[ax_ref[i, j] for j in range(fields)] for i in range(fields)]
+    pt = [[pt_ref[i, j] for j in range(fields)] for i in range(fields)]
     return ax, pt
 
 
@@ -246,14 +246,13 @@
     return u, ms, ghosts[0], ghosts[1]
 
 
-def first_kernel(peers, sc_ref, u_ref, ms_ref, glo_ref, gup_ref, left_ref, right_ref, a_ref, part_ref):
+def first_kernel(peers, ax_ref, pt_ref, vel_ref, u_ref, ms_ref, glo_ref, gup_ref, left_ref, right_ref, a_ref, part_ref):
     h = TIME_STEP
     fields = u_ref.shape[0]
     modes = ms_ref.shape[0]
     pitch = u_ref.shape[1]
-    jac = read_jacobians(sc_ref, fields)
-    base = 2 * fields * fields
-    vel = [sc_ref[base + m] for m in range(modes)]
+    jac = read_jacobians(ax_ref, pt_ref, fields)
+    vel = [vel_ref[0, m] for m in range(modes)]
     u0, ms, gl, gu = assemble(u_ref, ms_ref, glo_ref, gup_ref, left_ref, right_ref, fields, modes, pitch)
     inside, owned = lane_masks(peers, u0[0].shape, u_ref.shape[-1])
     push = vel[0] * ms[0]
@@ -289,14 +288,73 @@
             part_ref[k + m * modes + n : k + m * modes + n + 1, :] = lane_fold(weighted[m] * t)
 
 
-def second_kernel(peers, sc_ref, a_ref, u_ref, ms_ref, glo_ref, gup_ref, left_ref, right_ref, out_ref):
+def modal_steps(force_scale, tot_ref, stiff_ref, disp_ref, vel_ref, modes):
+    h = TIME_STEP
+    t = [force_scale * tot_ref[k] for k in range(4 * modes + modes * modes)]
+    force = [t[w * modes : (w + 1) * modes] for w in range(4)]
+    couple = [t[4 * modes + m * modes : 4 * modes + (m + 1) * modes] for m in range(modes)]
+    stiff = [stiff_ref[0, m] for m in range(modes)]
+    disp0 = [disp_ref[0, m] for m in range(modes)]
+    vel0 = [vel_ref[0, m] for m in range(modes)]
+
+    def accel(f, q, v):
+        return [f[m] - stiff[m] * q[m] - DAMPING * v[m] for m in range(modes)]
+
+    def axpy(x, a, y):
+        return [x[m] + a * y[m] for m in range(modes)]
+
+    acc1 = accel(force[0], disp0, vel0)
+    disp1m = axpy(disp0, h, vel0)
+    vel1m = axpy(vel0, h, acc1)
+    acc1m = accel(force[1], disp1m, vel1m)
+    disp1 = [disp0[m] + 0.5 * h * (vel0[m] + vel1m[m]) for m in range(modes)]
+    vel1 = [vel0[m] + 0.5 * h * (acc1[m] + acc1m[m]) for m in range(modes)]
+    acc2 = accel(force[2], disp1, vel1)
+    disp2m = axpy(disp1, h, vel1)
+    vel2m = axpy(vel1, h, acc2)
+    corr = 0.5 * h * h * COUPLING
+    force2m = []
+    for m in range(modes):
+        coupled = couple[m][0] * acc1[0]
+        for n in range(1, modes):
+            coupled = coupled + couple[m][n] * acc1[n]
+        force2m.append(force[2][m] + h * force[3][m] + h * corr * coupled)
+    acc2m = accel(force2m, disp2m, vel2m)
+    disp2 = [disp1[m] + 0.5 * h * (vel1[m] + vel2m[m]) for m in range(modes)]
+    vel2 = [vel1[m] + 0.5 * h * (acc2[m] + acc2m[m]) for m in range(modes)]
+    coef = [[corr * acc1[m] for m in range(modes)], vel1, vel2m]
+    return coef, disp2, vel2
+
+
+def second_kernel(
+    peers,
+    force_scale,
+    tot_ref,
+    stiff_ref,
+    disp_ref,
+    vel_ref,
+    ax_ref,
+    pt_ref,
+    a_ref,
+    u_ref,
+    ms_ref,
+    glo_ref,
+    gup_ref,
+    left_ref,
+    right_ref,
+    out_ref,
+    disp_out_ref,
+    vel_out_ref,
+):
     h = TIME_STEP
     fields = a_ref.shape[0]
     modes = ms_ref.shape[0]
     pitch = u_ref.shape[1]
-    jac = read_jacobians(sc_ref, fields)
-    base = 2 * fields * fields
-    coef = [[sc_ref[base + w * modes + m] for m in range(modes)] for w in range(3)]
+    jac = read_jacobians(ax_ref, pt_ref, fields)
+    coef, disp2, vel2 = modal_steps(force_scale, tot_ref, stiff_ref, disp_ref, vel_ref, modes)
+    for m in range(modes):
+        disp_out_ref[0, m] = disp2[m]
+        vel_out_ref[0, m] = vel2[m]
     _, ms, gl, gu = assemble(u_ref, ms_ref, glo_ref, gup_ref, left_ref, right_ref, fields, modes, pitch)
     inside, _ = lane_masks(peers, ms[0].shape, u_ref.shape[-1])
 
@@ -383,47 +441,26 @@
     lanes_wide = axial_cells + LANES
     ins = (state0, mode_shape, lower_ghosts, upper_ghosts, from_left, from_right)
 
-    jac_flat = jnp.concatenate([axial_jacobian.reshape(-1), pitch_jacobian.reshape(-1)])
     base1, part_lanes = pl.pallas_call(
         functools.partial(first_kernel, mesh_peers),
         out_shape=(
             jax.ShapeDtypeStruct((fields, pitch_cells, lanes_wide), state0.dtype),
             jax.ShapeDtypeStruct((4 * modes + modes * modes, LANES), state0.dtype),
         ),
-        in_specs=[smem_spec()] + [vmem_spec()] * 6,
+        in_specs=[smem_spec()] * 3 + [vmem_spec()] * 6,
         out_specs=(vmem_spec(), vmem_spec()),
-    )(jnp.concatenate([jac_flat, vel0]), *ins)
+    )(axial_jacobian, pitch_jacobian, velocity, *ins)
 
     totals = mesh_sum(jnp.sum(part_lanes, axis=1))
-    force0 = force_scale * totals[0:modes]
-    force1 = force_scale * totals[modes : 2 * modes]
-    force2 = force_scale * totals[2 * modes : 3 * modes]
-    force3 = force_scale * totals[3 * modes : 4 * modes]
-    couple = force_scale * totals[4 * modes :].reshape(modes, modes)
-
-    acc1 = force0 - blade_stiffness * disp0 - DAMPING * vel0
-    disp1m = disp0 + h * vel0
-    vel1m = vel0 + h * acc1
-    acc1m = force1 - blade_stiffness * disp1m - DAMPING * vel1m
-    disp1 = disp0 + 0.5 * h * (vel0 + vel1m)
-    vel1 = vel0 + 0.5 * h * (acc1 + acc1m)
-
-    acc2 = force2 - blade_stiffness * disp1 - DAMPING * vel1
-    disp2m = disp1 + h * vel1
-    vel2m = vel1 + h * acc2
-    corr = 0.5 * h * h * COUPLING
-    force2m = force2 + h * force3 + h * corr * jnp.dot(couple, acc1, precision=PRECISE)
-    acc2m = force2m - blade_stiffness * disp2m - DAMPING * vel2m
-    disp2 = disp1 + 0.5 * h * (vel1 + vel2m)
-    vel2 = vel1 + 0.5 * h * (acc2 + acc2m)
-
-    state2 = pl.pallas_call(
-        functools.partial(second_kernel, mesh_peers),
-        out_shape=jax.ShapeDtypeStruct(state0.shape, state0.dtype),
-        in_specs=[smem_spec()] + [vmem_spec()] * 7,
-        out_specs=vmem_spec(),
-    )(jnp.concatenate([jac_flat, corr * acc1, vel1, vel2m]), base1, *ins)
-    return (state2[None], disp2[None], vel2[None])
+
+    small = jax.ShapeDtypeStruct(displacement.shape, displacement.dtype)
+    state2, disp2, vel2 = pl.pallas_call(
+        functools.partial(second_kernel, mesh_peers, force_scale),
+        out_shape=(jax.ShapeDtypeStruct(state0.shape, state0.dtype), small, small),
+        in_specs=[smem_spec()] * 6 + [vmem_spec()] * 7,
+        out_specs=(vmem_spec(), smem_spec(), smem_spec()),
+    )(totals, stiffness, displacement, velocity, axial_jacobian, pitch_jacobian, base1, *ins)
+    return (state2[None], disp2, vel2)
 
 
 def solution(mesh):

time: 42.1 us -> 39.4 us (0.936)
  local copies, waits for them, and re-layouts: 7.18 us -> 5.87 us
  other arithmetic: 2.25 us -> 1.51 us
  matrix products: 0.65 us -> 0 us
    concatenate x1 -> x0, local copies, waits for them, and re-layouts: 0.66 us -> none  [on_device(): jnp.concatenate([jac_flat, corr * acc1, vel1, vel2m])]
    dot_general x1 -> x0, matrix products: 0.65 us -> none  [on_device(): jnp.dot(couple, acc1, precision=PRECISE)]
    broadcast_in_dim x1 -> x0, other arithmetic: 0.6 us -> none  [on_device(): return (state2[None], disp2[None], vel2[None])]
    concatenate x1 -> x0, other arithmetic: 0.59 us -> none  [on_device(): jnp.concatenate([jac_flat, vel0])]
    add x2, other arithmetic: 0.01 us -> 0.52 us  [mesh_sum(): value + lax.ppermute(value, 'mesh', [(i, i ^ step) for i in range(peers)])]
    unnamed x18 -> x8, local copies, waits for them, and re-layouts: 2.32 us -> 1.92 us
  transfers between devices with their start and end apart: 6 -> 6, of which waited for: 4 -> 4; matrix products, arithmetic and copies ran while one was open for 5% -> 4% of each run, Pallas kernels for 0% -> 0%
where the time goes in v7:
time: 39.4 us; the launch traced here: 39.1 us
  Pallas kernels  11.9 us (30%)
  waiting for transfers between devices  11.2 us (28%)
  starting transfers between devices  8.02 us (20%)
  local copies, waits for them, and re-layouts  5.87 us (15%)
  other arithmetic  1.51 us (4%)
  between operations  0.7 us (2%)
    ppermute x4, starting transfers between devices, shifted(): lax.ppermute(value, axis, [(i, (i + by) % peers) for i in range(peers)])  7.45 us
    ppermute x2, waiting for transfers between devices, mesh_sum(): lax.ppermute(value, 'mesh', [(i, i ^ step) for i in range(peers)])  6.56 us
    pallas_call x1, Pallas kernels, on_device(): pl.pallas_call(functools.partial(first_kernel, mesh_peers), out_shape=(ja...  5.69 us
    ppermute x4, waiting for transfers between devices, shifted(): lax.ppermute(value, axis, [(i, (i + by) % peers) for i in range(peers)])  4.59 us
    pallas_call x1, Pallas kernels, on_device(): pl.pallas_call(functools.partial(second_kernel, mesh_peers, force_scale),...  4.38 us
    unnamed x8, local copies, waits for them, and re-layouts  1.92 us
    pallas_call x1, Pallas kernels, on_device(): pl.pallas_call(functools.partial(pick_kernel, passages), out_shape=(row_s...  1.78 us
    reduce_sum x1, other arithmetic, on_device(): totals = mesh_sum(jnp.sum(part_lanes, axis=1))  0.83 us
  transfers between devices with their start and end apart: 6, of which 4 were waited for; matrix products, arithmetic and copies ran while one was open for 4% of the time, Pallas kernels for 0%

profile of v7, /device:TPU:0, one launch (start us, length us, event | category | flops | bytes accessed | tf_op | source)
XLA Modules:
  0.0 39.1 jit_solution(11413168174976812227)
XLA Ops:
  0.6 0.0 copy-start
  0.6 1.8 %shard_map.130 = (f32[2,5,256]{2,1,0:T(8,128)}, f32[2,5,256]{2,1,0:T(8,128)}) custom-call(s32[8]{0:T(128)} %lower_slot_ref.1, s32[8]{0:T(128)} %upper_slot_ref.1, f32[5,64,256]{2,1,0:T(8,128)} %bitcast.39, f32[5,64,256]{2,1,0:T(8,128)} %bitcast.40), custom_call_target="tpu_custom_call" | custom-call | tf_op jit(solution)/shard_map/pallas_call | solution.py:415
  2.4 0.5 %collective-permute-start = (f32[2,5,256]{2,1,0:T(8,128)}, f32[2,5,256]{2,1,0:T(8,128)S(1)}, u32[]{:S(2)}, u32[]{:S(2)}) collective-permute-start(f32[2,5,256]{2,1,0:T(8,128)} %get-tuple-element.10), channel_id=1, source_target_pairs={{0,4},{4,8},{8,12},{12,16},{16,20},{20,24},{24,28},{28,0},{1,5},{5... | collective-permute-start | bytes 30728 | tf_op jit(solution)/shard_map/ppermute | solution.py:23
  2.9 4.0 %collective-permute-start.1 = (f32[2,5,256]{2,1,0:T(8,128)}, f32[2,5,256]{2,1,0:T(8,128)S(1)}, u32[]{:S(2)}, u32[]{:S(2)}) collective-permute-start(f32[2,5,256]{2,1,0:T(8,128)} %get-tuple-element.11), channel_id=1, source_target_pairs={{0,28},{4,0},{8,4},{12,8},{16,12},{20,16},{24,20},{28,24},{1,29},{... | collective-permute-start | bytes 30728 | tf_op jit(solution)/shard_map/ppermute | solution.py:23
  6.9 0.0 copy-done
  6.9 0.0 copy-start.1
  6.9 0.1 fusion
  7.0 0.9 %copy-done.1 = f32[4,96,256]{2,1,0:T(8,128)S(1)} copy-done((f32[4,96,256]{2,1,0:T(8,128)S(1)}, f32[4,96,256]{2,1,0:T(8,128)}, u32[]{:S(2)}) %copy-start.1) | copy-done | bytes 393240
  7.9 0.1 fusion.1
  8.0 0.1 copy.30
  8.1 0.1 copy.25
  8.2 0.1 copy.29
  8.4 0.1 copy.24
  8.5 0.0 collective-permute-done.glo_ref
  8.5 0.0 copy-start.2
  8.5 0.1 slice_bitcast_fusion.1
  8.6 0.5 %copy-done.2 = f32[2,5,256]{2,1,0:T(8,128)} copy-done((f32[2,5,256]{2,1,0:T(8,128)}, f32[2,5,256]{2,1,0:T(8,128)S(1)}, u32[]{:S(2)}) %copy-start.2) | copy-done | bytes 10264
  9.1 0.1 copy.27
  9.2 0.1 reshape.51
  9.3 0.1 copy.22
  9.4 0.1 reshape.46
  9.5 0.0 collective-permute-done.1.gup_ref
  9.5 0.0 copy-start.3
  9.5 0.1 slice_bitcast_fusion
  9.6 0.5 %copy-done.3 = f32[2,5,256]{2,1,0:T(8,128)} copy-done((f32[2,5,256]{2,1,0:T(8,128)}, f32[2,5,256]{2,1,0:T(8,128)S(1)}, u32[]{:S(2)}) %copy-start.3) | copy-done | bytes 10264
  10.1 0.1 copy.28
  10.2 0.1 reshape.52
  10.3 0.1 copy.23
  10.4 0.1 reshape.47
  10.5 0.1 pad_maximum_fusion.1
  10.6 0.1 reshape.53
  10.6 3.0 %collective-permute-start.3 = (f32[3536]{0:T(1024)S(1)}, f32[3536]{0:T(1024)S(1)}, u32[]{:S(2)}, u32[]{:S(2)}) collective-permute-start(f32[3536]{0:T(1024)S(1)} %reshape.53), channel_id=1, source_target_pairs={{0,3},{1,0},{2,1},{3,2},{4,7},{5,4},{6,5},{7,6},{8,11},{9,8},{10,9... | collective-permute-start | bytes 42440 | tf_op jit(solution)/shard_map/ppermute | solution.py:23
  13.6 0.1 pad_maximum_fusion
  13.7 0.1 reshape.48
  13.8 0.0 collective-permute-start.2
  13.8 1.3 %collective-permute-done.3 = f32[3536]{0:T(1024)S(1)} collective-permute-done((f32[3536]{0:T(1024)S(1)}, f32[3536]{0:T(1024)S(1)}, u32[]{:S(2)}, u32[]{:S(2)}) %collective-permute-start.3) | collective-permute-done | bytes 14176 | tf_op jit(solution)/shard_map/ppermute | solution.py:23
  15.0 0.1 select_n.25
  15.1 3.3 %collective-permute-done.2 = f32[3536]{0:T(1024)S(1)} collective-permute-done((f32[3536]{0:T(1024)S(1)}, f32[3536]{0:T(1024)S(1)}, u32[]{:S(2)}, u32[]{:S(2)}) %collective-permute-start.2) | collective-permute-done | bytes 14176 | tf_op jit(solution)/shard_map/ppermute | solution.py:23
  18.4 0.1 select_n.22
  18.5 0.2 copy.26
  18.7 0.2 copy.31
  18.9 0.8 %pad.7.left_ref = f32[884,128]{1,0:T(8,128)} pad(f32[884,4]{1,0:T(8,128)S(1)} %bitcast.33, f32[]{:T(128)} %constant.2.clone.1), padding=0_0x0_124 | pad | bytes 466756 | tf_op jit(solution)/shard_map/jit(_pad)/pad | solution.py:439
  19.7 0.8 %pad.8.right_ref = f32[884,128]{1,0:T(8,128)} pad(f32[884,4]{1,0:T(8,128)S(1)} %bitcast.34, f32[]{:T(128)} %constant.2.clone.1), padding=0_0x0_124 | pad | bytes 466756 | tf_op jit(solution)/shard_map/jit(_pad)/pad | solution.py:440
  20.5 5.7 %shard_map.131 = (f32[5,96,384]{2,1,0:T(8,128)}, f32[32,128]{1,0:T(8,128)}) custom-call(f32[5,5]{1,0:T(8,128)} %ax_ref.3, f32[5,5]{1,0:T(8,128)} %pt_ref.3, f32[1,4]{1,0:T(1,128)} %vel_ref.3, f32[5,96,256]{2,1,0:T(8,128)} %bitcast.30, f32[4,96,256]{2,1,0:T(8,128)} %ms_ref.3, f32[2,5,256]{2,1,0:T(8,128)} %copy-done.2, f32[2,5,256]{2,1,0:T(8,128)} %copy-done.3, ...), custom_call_target="tpu_custom_call" | custom-call | tf_op jit(solution)/shard_map/pallas_call | solution.py:444
  26.2 0.8 %reduce_sum.9 = f32[32]{0:T(128)S(1)} reduce(f32[32,128]{1,0:T(8,128)} %get-tuple-element.12, f32[]{:T(128)} %constant.2.clone.1), dimensions={1}, to_apply=%region_0.1 | reduce | flops 4064 | bytes 16516 | tf_op jit(solution)/shard_map/reduce_sum | solution.py:454
  27.1 0.1 collective-permute-start.4
  27.1 3.5 %collective-permute-done.4 = f32[32]{0:T(128)S(1)} collective-permute-done((f32[32]{0:T(128)S(1)}, f32[32]{0:T(128)S(1)}, u32[]{:S(2)}, u32[]{:S(2)}) %collective-permute-start.4) | collective-permute-done | bytes 160 | tf_op jit(solution)/shard_map/ppermute | solution.py:42
  30.7 0.5 %collective-permute-start.5 = (f32[32]{0:T(128)S(1)}, f32[32]{0:T(128)S(1)}, u32[]{:S(2)}, u32[]{:S(2)}) collective-permute-start(f32[32]{0:T(128)S(1)} %add.10), channel_id=1, source_target_pairs={{0,2},{1,3},{2,0},{3,1},{4,6},{5,7},{6,4},{7,5},{8,10},{9,11},{10,... | collective-permute-start | bytes 392 | tf_op jit(solution)/shard_map/ppermute | solution.py:42
  31.2 3.0 %collective-permute-done.5 = f32[32]{0:T(128)S(1)} collective-permute-done((f32[32]{0:T(128)S(1)}, f32[32]{0:T(128)S(1)}, u32[]{:S(2)}, u32[]{:S(2)}) %collective-permute-start.5) | collective-permute-done | bytes 160 | tf_op jit(solution)/shard_map/ppermute | solution.py:42
  34.2 0.5 %add.11.tot_ref = f32[32]{0:T(128)} add(f32[32]{0:T(128)S(1)} %add.10, f32[32]{0:T(128)S(1)} %collective-permute-done.5) | non-fusion elementwise | flops 32 | bytes 384 | tf_op jit(solution)/shard_map/add | solution.py:42
  34.7 4.4 %shard_map.132 = (f32[5,96,256]{2,1,0:T(8,128)}, f32[1,4]{1,0:T(1,128)}, f32[1,4]{1,0:T(1,128)}) custom-call(f32[32]{0:T(128)} %add.11.tot_ref, f32[1,4]{1,0:T(1,128)} %stiff_ref.1, f32[1,4]{1,0:T(1,128)} %disp_ref.1, f32[1,4]{1,0:T(1,128)} %vel_ref.3, f32[5,5]{1,0:T(8,128)} %ax_ref.3, f32[5,5]{1,0:T(8,128)} %pt_ref.3, ...), custom_call_target="tpu_custom_call" | custom-call | tf_op jit(solution)/shard_map/pallas_call | solution.py:457
  (3 shorter events, 0.0 us)
Async XLA Ops:
  0.6 6.3 %copy-start = (f32[1,5,96,256]{3,2,1,0:T(8,128)S(1)}, f32[1,5,96,256]{3,2,1,0:T(8,128)}, u32[]{:S(2)}) copy-start(f32[1,5,96,256]{3,2,1,0:T(8,128)} %param.11) | copy-start | bytes 1474564
  2.4 6.1 %collective-permute-start = (f32[2,5,256]{2,1,0:T(8,128)}, f32[2,5,256]{2,1,0:T(8,128)S(1)}, u32[]{:S(2)}, u32[]{:S(2)}) collective-permute-start(f32[2,5,256]{2,1,0:T(8,128)} %get-tuple-element.10), channel_id=1, source_target_pairs={{0,4},{4,8},{8,12},{12,16},{16,20},{20,24},{24,28},{28,0},{1,5},{5... | collective-permute-start | bytes 30728 | tf_op jit(solution)/shard_map/ppermute | solution.py:23
  2.9 6.6 %collective-permute-start.1 = (f32[2,5,256]{2,1,0:T(8,128)}, f32[2,5,256]{2,1,0:T(8,128)S(1)}, u32[]{:S(2)}, u32[]{:S(2)}) collective-permute-start(f32[2,5,256]{2,1,0:T(8,128)} %get-tuple-element.11), channel_id=1, source_target_pairs={{0,28},{4,0},{8,4},{12,8},{16,12},{20,16},{24,20},{28,24},{1,29},{... | collective-permute-start | bytes 30728 | tf_op jit(solution)/shard_map/ppermute | solution.py:23
  6.9 1.0 %copy-start.1 = (f32[4,96,256]{2,1,0:T(8,128)S(1)}, f32[4,96,256]{2,1,0:T(8,128)}, u32[]{:S(2)}) copy-start(f32[4,96,256]{2,1,0:T(8,128)} %ms_ref.3) | copy-start | bytes 1179652
  8.5 0.6 %copy-start.2 = (f32[2,5,256]{2,1,0:T(8,128)}, f32[2,5,256]{2,1,0:T(8,128)S(1)}, u32[]{:S(2)}) copy-start(f32[2,5,256]{2,1,0:T(8,128)S(1)} %collective-permute-done.glo_ref) | copy-start | bytes 30724
  9.5 0.6 %copy-start.3 = (f32[2,5,256]{2,1,0:T(8,128)}, f32[2,5,256]{2,1,0:T(8,128)S(1)}, u32[]{:S(2)}) copy-start(f32[2,5,256]{2,1,0:T(8,128)S(1)} %collective-permute-done.1.gup_ref) | copy-start | bytes 30724
  10.6 4.4 %collective-permute-start.3 = (f32[3536]{0:T(1024)S(1)}, f32[3536]{0:T(1024)S(1)}, u32[]{:S(2)}, u32[]{:S(2)}) collective-permute-start(f32[3536]{0:T(1024)S(1)} %reshape.53), channel_id=1, source_target_pairs={{0,3},{1,0},{2,1},{3,2},{4,7},{5,4},{6,5},{7,6},{8,11},{9,8},{10,9... | collective-permute-start | bytes 42440 | tf_op jit(solution)/shard_map/ppermute | solution.py:23
  13.8 4.6 %collective-permute-start.2 = (f32[3536]{0:T(1024)S(1)}, f32[3536]{0:T(1024)S(1)}, u32[]{:S(2)}, u32[]{:S(2)}) collective-permute-start(f32[3536]{0:T(1024)S(1)} %reshape.48), channel_id=1, source_target_pairs={{0,1},{1,2},{2,3},{3,0},{4,5},{5,6},{6,7},{7,4},{8,9},{9,10},{10,1... | collective-permute-start | bytes 42440 | tf_op jit(solution)/shard_map/ppermute | solution.py:23
  27.1 3.6 %collective-permute-start.4 = (f32[32]{0:T(128)S(1)}, f32[32]{0:T(128)S(1)}, u32[]{:S(2)}, u32[]{:S(2)}) collective-permute-start(f32[32]{0:T(128)S(1)} %reduce_sum.9), channel_id=1, source_target_pairs={{0,1},{1,0},{2,3},{3,2},{4,5},{5,4},{6,7},{7,6},{8,9},{9,8},{10,11... | collective-permute-start | bytes 392 | tf_op jit(solution)/shard_map/ppermute | solution.py:42
  30.7 3.5 %collective-permute-start.5 = (f32[32]{0:T(128)S(1)}, f32[32]{0:T(128)S(1)}, u32[]{:S(2)}, u32[]{:S(2)}) collective-permute-start(f32[32]{0:T(128)S(1)} %add.10), channel_id=1, source_target_pairs={{0,2},{1,3},{2,0},{3,1},{4,6},{5,7},{6,4},{7,5},{8,10},{9,11},{10,... | collective-permute-start | bytes 392 | tf_op jit(solution)/shard_map/ppermute | solution.py:42

commit v8 on v7

--- a/solution.py
+++ b/solution.py
@@ -206,8 +206,7 @@
             down_ref[s, f : f + 1, :] = lower_hist_ref[f, pl.ds(down_at, 1), :]
 
 
-def widened(own, left, right):
-    tile = right + lane_roll(left, -2 * STEP_COUNT)
+def widened(own, tile):
     return jnp.concatenate([own, tile], axis=-1)
 
 
@@ -223,15 +222,15 @@
     return inside.astype(jnp.float32), owned.astype(jnp.float32)
 
 
-def assemble(u_ref, ms_ref, glo_ref, gup_ref, left_ref, right_ref, fields, modes, pitch):
+def assemble(u_ref, ms_ref, glo_ref, gup_ref, halo_ref, fields, modes, pitch):
     u = []
     for j in range(fields):
         rows = slice(j * pitch, (j + 1) * pitch)
-        u.append(widened(u_ref[j], left_ref[rows, :], right_ref[rows, :]))
+        u.append(widened(u_ref[j], halo_ref[rows, :]))
     ms = []
     for m in range(modes):
         rows = slice((fields + m) * pitch, (fields + m + 1) * pitch)
-        ms.append(widened(ms_ref[m], left_ref[rows, :], right_ref[rows, :]))
+        ms.append(widened(ms_ref[m], halo_ref[rows, :]))
     base = (fields + modes) * pitch
     steps = glo_ref.shape[0]
     ghosts = []
@@ -240,20 +239,20 @@
         for s in range(steps):
             start = base + (side * steps + s) * fields
             rows = slice(start, start + fields)
-            block = widened(ref[s], left_ref[rows, :], right_ref[rows, :])
+            block = widened(ref[s], halo_ref[rows, :])
             per_step.append([block[j : j + 1, :] for j in range(fields)])
         ghosts.append(per_step)
     return u, ms, ghosts[0], ghosts[1]
 
 
-def first_kernel(peers, ax_ref, pt_ref, vel_ref, u_ref, ms_ref, glo_ref, gup_ref, left_ref, right_ref, a_ref, part_ref):
+def first_kernel(peers, ax_ref, pt_ref, vel_ref, u_ref, ms_ref, glo_ref, gup_ref, halo_ref, a_ref, part_ref):
     h = TIME_STEP
     fields = u_ref.shape[0]
     modes = ms_ref.shape[0]
     pitch = u_ref.shape[1]
     jac = read_jacobians(ax_ref, pt_ref, fields)
     vel = [vel_ref[0, m] for m in range(modes)]
-    u0, ms, gl, gu = assemble(u_ref, ms_ref, glo_ref, gup_ref, left_ref, right_ref, fields, modes, pitch)
+    u0, ms, gl, gu = assemble(u_ref, ms_ref, glo_ref, gup_ref, halo_ref, fields, modes, pitch)
     inside, owned = lane_masks(peers, u0[0].shape, u_ref.shape[-1])
     push = vel[0] * ms[0]
     for m in range(1, modes):
@@ -340,8 +339,7 @@
     ms_ref,
     glo_ref,
     gup_ref,
-    left_ref,
-    right_ref,
+    halo_ref,
     out_ref,
     disp_out_ref,
     vel_out_ref,
@@ -355,7 +353,7 @@
     for m in range(modes):
         disp_out_ref[0, m] = disp2[m]
         vel_out_ref[0, m] = vel2[m]
-    _, ms, gl, gu = assemble(u_ref, ms_ref, glo_ref, gup_ref, left_ref, right_ref, fields, modes, pitch)
+    _, ms, gl, gu = assemble(u_ref, ms_ref, glo_ref, gup_ref, halo_ref, fields, modes, pitch)
     inside, _ = lane_masks(peers, ms[0].shape, u_ref.shape[-1])
 
     def combine(weights):
@@ -435,11 +433,10 @@
     from_right = from_right.reshape(reach, -1)
     from_left = jnp.where(me > 0, from_left, jnp.zeros_like(from_left))
     from_right = jnp.where(me < mesh_peers - 1, from_right, jnp.zeros_like(from_right))
-    pad = [(0, 0), (0, LANES - reach)]
-    from_left = jnp.pad(from_left.T, pad)
-    from_right = jnp.pad(from_right.T, pad)
+    gap = jnp.zeros((from_left.shape[1], LANES - 2 * reach), from_left.dtype)
+    halo_tile = jnp.concatenate([from_right.T, gap, from_left.T], axis=1)
     lanes_wide = axial_cells + LANES
-    ins = (state0, mode_shape, lower_ghosts, upper_ghosts, from_left, from_right)
+    ins = (state0, mode_shape, lower_ghosts, upper_ghosts, halo_tile)
 
     base1, part_lanes = pl.pallas_call(
         functools.partial(first_kernel, mesh_peers),
@@ -447,7 +444,7 @@
             jax.ShapeDtypeStruct((fields, pitch_cells, lanes_wide), state0.dtype),
             jax.ShapeDtypeStruct((4 * modes + modes * modes, LANES), state0.dtype),
         ),
-        in_specs=[smem_spec()] * 3 + [vmem_spec()] * 6,
+        in_specs=[smem_spec()] * 3 + [vmem_spec()] * 5,
         out_specs=(vmem_spec(), vmem_spec()),
     )(axial_jacobian, pitch_jacobian, velocity, *ins)
 
@@ -457,7 +454,7 @@
     state2, disp2, vel2 = pl.pallas_call(
         functools.partial(second_kernel, mesh_peers, force_scale),
         out_shape=(jax.ShapeDtypeStruct(state0.shape, state0.dtype), small, small),
-        in_specs=[smem_spec()] * 6 + [vmem_spec()] * 7,
+        in_specs=[smem_spec()] * 6 + [vmem_spec()] * 6,
         out_specs=(vmem_spec(), smem_spec(), smem_spec()),
     )(totals, stiffness, displacement, velocity, axial_jacobian, pitch_jacobian, base1, *ins)
     return (state2[None], disp2, vel2)

time: 39.4 us -> 38.4 us (0.975)
  local copies, waits for them, and re-layouts: 5.87 us -> 4.34 us
  other arithmetic: 1.51 us -> 2.49 us
  Pallas kernels: 11.9 us -> 11.5 us
    pad x2 -> x0, local copies, waits for them, and re-layouts: 1.62 us -> none  [the longest x1 0.81 us: on_device(): from_right = jnp.pad(from_right.T, pad)]
    concatenate x0 -> x1, other arithmetic: none -> 0.97 us  [on_device(): halo_tile = jnp.concatenate([from_right.T, gap, from_left.T], axis=1)]
where the time goes in v8:
time: 38.4 us; the launch traced here: 38.1 us
  Pallas kernels  11.5 us (30%)
  waiting for transfers between devices  11.1 us (29%)
  starting transfers between devices  8.02 us (21%)
  local copies, waits for them, and re-layouts  4.34 us (11%)
  other arithmetic  2.49 us (6%)
  between operations  0.7 us (2%)
    ppermute x4, starting transfers between devices, shifted(): lax.ppermute(value, axis, [(i, (i + by) % peers) for i in range(peers)])  7.44 us
    ppermute x2, waiting for transfers between devices, mesh_sum(): lax.ppermute(value, 'mesh', [(i, i ^ step) for i in range(peers)])  6.56 us
    pallas_call x1, Pallas kernels, on_device(): pl.pallas_call(functools.partial(first_kernel, mesh_peers), out_shape=(ja...  5.47 us
    ppermute x4, waiting for transfers between devices, shifted(): lax.ppermute(value, axis, [(i, (i + by) % peers) for i in range(peers)])  4.55 us
    pallas_call x1, Pallas kernels, on_device(): pl.pallas_call(functools.partial(second_kernel, mesh_peers, force_scale),...  4.2 us
    unnamed x8, local copies, waits for them, and re-layouts  1.93 us
    pallas_call x1, Pallas kernels, on_device(): pl.pallas_call(functools.partial(pick_kernel, passages), out_shape=(row_s...  1.78 us
    concatenate x1, other arithmetic, on_device(): halo_tile = jnp.concatenate([from_right.T, gap, from_left.T], axis=1)  0.97 us
  transfers between devices with their start and end apart: 6, of which 4 were waited for; matrix products, arithmetic and copies ran while one was open for 4% of the time, Pallas kernels for 0%

profile of v8, /device:TPU:0, one launch (start us, length us, event | category | flops | bytes accessed | tf_op | source)
XLA Modules:
  0.0 38.1 jit_solution(1917206498155664284)
XLA Ops:
  0.6 0.0 copy-start
  0.6 1.8 %shard_map.130 = (f32[2,5,256]{2,1,0:T(8,128)}, f32[2,5,256]{2,1,0:T(8,128)}) custom-call(s32[8]{0:T(128)} %lower_slot_ref.1, s32[8]{0:T(128)} %upper_slot_ref.1, f32[5,64,256]{2,1,0:T(8,128)} %bitcast.39, f32[5,64,256]{2,1,0:T(8,128)} %bitcast.40), custom_call_target="tpu_custom_call" | custom-call | tf_op jit(solution)/shard_map/pallas_call | solution.py:413
  2.4 0.5 %collective-permute-start = (f32[2,5,256]{2,1,0:T(8,128)}, f32[2,5,256]{2,1,0:T(8,128)S(1)}, u32[]{:S(2)}, u32[]{:S(2)}) collective-permute-start(f32[2,5,256]{2,1,0:T(8,128)} %get-tuple-element.10), channel_id=1, source_target_pairs={{0,4},{4,8},{8,12},{12,16},{16,20},{20,24},{24,28},{28,0},{1,5},{5... | collective-permute-start | bytes 30728 | tf_op jit(solution)/shard_map/ppermute | solution.py:23
  2.9 4.0 %collective-permute-start.1 = (f32[2,5,256]{2,1,0:T(8,128)}, f32[2,5,256]{2,1,0:T(8,128)S(1)}, u32[]{:S(2)}, u32[]{:S(2)}) collective-permute-start(f32[2,5,256]{2,1,0:T(8,128)} %get-tuple-element.11), channel_id=1, source_target_pairs={{0,28},{4,0},{8,4},{12,8},{16,12},{20,16},{24,20},{28,24},{1,29},{... | collective-permute-start | bytes 30728 | tf_op jit(solution)/shard_map/ppermute | solution.py:23
  6.9 0.0 copy-done
  6.9 0.0 copy-start.1
  6.9 0.1 fusion
  7.0 0.9 %copy-done.1 = f32[4,96,256]{2,1,0:T(8,128)S(1)} copy-done((f32[4,96,256]{2,1,0:T(8,128)S(1)}, f32[4,96,256]{2,1,0:T(8,128)}, u32[]{:S(2)}) %copy-start.1) | copy-done | bytes 393240
  7.9 0.1 fusion.1
  8.0 0.1 copy.25
  8.1 0.1 copy.30
  8.2 0.1 copy.24
  8.4 0.1 copy.29
  8.5 0.1 pad.1.clone
  8.6 0.0 collective-permute-done.glo_ref
  8.6 0.0 copy-start.2
  8.6 0.1 slice_bitcast_fusion.3
  8.7 0.5 %copy-done.2 = f32[2,5,256]{2,1,0:T(8,128)} copy-done((f32[2,5,256]{2,1,0:T(8,128)}, f32[2,5,256]{2,1,0:T(8,128)S(1)}, u32[]{:S(2)}) %copy-start.2) | copy-done | bytes 10264
  9.2 0.1 copy.22
  9.3 0.1 reshape.46
  9.4 0.1 copy.27
  9.5 0.1 reshape.51
  9.6 0.0 collective-permute-done.1.gup_ref
  9.6 0.0 copy-start.3
  9.6 0.1 slice_bitcast_fusion.2
  9.6 0.5 %copy-done.3 = f32[2,5,256]{2,1,0:T(8,128)} copy-done((f32[2,5,256]{2,1,0:T(8,128)}, f32[2,5,256]{2,1,0:T(8,128)S(1)}, u32[]{:S(2)}) %copy-start.3) | copy-done | bytes 10264
  10.2 0.1 copy.23
  10.3 0.1 reshape.47
  10.3 0.1 copy.28
  10.4 0.1 reshape.52
  10.5 0.1 pad_maximum_fusion.1
  10.6 0.1 reshape.48
  10.7 2.9 %collective-permute-start.2 = (f32[3536]{0:T(1024)S(1)}, f32[3536]{0:T(1024)S(1)}, u32[]{:S(2)}, u32[]{:S(2)}) collective-permute-start(f32[3536]{0:T(1024)S(1)} %reshape.48), channel_id=1, source_target_pairs={{0,3},{1,0},{2,1},{3,2},{4,7},{5,4},{6,5},{7,6},{8,11},{9,8},{10,9... | collective-permute-start | bytes 42440 | tf_op jit(solution)/shard_map/ppermute | solution.py:23
  13.6 0.1 pad_maximum_fusion.2
  13.7 0.1 reshape.53
  13.8 0.0 collective-permute-start.3
  13.8 1.3 %collective-permute-done.2 = f32[3536]{0:T(1024)S(1)} collective-permute-done((f32[3536]{0:T(1024)S(1)}, f32[3536]{0:T(1024)S(1)}, u32[]{:S(2)}, u32[]{:S(2)}) %collective-permute-start.2) | collective-permute-done | bytes 14176 | tf_op jit(solution)/shard_map/ppermute | solution.py:23
  15.1 0.1 select_n.22
  15.2 3.3 %collective-permute-done.3 = f32[3536]{0:T(1024)S(1)} collective-permute-done((f32[3536]{0:T(1024)S(1)}, f32[3536]{0:T(1024)S(1)}, u32[]{:S(2)}, u32[]{:S(2)}) %collective-permute-start.3) | collective-permute-done | bytes 14176 | tf_op jit(solution)/shard_map/ppermute | solution.py:23
  18.4 0.1 select_n.25
  18.5 0.2 copy.31
  18.7 0.2 copy.26
  19.0 1.0 %pad_maximum_fusion.halo_ref = f32[884,128]{1,0:T(8,128)} fusion(f32[884,4]{1,0:T(8,128)S(1)} %bitcast.33, f32[884,4]{1,0:T(8,128)S(1)} %bitcast.34, f32[128]{0:T(128)S(1)} %pad.1.clone), kind=kLoop, calls=%fused_computation | loop fusion | flops 226304 | bytes 481408 | tf_op jit(solution)/shard_map/concatenate | solution.py:437
  19.9 5.5 %shard_map.131 = (f32[5,96,384]{2,1,0:T(8,128)}, f32[32,128]{1,0:T(8,128)}) custom-call(f32[5,5]{1,0:T(8,128)} %ax_ref.3, f32[5,5]{1,0:T(8,128)} %pt_ref.3, f32[1,4]{1,0:T(1,128)} %vel_ref.3, f32[5,96,256]{2,1,0:T(8,128)} %bitcast.30, f32[4,96,256]{2,1,0:T(8,128)} %ms_ref.3, f32[2,5,256]{2,1,0:T(8,128)} %copy-done.2, f32[2,5,256]{2,1,0:T(8,128)} %copy-done.3, ...), custom_call_target="tpu_custom_call" | custom-call | tf_op jit(solution)/shard_map/pallas_call | solution.py:441
  25.4 0.8 %reduce_sum.9 = f32[32]{0:T(128)S(1)} reduce(f32[32,128]{1,0:T(8,128)} %get-tuple-element.12, f32[]{:T(128)} %constant.6.clone.1), dimensions={1}, to_apply=%region_0.1 | reduce | flops 4064 | bytes 16516 | tf_op jit(solution)/shard_map/reduce_sum | solution.py:451
  26.2 0.1 collective-permute-start.4
  26.3 3.5 %collective-permute-done.4 = f32[32]{0:T(128)S(1)} collective-permute-done((f32[32]{0:T(128)S(1)}, f32[32]{0:T(128)S(1)}, u32[]{:S(2)}, u32[]{:S(2)}) %collective-permute-start.4) | collective-permute-done | bytes 160 | tf_op jit(solution)/shard_map/ppermute | solution.py:42
  29.8 0.5 %collective-permute-start.5 = (f32[32]{0:T(128)S(1)}, f32[32]{0:T(128)S(1)}, u32[]{:S(2)}, u32[]{:S(2)}) collective-permute-start(f32[32]{0:T(128)S(1)} %add.6), channel_id=1, source_target_pairs={{0,2},{1,3},{2,0},{3,1},{4,6},{5,7},{6,4},{7,5},{8,10},{9,11},{10,... | collective-permute-start | bytes 392 | tf_op jit(solution)/shard_map/ppermute | solution.py:42
  30.3 3.0 %collective-permute-done.5 = f32[32]{0:T(128)S(1)} collective-permute-done((f32[32]{0:T(128)S(1)}, f32[32]{0:T(128)S(1)}, u32[]{:S(2)}, u32[]{:S(2)}) %collective-permute-start.5) | collective-permute-done | bytes 160 | tf_op jit(solution)/shard_map/ppermute | solution.py:42
  33.4 0.5 %add.7.tot_ref = f32[32]{0:T(128)} add(f32[32]{0:T(128)S(1)} %add.6, f32[32]{0:T(128)S(1)} %collective-permute-done.5) | non-fusion elementwise | flops 32 | bytes 384 | tf_op jit(solution)/shard_map/add | solution.py:42
  33.9 4.2 %shard_map.132 = (f32[5,96,256]{2,1,0:T(8,128)}, f32[1,4]{1,0:T(1,128)}, f32[1,4]{1,0:T(1,128)}) custom-call(f32[32]{0:T(128)} %add.7.tot_ref, f32[1,4]{1,0:T(1,128)} %stiff_ref.1, f32[1,4]{1,0:T(1,128)} %disp_ref.1, f32[1,4]{1,0:T(1,128)} %vel_ref.3, f32[5,5]{1,0:T(8,128)} %ax_ref.3, f32[5,5]{1,0:T(8,128)} %pt_ref.3, ...), custom_call_target="tpu_custom_call" | custom-call | tf_op jit(solution)/shard_map/pallas_call | solution.py:454
  (4 shorter events, 0.0 us)
Async XLA Ops:
  0.6 6.3 %copy-start = (f32[1,5,96,256]{3,2,1,0:T(8,128)S(1)}, f32[1,5,96,256]{3,2,1,0:T(8,128)}, u32[]{:S(2)}) copy-start(f32[1,5,96,256]{3,2,1,0:T(8,128)} %param.11) | copy-start | bytes 1474564
  2.4 6.2 %collective-permute-start = (f32[2,5,256]{2,1,0:T(8,128)}, f32[2,5,256]{2,1,0:T(8,128)S(1)}, u32[]{:S(2)}, u32[]{:S(2)}) collective-permute-start(f32[2,5,256]{2,1,0:T(8,128)} %get-tuple-element.10), channel_id=1, source_target_pairs={{0,4},{4,8},{8,12},{12,16},{16,20},{20,24},{24,28},{28,0},{1,5},{5... | collective-permute-start | bytes 30728 | tf_op jit(solution)/shard_map/ppermute | solution.py:23
  2.9 6.7 %collective-permute-start.1 = (f32[2,5,256]{2,1,0:T(8,128)}, f32[2,5,256]{2,1,0:T(8,128)S(1)}, u32[]{:S(2)}, u32[]{:S(2)}) collective-permute-start(f32[2,5,256]{2,1,0:T(8,128)} %get-tuple-element.11), channel_id=1, source_target_pairs={{0,28},{4,0},{8,4},{12,8},{16,12},{20,16},{24,20},{28,24},{1,29},{... | collective-permute-start | bytes 30728 | tf_op jit(solution)/shard_map/ppermute | solution.py:23
  6.9 1.0 %copy-start.1 = (f32[4,96,256]{2,1,0:T(8,128)S(1)}, f32[4,96,256]{2,1,0:T(8,128)}, u32[]{:S(2)}) copy-start(f32[4,96,256]{2,1,0:T(8,128)} %ms_ref.3) | copy-start | bytes 1179652
  8.6 0.6 %copy-start.2 = (f32[2,5,256]{2,1,0:T(8,128)}, f32[2,5,256]{2,1,0:T(8,128)S(1)}, u32[]{:S(2)}) copy-start(f32[2,5,256]{2,1,0:T(8,128)S(1)} %collective-permute-done.glo_ref) | copy-start | bytes 30724
  9.6 0.6 %copy-start.3 = (f32[2,5,256]{2,1,0:T(8,128)}, f32[2,5,256]{2,1,0:T(8,128)S(1)}, u32[]{:S(2)}) copy-start(f32[2,5,256]{2,1,0:T(8,128)S(1)} %collective-permute-done.1.gup_ref) | copy-start | bytes 30724
  10.7 4.4 %collective-permute-start.2 = (f32[3536]{0:T(1024)S(1)}, f32[3536]{0:T(1024)S(1)}, u32[]{:S(2)}, u32[]{:S(2)}) collective-permute-start(f32[3536]{0:T(1024)S(1)} %reshape.48), channel_id=1, source_target_pairs={{0,3},{1,0},{2,1},{3,2},{4,7},{5,4},{6,5},{7,6},{8,11},{9,8},{10,9... | collective-permute-start | bytes 42440 | tf_op jit(solution)/shard_map/ppermute | solution.py:23
  13.8 4.6 %collective-permute-start.3 = (f32[3536]{0:T(1024)S(1)}, f32[3536]{0:T(1024)S(1)}, u32[]{:S(2)}, u32[]{:S(2)}) collective-permute-start(f32[3536]{0:T(1024)S(1)} %reshape.53), channel_id=1, source_target_pairs={{0,1},{1,2},{2,3},{3,0},{4,5},{5,6},{6,7},{7,4},{8,9},{9,10},{10,1... | collective-permute-start | bytes 42440 | tf_op jit(solution)/shard_map/ppermute | solution.py:23
  26.2 3.6 %collective-permute-start.4 = (f32[32]{0:T(128)S(1)}, f32[32]{0:T(128)S(1)}, u32[]{:S(2)}, u32[]{:S(2)}) collective-permute-start(f32[32]{0:T(128)S(1)} %reduce_sum.9), channel_id=1, source_target_pairs={{0,1},{1,0},{2,3},{3,2},{4,5},{5,4},{6,7},{7,6},{8,9},{9,8},{10,11... | collective-permute-start | bytes 392 | tf_op jit(solution)/shard_map/ppermute | solution.py:42
  29.8 3.5 %collective-permute-start.5 = (f32[32]{0:T(128)S(1)}, f32[32]{0:T(128)S(1)}, u32[]{:S(2)}, u32[]{:S(2)}) collective-permute-start(f32[32]{0:T(128)S(1)} %add.6), channel_id=1, source_target_pairs={{0,2},{1,3},{2,0},{3,1},{4,6},{5,7},{6,4},{7,5},{8,10},{9,11},{10,... | collective-permute-start | bytes 392 | tf_op jit(solution)/shard_map/ppermute | solution.py:42

commit v9 on v8

--- a/solution.py
+++ b/solution.py
@@ -325,6 +325,20 @@
     return coef, disp2, vel2
 
 
+def step2_rate_kernel(peers, ax_ref, pt_ref, a_ref, u_ref, ms_ref, glo_ref, gup_ref, halo_ref, ra_ref):
+    fields = a_ref.shape[0]
+    modes = ms_ref.shape[0]
+    pitch = u_ref.shape[1]
+    jac = read_jacobians(ax_ref, pt_ref, fields)
+    _, ms, gl, gu = assemble(u_ref, ms_ref, glo_ref, gup_ref, halo_ref, fields, modes, pitch)
+    inside, _ = lane_masks(peers, ms[0].shape, u_ref.shape[-1])
+    every = list(range(fields))
+    a = [a_ref[j] for j in every]
+    ra = kernel_rate(a, gl[1], gu[1], jac, None, inside, every)
+    for j in every:
+        ra_ref[j] = ra[j]
+
+
 def second_kernel(
     peers,
     force_scale,
@@ -335,6 +349,7 @@
     ax_ref,
     pt_ref,
     a_ref,
+    ra_ref,
     u_ref,
     ms_ref,
     glo_ref,
@@ -365,8 +380,24 @@
     gl2, gu2 = gl[1], gu[1]
     every = list(range(fields))
     s1 = [a_ref[j] for j in every]
-    s1[1] = s1[1] + combine(coef[0])
-    k1 = kernel_rate(s1, gl2, gu2, jac, COUPLING * combine(coef[1]), inside, every)
+    correction = combine(coef[0])
+    s1[1] = s1[1] + correction
+    rows = correction.shape[0]
+    row = lax.broadcasted_iota(jnp.int32, correction.shape, 0)
+    east, west = lane_roll(correction, -1), lane_roll(correction, 1)
+    north = jnp.where(row == rows - 1, 0.0, row_roll(correction, -1))
+    south = jnp.where(row == 0, 0.0, row_roll(correction, 1))
+    ga = 0.5 * (east - west)
+    gp = 0.5 * (north - south)
+    lap = east + west + north + south - 4.0 * correction
+    ax, pt = jac
+    push1 = COUPLING * combine(coef[1])
+    k1 = []
+    for i in every:
+        r = -ax[i][1] * ga - pt[i][1] * gp
+        if i == 1:
+            r = r + DIFFUSION * lap + push1
+        k1.append(ra_ref[i] + r * inside)
     mid = [s1[j] + h * k1[j] for j in every]
     k2 = kernel_rate(mid, gl2, gu2, jac, COUPLING * combine(coef[2]), inside, every)
     width = out_ref.shape[-1]
@@ -450,13 +481,20 @@
 
     totals = mesh_sum(jnp.sum(part_lanes, axis=1))
 
+    rate_a = pl.pallas_call(
+        functools.partial(step2_rate_kernel, mesh_peers),
+        out_shape=jax.ShapeDtypeStruct(base1.shape, base1.dtype),
+        in_specs=[smem_spec()] * 2 + [vmem_spec()] * 6,
+        out_specs=vmem_spec(),
+    )(axial_jacobian, pitch_jacobian, base1, *ins)
+
     small = jax.ShapeDtypeStruct(displacement.shape, displacement.dtype)
     state2, disp2, vel2 = pl.pallas_call(
         functools.partial(second_kernel, mesh_peers, force_scale),
         out_shape=(jax.ShapeDtypeStruct(state0.shape, state0.dtype), small, small),
-        in_specs=[smem_spec()] * 6 + [vmem_spec()] * 6,
+        in_specs=[smem_spec()] * 6 + [vmem_spec()] * 7,
         out_specs=(vmem_spec(), smem_spec(), smem_spec()),
-    )(totals, stiffness, displacement, velocity, axial_jacobian, pitch_jacobian, base1, *ins)
+    )(totals, stiffness, displacement, velocity, axial_jacobian, pitch_jacobian, base1, rate_a, *ins)
     return (state2[None], disp2, vel2)
 
 

time: 38.4 us -> 38.4 us (level)
  waiting for transfers between devices: 11.1 us -> 8.08 us
  Pallas kernels: 11.5 us -> 14.4 us
    pallas_call x0 -> x1, Pallas kernels: none -> 3.49 us  [on_device(): pl.pallas_call(functools.partial(step2_rate_kernel, mesh_peers), out_shap...]
    ppermute x2, waiting for transfers between devices: 6.56 us -> 3.53 us  [mesh_sum(): lax.ppermute(value, 'mesh', [(i, i ^ step) for i in range(peers)])]
    pallas_call x1, Pallas kernels: 4.2 us -> 3.66 us  [on_device(): pl.pallas_call(functools.partial(second_kernel, mesh_peers, force_scale),...]
  transfers between devices with their start and end apart: 6 -> 6, of which waited for: 4 -> 3; matrix products, arithmetic and copies ran while one was open for 4% -> 4% of each run, Pallas kernels for 0% -> 9%
where the time goes in v9:
time: 38.4 us; the launch traced here: 38.1 us
  Pallas kernels  14.4 us (38%)
  waiting for transfers between devices  8.08 us (21%)
  starting transfers between devices  8.02 us (21%)
  local copies, waits for them, and re-layouts  4.34 us (11%)
  other arithmetic  2.53 us (7%)
  between operations  0.7 us (2%)
    ppermute x4, starting transfers between devices, shifted(): lax.ppermute(value, axis, [(i, (i + by) % peers) for i in range(peers)])  7.44 us
    pallas_call x1, Pallas kernels, on_device(): pl.pallas_call(functools.partial(first_kernel, mesh_peers), out_shape=(ja...  5.47 us
    ppermute x4, waiting for transfers between devices, shifted(): lax.ppermute(value, axis, [(i, (i + by) % peers) for i in range(peers)])  4.55 us
    pallas_call x1, Pallas kernels, on_device(): pl.pallas_call(functools.partial(second_kernel, mesh_peers, force_scale),...  3.66 us
    ppermute x2, waiting for transfers between devices, mesh_sum(): lax.ppermute(value, 'mesh', [(i, i ^ step) for i in range(peers)])  3.53 us
    pallas_call x1, Pallas kernels, on_device(): pl.pallas_call(functools.partial(step2_rate_kernel, mesh_peers), out_shap...  3.49 us
    unnamed x8, local copies, waits for them, and re-layouts  1.93 us
    pallas_call x1, Pallas kernels, on_device(): pl.pallas_call(functools.partial(pick_kernel, passages), out_shape=(row_s...  1.78 us
  transfers between devices with their start and end apart: 6, of which 3 were waited for; matrix products, arithmetic and copies ran while one was open for 4% of the time, Pallas kernels for 9%

profile of v9, /device:TPU:0, one launch (start us, length us, event | category | flops | bytes accessed | tf_op | source)
XLA Modules:
  0.0 38.1 jit_solution(8190763479441958107)
XLA Ops:
  0.6 0.0 copy-start
  0.6 1.8 %shard_map.130 = (f32[2,5,256]{2,1,0:T(8,128)}, f32[2,5,256]{2,1,0:T(8,128)}) custom-call(s32[8]{0:T(128)} %lower_slot_ref.1, s32[8]{0:T(128)} %upper_slot_ref.1, f32[5,64,256]{2,1,0:T(8,128)} %bitcast.40, f32[5,64,256]{2,1,0:T(8,128)} %bitcast.41), custom_call_target="tpu_custom_call" | custom-call | tf_op jit(solution)/shard_map/pallas_call | solution.py:444
  2.4 0.5 %collective-permute-start = (f32[2,5,256]{2,1,0:T(8,128)}, f32[2,5,256]{2,1,0:T(8,128)S(1)}, u32[]{:S(2)}, u32[]{:S(2)}) collective-permute-start(f32[2,5,256]{2,1,0:T(8,128)} %get-tuple-element.10), channel_id=1, source_target_pairs={{0,4},{4,8},{8,12},{12,16},{16,20},{20,24},{24,28},{28,0},{1,5},{5... | collective-permute-start | bytes 30728 | tf_op jit(solution)/shard_map/ppermute | solution.py:23
  2.9 4.0 %collective-permute-start.1 = (f32[2,5,256]{2,1,0:T(8,128)}, f32[2,5,256]{2,1,0:T(8,128)S(1)}, u32[]{:S(2)}, u32[]{:S(2)}) collective-permute-start(f32[2,5,256]{2,1,0:T(8,128)} %get-tuple-element.11), channel_id=1, source_target_pairs={{0,28},{4,0},{8,4},{12,8},{16,12},{20,16},{24,20},{28,24},{1,29},{... | collective-permute-start | bytes 30728 | tf_op jit(solution)/shard_map/ppermute | solution.py:23
  6.9 0.0 copy-done
  6.9 0.0 copy-start.1
  6.9 0.1 fusion
  7.0 0.9 %copy-done.1 = f32[4,96,256]{2,1,0:T(8,128)S(1)} copy-done((f32[4,96,256]{2,1,0:T(8,128)S(1)}, f32[4,96,256]{2,1,0:T(8,128)}, u32[]{:S(2)}) %copy-start.1) | copy-done | bytes 393240
  7.9 0.1 fusion.1
  8.0 0.1 copy.25
  8.1 0.1 copy.30
  8.2 0.1 copy.24
  8.4 0.1 copy.29
  8.5 0.1 pad.1.clone
  8.6 0.0 collective-permute-done.glo_ref
  8.6 0.0 copy-start.2
  8.6 0.1 slice_bitcast_fusion.3
  8.7 0.5 %copy-done.2 = f32[2,5,256]{2,1,0:T(8,128)} copy-done((f32[2,5,256]{2,1,0:T(8,128)}, f32[2,5,256]{2,1,0:T(8,128)S(1)}, u32[]{:S(2)}) %copy-start.2) | copy-done | bytes 10264
  9.2 0.1 copy.22
  9.3 0.1 reshape.46
  9.4 0.1 copy.27
  9.5 0.1 reshape.51
  9.6 0.0 collective-permute-done.1.gup_ref
  9.6 0.0 copy-start.3
  9.6 0.1 slice_bitcast_fusion.2
  9.6 0.5 %copy-done.3 = f32[2,5,256]{2,1,0:T(8,128)} copy-done((f32[2,5,256]{2,1,0:T(8,128)}, f32[2,5,256]{2,1,0:T(8,128)S(1)}, u32[]{:S(2)}) %copy-start.3) | copy-done | bytes 10264
  10.2 0.1 copy.23
  10.3 0.1 reshape.47
  10.3 0.1 copy.28
  10.4 0.1 reshape.52
  10.5 0.1 pad_maximum_fusion.1
  10.6 0.1 reshape.48
  10.7 2.9 %collective-permute-start.2 = (f32[3536]{0:T(1024)S(1)}, f32[3536]{0:T(1024)S(1)}, u32[]{:S(2)}, u32[]{:S(2)}) collective-permute-start(f32[3536]{0:T(1024)S(1)} %reshape.48), channel_id=1, source_target_pairs={{0,3},{1,0},{2,1},{3,2},{4,7},{5,4},{6,5},{7,6},{8,11},{9,8},{10,9... | collective-permute-start | bytes 42440 | tf_op jit(solution)/shard_map/ppermute | solution.py:23
  13.6 0.1 pad_maximum_fusion.2
  13.7 0.1 reshape.53
  13.8 0.0 collective-permute-start.3
  13.8 1.3 %collective-permute-done.2 = f32[3536]{0:T(1024)S(1)} collective-permute-done((f32[3536]{0:T(1024)S(1)}, f32[3536]{0:T(1024)S(1)}, u32[]{:S(2)}, u32[]{:S(2)}) %collective-permute-start.2) | collective-permute-done | bytes 14176 | tf_op jit(solution)/shard_map/ppermute | solution.py:23
  15.1 0.1 select_n.22
  15.2 3.3 %collective-permute-done.3 = f32[3536]{0:T(1024)S(1)} collective-permute-done((f32[3536]{0:T(1024)S(1)}, f32[3536]{0:T(1024)S(1)}, u32[]{:S(2)}, u32[]{:S(2)}) %collective-permute-start.3) | collective-permute-done | bytes 14176 | tf_op jit(solution)/shard_map/ppermute | solution.py:23
  18.4 0.1 select_n.25
  18.5 0.2 copy.31
  18.7 0.2 copy.26
  19.0 1.0 %pad_maximum_fusion.halo_ref = f32[884,128]{1,0:T(8,128)} fusion(f32[884,4]{1,0:T(8,128)S(1)} %bitcast.34, f32[884,4]{1,0:T(8,128)S(1)} %bitcast.35, f32[128]{0:T(128)S(1)} %pad.1.clone), kind=kLoop, calls=%fused_computation | loop fusion | flops 226304 | bytes 481408 | tf_op jit(solution)/shard_map/concatenate | solution.py:468
  19.9 5.5 %shard_map.131 = (f32[5,96,384]{2,1,0:T(8,128)}, f32[32,128]{1,0:T(8,128)}) custom-call(f32[5,5]{1,0:T(8,128)} %ax_ref.5, f32[5,5]{1,0:T(8,128)} %pt_ref.5, f32[1,4]{1,0:T(1,128)} %vel_ref.3, f32[5,96,256]{2,1,0:T(8,128)} %bitcast.30, f32[4,96,256]{2,1,0:T(8,128)} %ms_ref.5, f32[2,5,256]{2,1,0:T(8,128)} %copy-done.2, f32[2,5,256]{2,1,0:T(8,128)} %copy-done.3, ...), custom_call_target="tpu_custom_call" | custom-call | tf_op jit(solution)/shard_map/pallas_call | solution.py:472
  25.4 0.8 %reduce_sum.9 = f32[32]{0:T(128)S(1)} reduce(f32[32,128]{1,0:T(8,128)} %get-tuple-element.12, f32[]{:T(128)} %constant.6.clone.1), dimensions={1}, to_apply=%region_0.1 | reduce | flops 4064 | bytes 16516 | tf_op jit(solution)/shard_map/reduce_sum | solution.py:482
  26.2 0.1 collective-permute-start.4
  26.3 3.5 %collective-permute-done.4 = f32[32]{0:T(128)S(1)} collective-permute-done((f32[32]{0:T(128)S(1)}, f32[32]{0:T(128)S(1)}, u32[]{:S(2)}, u32[]{:S(2)}) %collective-permute-start.4) | collective-permute-done | bytes 160 | tf_op jit(solution)/shard_map/ppermute | solution.py:42
  29.8 0.5 %collective-permute-start.5 = (f32[32]{0:T(128)S(1)}, f32[32]{0:T(128)S(1)}, u32[]{:S(2)}, u32[]{:S(2)}) collective-permute-start(f32[32]{0:T(128)S(1)} %add.6), channel_id=1, source_target_pairs={{0,2},{1,3},{2,0},{3,1},{4,6},{5,7},{6,4},{7,5},{8,10},{9,11},{10,... | collective-permute-start | bytes 392 | tf_op jit(solution)/shard_map/ppermute | solution.py:42
  30.3 3.5 %shard_map.132.ra_ref = f32[5,96,384]{2,1,0:T(8,128)} custom-call(f32[5,5]{1,0:T(8,128)} %ax_ref.5, f32[5,5]{1,0:T(8,128)} %pt_ref.5, f32[5,96,384]{2,1,0:T(8,128)} %get-tuple-element.13.a_ref, f32[5,96,256]{2,1,0:T(8,128)} %bitcast.31, f32[4,96,256]{2,1,0:T(8,128)} %ms_ref.5, f32[2,5,256]{2,1,0:T(8,128)} %copy-done.2, f32[2,5,256]{2,1,0:T(8,128)} %copy-done.3, ...), custom_call_target="tpu_custom_call" | custom-call | tf_op jit(solution)/shard_map/pallas_call | solution.py:484
  33.8 0.0 collective-permute-done.5
  33.8 0.6 %add.7.tot_ref = f32[32]{0:T(128)} add(f32[32]{0:T(128)S(1)} %add.6, f32[32]{0:T(128)S(1)} %collective-permute-done.5) | non-fusion elementwise | flops 32 | bytes 384 | tf_op jit(solution)/shard_map/add | solution.py:42
  34.4 3.7 %shard_map.133 = (f32[5,96,256]{2,1,0:T(8,128)}, f32[1,4]{1,0:T(1,128)}, f32[1,4]{1,0:T(1,128)}) custom-call(f32[32]{0:T(128)} %add.7.tot_ref, f32[1,4]{1,0:T(1,128)} %stiff_ref.1, f32[1,4]{1,0:T(1,128)} %disp_ref.1, f32[1,4]{1,0:T(1,128)} %vel_ref.3, f32[5,5]{1,0:T(8,128)} %ax_ref.5, f32[5,5]{1,0:T(8,128)} %pt_ref.5, ...), custom_call_target="tpu_custom_call" | custom-call | tf_op jit(solution)/shard_map/pallas_call | solution.py:492
  (4 shorter events, 0.0 us)
Async XLA Ops:
  0.6 6.3 %copy-start = (f32[1,5,96,256]{3,2,1,0:T(8,128)S(1)}, f32[1,5,96,256]{3,2,1,0:T(8,128)}, u32[]{:S(2)}) copy-start(f32[1,5,96,256]{3,2,1,0:T(8,128)} %param.11) | copy-start | bytes 1474564
  2.4 6.2 %collective-permute-start = (f32[2,5,256]{2,1,0:T(8,128)}, f32[2,5,256]{2,1,0:T(8,128)S(1)}, u32[]{:S(2)}, u32[]{:S(2)}) collective-permute-start(f32[2,5,256]{2,1,0:T(8,128)} %get-tuple-element.10), channel_id=1, source_target_pairs={{0,4},{4,8},{8,12},{12,16},{16,20},{20,24},{24,28},{28,0},{1,5},{5... | collective-permute-start | bytes 30728 | tf_op jit(solution)/shard_map/ppermute | solution.py:23
  2.9 6.7 %collective-permute-start.1 = (f32[2,5,256]{2,1,0:T(8,128)}, f32[2,5,256]{2,1,0:T(8,128)S(1)}, u32[]{:S(2)}, u32[]{:S(2)}) collective-permute-start(f32[2,5,256]{2,1,0:T(8,128)} %get-tuple-element.11), channel_id=1, source_target_pairs={{0,28},{4,0},{8,4},{12,8},{16,12},{20,16},{24,20},{28,24},{1,29},{... | collective-permute-start | bytes 30728 | tf_op jit(solution)/shard_map/ppermute | solution.py:23
  6.9 1.0 %copy-start.1 = (f32[4,96,256]{2,1,0:T(8,128)S(1)}, f32[4,96,256]{2,1,0:T(8,128)}, u32[]{:S(2)}) copy-start(f32[4,96,256]{2,1,0:T(8,128)} %ms_ref.5) | copy-start | bytes 1179652
  8.6 0.6 %copy-start.2 = (f32[2,5,256]{2,1,0:T(8,128)}, f32[2,5,256]{2,1,0:T(8,128)S(1)}, u32[]{:S(2)}) copy-start(f32[2,5,256]{2,1,0:T(8,128)S(1)} %collective-permute-done.glo_ref) | copy-start | bytes 30724
  9.6 0.6 %copy-start.3 = (f32[2,5,256]{2,1,0:T(8,128)}, f32[2,5,256]{2,1,0:T(8,128)S(1)}, u32[]{:S(2)}) copy-start(f32[2,5,256]{2,1,0:T(8,128)S(1)} %collective-permute-done.1.gup_ref) | copy-start | bytes 30724
  10.7 4.4 %collective-permute-start.2 = (f32[3536]{0:T(1024)S(1)}, f32[3536]{0:T(1024)S(1)}, u32[]{:S(2)}, u32[]{:S(2)}) collective-permute-start(f32[3536]{0:T(1024)S(1)} %reshape.48), channel_id=1, source_target_pairs={{0,3},{1,0},{2,1},{3,2},{4,7},{5,4},{6,5},{7,6},{8,11},{9,8},{10,9... | collective-permute-start | bytes 42440 | tf_op jit(solution)/shard_map/ppermute | solution.py:23
  13.8 4.6 %collective-permute-start.3 = (f32[3536]{0:T(1024)S(1)}, f32[3536]{0:T(1024)S(1)}, u32[]{:S(2)}, u32[]{:S(2)}) collective-permute-start(f32[3536]{0:T(1024)S(1)} %reshape.53), channel_id=1, source_target_pairs={{0,1},{1,2},{2,3},{3,0},{4,5},{5,6},{6,7},{7,4},{8,9},{9,10},{10,1... | collective-permute-start | bytes 42440 | tf_op jit(solution)/shard_map/ppermute | solution.py:23
  26.2 3.6 %collective-permute-start.4 = (f32[32]{0:T(128)S(1)}, f32[32]{0:T(128)S(1)}, u32[]{:S(2)}, u32[]{:S(2)}) collective-permute-start(f32[32]{0:T(128)S(1)} %reduce_sum.9), channel_id=1, source_target_pairs={{0,1},{1,0},{2,3},{3,2},{4,5},{5,4},{6,7},{7,6},{8,9},{9,8},{10,11... | collective-permute-start | bytes 392 | tf_op jit(solution)/shard_map/ppermute | solution.py:42
  29.8 4.0 %collective-permute-start.5 = (f32[32]{0:T(128)S(1)}, f32[32]{0:T(128)S(1)}, u32[]{:S(2)}, u32[]{:S(2)}) collective-permute-start(f32[32]{0:T(128)S(1)} %add.6), channel_id=1, source_target_pairs={{0,2},{1,3},{2,0},{3,1},{4,6},{5,7},{6,4},{7,5},{8,10},{9,11},{10,... | collective-permute-start | bytes 392 | tf_op jit(solution)/shard_map/ppermute | solution.py:42

commit v10 on v9

--- a/solution.py
+++ b/solution.py
@@ -155,27 +155,42 @@
     return pltpu.roll(x, shift % x.shape[0], 0)
 
 
+def pitch_neighbours(s, lower, upper):
+    rows = s.shape[0]
+    tile = 8
+    edge = lax.broadcasted_iota(jnp.int32, (tile,) + s.shape[1:], 0)
+    north = row_roll(s, -1)
+    south = row_roll(s, 1)
+    north = jnp.concatenate(
+        [north[: rows - tile], jnp.where(edge == tile - 1, upper, north[rows - tile :])], axis=0
+    )
+    south = jnp.concatenate([jnp.where(edge == 0, lower, south[:tile]), south[tile:]], axis=0)
+    return north, south
+
+
+def masked(r, inside):
+    cut = r.shape[-1] - LANES
+    return jnp.concatenate([r[:, :cut], r[:, cut:] * inside[:, cut:]], axis=1)
+
+
 def kernel_rate(state, lower, upper, jac, push, inside, fields_out):
     ax, pt = jac
-    rows = state[0].shape[0]
-    row = lax.broadcasted_iota(jnp.int32, state[0].shape, 0)
-    grads_a, grads_p, laps = [], [], []
+    diffs_a, diffs_p, laps = [], [], []
     for j, s in enumerate(state):
         east = lane_roll(s, -1)
         west = lane_roll(s, 1)
-        north = jnp.where(row == rows - 1, upper[j], row_roll(s, -1))
-        south = jnp.where(row == 0, lower[j], row_roll(s, 1))
-        grads_a.append(0.5 * (east - west))
-        grads_p.append(0.5 * (north - south))
-        laps.append(east + west + north + south - 4.0 * s)
+        north, south = pitch_neighbours(s, lower[j], upper[j])
+        diffs_a.append(east - west)
+        diffs_p.append(north - south)
+        laps.append((east + west) + (north + south) - 4.0 * s)
     out = []
     for i in fields_out:
         r = DIFFUSION * laps[i]
         for j in range(len(state)):
-            r = r - ax[i][j] * grads_a[j] - pt[i][j] * grads_p[j]
+            r = r - (0.5 * ax[i][j]) * diffs_a[j] - (0.5 * pt[i][j]) * diffs_p[j]
         if i == 1 and push is not None:
             r = r + push
-        out.append(r * inside)
+        out.append(masked(r, inside))
     return out
 
 
@@ -224,7 +239,7 @@
 
 def assemble(u_ref, ms_ref, glo_ref, gup_ref, halo_ref, fields, modes, pitch):
     u = []
-    for j in range(fields):
+    for j in range(fields if u_ref is not None else 0):
         rows = slice(j * pitch, (j + 1) * pitch)
         u.append(widened(u_ref[j], halo_ref[rows, :]))
     ms = []
@@ -325,13 +340,13 @@
     return coef, disp2, vel2
 
 
-def step2_rate_kernel(peers, ax_ref, pt_ref, a_ref, u_ref, ms_ref, glo_ref, gup_ref, halo_ref, ra_ref):
+def step2_rate_kernel(peers, ax_ref, pt_ref, a_ref, ms_ref, glo_ref, gup_ref, halo_ref, ra_ref):
     fields = a_ref.shape[0]
     modes = ms_ref.shape[0]
-    pitch = u_ref.shape[1]
+    pitch = ms_ref.shape[1]
     jac = read_jacobians(ax_ref, pt_ref, fields)
-    _, ms, gl, gu = assemble(u_ref, ms_ref, glo_ref, gup_ref, halo_ref, fields, modes, pitch)
-    inside, _ = lane_masks(peers, ms[0].shape, u_ref.shape[-1])
+    _, ms, gl, gu = assemble(None, ms_ref, glo_ref, gup_ref, halo_ref, fields, modes, pitch)
+    inside, _ = lane_masks(peers, ms[0].shape, ms_ref.shape[-1])
     every = list(range(fields))
     a = [a_ref[j] for j in every]
     ra = kernel_rate(a, gl[1], gu[1], jac, None, inside, every)
@@ -350,7 +365,6 @@
     pt_ref,
     a_ref,
     ra_ref,
-    u_ref,
     ms_ref,
     glo_ref,
     gup_ref,
@@ -362,14 +376,14 @@
     h = TIME_STEP
     fields = a_ref.shape[0]
     modes = ms_ref.shape[0]
-    pitch = u_ref.shape[1]
+    pitch = ms_ref.shape[1]
     jac = read_jacobians(ax_ref, pt_ref, fields)
     coef, disp2, vel2 = modal_steps(force_scale, tot_ref, stiff_ref, disp_ref, vel_ref, modes)
     for m in range(modes):
         disp_out_ref[0, m] = disp2[m]
         vel_out_ref[0, m] = vel2[m]
-    _, ms, gl, gu = assemble(u_ref, ms_ref, glo_ref, gup_ref, halo_ref, fields, modes, pitch)
-    inside, _ = lane_masks(peers, ms[0].shape, u_ref.shape[-1])
+    _, ms, gl, gu = assemble(None, ms_ref, glo_ref, gup_ref, halo_ref, fields, modes, pitch)
+    inside, _ = lane_masks(peers, ms[0].shape, ms_ref.shape[-1])
 
     def combine(weights):
         total = weights[0] * ms[0]
@@ -397,7 +411,7 @@
         r = -ax[i][1] * ga - pt[i][1] * gp
         if i == 1:
             r = r + DIFFUSION * lap + push1
-        k1.append(ra_ref[i] + r * inside)
+        k1.append(ra_ref[i] + masked(r, inside))
     mid = [s1[j] + h * k1[j] for j in every]
     k2 = kernel_rate(mid, gl2, gu2, jac, COUPLING * combine(coef[2]), inside, every)
     width = out_ref.shape[-1]
@@ -484,17 +498,17 @@
     rate_a = pl.pallas_call(
         functools.partial(step2_rate_kernel, mesh_peers),
         out_shape=jax.ShapeDtypeStruct(base1.shape, base1.dtype),
-        in_specs=[smem_spec()] * 2 + [vmem_spec()] * 6,
+        in_specs=[smem_spec()] * 2 + [vmem_spec()] * 5,
         out_specs=vmem_spec(),
-    )(axial_jacobian, pitch_jacobian, base1, *ins)
+    )(axial_jacobian, pitch_jacobian, base1, *ins[1:])
 
     small = jax.ShapeDtypeStruct(displacement.shape, displacement.dtype)
     state2, disp2, vel2 = pl.pallas_call(
         functools.partial(second_kernel, mesh_peers, force_scale),
         out_shape=(jax.ShapeDtypeStruct(state0.shape, state0.dtype), small, small),
-        in_specs=[smem_spec()] * 6 + [vmem_spec()] * 7,
+        in_specs=[smem_spec()] * 6 + [vmem_spec()] * 6,
         out_specs=(vmem_spec(), smem_spec(), smem_spec()),
-    )(totals, stiffness, displacement, velocity, axial_jacobian, pitch_jacobian, base1, rate_a, *ins)
+    )(totals, stiffness, displacement, velocity, axial_jacobian, pitch_jacobian, base1, rate_a, *ins[1:])
     return (state2[None], disp2, vel2)
 
 

time: 38.4 us -> 37.8 us (0.984)
  Pallas kernels: 14.4 us -> 13.9 us
where the time goes in v10:
time: 37.8 us; the launch traced here: 37.5 us
  Pallas kernels  13.9 us (37%)
  waiting for transfers between devices  8.08 us (21%)
  starting transfers between devices  8.02 us (21%)
  local copies, waits for them, and re-layouts  4.34 us (11%)
  other arithmetic  2.53 us (7%)
  between operations  0.7 us (2%)
    ppermute x4, starting transfers between devices, shifted(): lax.ppermute(value, axis, [(i, (i + by) % peers) for i in range(peers)])  7.44 us
    pallas_call x1, Pallas kernels, on_device(): pl.pallas_call(functools.partial(first_kernel, mesh_peers), out_shape=(ja...  5.31 us
    ppermute x4, waiting for transfers between devices, shifted(): lax.ppermute(value, axis, [(i, (i + by) % peers) for i in range(peers)])  4.55 us
    ppermute x2, waiting for transfers between devices, mesh_sum(): lax.ppermute(value, 'mesh', [(i, i ^ step) for i in range(peers)])  3.53 us
    pallas_call x1, Pallas kernels, on_device(): pl.pallas_call(functools.partial(second_kernel, mesh_peers, force_scale),...  3.49 us
    pallas_call x1, Pallas kernels, on_device(): pl.pallas_call(functools.partial(step2_rate_kernel, mesh_peers), out_shap...  3.29 us
    unnamed x8, local copies, waits for them, and re-layouts  1.93 us
    pallas_call x1, Pallas kernels, on_device(): pl.pallas_call(functools.partial(pick_kernel, passages), out_shape=(row_s...  1.78 us
  transfers between devices with their start and end apart: 6, of which 3 were waited for; matrix products, arithmetic and copies ran while one was open for 4% of the time, Pallas kernels for 9%

profile of v10, /device:TPU:0, one launch (start us, length us, event | category | flops | bytes accessed | tf_op | source)
XLA Modules:
  0.0 37.5 jit_solution(7640253443770049753)
XLA Ops:
  0.6 0.0 copy-start.1
  0.6 1.8 %shard_map.130 = (f32[2,5,256]{2,1,0:T(8,128)}, f32[2,5,256]{2,1,0:T(8,128)}) custom-call(s32[8]{0:T(128)} %lower_slot_ref.1, s32[8]{0:T(128)} %upper_slot_ref.1, f32[5,64,256]{2,1,0:T(8,128)} %bitcast.38, f32[5,64,256]{2,1,0:T(8,128)} %bitcast.39), custom_call_target="tpu_custom_call" | custom-call | tf_op jit(solution)/shard_map/pallas_call | solution.py:458
  2.4 0.5 %collective-permute-start = (f32[2,5,256]{2,1,0:T(8,128)}, f32[2,5,256]{2,1,0:T(8,128)S(1)}, u32[]{:S(2)}, u32[]{:S(2)}) collective-permute-start(f32[2,5,256]{2,1,0:T(8,128)} %get-tuple-element.10), channel_id=1, source_target_pairs={{0,4},{4,8},{8,12},{12,16},{16,20},{20,24},{24,28},{28,0},{1,5},{5... | collective-permute-start | bytes 30728 | tf_op jit(solution)/shard_map/ppermute | solution.py:23
  2.9 4.0 %collective-permute-start.1 = (f32[2,5,256]{2,1,0:T(8,128)}, f32[2,5,256]{2,1,0:T(8,128)S(1)}, u32[]{:S(2)}, u32[]{:S(2)}) collective-permute-start(f32[2,5,256]{2,1,0:T(8,128)} %get-tuple-element.11), channel_id=1, source_target_pairs={{0,28},{4,0},{8,4},{12,8},{16,12},{20,16},{24,20},{28,24},{1,29},{... | collective-permute-start | bytes 30728 | tf_op jit(solution)/shard_map/ppermute | solution.py:23
  6.9 0.0 copy-done.1
  6.9 0.0 copy-start
  6.9 0.1 fusion
  7.0 0.9 %copy-done = f32[4,96,256]{2,1,0:T(8,128)S(1)} copy-done((f32[4,96,256]{2,1,0:T(8,128)S(1)}, f32[4,96,256]{2,1,0:T(8,128)}, u32[]{:S(2)}) %copy-start) | copy-done | bytes 393240
  7.9 0.1 fusion.1
  8.0 0.1 copy.25
  8.1 0.1 copy.30
  8.2 0.1 copy.24
  8.4 0.1 copy.29
  8.5 0.1 pad.1.clone
  8.6 0.0 collective-permute-done.glo_ref
  8.6 0.0 copy-start.2
  8.6 0.1 slice_bitcast_fusion.3
  8.7 0.5 %copy-done.2 = f32[2,5,256]{2,1,0:T(8,128)} copy-done((f32[2,5,256]{2,1,0:T(8,128)}, f32[2,5,256]{2,1,0:T(8,128)S(1)}, u32[]{:S(2)}) %copy-start.2) | copy-done | bytes 10264
  9.2 0.1 copy.22
  9.3 0.1 reshape.46
  9.4 0.1 copy.27
  9.5 0.1 reshape.51
  9.6 0.0 collective-permute-done.1.gup_ref
  9.6 0.0 copy-start.3
  9.6 0.1 slice_bitcast_fusion.2
  9.6 0.5 %copy-done.3 = f32[2,5,256]{2,1,0:T(8,128)} copy-done((f32[2,5,256]{2,1,0:T(8,128)}, f32[2,5,256]{2,1,0:T(8,128)S(1)}, u32[]{:S(2)}) %copy-start.3) | copy-done | bytes 10264
  10.2 0.1 copy.23
  10.3 0.1 reshape.47
  10.3 0.1 copy.28
  10.4 0.1 reshape.52
  10.5 0.1 pad_maximum_fusion.1
  10.6 0.1 reshape.48
  10.7 2.9 %collective-permute-start.2 = (f32[3536]{0:T(1024)S(1)}, f32[3536]{0:T(1024)S(1)}, u32[]{:S(2)}, u32[]{:S(2)}) collective-permute-start(f32[3536]{0:T(1024)S(1)} %reshape.48), channel_id=1, source_target_pairs={{0,3},{1,0},{2,1},{3,2},{4,7},{5,4},{6,5},{7,6},{8,11},{9,8},{10,9... | collective-permute-start | bytes 42440 | tf_op jit(solution)/shard_map/ppermute | solution.py:23
  13.6 0.1 pad_maximum_fusion.2
  13.7 0.1 reshape.53
  13.8 0.0 collective-permute-start.3
  13.8 1.3 %collective-permute-done.2 = f32[3536]{0:T(1024)S(1)} collective-permute-done((f32[3536]{0:T(1024)S(1)}, f32[3536]{0:T(1024)S(1)}, u32[]{:S(2)}, u32[]{:S(2)}) %collective-permute-start.2) | collective-permute-done | bytes 14176 | tf_op jit(solution)/shard_map/ppermute | solution.py:23
  15.1 0.1 select_n.22
  15.2 3.3 %collective-permute-done.3 = f32[3536]{0:T(1024)S(1)} collective-permute-done((f32[3536]{0:T(1024)S(1)}, f32[3536]{0:T(1024)S(1)}, u32[]{:S(2)}, u32[]{:S(2)}) %collective-permute-start.3) | collective-permute-done | bytes 14176 | tf_op jit(solution)/shard_map/ppermute | solution.py:23
  18.4 0.1 select_n.25
  18.5 0.2 copy.31
  18.7 0.2 copy.26
  19.0 1.0 %pad_maximum_fusion.halo_ref = f32[884,128]{1,0:T(8,128)} fusion(f32[884,4]{1,0:T(8,128)S(1)} %bitcast.32, f32[884,4]{1,0:T(8,128)S(1)} %bitcast.33, f32[128]{0:T(128)S(1)} %pad.1.clone), kind=kLoop, calls=%fused_computation | loop fusion | flops 226304 | bytes 481408 | tf_op jit(solution)/shard_map/concatenate | solution.py:482
  19.9 5.3 %shard_map.131 = (f32[5,96,384]{2,1,0:T(8,128)}, f32[32,128]{1,0:T(8,128)}) custom-call(f32[5,5]{1,0:T(8,128)} %ax_ref.5, f32[5,5]{1,0:T(8,128)} %pt_ref.5, f32[1,4]{1,0:T(1,128)} %vel_ref.3, f32[5,96,256]{2,1,0:T(8,128)} %bitcast.30, f32[4,96,256]{2,1,0:T(8,128)} %ms_ref.5, f32[2,5,256]{2,1,0:T(8,128)} %copy-done.2, f32[2,5,256]{2,1,0:T(8,128)} %copy-done.3, ...), custom_call_target="tpu_custom_call" | custom-call | tf_op jit(solution)/shard_map/pallas_call | solution.py:486
  25.2 0.8 %reduce_sum.9 = f32[32]{0:T(128)S(1)} reduce(f32[32,128]{1,0:T(8,128)} %get-tuple-element.12, f32[]{:T(128)} %constant.6.clone.1), dimensions={1}, to_apply=%region_0.1 | reduce | flops 4064 | bytes 16516 | tf_op jit(solution)/shard_map/reduce_sum | solution.py:496
  26.1 0.1 collective-permute-start.4
  26.1 3.5 %collective-permute-done.4 = f32[32]{0:T(128)S(1)} collective-permute-done((f32[32]{0:T(128)S(1)}, f32[32]{0:T(128)S(1)}, u32[]{:S(2)}, u32[]{:S(2)}) %collective-permute-start.4) | collective-permute-done | bytes 160 | tf_op jit(solution)/shard_map/ppermute | solution.py:42
  29.7 0.5 %collective-permute-start.5 = (f32[32]{0:T(128)S(1)}, f32[32]{0:T(128)S(1)}, u32[]{:S(2)}, u32[]{:S(2)}) collective-permute-start(f32[32]{0:T(128)S(1)} %add.6), channel_id=1, source_target_pairs={{0,2},{1,3},{2,0},{3,1},{4,6},{5,7},{6,4},{7,5},{8,10},{9,11},{10,... | collective-permute-start | bytes 392 | tf_op jit(solution)/shard_map/ppermute | solution.py:42
  30.2 3.3 %shard_map.132.ra_ref = f32[5,96,384]{2,1,0:T(8,128)} custom-call(f32[5,5]{1,0:T(8,128)} %ax_ref.5, f32[5,5]{1,0:T(8,128)} %pt_ref.5, f32[5,96,384]{2,1,0:T(8,128)} %get-tuple-element.13.a_ref, f32[4,96,256]{2,1,0:T(8,128)} %ms_ref.5, f32[2,5,256]{2,1,0:T(8,128)} %copy-done.2, f32[2,5,256]{2,1,0:T(8,128)} %copy-done.3, f32[884,128]{1,0:T(8,128)} %pad_maximum_fusion.halo_ref), custom_call_target="tpu_custom_call" | custom-call | tf_op jit(solution)/shard_map/pallas_call | solution.py:498
  33.5 0.0 collective-permute-done.5
  33.5 0.6 %add.7.tot_ref = f32[32]{0:T(128)} add(f32[32]{0:T(128)S(1)} %add.6, f32[32]{0:T(128)S(1)} %collective-permute-done.5) | non-fusion elementwise | flops 32 | bytes 384 | tf_op jit(solution)/shard_map/add | solution.py:42
  34.0 3.5 %shard_map.133 = (f32[5,96,256]{2,1,0:T(8,128)}, f32[1,4]{1,0:T(1,128)}, f32[1,4]{1,0:T(1,128)}) custom-call(f32[32]{0:T(128)} %add.7.tot_ref, f32[1,4]{1,0:T(1,128)} %stiff_ref.1, f32[1,4]{1,0:T(1,128)} %disp_ref.1, f32[1,4]{1,0:T(1,128)} %vel_ref.3, f32[5,5]{1,0:T(8,128)} %ax_ref.5, f32[5,5]{1,0:T(8,128)} %pt_ref.5, ...), custom_call_target="tpu_custom_call" | custom-call | tf_op jit(solution)/shard_map/pallas_call | solution.py:506
  (4 shorter events, 0.0 us)
Async XLA Ops:
  0.6 6.3 %copy-start.1 = (f32[1,5,96,256]{3,2,1,0:T(8,128)S(1)}, f32[1,5,96,256]{3,2,1,0:T(8,128)}, u32[]{:S(2)}) copy-start(f32[1,5,96,256]{3,2,1,0:T(8,128)} %param.11) | copy-start | bytes 1474564
  2.4 6.2 %collective-permute-start = (f32[2,5,256]{2,1,0:T(8,128)}, f32[2,5,256]{2,1,0:T(8,128)S(1)}, u32[]{:S(2)}, u32[]{:S(2)}) collective-permute-start(f32[2,5,256]{2,1,0:T(8,128)} %get-tuple-element.10), channel_id=1, source_target_pairs={{0,4},{4,8},{8,12},{12,16},{16,20},{20,24},{24,28},{28,0},{1,5},{5... | collective-permute-start | bytes 30728 | tf_op jit(solution)/shard_map/ppermute | solution.py:23
  2.9 6.7 %collective-permute-start.1 = (f32[2,5,256]{2,1,0:T(8,128)}, f32[2,5,256]{2,1,0:T(8,128)S(1)}, u32[]{:S(2)}, u32[]{:S(2)}) collective-permute-start(f32[2,5,256]{2,1,0:T(8,128)} %get-tuple-element.11), channel_id=1, source_target_pairs={{0,28},{4,0},{8,4},{12,8},{16,12},{20,16},{24,20},{28,24},{1,29},{... | collective-permute-start | bytes 30728 | tf_op jit(solution)/shard_map/ppermute | solution.py:23
  6.9 1.0 %copy-start = (f32[4,96,256]{2,1,0:T(8,128)S(1)}, f32[4,96,256]{2,1,0:T(8,128)}, u32[]{:S(2)}) copy-start(f32[4,96,256]{2,1,0:T(8,128)} %ms_ref.5) | copy-start | bytes 1179652
  8.6 0.6 %copy-start.2 = (f32[2,5,256]{2,1,0:T(8,128)}, f32[2,5,256]{2,1,0:T(8,128)S(1)}, u32[]{:S(2)}) copy-start(f32[2,5,256]{2,1,0:T(8,128)S(1)} %collective-permute-done.glo_ref) | copy-start | bytes 30724
  9.6 0.6 %copy-start.3 = (f32[2,5,256]{2,1,0:T(8,128)}, f32[2,5,256]{2,1,0:T(8,128)S(1)}, u32[]{:S(2)}) copy-start(f32[2,5,256]{2,1,0:T(8,128)S(1)} %collective-permute-done.1.gup_ref) | copy-start | bytes 30724
  10.7 4.4 %collective-permute-start.2 = (f32[3536]{0:T(1024)S(1)}, f32[3536]{0:T(1024)S(1)}, u32[]{:S(2)}, u32[]{:S(2)}) collective-permute-start(f32[3536]{0:T(1024)S(1)} %reshape.48), channel_id=1, source_target_pairs={{0,3},{1,0},{2,1},{3,2},{4,7},{5,4},{6,5},{7,6},{8,11},{9,8},{10,9... | collective-permute-start | bytes 42440 | tf_op jit(solution)/shard_map/ppermute | solution.py:23
  13.8 4.6 %collective-permute-start.3 = (f32[3536]{0:T(1024)S(1)}, f32[3536]{0:T(1024)S(1)}, u32[]{:S(2)}, u32[]{:S(2)}) collective-permute-start(f32[3536]{0:T(1024)S(1)} %reshape.53), channel_id=1, source_target_pairs={{0,1},{1,2},{2,3},{3,0},{4,5},{5,6},{6,7},{7,4},{8,9},{9,10},{10,1... | collective-permute-start | bytes 42440 | tf_op jit(solution)/shard_map/ppermute | solution.py:23
  26.1 3.6 %collective-permute-start.4 = (f32[32]{0:T(128)S(1)}, f32[32]{0:T(128)S(1)}, u32[]{:S(2)}, u32[]{:S(2)}) collective-permute-start(f32[32]{0:T(128)S(1)} %reduce_sum.9), channel_id=1, source_target_pairs={{0,1},{1,0},{2,3},{3,2},{4,5},{5,4},{6,7},{7,6},{8,9},{9,8},{10,11... | collective-permute-start | bytes 392 | tf_op jit(solution)/shard_map/ppermute | solution.py:42
  29.7 3.8 %collective-permute-start.5 = (f32[32]{0:T(128)S(1)}, f32[32]{0:T(128)S(1)}, u32[]{:S(2)}, u32[]{:S(2)}) collective-permute-start(f32[32]{0:T(128)S(1)} %add.6), channel_id=1, source_target_pairs={{0,2},{1,3},{2,0},{3,1},{4,6},{5,7},{6,4},{7,5},{8,10},{9,11},{10,... | collective-permute-start | bytes 392 | tf_op jit(solution)/shard_map/ppermute | solution.py:42

commit v11 on v10

--- a/solution.py
+++ b/solution.py
@@ -268,7 +268,7 @@
     jac = read_jacobians(ax_ref, pt_ref, fields)
     vel = [vel_ref[0, m] for m in range(modes)]
     u0, ms, gl, gu = assemble(u_ref, ms_ref, glo_ref, gup_ref, halo_ref, fields, modes, pitch)
-    inside, owned = lane_masks(peers, u0[0].shape, u_ref.shape[-1])
+    inside, _ = lane_masks(peers, u0[0].shape, u_ref.shape[-1])
     push = vel[0] * ms[0]
     for m in range(1, modes):
         push = push + vel[m] * ms[m]
@@ -282,22 +282,21 @@
     for j in every:
         a_ref[j] = a[j]
     (ra4,) = kernel_rate(a, gl2, gu2, jac, None, inside, [4])
-    weighted = [ms[m] * owned for m in range(modes)]
+    own = u_ref.shape[-1]
+    weighted = [ms_ref[m] for m in range(modes)]
     k = 0
     for field in (u0[4], mid[4], a[4], ra4):
+        field = field[:, :own]
         for m in range(modes):
             part_ref[k : k + 1, :] = lane_fold(weighted[m] * field)
             k += 1
-    ax41, pt41 = jac[0][4][1], jac[1][4][1]
-    rows = ms[0].shape[0]
-    row = lax.broadcasted_iota(jnp.int32, ms[0].shape, 0)
+    ax41, pt41 = 0.5 * jac[0][4][1], 0.5 * jac[1][4][1]
+    no_ghost = jnp.zeros((1, ms[0].shape[1]), ms[0].dtype)
     for n in range(modes):
         s = ms[n]
-        ga = 0.5 * (lane_roll(s, -1) - lane_roll(s, 1))
-        north = jnp.where(row == rows - 1, 0.0, row_roll(s, -1))
-        south = jnp.where(row == 0, 0.0, row_roll(s, 1))
-        gp = 0.5 * (north - south)
-        t = -(ax41 * ga + pt41 * gp)
+        north, south = pitch_neighbours(s, no_ghost, no_ghost)
+        t = -(ax41 * (lane_roll(s, -1) - lane_roll(s, 1)) + pt41 * (north - south))
+        t = t[:, :own]
         for m in range(modes):
             part_ref[k + m * modes + n : k + m * modes + n + 1, :] = lane_fold(weighted[m] * t)
 

time: 37.8 us -> 37.6 us (level)
  no operation moved by 1% of the time
where the time goes in v11:
time: 37.6 us; the launch traced here: 37.2 us
  Pallas kernels  13.6 us (36%)
  waiting for transfers between devices  8.08 us (21%)
  starting transfers between devices  8.02 us (21%)
  local copies, waits for them, and re-layouts  4.34 us (12%)
  other arithmetic  2.53 us (7%)
  between operations  0.7 us (2%)
    ppermute x4, starting transfers between devices, shifted(): lax.ppermute(value, axis, [(i, (i + by) % peers) for i in range(peers)])  7.44 us
    pallas_call x1, Pallas kernels, on_device(): pl.pallas_call(functools.partial(first_kernel, mesh_peers), out_shape=(ja...  5.02 us
    ppermute x4, waiting for transfers between devices, shifted(): lax.ppermute(value, axis, [(i, (i + by) % peers) for i in range(peers)])  4.55 us
    ppermute x2, waiting for transfers between devices, mesh_sum(): lax.ppermute(value, 'mesh', [(i, i ^ step) for i in range(peers)])  3.53 us
    pallas_call x1, Pallas kernels, on_device(): pl.pallas_call(functools.partial(second_kernel, mesh_peers, force_scale),...  3.49 us
    pallas_call x1, Pallas kernels, on_device(): pl.pallas_call(functools.partial(step2_rate_kernel, mesh_peers), out_shap...  3.28 us
    unnamed x8, local copies, waits for them, and re-layouts  1.93 us
    pallas_call x1, Pallas kernels, on_device(): pl.pallas_call(functools.partial(pick_kernel, passages), out_shape=(row_s...  1.78 us
  transfers between devices with their start and end apart: 6, of which 3 were waited for; matrix products, arithmetic and copies ran while one was open for 4% of the time, Pallas kernels for 9%

profile of v11, /device:TPU:0, one launch (start us, length us, event | category | flops | bytes accessed | tf_op | source)
XLA Modules:
  0.0 37.2 jit_solution(7181701372310913012)
XLA Ops:
  0.6 0.0 copy-start.1
  0.6 1.8 %shard_map.130 = (f32[2,5,256]{2,1,0:T(8,128)}, f32[2,5,256]{2,1,0:T(8,128)}) custom-call(s32[8]{0:T(128)} %lower_slot_ref.1, s32[8]{0:T(128)} %upper_slot_ref.1, f32[5,64,256]{2,1,0:T(8,128)} %bitcast.38, f32[5,64,256]{2,1,0:T(8,128)} %bitcast.39), custom_call_target="tpu_custom_call" | custom-call | tf_op jit(solution)/shard_map/pallas_call | solution.py:457
  2.4 0.5 %collective-permute-start = (f32[2,5,256]{2,1,0:T(8,128)}, f32[2,5,256]{2,1,0:T(8,128)S(1)}, u32[]{:S(2)}, u32[]{:S(2)}) collective-permute-start(f32[2,5,256]{2,1,0:T(8,128)} %get-tuple-element.10), channel_id=1, source_target_pairs={{0,4},{4,8},{8,12},{12,16},{16,20},{20,24},{24,28},{28,0},{1,5},{5... | collective-permute-start | bytes 30728 | tf_op jit(solution)/shard_map/ppermute | solution.py:23
  2.9 4.0 %collective-permute-start.1 = (f32[2,5,256]{2,1,0:T(8,128)}, f32[2,5,256]{2,1,0:T(8,128)S(1)}, u32[]{:S(2)}, u32[]{:S(2)}) collective-permute-start(f32[2,5,256]{2,1,0:T(8,128)} %get-tuple-element.11), channel_id=1, source_target_pairs={{0,28},{4,0},{8,4},{12,8},{16,12},{20,16},{24,20},{28,24},{1,29},{... | collective-permute-start | bytes 30728 | tf_op jit(solution)/shard_map/ppermute | solution.py:23
  6.9 0.0 copy-done.1
  6.9 0.0 copy-start
  6.9 0.1 fusion
  7.0 0.9 %copy-done = f32[4,96,256]{2,1,0:T(8,128)S(1)} copy-done((f32[4,96,256]{2,1,0:T(8,128)S(1)}, f32[4,96,256]{2,1,0:T(8,128)}, u32[]{:S(2)}) %copy-start) | copy-done | bytes 393240
  7.9 0.1 fusion.1
  8.0 0.1 copy.25
  8.1 0.1 copy.30
  8.2 0.1 copy.24
  8.4 0.1 copy.29
  8.5 0.1 pad.1.clone
  8.6 0.0 collective-permute-done.glo_ref
  8.6 0.0 copy-start.2
  8.6 0.1 slice_bitcast_fusion.3
  8.7 0.5 %copy-done.2 = f32[2,5,256]{2,1,0:T(8,128)} copy-done((f32[2,5,256]{2,1,0:T(8,128)}, f32[2,5,256]{2,1,0:T(8,128)S(1)}, u32[]{:S(2)}) %copy-start.2) | copy-done | bytes 10264
  9.2 0.1 copy.22
  9.3 0.1 reshape.46
  9.4 0.1 copy.27
  9.5 0.1 reshape.51
  9.6 0.0 collective-permute-done.1.gup_ref
  9.6 0.0 copy-start.3
  9.6 0.1 slice_bitcast_fusion.2
  9.6 0.5 %copy-done.3 = f32[2,5,256]{2,1,0:T(8,128)} copy-done((f32[2,5,256]{2,1,0:T(8,128)}, f32[2,5,256]{2,1,0:T(8,128)S(1)}, u32[]{:S(2)}) %copy-start.3) | copy-done | bytes 10264
  10.2 0.1 copy.23
  10.3 0.1 reshape.47
  10.3 0.1 copy.28
  10.4 0.1 reshape.52
  10.5 0.1 pad_maximum_fusion.1
  10.6 0.1 reshape.48
  10.7 2.9 %collective-permute-start.2 = (f32[3536]{0:T(1024)S(1)}, f32[3536]{0:T(1024)S(1)}, u32[]{:S(2)}, u32[]{:S(2)}) collective-permute-start(f32[3536]{0:T(1024)S(1)} %reshape.48), channel_id=1, source_target_pairs={{0,3},{1,0},{2,1},{3,2},{4,7},{5,4},{6,5},{7,6},{8,11},{9,8},{10,9... | collective-permute-start | bytes 42440 | tf_op jit(solution)/shard_map/ppermute | solution.py:23
  13.6 0.1 pad_maximum_fusion.2
  13.7 0.1 reshape.53
  13.8 0.0 collective-permute-start.3
  13.8 1.3 %collective-permute-done.2 = f32[3536]{0:T(1024)S(1)} collective-permute-done((f32[3536]{0:T(1024)S(1)}, f32[3536]{0:T(1024)S(1)}, u32[]{:S(2)}, u32[]{:S(2)}) %collective-permute-start.2) | collective-permute-done | bytes 14176 | tf_op jit(solution)/shard_map/ppermute | solution.py:23
  15.1 0.1 select_n.22
  15.2 3.3 %collective-permute-done.3 = f32[3536]{0:T(1024)S(1)} collective-permute-done((f32[3536]{0:T(1024)S(1)}, f32[3536]{0:T(1024)S(1)}, u32[]{:S(2)}, u32[]{:S(2)}) %collective-permute-start.3) | collective-permute-done | bytes 14176 | tf_op jit(solution)/shard_map/ppermute | solution.py:23
  18.4 0.1 select_n.25
  18.5 0.2 copy.31
  18.7 0.2 copy.26
  19.0 1.0 %pad_maximum_fusion.halo_ref = f32[884,128]{1,0:T(8,128)} fusion(f32[884,4]{1,0:T(8,128)S(1)} %bitcast.32, f32[884,4]{1,0:T(8,128)S(1)} %bitcast.33, f32[128]{0:T(128)S(1)} %pad.1.clone), kind=kLoop, calls=%fused_computation | loop fusion | flops 226304 | bytes 481408 | tf_op jit(solution)/shard_map/concatenate | solution.py:481
  19.9 5.0 %shard_map.131 = (f32[5,96,384]{2,1,0:T(8,128)}, f32[32,128]{1,0:T(8,128)}) custom-call(f32[5,5]{1,0:T(8,128)} %ax_ref.5, f32[5,5]{1,0:T(8,128)} %pt_ref.5, f32[1,4]{1,0:T(1,128)} %vel_ref.3, f32[5,96,256]{2,1,0:T(8,128)} %bitcast.30, f32[4,96,256]{2,1,0:T(8,128)} %ms_ref.5, f32[2,5,256]{2,1,0:T(8,128)} %copy-done.2, f32[2,5,256]{2,1,0:T(8,128)} %copy-done.3, ...), custom_call_target="tpu_custom_call" | custom-call | tf_op jit(solution)/shard_map/pallas_call | solution.py:485
  24.9 0.8 %reduce_sum.9 = f32[32]{0:T(128)S(1)} reduce(f32[32,128]{1,0:T(8,128)} %get-tuple-element.12, f32[]{:T(128)} %constant.6.clone.1), dimensions={1}, to_apply=%region_0.1 | reduce | flops 4064 | bytes 16516 | tf_op jit(solution)/shard_map/reduce_sum | solution.py:495
  25.8 0.1 collective-permute-start.4
  25.8 3.5 %collective-permute-done.4 = f32[32]{0:T(128)S(1)} collective-permute-done((f32[32]{0:T(128)S(1)}, f32[32]{0:T(128)S(1)}, u32[]{:S(2)}, u32[]{:S(2)}) %collective-permute-start.4) | collective-permute-done | bytes 160 | tf_op jit(solution)/shard_map/ppermute | solution.py:42
  29.4 0.5 %collective-permute-start.5 = (f32[32]{0:T(128)S(1)}, f32[32]{0:T(128)S(1)}, u32[]{:S(2)}, u32[]{:S(2)}) collective-permute-start(f32[32]{0:T(128)S(1)} %add.6), channel_id=1, source_target_pairs={{0,2},{1,3},{2,0},{3,1},{4,6},{5,7},{6,4},{7,5},{8,10},{9,11},{10,... | collective-permute-start | bytes 392 | tf_op jit(solution)/shard_map/ppermute | solution.py:42
  29.9 3.3 %shard_map.132.ra_ref = f32[5,96,384]{2,1,0:T(8,128)} custom-call(f32[5,5]{1,0:T(8,128)} %ax_ref.5, f32[5,5]{1,0:T(8,128)} %pt_ref.5, f32[5,96,384]{2,1,0:T(8,128)} %get-tuple-element.13.a_ref, f32[4,96,256]{2,1,0:T(8,128)} %ms_ref.5, f32[2,5,256]{2,1,0:T(8,128)} %copy-done.2, f32[2,5,256]{2,1,0:T(8,128)} %copy-done.3, f32[884,128]{1,0:T(8,128)} %pad_maximum_fusion.halo_ref), custom_call_target="tpu_custom_call" | custom-call | tf_op jit(solution)/shard_map/pallas_call | solution.py:497
  33.2 0.0 collective-permute-done.5
  33.2 0.6 %add.7.tot_ref = f32[32]{0:T(128)} add(f32[32]{0:T(128)S(1)} %add.6, f32[32]{0:T(128)S(1)} %collective-permute-done.5) | non-fusion elementwise | flops 32 | bytes 384 | tf_op jit(solution)/shard_map/add | solution.py:42
  33.8 3.5 %shard_map.133 = (f32[5,96,256]{2,1,0:T(8,128)}, f32[1,4]{1,0:T(1,128)}, f32[1,4]{1,0:T(1,128)}) custom-call(f32[32]{0:T(128)} %add.7.tot_ref, f32[1,4]{1,0:T(1,128)} %stiff_ref.1, f32[1,4]{1,0:T(1,128)} %disp_ref.1, f32[1,4]{1,0:T(1,128)} %vel_ref.3, f32[5,5]{1,0:T(8,128)} %ax_ref.5, f32[5,5]{1,0:T(8,128)} %pt_ref.5, ...), custom_call_target="tpu_custom_call" | custom-call | tf_op jit(solution)/shard_map/pallas_call | solution.py:505
  (4 shorter events, 0.0 us)
Async XLA Ops:
  0.6 6.3 %copy-start.1 = (f32[1,5,96,256]{3,2,1,0:T(8,128)S(1)}, f32[1,5,96,256]{3,2,1,0:T(8,128)}, u32[]{:S(2)}) copy-start(f32[1,5,96,256]{3,2,1,0:T(8,128)} %param.11) | copy-start | bytes 1474564
  2.4 6.2 %collective-permute-start = (f32[2,5,256]{2,1,0:T(8,128)}, f32[2,5,256]{2,1,0:T(8,128)S(1)}, u32[]{:S(2)}, u32[]{:S(2)}) collective-permute-start(f32[2,5,256]{2,1,0:T(8,128)} %get-tuple-element.10), channel_id=1, source_target_pairs={{0,4},{4,8},{8,12},{12,16},{16,20},{20,24},{24,28},{28,0},{1,5},{5... | collective-permute-start | bytes 30728 | tf_op jit(solution)/shard_map/ppermute | solution.py:23
  2.9 6.7 %collective-permute-start.1 = (f32[2,5,256]{2,1,0:T(8,128)}, f32[2,5,256]{2,1,0:T(8,128)S(1)}, u32[]{:S(2)}, u32[]{:S(2)}) collective-permute-start(f32[2,5,256]{2,1,0:T(8,128)} %get-tuple-element.11), channel_id=1, source_target_pairs={{0,28},{4,0},{8,4},{12,8},{16,12},{20,16},{24,20},{28,24},{1,29},{... | collective-permute-start | bytes 30728 | tf_op jit(solution)/shard_map/ppermute | solution.py:23
  6.9 1.0 %copy-start = (f32[4,96,256]{2,1,0:T(8,128)S(1)}, f32[4,96,256]{2,1,0:T(8,128)}, u32[]{:S(2)}) copy-start(f32[4,96,256]{2,1,0:T(8,128)} %ms_ref.5) | copy-start | bytes 1179652
  8.6 0.6 %copy-start.2 = (f32[2,5,256]{2,1,0:T(8,128)}, f32[2,5,256]{2,1,0:T(8,128)S(1)}, u32[]{:S(2)}) copy-start(f32[2,5,256]{2,1,0:T(8,128)S(1)} %collective-permute-done.glo_ref) | copy-start | bytes 30724
  9.6 0.6 %copy-start.3 = (f32[2,5,256]{2,1,0:T(8,128)}, f32[2,5,256]{2,1,0:T(8,128)S(1)}, u32[]{:S(2)}) copy-start(f32[2,5,256]{2,1,0:T(8,128)S(1)} %collective-permute-done.1.gup_ref) | copy-start | bytes 30724
  10.7 4.4 %collective-permute-start.2 = (f32[3536]{0:T(1024)S(1)}, f32[3536]{0:T(1024)S(1)}, u32[]{:S(2)}, u32[]{:S(2)}) collective-permute-start(f32[3536]{0:T(1024)S(1)} %reshape.48), channel_id=1, source_target_pairs={{0,3},{1,0},{2,1},{3,2},{4,7},{5,4},{6,5},{7,6},{8,11},{9,8},{10,9... | collective-permute-start | bytes 42440 | tf_op jit(solution)/shard_map/ppermute | solution.py:23
  13.8 4.6 %collective-permute-start.3 = (f32[3536]{0:T(1024)S(1)}, f32[3536]{0:T(1024)S(1)}, u32[]{:S(2)}, u32[]{:S(2)}) collective-permute-start(f32[3536]{0:T(1024)S(1)} %reshape.53), channel_id=1, source_target_pairs={{0,1},{1,2},{2,3},{3,0},{4,5},{5,6},{6,7},{7,4},{8,9},{9,10},{10,1... | collective-permute-start | bytes 42440 | tf_op jit(solution)/shard_map/ppermute | solution.py:23
  25.8 3.6 %collective-permute-start.4 = (f32[32]{0:T(128)S(1)}, f32[32]{0:T(128)S(1)}, u32[]{:S(2)}, u32[]{:S(2)}) collective-permute-start(f32[32]{0:T(128)S(1)} %reduce_sum.9), channel_id=1, source_target_pairs={{0,1},{1,0},{2,3},{3,2},{4,5},{5,4},{6,7},{7,6},{8,9},{9,8},{10,11... | collective-permute-start | bytes 392 | tf_op jit(solution)/shard_map/ppermute | solution.py:42
  29.4 3.8 %collective-permute-start.5 = (f32[32]{0:T(128)S(1)}, f32[32]{0:T(128)S(1)}, u32[]{:S(2)}, u32[]{:S(2)}) collective-permute-start(f32[32]{0:T(128)S(1)} %add.6), channel_id=1, source_target_pairs={{0,2},{1,3},{2,0},{3,1},{4,6},{5,7},{6,4},{7,5},{8,10},{9,11},{10,... | collective-permute-start | bytes 392 | tf_op jit(solution)/shard_map/ppermute | solution.py:42

commit v12 on v11

--- a/solution.py
+++ b/solution.py
@@ -339,7 +339,8 @@
     return coef, disp2, vel2
 
 
-def step2_rate_kernel(peers, ax_ref, pt_ref, a_ref, ms_ref, glo_ref, gup_ref, halo_ref, ra_ref):
+def step2_rate_kernel(peers, first, ax_ref, pt_ref, *refs):
+    a_ref, ms_ref, glo_ref, gup_ref, halo_ref, ra_ref = refs[-6:]
     fields = a_ref.shape[0]
     modes = ms_ref.shape[0]
     pitch = ms_ref.shape[1]
@@ -348,9 +349,10 @@
     inside, _ = lane_masks(peers, ms[0].shape, ms_ref.shape[-1])
     every = list(range(fields))
     a = [a_ref[j] for j in every]
-    ra = kernel_rate(a, gl[1], gu[1], jac, None, inside, every)
-    for j in every:
-        ra_ref[j] = ra[j]
+    wanted = list(range(first, first + ra_ref.shape[0]))
+    ra = kernel_rate(a, gl[1], gu[1], jac, None, inside, wanted)
+    for j, r in enumerate(ra):
+        ra_ref[j] = r
 
 
 def second_kernel(
@@ -363,7 +365,8 @@
     ax_ref,
     pt_ref,
     a_ref,
-    ra_ref,
+    ra_low_ref,
+    ra_high_ref,
     ms_ref,
     glo_ref,
     gup_ref,
@@ -410,7 +413,9 @@
         r = -ax[i][1] * ga - pt[i][1] * gp
         if i == 1:
             r = r + DIFFUSION * lap + push1
-        k1.append(ra_ref[i] + masked(r, inside))
+        split = ra_low_ref.shape[0]
+        ra_i = ra_low_ref[i] if i < split else ra_high_ref[i - split]
+        k1.append(ra_i + masked(r, inside))
     mid = [s1[j] + h * k1[j] for j in every]
     k2 = kernel_rate(mid, gl2, gu2, jac, COUPLING * combine(coef[2]), inside, every)
     width = out_ref.shape[-1]
@@ -492,22 +497,38 @@
         out_specs=(vmem_spec(), vmem_spec()),
     )(axial_jacobian, pitch_jacobian, velocity, *ins)
 
-    totals = mesh_sum(jnp.sum(part_lanes, axis=1))
-
-    rate_a = pl.pallas_call(
-        functools.partial(step2_rate_kernel, mesh_peers),
-        out_shape=jax.ShapeDtypeStruct(base1.shape, base1.dtype),
-        in_specs=[smem_spec()] * 2 + [vmem_spec()] * 5,
-        out_specs=vmem_spec(),
-    )(axial_jacobian, pitch_jacobian, base1, *ins[1:])
+    split = fields // 2
+
+    def rate_part(first, count, *order):
+        return pl.pallas_call(
+            functools.partial(step2_rate_kernel, mesh_peers, first),
+            out_shape=jax.ShapeDtypeStruct((count,) + base1.shape[1:], base1.dtype),
+            in_specs=[smem_spec()] * (2 + len(order)) + [vmem_spec()] * 5,
+            out_specs=vmem_spec(),
+        )(axial_jacobian, pitch_jacobian, *order, base1, *ins[1:])
+
+    rate_low = rate_part(0, split)
+    totals = jnp.sum(part_lanes, axis=1)
+    peers = mesh_peers
+    if peers & (peers - 1) or peers < 2:
+        totals = lax.psum(totals, "mesh")
+        rate_high = rate_part(split, fields - split)
+    else:
+        step = 1
+        while step < peers:
+            totals = totals + lax.ppermute(totals, "mesh", [(i, i ^ step) for i in range(peers)])
+            if step == 1:
+                totals, rate_low = lax.optimization_barrier((totals, rate_low))
+                rate_high = rate_part(split, fields - split, totals)
+            step *= 2
 
     small = jax.ShapeDtypeStruct(displacement.shape, displacement.dtype)
     state2, disp2, vel2 = pl.pallas_call(
         functools.partial(second_kernel, mesh_peers, force_scale),
         out_shape=(jax.ShapeDtypeStruct(state0.shape, state0.dtype), small, small),
-        in_specs=[smem_spec()] * 6 + [vmem_spec()] * 6,
+        in_specs=[smem_spec()] * 6 + [vmem_spec()] * 7,
         out_specs=(vmem_spec(), smem_spec(), smem_spec()),
-    )(totals, stiffness, displacement, velocity, axial_jacobian, pitch_jacobian, base1, rate_a, *ins[1:])
+    )(totals, stiffness, displacement, velocity, axial_jacobian, pitch_jacobian, base1, rate_low, rate_high, *ins[1:])
     return (state2[None], disp2, vel2)
 
 

time: 37.6 us -> 38 us (1.011)
  waiting for transfers between devices: 8.08 us -> 5.44 us
  Pallas kernels: 13.6 us -> 15.9 us
  other arithmetic: 2.53 us -> 3.2 us
    ppermute x2, waiting for transfers between devices: 3.53 us -> 0.89 us  [on_device(): lax.ppermute(totals, 'mesh', [(i, i ^ step) for i in range(peers)])]
    pallas_call x1 -> x2, Pallas kernels: 3.28 us -> 5.66 us  [rate_part(): pl.pallas_call(functools.partial(step2_rate_kernel, mesh_peers, first), o...]
    add x2, other arithmetic: 0.58 us -> 1.24 us  [on_device(): totals + lax.ppermute(totals, 'mesh', [(i, i ^ step) for i in range(peers)])]
    unnamed x8 -> x10, local copies, waits for them, and re-layouts: 1.93 us -> 1.93 us
  transfers between devices with their start and end apart: 6 -> 6, of which waited for: 3 -> 4; matrix products, arithmetic and copies ran while one was open for 4% -> 4% of each run, Pallas kernels for 9% -> 15%
where the time goes in v12:
time: 38 us; the launch traced here: 37.7 us
  Pallas kernels  15.9 us (42%)
  starting transfers between devices  8.02 us (21%)
  waiting for transfers between devices  5.44 us (14%)
  local copies, waits for them, and re-layouts  4.34 us (11%)
  other arithmetic  3.2 us (8%)
  between operations  0.7 us (2%)
    ppermute x4, starting transfers between devices, shifted(): lax.ppermute(value, axis, [(i, (i + by) % peers) for i in range(peers)])  7.44 us
    pallas_call x2, Pallas kernels, rate_part(): pl.pallas_call(functools.partial(step2_rate_kernel, mesh_peers, first), o...  5.66 us
    pallas_call x1, Pallas kernels, on_device(): pl.pallas_call(functools.partial(first_kernel, mesh_peers), out_shape=(ja...  5.02 us
    ppermute x4, waiting for transfers between devices, shifted(): lax.ppermute(value, axis, [(i, (i + by) % peers) for i in range(peers)])  4.55 us
    pallas_call x1, Pallas kernels, on_device(): pl.pallas_call(functools.partial(second_kernel, mesh_peers, force_scale),...  3.49 us
    unnamed x10, local copies, waits for them, and re-layouts  1.93 us
    pallas_call x1, Pallas kernels, on_device(): pl.pallas_call(functools.partial(pick_kernel, passages), out_shape=(row_s...  1.78 us
    add x2, other arithmetic, on_device(): totals + lax.ppermute(totals, 'mesh', [(i, i ^ step) for i in range(peers)])  1.24 us
  transfers between devices with their start and end apart: 6, of which 4 were waited for; matrix products, arithmetic and copies ran while one was open for 4% of the time, Pallas kernels for 15%

profile of v12, /device:TPU:0, one launch (start us, length us, event | category | flops | bytes accessed | tf_op | source)
XLA Modules:
  0.0 37.7 jit_solution(6672347472967168954)
XLA Ops:
  0.6 0.0 copy-start.1
  0.6 1.8 %shard_map.130 = (f32[2,5,256]{2,1,0:T(8,128)}, f32[2,5,256]{2,1,0:T(8,128)}) custom-call(s32[8]{0:T(128)} %lower_slot_ref.1, s32[8]{0:T(128)} %upper_slot_ref.1, f32[5,64,256]{2,1,0:T(8,128)} %bitcast.38, f32[5,64,256]{2,1,0:T(8,128)} %bitcast.39), custom_call_target="tpu_custom_call" | custom-call | tf_op jit(solution)/shard_map/pallas_call | solution.py:462
  2.4 0.5 %collective-permute-start = (f32[2,5,256]{2,1,0:T(8,128)}, f32[2,5,256]{2,1,0:T(8,128)S(1)}, u32[]{:S(2)}, u32[]{:S(2)}) collective-permute-start(f32[2,5,256]{2,1,0:T(8,128)} %get-tuple-element.12), channel_id=1, source_target_pairs={{0,4},{4,8},{8,12},{12,16},{16,20},{20,24},{24,28},{28,0},{1,5},{5... | collective-permute-start | bytes 30728 | tf_op jit(solution)/shard_map/ppermute | solution.py:23
  2.9 4.0 %collective-permute-start.1 = (f32[2,5,256]{2,1,0:T(8,128)}, f32[2,5,256]{2,1,0:T(8,128)S(1)}, u32[]{:S(2)}, u32[]{:S(2)}) collective-permute-start(f32[2,5,256]{2,1,0:T(8,128)} %get-tuple-element.13), channel_id=1, source_target_pairs={{0,28},{4,0},{8,4},{12,8},{16,12},{20,16},{24,20},{28,24},{1,29},{... | collective-permute-start | bytes 30728 | tf_op jit(solution)/shard_map/ppermute | solution.py:23
  6.9 0.0 copy-done.1
  6.9 0.0 copy-start
  6.9 0.1 fusion
  7.0 0.9 %copy-done = f32[4,96,256]{2,1,0:T(8,128)S(1)} copy-done((f32[4,96,256]{2,1,0:T(8,128)S(1)}, f32[4,96,256]{2,1,0:T(8,128)}, u32[]{:S(2)}) %copy-start) | copy-done | bytes 393240
  7.9 0.1 fusion.1
  8.0 0.1 copy.25
  8.1 0.1 copy.30
  8.2 0.1 copy.24
  8.4 0.1 copy.29
  8.5 0.1 pad.1.clone
  8.6 0.0 collective-permute-done.glo_ref.refs_2_.refs_3_
  8.6 0.0 copy-start.2
  8.6 0.1 slice_bitcast_fusion.3
  8.7 0.5 %copy-done.2 = f32[2,5,256]{2,1,0:T(8,128)} copy-done((f32[2,5,256]{2,1,0:T(8,128)}, f32[2,5,256]{2,1,0:T(8,128)S(1)}, u32[]{:S(2)}) %copy-start.2) | copy-done | bytes 10264
  9.2 0.1 copy.22
  9.3 0.1 reshape.46
  9.4 0.1 copy.27
  9.5 0.1 reshape.51
  9.6 0.0 collective-permute-done.1.gup_ref.refs_3_.refs_4_
  9.6 0.0 copy-start.3
  9.6 0.1 slice_bitcast_fusion.2
  9.6 0.5 %copy-done.3 = f32[2,5,256]{2,1,0:T(8,128)} copy-done((f32[2,5,256]{2,1,0:T(8,128)}, f32[2,5,256]{2,1,0:T(8,128)S(1)}, u32[]{:S(2)}) %copy-start.3) | copy-done | bytes 10264
  10.2 0.1 copy.23
  10.3 0.1 reshape.47
  10.3 0.1 copy.28
  10.4 0.1 reshape.52
  10.5 0.1 pad_maximum_fusion.1
  10.6 0.1 reshape.48
  10.7 2.9 %collective-permute-start.2 = (f32[3536]{0:T(1024)S(1)}, f32[3536]{0:T(1024)S(1)}, u32[]{:S(2)}, u32[]{:S(2)}) collective-permute-start(f32[3536]{0:T(1024)S(1)} %reshape.48), channel_id=1, source_target_pairs={{0,3},{1,0},{2,1},{3,2},{4,7},{5,4},{6,5},{7,6},{8,11},{9,8},{10,9... | collective-permute-start | bytes 42440 | tf_op jit(solution)/shard_map/ppermute | solution.py:23
  13.6 0.1 pad_maximum_fusion.2
  13.7 0.1 reshape.53
  13.8 0.0 collective-permute-start.3
  13.8 1.3 %collective-permute-done.2 = f32[3536]{0:T(1024)S(1)} collective-permute-done((f32[3536]{0:T(1024)S(1)}, f32[3536]{0:T(1024)S(1)}, u32[]{:S(2)}, u32[]{:S(2)}) %collective-permute-start.2) | collective-permute-done | bytes 14176 | tf_op jit(solution)/shard_map/ppermute | solution.py:23
  15.1 0.1 select_n.22
  15.2 3.3 %collective-permute-done.3 = f32[3536]{0:T(1024)S(1)} collective-permute-done((f32[3536]{0:T(1024)S(1)}, f32[3536]{0:T(1024)S(1)}, u32[]{:S(2)}, u32[]{:S(2)}) %collective-permute-start.3) | collective-permute-done | bytes 14176 | tf_op jit(solution)/shard_map/ppermute | solution.py:23
  18.4 0.1 select_n.25
  18.5 0.2 copy.31
  18.7 0.2 copy.26
  19.0 1.0 %pad_maximum_fusion.halo_ref.refs_4_.refs_5_ = f32[884,128]{1,0:T(8,128)} fusion(f32[884,4]{1,0:T(8,128)S(1)} %bitcast.32, f32[884,4]{1,0:T(8,128)S(1)} %bitcast.33, f32[128]{0:T(128)S(1)} %pad.1.clone), kind=kLoop, calls=%fused_computation | loop fusion | flops 226304 | bytes 481408 | tf_op jit(solution)/shard_map/concatenate | solution.py:486
  19.9 5.0 %shard_map.131 = (f32[5,96,384]{2,1,0:T(8,128)}, f32[32,128]{1,0:T(8,128)}) custom-call(f32[5,5]{1,0:T(8,128)} %ax_ref.7, f32[5,5]{1,0:T(8,128)} %pt_ref.7, f32[1,4]{1,0:T(1,128)} %vel_ref.3, f32[5,96,256]{2,1,0:T(8,128)} %bitcast.30, f32[4,96,256]{2,1,0:T(8,128)} %ms_ref.3, f32[2,5,256]{2,1,0:T(8,128)} %copy-done.2, f32[2,5,256]{2,1,0:T(8,128)} %copy-done.3, ...), custom_call_target="tpu_custom_call" | custom-call | tf_op jit(solution)/shard_map/pallas_call | solution.py:490
  25.0 0.8 %reduce_sum.9 = f32[32]{0:T(128)S(1)} reduce(f32[32,128]{1,0:T(8,128)} %get-tuple-element.14, f32[]{:T(128)} %constant.6.clone.1), dimensions={1}, to_apply=%region_0.1 | reduce | flops 4064 | bytes 16516 | tf_op jit(solution)/shard_map/reduce_sum | solution.py:511
  25.8 0.1 collective-permute-start.4
  25.9 2.7 %shard_map.132.ra_low_ref = f32[2,96,384]{2,1,0:T(8,128)} custom-call(f32[5,5]{1,0:T(8,128)} %ax_ref.7, f32[5,5]{1,0:T(8,128)} %pt_ref.7, f32[5,96,384]{2,1,0:T(8,128)} %get-tuple-element.15.refs_0_.refs_1_.a_ref, f32[4,96,256]{2,1,0:T(8,128)} %ms_ref.3, f32[2,5,256]{2,1,0:T(8,128)} %copy-done.2, f32[2,5,256]{2,1,0:T(8,128)} %copy-done.3, ...), custom_call_target="tpu_custom_call" | custom-call | tf_op jit(solution)/shard_map/pallas_call | solution.py:503
  28.6 0.8 %collective-permute-done.4 = f32[32]{0:T(128)S(1)} collective-permute-done((f32[32]{0:T(128)S(1)}, f32[32]{0:T(128)S(1)}, u32[]{:S(2)}, u32[]{:S(2)}) %collective-permute-start.4) | collective-permute-done | bytes 160 | tf_op jit(solution)/shard_map/ppermute | solution.py:519
  29.4 0.0 copy-start.4
  29.4 0.5 %collective-permute-start.5 = (f32[32]{0:T(128)S(1)}, f32[32]{0:T(128)S(1)}, u32[]{:S(2)}, u32[]{:S(2)}) collective-permute-start(f32[32]{0:T(128)S(1)} %add.6.refs_0_), channel_id=1, source_target_pairs={{0,2},{1,3},{2,0},{3,1},{4,6},{5,7},{6,4},{7,5},{8,10},{9,11},{10,... | collective-permute-start | bytes 392 | tf_op jit(solution)/shard_map/ppermute | solution.py:519
  29.9 0.0 copy-done.4
  29.9 3.0 %shard_map.133.ra_high_ref = f32[3,96,384]{2,1,0:T(8,128)} custom-call(f32[5,5]{1,0:T(8,128)} %ax_ref.7, f32[5,5]{1,0:T(8,128)} %pt_ref.7, f32[32]{0:T(128)} %copy-done.4, f32[5,96,384]{2,1,0:T(8,128)} %get-tuple-element.15.refs_0_.refs_1_.a_ref, f32[4,96,256]{2,1,0:T(8,128)} %ms_ref.3, f32[2,5,256]{2,1,0:T(8,128)} %copy-done.2, f32[2,5,256]{2,1,0:T(8,128)} %copy-done.3, ...), custom_call_target="tpu_custom_call" | custom-call | tf_op jit(solution)/shard_map/pallas_call | solution.py:503
  32.9 0.1 collective-permute-done.5
  32.9 1.2 %add.7.tot_ref = f32[32]{0:T(128)} add(f32[32]{0:T(128)} %copy-done.4, f32[32]{0:T(128)S(1)} %collective-permute-done.5) | non-fusion elementwise | flops 32 | bytes 384 | tf_op jit(solution)/shard_map/add | solution.py:519
  34.2 3.5 %shard_map.134 = (f32[5,96,256]{2,1,0:T(8,128)}, f32[1,4]{1,0:T(1,128)}, f32[1,4]{1,0:T(1,128)}) custom-call(f32[32]{0:T(128)} %add.7.tot_ref, f32[1,4]{1,0:T(1,128)} %stiff_ref.1, f32[1,4]{1,0:T(1,128)} %disp_ref.1, f32[1,4]{1,0:T(1,128)} %vel_ref.3, f32[5,5]{1,0:T(8,128)} %ax_ref.7, f32[5,5]{1,0:T(8,128)} %pt_ref.7, ...), custom_call_target="tpu_custom_call" | custom-call | tf_op jit(solution)/shard_map/pallas_call | solution.py:526
  (4 shorter events, 0.0 us)
Async XLA Ops:
  0.6 6.3 %copy-start.1 = (f32[1,5,96,256]{3,2,1,0:T(8,128)S(1)}, f32[1,5,96,256]{3,2,1,0:T(8,128)}, u32[]{:S(2)}) copy-start(f32[1,5,96,256]{3,2,1,0:T(8,128)} %param.11) | copy-start | bytes 1474564
  2.4 6.2 %collective-permute-start = (f32[2,5,256]{2,1,0:T(8,128)}, f32[2,5,256]{2,1,0:T(8,128)S(1)}, u32[]{:S(2)}, u32[]{:S(2)}) collective-permute-start(f32[2,5,256]{2,1,0:T(8,128)} %get-tuple-element.12), channel_id=1, source_target_pairs={{0,4},{4,8},{8,12},{12,16},{16,20},{20,24},{24,28},{28,0},{1,5},{5... | collective-permute-start | bytes 30728 | tf_op jit(solution)/shard_map/ppermute | solution.py:23
  2.9 6.7 %collective-permute-start.1 = (f32[2,5,256]{2,1,0:T(8,128)}, f32[2,5,256]{2,1,0:T(8,128)S(1)}, u32[]{:S(2)}, u32[]{:S(2)}) collective-permute-start(f32[2,5,256]{2,1,0:T(8,128)} %get-tuple-element.13), channel_id=1, source_target_pairs={{0,28},{4,0},{8,4},{12,8},{16,12},{20,16},{24,20},{28,24},{1,29},{... | collective-permute-start | bytes 30728 | tf_op jit(solution)/shard_map/ppermute | solution.py:23
  6.9 1.0 %copy-start = (f32[4,96,256]{2,1,0:T(8,128)S(1)}, f32[4,96,256]{2,1,0:T(8,128)}, u32[]{:S(2)}) copy-start(f32[4,96,256]{2,1,0:T(8,128)} %ms_ref.3) | copy-start | bytes 1179652
  8.6 0.6 %copy-start.2 = (f32[2,5,256]{2,1,0:T(8,128)}, f32[2,5,256]{2,1,0:T(8,128)S(1)}, u32[]{:S(2)}) copy-start(f32[2,5,256]{2,1,0:T(8,128)S(1)} %collective-permute-done.glo_ref.refs_2_.refs_3_) | copy-start | bytes 30724
  9.6 0.6 %copy-start.3 = (f32[2,5,256]{2,1,0:T(8,128)}, f32[2,5,256]{2,1,0:T(8,128)S(1)}, u32[]{:S(2)}) copy-start(f32[2,5,256]{2,1,0:T(8,128)S(1)} %collective-permute-done.1.gup_ref.refs_3_.refs_4_) | copy-start | bytes 30724
  10.7 4.4 %collective-permute-start.2 = (f32[3536]{0:T(1024)S(1)}, f32[3536]{0:T(1024)S(1)}, u32[]{:S(2)}, u32[]{:S(2)}) collective-permute-start(f32[3536]{0:T(1024)S(1)} %reshape.48), channel_id=1, source_target_pairs={{0,3},{1,0},{2,1},{3,2},{4,7},{5,4},{6,5},{7,6},{8,11},{9,8},{10,9... | collective-permute-start | bytes 42440 | tf_op jit(solution)/shard_map/ppermute | solution.py:23
  13.8 4.6 %collective-permute-start.3 = (f32[3536]{0:T(1024)S(1)}, f32[3536]{0:T(1024)S(1)}, u32[]{:S(2)}, u32[]{:S(2)}) collective-permute-start(f32[3536]{0:T(1024)S(1)} %reshape.53), channel_id=1, source_target_pairs={{0,1},{1,2},{2,3},{3,0},{4,5},{5,6},{6,7},{7,4},{8,9},{9,10},{10,1... | collective-permute-start | bytes 42440 | tf_op jit(solution)/shard_map/ppermute | solution.py:23
  25.8 3.6 %collective-permute-start.4 = (f32[32]{0:T(128)S(1)}, f32[32]{0:T(128)S(1)}, u32[]{:S(2)}, u32[]{:S(2)}) collective-permute-start(f32[32]{0:T(128)S(1)} %reduce_sum.9), channel_id=1, source_target_pairs={{0,1},{1,0},{2,3},{3,2},{4,5},{5,4},{6,7},{7,6},{8,9},{9,8},{10,11... | collective-permute-start | bytes 392 | tf_op jit(solution)/shard_map/ppermute | solution.py:519
  29.4 0.5 %copy-start.4 = (f32[32]{0:T(128)}, f32[32]{0:T(128)S(1)}, u32[]{:S(2)}) copy-start(f32[32]{0:T(128)S(1)} %add.6.refs_0_) | copy-start | bytes 388
  29.4 3.5 %collective-permute-start.5 = (f32[32]{0:T(128)S(1)}, f32[32]{0:T(128)S(1)}, u32[]{:S(2)}, u32[]{:S(2)}) collective-permute-start(f32[32]{0:T(128)S(1)} %add.6.refs_0_), channel_id=1, source_target_pairs={{0,2},{1,3},{2,0},{3,1},{4,6},{5,7},{6,4},{7,5},{8,10},{9,11},{10,... | collective-permute-start | bytes 392 | tf_op jit(solution)/shard_map/ppermute | solution.py:519

commit v13 on v11

--- a/solution.py
+++ b/solution.py
@@ -222,7 +222,13 @@
 
 
 def widened(own, tile):
-    return jnp.concatenate([own, tile], axis=-1)
+    return jnp.concatenate([own, lane_roll(tile, -2 * STEP_COUNT)], axis=-1)
+
+
+def unfold_halo(halo_ref, columns_ref):
+    block = halo_ref[...]
+    spare = jnp.zeros((LANES - block.shape[0], block.shape[1]), block.dtype)
+    columns_ref[...] = jnp.concatenate([block, spare], axis=0).T
 
 
 def lane_masks(peers, shape, own_width):
@@ -260,8 +266,9 @@
     return u, ms, ghosts[0], ghosts[1]
 
 
-def first_kernel(peers, ax_ref, pt_ref, vel_ref, u_ref, ms_ref, glo_ref, gup_ref, halo_ref, a_ref, part_ref):
+def first_kernel(peers, ax_ref, pt_ref, vel_ref, u_ref, ms_ref, glo_ref, gup_ref, packed_ref, a_ref, part_ref, halo_ref):
     h = TIME_STEP
+    unfold_halo(packed_ref, halo_ref)
     fields = u_ref.shape[0]
     modes = ms_ref.shape[0]
     pitch = u_ref.shape[1]
@@ -339,7 +346,8 @@
     return coef, disp2, vel2
 
 
-def step2_rate_kernel(peers, ax_ref, pt_ref, a_ref, ms_ref, glo_ref, gup_ref, halo_ref, ra_ref):
+def step2_rate_kernel(peers, ax_ref, pt_ref, a_ref, ms_ref, glo_ref, gup_ref, packed_ref, ra_ref, halo_ref):
+    unfold_halo(packed_ref, halo_ref)
     fields = a_ref.shape[0]
     modes = ms_ref.shape[0]
     pitch = ms_ref.shape[1]
@@ -367,12 +375,14 @@
     ms_ref,
     glo_ref,
     gup_ref,
-    halo_ref,
+    packed_ref,
     out_ref,
     disp_out_ref,
     vel_out_ref,
+    halo_ref,
 ):
     h = TIME_STEP
+    unfold_halo(packed_ref, halo_ref)
     fields = a_ref.shape[0]
     modes = ms_ref.shape[0]
     pitch = ms_ref.shape[1]
@@ -477,8 +487,12 @@
     from_right = from_right.reshape(reach, -1)
     from_left = jnp.where(me > 0, from_left, jnp.zeros_like(from_left))
     from_right = jnp.where(me < mesh_peers - 1, from_right, jnp.zeros_like(from_right))
-    gap = jnp.zeros((from_left.shape[1], LANES - 2 * reach), from_left.dtype)
-    halo_tile = jnp.concatenate([from_right.T, gap, from_left.T], axis=1)
+    packed_rows = from_left.shape[1]
+    padded_rows = -(-packed_rows // LANES) * LANES
+    halo_tile = jnp.pad(
+        jnp.concatenate([from_left, from_right], axis=0), [(0, 0), (0, padded_rows - packed_rows)]
+    )
+    columns = [pltpu.VMEM((padded_rows, LANES), state0.dtype)]
     lanes_wide = axial_cells + LANES
     ins = (state0, mode_shape, lower_ghosts, upper_ghosts, halo_tile)
 
@@ -490,6 +504,7 @@
         ),
         in_specs=[smem_spec()] * 3 + [vmem_spec()] * 5,
         out_specs=(vmem_spec(), vmem_spec()),
+        scratch_shapes=columns,
     )(axial_jacobian, pitch_jacobian, velocity, *ins)
 
     totals = mesh_sum(jnp.sum(part_lanes, axis=1))
@@ -499,6 +514,7 @@
         out_shape=jax.ShapeDtypeStruct(base1.shape, base1.dtype),
         in_specs=[smem_spec()] * 2 + [vmem_spec()] * 5,
         out_specs=vmem_spec(),
+        scratch_shapes=columns,
     )(axial_jacobian, pitch_jacobian, base1, *ins[1:])
 
     small = jax.ShapeDtypeStruct(displacement.shape, displacement.dtype)
@@ -507,6 +523,7 @@
         out_shape=(jax.ShapeDtypeStruct(state0.shape, state0.dtype), small, small),
         in_specs=[smem_spec()] * 6 + [vmem_spec()] * 6,
         out_specs=(vmem_spec(), smem_spec(), smem_spec()),
+        scratch_shapes=columns,
     )(totals, stiffness, displacement, velocity, axial_jacobian, pitch_jacobian, base1, rate_a, *ins[1:])
     return (state2[None], disp2, vel2)
 

time: 37.6 us -> 36 us (0.957)
  waiting for transfers between devices: 8.08 us -> 4.26 us
  starting transfers between devices: 8.02 us -> 11.1 us
  local copies, waits for them, and re-layouts: 4.34 us -> 3.83 us
    ppermute x2, starting transfers between devices: 0.57 us -> 3.6 us  [mesh_sum(): lax.ppermute(value, 'mesh', [(i, i ^ step) for i in range(peers)])]
    ppermute x2, waiting for transfers between devices: 3.53 us -> 1.52 us  [mesh_sum(): lax.ppermute(value, 'mesh', [(i, i ^ step) for i in range(peers)])]
    ppermute x4, waiting for transfers between devices: 4.55 us -> 2.74 us  [shifted(): lax.ppermute(value, axis, [(i, (i + by) % peers) for i in range(peers)])]
where the time goes in v13:
time: 36 us; the launch traced here: 35.7 us
  Pallas kernels  13.7 us (38%)
  starting transfers between devices  11.1 us (31%)
  waiting for transfers between devices  4.26 us (12%)
  local copies, waits for them, and re-layouts  3.83 us (11%)
  other arithmetic  2.16 us (6%)
  between operations  0.68 us (2%)
    ppermute x4, starting transfers between devices, shifted(): lax.ppermute(value, axis, [(i, (i + by) % peers) for i in range(peers)])  7.46 us
    pallas_call x1, Pallas kernels, on_device(): pl.pallas_call(functools.partial(first_kernel, mesh_peers), out_shape=(ja...  5.11 us
    ppermute x2, starting transfers between devices, mesh_sum(): lax.ppermute(value, 'mesh', [(i, i ^ step) for i in range(peers)])  3.6 us
    pallas_call x1, Pallas kernels, on_device(): pl.pallas_call(functools.partial(second_kernel, mesh_peers, force_scale),...  3.5 us
    pallas_call x1, Pallas kernels, on_device(): pl.pallas_call(functools.partial(step2_rate_kernel, mesh_peers), out_shap...  3.34 us
    ppermute x4, waiting for transfers between devices, shifted(): lax.ppermute(value, axis, [(i, (i + by) % peers) for i in range(peers)])  2.74 us
    unnamed x8, local copies, waits for them, and re-layouts  1.92 us
    pallas_call x1, Pallas kernels, on_device(): pl.pallas_call(functools.partial(pick_kernel, passages), out_shape=(row_s...  1.78 us
  transfers between devices with their start and end apart: 6, of which 3 were waited for; matrix products, arithmetic and copies ran while one was open for 4% of the time, Pallas kernels for 9%

profile of v13, /device:TPU:0, one launch (start us, length us, event | category | flops | bytes accessed | tf_op | source)
XLA Modules:
  0.0 35.7 jit_solution(11869534607876196756)
XLA Ops:
  0.6 0.0 copy-start.1
  0.6 1.8 %shard_map.130 = (f32[2,5,256]{2,1,0:T(8,128)}, f32[2,5,256]{2,1,0:T(8,128)}) custom-call(s32[8]{0:T(128)} %lower_slot_ref.1, s32[8]{0:T(128)} %upper_slot_ref.1, f32[5,64,256]{2,1,0:T(8,128)} %bitcast.34, f32[5,64,256]{2,1,0:T(8,128)} %bitcast.35), custom_call_target="tpu_custom_call" | custom-call | tf_op jit(solution)/shard_map/pallas_call | solution.py:467
  2.4 0.5 %collective-permute-start = (f32[2,5,256]{2,1,0:T(8,128)}, f32[2,5,256]{2,1,0:T(8,128)S(1)}, u32[]{:S(2)}, u32[]{:S(2)}) collective-permute-start(f32[2,5,256]{2,1,0:T(8,128)} %get-tuple-element.10), channel_id=1, source_target_pairs={{0,4},{4,8},{8,12},{12,16},{16,20},{20,24},{24,28},{28,0},{1,5},{5... | collective-permute-start | bytes 30728 | tf_op jit(solution)/shard_map/ppermute | solution.py:23
  2.9 4.0 %collective-permute-start.1 = (f32[2,5,256]{2,1,0:T(8,128)}, f32[2,5,256]{2,1,0:T(8,128)S(1)}, u32[]{:S(2)}, u32[]{:S(2)}) collective-permute-start(f32[2,5,256]{2,1,0:T(8,128)} %get-tuple-element.11), channel_id=1, source_target_pairs={{0,28},{4,0},{8,4},{12,8},{16,12},{20,16},{24,20},{28,24},{1,29},{... | collective-permute-start | bytes 30728 | tf_op jit(solution)/shard_map/ppermute | solution.py:23
  6.9 0.0 copy-done.1
  6.9 0.0 copy-start
  6.9 0.1 fusion
  7.0 0.9 %copy-done = f32[4,96,256]{2,1,0:T(8,128)S(1)} copy-done((f32[4,96,256]{2,1,0:T(8,128)S(1)}, f32[4,96,256]{2,1,0:T(8,128)}, u32[]{:S(2)}) %copy-start) | copy-done | bytes 393240
  7.9 0.1 fusion.1
  8.0 0.1 copy.25
  8.1 0.1 copy.29
  8.2 0.1 copy.24
  8.4 0.1 copy.28
  8.5 0.0 collective-permute-done.glo_ref
  8.5 0.0 copy-start.2
  8.5 0.1 slice_bitcast_fusion.3
  8.6 0.5 %copy-done.2 = f32[2,5,256]{2,1,0:T(8,128)} copy-done((f32[2,5,256]{2,1,0:T(8,128)}, f32[2,5,256]{2,1,0:T(8,128)S(1)}, u32[]{:S(2)}) %copy-start.2) | copy-done | bytes 10264
  9.1 0.1 copy.22
  9.2 0.1 reshape.46
  9.3 0.1 copy.26
  9.4 0.1 reshape.51
  9.5 0.0 collective-permute-done.1.gup_ref
  9.5 0.0 copy-start.3
  9.5 0.1 slice_bitcast_fusion.2
  9.6 0.5 %copy-done.3 = f32[2,5,256]{2,1,0:T(8,128)} copy-done((f32[2,5,256]{2,1,0:T(8,128)}, f32[2,5,256]{2,1,0:T(8,128)S(1)}, u32[]{:S(2)}) %copy-start.3) | copy-done | bytes 10264
  10.1 0.1 copy.23
  10.2 0.1 reshape.47
  10.3 0.1 copy.27
  10.4 0.1 reshape.52
  10.5 0.1 pad_maximum_fusion
  10.6 0.1 reshape.48
  10.6 2.0 %collective-permute-start.2 = (f32[3536]{0:T(1024)S(1)}, f32[3536]{0:T(1024)S(1)}, u32[]{:S(2)}, u32[]{:S(2)}) collective-permute-start(f32[3536]{0:T(1024)S(1)} %reshape.48), channel_id=1, source_target_pairs={{0,1},{1,2},{2,3},{3,0},{4,5},{5,6},{6,7},{7,4},{8,9},{9,10},{10,1... | collective-permute-start | bytes 42440 | tf_op jit(solution)/shard_map/ppermute | solution.py:23
  12.6 0.1 pad_maximum_fusion.1
  12.7 0.1 reshape.53
  12.8 1.0 %collective-permute-start.3 = (f32[3536]{0:T(1024)S(1)}, f32[3536]{0:T(1024)S(1)}, u32[]{:S(2)}, u32[]{:S(2)}) collective-permute-start(f32[3536]{0:T(1024)S(1)} %reshape.53), channel_id=1, source_target_pairs={{0,3},{1,0},{2,1},{3,2},{4,7},{5,4},{6,5},{7,6},{8,11},{9,8},{10,9... | collective-permute-start | bytes 42440 | tf_op jit(solution)/shard_map/ppermute | solution.py:23
  13.8 1.6 %collective-permute-done.2 = f32[3536]{0:T(1024)S(1)} collective-permute-done((f32[3536]{0:T(1024)S(1)}, f32[3536]{0:T(1024)S(1)}, u32[]{:S(2)}, u32[]{:S(2)}) %collective-permute-start.2) | collective-permute-done | bytes 14176 | tf_op jit(solution)/shard_map/ppermute | solution.py:23
  15.4 0.1 select_n.22
  15.5 1.0 %collective-permute-done.3 = f32[3536]{0:T(1024)S(1)} collective-permute-done((f32[3536]{0:T(1024)S(1)}, f32[3536]{0:T(1024)S(1)}, u32[]{:S(2)}, u32[]{:S(2)}) %collective-permute-start.3) | collective-permute-done | bytes 14176 | tf_op jit(solution)/shard_map/ppermute | solution.py:23
  16.5 0.1 select_n.25
  16.6 0.6 %select_maximum_fusion.packed_ref = f32[8,896]{1,0:T(8,128)} fusion(f32[4,884]{1,0:T(4,128)S(1)} %select_n.25, f32[4,884]{1,0:T(4,128)S(1)} %select_n.22), kind=kLoop, calls=%fused_computation | loop fusion | flops 28672 | bytes 56960 | tf_op jit(solution)/shard_map/concatenate | solution.py:493
  17.3 5.1 %shard_map.131 = (f32[5,96,384]{2,1,0:T(8,128)}, f32[32,128]{1,0:T(8,128)}) custom-call(f32[5,5]{1,0:T(8,128)} %ax_ref.5, f32[5,5]{1,0:T(8,128)} %pt_ref.5, f32[1,4]{1,0:T(1,128)} %vel_ref.3, f32[5,96,256]{2,1,0:T(8,128)} %bitcast.28, f32[4,96,256]{2,1,0:T(8,128)} %ms_ref.5, f32[2,5,256]{2,1,0:T(8,128)} %copy-done.2, f32[2,5,256]{2,1,0:T(8,128)} %copy-done.3, ...), custom_call_target="tpu_custom_call" | custom-call | tf_op jit(solution)/shard_map/pallas_call | solution.py:499
  22.4 0.8 %reduce_sum.9 = f32[32]{0:T(128)S(1)} reduce(f32[32,128]{1,0:T(8,128)} %get-tuple-element.12, f32[]{:T(128)} %constant.2.clone.1), dimensions={1}, to_apply=%region_0.1 | reduce | flops 4064 | bytes 16516 | tf_op jit(solution)/shard_map/reduce_sum | solution.py:510
  23.2 2.5 %collective-permute-start.4 = (f32[32]{0:T(128)S(1)}, f32[32]{0:T(128)S(1)}, u32[]{:S(2)}, u32[]{:S(2)}) collective-permute-start(f32[32]{0:T(128)S(1)} %reduce_sum.9), channel_id=1, source_target_pairs={{0,1},{1,0},{2,3},{3,2},{4,5},{5,4},{6,7},{7,6},{8,9},{9,8},{10,11... | collective-permute-start | bytes 392 | tf_op jit(solution)/shard_map/ppermute | solution.py:42
  25.6 1.5 %collective-permute-done.4 = f32[32]{0:T(128)S(1)} collective-permute-done((f32[32]{0:T(128)S(1)}, f32[32]{0:T(128)S(1)}, u32[]{:S(2)}, u32[]{:S(2)}) %collective-permute-start.4) | collective-permute-done | bytes 160 | tf_op jit(solution)/shard_map/ppermute | solution.py:42
  27.2 1.1 %collective-permute-start.5 = (f32[32]{0:T(128)S(1)}, f32[32]{0:T(128)S(1)}, u32[]{:S(2)}, u32[]{:S(2)}) collective-permute-start(f32[32]{0:T(128)S(1)} %add.8), channel_id=1, source_target_pairs={{0,2},{1,3},{2,0},{3,1},{4,6},{5,7},{6,4},{7,5},{8,10},{9,11},{10,... | collective-permute-start | bytes 392 | tf_op jit(solution)/shard_map/ppermute | solution.py:42
  28.3 3.3 %shard_map.132.ra_ref = f32[5,96,384]{2,1,0:T(8,128)} custom-call(f32[5,5]{1,0:T(8,128)} %ax_ref.5, f32[5,5]{1,0:T(8,128)} %pt_ref.5, f32[5,96,384]{2,1,0:T(8,128)} %get-tuple-element.13.a_ref, f32[4,96,256]{2,1,0:T(8,128)} %ms_ref.5, f32[2,5,256]{2,1,0:T(8,128)} %copy-done.2, f32[2,5,256]{2,1,0:T(8,128)} %copy-done.3, f32[8,896]{1,0:T(8,128)} %select_maximum_fusion.packed_ref), custom_call_target="tpu_custom_call" | custom-call | tf_op jit(solution)/shard_map/pallas_call | solution.py:512
  31.7 0.0 collective-permute-done.5
  31.7 0.5 %add.9.tot_ref = f32[32]{0:T(128)} add(f32[32]{0:T(128)S(1)} %add.8, f32[32]{0:T(128)S(1)} %collective-permute-done.5) | non-fusion elementwise | flops 32 | bytes 384 | tf_op jit(solution)/shard_map/add | solution.py:42
  32.2 3.5 %shard_map.133 = (f32[5,96,256]{2,1,0:T(8,128)}, f32[1,4]{1,0:T(1,128)}, f32[1,4]{1,0:T(1,128)}) custom-call(f32[32]{0:T(128)} %add.9.tot_ref, f32[1,4]{1,0:T(1,128)} %stiff_ref.1, f32[1,4]{1,0:T(1,128)} %disp_ref.1, f32[1,4]{1,0:T(1,128)} %vel_ref.3, f32[5,5]{1,0:T(8,128)} %ax_ref.5, f32[5,5]{1,0:T(8,128)} %pt_ref.5, ...), custom_call_target="tpu_custom_call" | custom-call | tf_op jit(solution)/shard_map/pallas_call | solution.py:521
  (3 shorter events, 0.0 us)
Async XLA Ops:
  0.6 6.3 %copy-start.1 = (f32[1,5,96,256]{3,2,1,0:T(8,128)S(1)}, f32[1,5,96,256]{3,2,1,0:T(8,128)}, u32[]{:S(2)}) copy-start(f32[1,5,96,256]{3,2,1,0:T(8,128)} %param.11) | copy-start | bytes 1474564
  2.4 6.1 %collective-permute-start = (f32[2,5,256]{2,1,0:T(8,128)}, f32[2,5,256]{2,1,0:T(8,128)S(1)}, u32[]{:S(2)}, u32[]{:S(2)}) collective-permute-start(f32[2,5,256]{2,1,0:T(8,128)} %get-tuple-element.10), channel_id=1, source_target_pairs={{0,4},{4,8},{8,12},{12,16},{16,20},{20,24},{24,28},{28,0},{1,5},{5... | collective-permute-start | bytes 30728 | tf_op jit(solution)/shard_map/ppermute | solution.py:23
  2.9 6.6 %collective-permute-start.1 = (f32[2,5,256]{2,1,0:T(8,128)}, f32[2,5,256]{2,1,0:T(8,128)S(1)}, u32[]{:S(2)}, u32[]{:S(2)}) collective-permute-start(f32[2,5,256]{2,1,0:T(8,128)} %get-tuple-element.11), channel_id=1, source_target_pairs={{0,28},{4,0},{8,4},{12,8},{16,12},{20,16},{24,20},{28,24},{1,29},{... | collective-permute-start | bytes 30728 | tf_op jit(solution)/shard_map/ppermute | solution.py:23
  6.9 1.0 %copy-start = (f32[4,96,256]{2,1,0:T(8,128)S(1)}, f32[4,96,256]{2,1,0:T(8,128)}, u32[]{:S(2)}) copy-start(f32[4,96,256]{2,1,0:T(8,128)} %ms_ref.5) | copy-start | bytes 1179652
  8.5 0.6 %copy-start.2 = (f32[2,5,256]{2,1,0:T(8,128)}, f32[2,5,256]{2,1,0:T(8,128)S(1)}, u32[]{:S(2)}) copy-start(f32[2,5,256]{2,1,0:T(8,128)S(1)} %collective-permute-done.glo_ref) | copy-start | bytes 30724
  9.5 0.6 %copy-start.3 = (f32[2,5,256]{2,1,0:T(8,128)}, f32[2,5,256]{2,1,0:T(8,128)S(1)}, u32[]{:S(2)}) copy-start(f32[2,5,256]{2,1,0:T(8,128)S(1)} %collective-permute-done.1.gup_ref) | copy-start | bytes 30724
  10.6 4.8 %collective-permute-start.2 = (f32[3536]{0:T(1024)S(1)}, f32[3536]{0:T(1024)S(1)}, u32[]{:S(2)}, u32[]{:S(2)}) collective-permute-start(f32[3536]{0:T(1024)S(1)} %reshape.48), channel_id=1, source_target_pairs={{0,1},{1,2},{2,3},{3,0},{4,5},{5,6},{6,7},{7,4},{8,9},{9,10},{10,1... | collective-permute-start | bytes 42440 | tf_op jit(solution)/shard_map/ppermute | solution.py:23
  12.8 3.7 %collective-permute-start.3 = (f32[3536]{0:T(1024)S(1)}, f32[3536]{0:T(1024)S(1)}, u32[]{:S(2)}, u32[]{:S(2)}) collective-permute-start(f32[3536]{0:T(1024)S(1)} %reshape.53), channel_id=1, source_target_pairs={{0,3},{1,0},{2,1},{3,2},{4,7},{5,4},{6,5},{7,6},{8,11},{9,8},{10,9... | collective-permute-start | bytes 42440 | tf_op jit(solution)/shard_map/ppermute | solution.py:23
  23.2 4.0 %collective-permute-start.4 = (f32[32]{0:T(128)S(1)}, f32[32]{0:T(128)S(1)}, u32[]{:S(2)}, u32[]{:S(2)}) collective-permute-start(f32[32]{0:T(128)S(1)} %reduce_sum.9), channel_id=1, source_target_pairs={{0,1},{1,0},{2,3},{3,2},{4,5},{5,4},{6,7},{7,6},{8,9},{9,8},{10,11... | collective-permute-start | bytes 392 | tf_op jit(solution)/shard_map/ppermute | solution.py:42
  27.2 4.5 %collective-permute-start.5 = (f32[32]{0:T(128)S(1)}, f32[32]{0:T(128)S(1)}, u32[]{:S(2)}, u32[]{:S(2)}) collective-permute-start(f32[32]{0:T(128)S(1)} %add.8), channel_id=1, source_target_pairs={{0,2},{1,3},{2,0},{3,1},{4,6},{5,7},{6,4},{7,5},{8,10},{9,11},{10,... | collective-permute-start | bytes 392 | tf_op jit(solution)/shard_map/ppermute | solution.py:42

commit v14 on v13

--- a/solution.py
+++ b/solution.py
@@ -208,17 +208,24 @@
     return total
 
 
-def pick_kernel(peers, lower_slot_ref, upper_slot_ref, upper_hist_ref, lower_hist_ref, up_ref, down_ref):
+def pick_kernel(peers, lower_slot_ref, upper_slot_ref, upper_hist_ref, lower_hist_ref, up_ref, down_ref, sems):
     fields, slots = upper_hist_ref.shape[0], upper_hist_ref.shape[1]
     position = lax.axis_index("blk")
     slot_next = lower_slot_ref[(position + 1) % peers]
     slot_prev = upper_slot_ref[(position + peers - 1) % peers]
+    copies = []
     for s in range(up_ref.shape[0]):
         up_at = (slot_next + s) % slots
         down_at = (slot_prev + s) % slots
         for f in range(fields):
-            up_ref[s, f : f + 1, :] = upper_hist_ref[f, pl.ds(up_at, 1), :]
-            down_ref[s, f : f + 1, :] = lower_hist_ref[f, pl.ds(down_at, 1), :]
+            for hist, at, out in ((upper_hist_ref, up_at, up_ref), (lower_hist_ref, down_at, down_ref)):
+                copy = pltpu.make_async_copy(
+                    hist.at[f, pl.ds(at, 1), :], out.at[s, pl.ds(f, 1), :], sems.at[len(copies)]
+                )
+                copy.start()
+                copies.append(copy)
+    for copy in copies:
+        copy.wait()
 
 
 def widened(own, tile):
@@ -433,6 +440,10 @@
     return pl.BlockSpec(memory_space=pltpu.VMEM)
 
 
+def any_spec():
+    return pl.BlockSpec(memory_space=pl.ANY)
+
+
 def smem_spec():
     return pl.BlockSpec(memory_space=pltpu.SMEM)
 
@@ -467,8 +478,9 @@
     rows_up, rows_down = pl.pallas_call(
         functools.partial(pick_kernel, passages),
         out_shape=(row_shape, row_shape),
-        in_specs=[smem_spec(), smem_spec(), vmem_spec(), vmem_spec()],
+        in_specs=[smem_spec(), smem_spec(), any_spec(), any_spec()],
         out_specs=(vmem_spec(), vmem_spec()),
+        scratch_shapes=[pltpu.SemaphoreType.DMA((2 * STEP_COUNT * upper_row_history.shape[2],))],
     )(
         lower_lag_slot,
         upper_lag_slot,

time: 36 us -> 36.8 us (1.022)
  Pallas kernels: 13.7 us -> 14.4 us
    pallas_call x1, Pallas kernels: 1.78 us -> 2.47 us  [on_device(): pl.pallas_call(functools.partial(pick_kernel, passages), out_shape=(row_s...]
where the time goes in v14:
time: 36.8 us; the launch traced here: 36.5 us
  Pallas kernels  14.4 us (39%)
  starting transfers between devices  11.1 us (30%)
  waiting for transfers between devices  4.21 us (11%)
  local copies, waits for them, and re-layouts  3.84 us (10%)
  other arithmetic  2.16 us (6%)
  between operations  0.68 us (2%)
    ppermute x4, starting transfers between devices, shifted(): lax.ppermute(value, axis, [(i, (i + by) % peers) for i in range(peers)])  7.54 us
    pallas_call x1, Pallas kernels, on_device(): pl.pallas_call(functools.partial(first_kernel, mesh_peers), out_shape=(ja...  5.11 us
    ppermute x2, starting transfers between devices, mesh_sum(): lax.ppermute(value, 'mesh', [(i, i ^ step) for i in range(peers)])  3.6 us
    pallas_call x1, Pallas kernels, on_device(): pl.pallas_call(functools.partial(second_kernel, mesh_peers, force_scale),...  3.5 us
    pallas_call x1, Pallas kernels, on_device(): pl.pallas_call(functools.partial(step2_rate_kernel, mesh_peers), out_shap...  3.34 us
    ppermute x4, waiting for transfers between devices, shifted(): lax.ppermute(value, axis, [(i, (i + by) % peers) for i in range(peers)])  2.69 us
    pallas_call x1, Pallas kernels, on_device(): pl.pallas_call(functools.partial(pick_kernel, passages), out_shape=(row_s...  2.47 us
    unnamed x8, local copies, waits for them, and re-layouts  1.93 us
  transfers between devices with their start and end apart: 6, of which 3 were waited for; matrix products, arithmetic and copies ran while one was open for 4% of the time, Pallas kernels for 9%

profile of v14, /device:TPU:0, one launch (start us, length us, event | category | flops | bytes accessed | tf_op | source)
XLA Modules:
  0.0 36.5 jit_solution(13370906620527591217)
XLA Ops:
  0.6 0.0 copy-start.1
  0.6 2.5 %shard_map.130 = (f32[2,5,256]{2,1,0:T(8,128)}, f32[2,5,256]{2,1,0:T(8,128)}) custom-call(s32[8]{0:T(128)} %lower_slot_ref.1, s32[8]{0:T(128)} %upper_slot_ref.1, f32[5,64,256]{2,1,0:T(8,128)} %bitcast.34, f32[5,64,256]{2,1,0:T(8,128)} %bitcast.35), custom_call_target="tpu_custom_call" | custom-call | tf_op jit(solution)/shard_map/pallas_call | solution.py:478
  3.1 0.5 %collective-permute-start = (f32[2,5,256]{2,1,0:T(8,128)}, f32[2,5,256]{2,1,0:T(8,128)S(1)}, u32[]{:S(2)}, u32[]{:S(2)}) collective-permute-start(f32[2,5,256]{2,1,0:T(8,128)} %get-tuple-element.10), channel_id=1, source_target_pairs={{0,4},{4,8},{8,12},{12,16},{16,20},{20,24},{24,28},{28,0},{1,5},{5... | collective-permute-start | bytes 30728 | tf_op jit(solution)/shard_map/ppermute | solution.py:23
  3.6 4.1 %collective-permute-start.1 = (f32[2,5,256]{2,1,0:T(8,128)}, f32[2,5,256]{2,1,0:T(8,128)S(1)}, u32[]{:S(2)}, u32[]{:S(2)}) collective-permute-start(f32[2,5,256]{2,1,0:T(8,128)} %get-tuple-element.11), channel_id=1, source_target_pairs={{0,28},{4,0},{8,4},{12,8},{16,12},{20,16},{24,20},{28,24},{1,29},{... | collective-permute-start | bytes 30728 | tf_op jit(solution)/shard_map/ppermute | solution.py:23
  7.7 0.0 copy-done.1
  7.7 0.0 copy-start
  7.7 0.1 fusion
  7.9 0.9 %copy-done = f32[4,96,256]{2,1,0:T(8,128)S(1)} copy-done((f32[4,96,256]{2,1,0:T(8,128)S(1)}, f32[4,96,256]{2,1,0:T(8,128)}, u32[]{:S(2)}) %copy-start) | copy-done | bytes 393240
  8.7 0.1 fusion.1
  8.9 0.1 copy.25
  8.9 0.1 copy.29
  9.1 0.1 copy.24
  9.2 0.1 copy.28
  9.3 0.0 collective-permute-done.glo_ref
  9.3 0.0 copy-start.2
  9.3 0.1 slice_bitcast_fusion.3
  9.4 0.5 %copy-done.2 = f32[2,5,256]{2,1,0:T(8,128)} copy-done((f32[2,5,256]{2,1,0:T(8,128)}, f32[2,5,256]{2,1,0:T(8,128)S(1)}, u32[]{:S(2)}) %copy-start.2) | copy-done | bytes 10264
  9.9 0.1 copy.22
  10.0 0.1 reshape.46
  10.1 0.1 copy.26
  10.2 0.1 reshape.51
  10.3 0.0 collective-permute-done.1.gup_ref
  10.3 0.0 copy-start.3
  10.3 0.1 slice_bitcast_fusion.2
  10.4 0.5 %copy-done.3 = f32[2,5,256]{2,1,0:T(8,128)} copy-done((f32[2,5,256]{2,1,0:T(8,128)}, f32[2,5,256]{2,1,0:T(8,128)S(1)}, u32[]{:S(2)}) %copy-start.3) | copy-done | bytes 10264
  10.9 0.1 copy.23
  11.0 0.1 reshape.47
  11.1 0.1 copy.27
  11.2 0.1 reshape.52
  11.3 0.1 pad_maximum_fusion
  11.3 0.1 reshape.48
  11.4 2.0 %collective-permute-start.2 = (f32[3536]{0:T(1024)S(1)}, f32[3536]{0:T(1024)S(1)}, u32[]{:S(2)}, u32[]{:S(2)}) collective-permute-start(f32[3536]{0:T(1024)S(1)} %reshape.48), channel_id=1, source_target_pairs={{0,1},{1,2},{2,3},{3,0},{4,5},{5,6},{6,7},{7,4},{8,9},{9,10},{10,1... | collective-permute-start | bytes 42440 | tf_op jit(solution)/shard_map/ppermute | solution.py:23
  13.4 0.1 pad_maximum_fusion.1
  13.5 0.1 reshape.53
  13.6 1.0 %collective-permute-start.3 = (f32[3536]{0:T(1024)S(1)}, f32[3536]{0:T(1024)S(1)}, u32[]{:S(2)}, u32[]{:S(2)}) collective-permute-start(f32[3536]{0:T(1024)S(1)} %reshape.53), channel_id=1, source_target_pairs={{0,3},{1,0},{2,1},{3,2},{4,7},{5,4},{6,5},{7,6},{8,11},{9,8},{10,9... | collective-permute-start | bytes 42440 | tf_op jit(solution)/shard_map/ppermute | solution.py:23
  14.5 1.6 %collective-permute-done.2 = f32[3536]{0:T(1024)S(1)} collective-permute-done((f32[3536]{0:T(1024)S(1)}, f32[3536]{0:T(1024)S(1)}, u32[]{:S(2)}, u32[]{:S(2)}) %collective-permute-start.2) | collective-permute-done | bytes 14176 | tf_op jit(solution)/shard_map/ppermute | solution.py:23
  16.2 0.1 select_n.22
  16.3 1.0 %collective-permute-done.3 = f32[3536]{0:T(1024)S(1)} collective-permute-done((f32[3536]{0:T(1024)S(1)}, f32[3536]{0:T(1024)S(1)}, u32[]{:S(2)}, u32[]{:S(2)}) %collective-permute-start.3) | collective-permute-done | bytes 14176 | tf_op jit(solution)/shard_map/ppermute | solution.py:23
  17.3 0.1 select_n.25
  17.4 0.6 %select_maximum_fusion.packed_ref = f32[8,896]{1,0:T(8,128)} fusion(f32[4,884]{1,0:T(4,128)S(1)} %select_n.25, f32[4,884]{1,0:T(4,128)S(1)} %select_n.22), kind=kLoop, calls=%fused_computation | loop fusion | flops 28672 | bytes 56960 | tf_op jit(solution)/shard_map/concatenate | solution.py:505
  18.0 5.1 %shard_map.131 = (f32[5,96,384]{2,1,0:T(8,128)}, f32[32,128]{1,0:T(8,128)}) custom-call(f32[5,5]{1,0:T(8,128)} %ax_ref.5, f32[5,5]{1,0:T(8,128)} %pt_ref.5, f32[1,4]{1,0:T(1,128)} %vel_ref.3, f32[5,96,256]{2,1,0:T(8,128)} %bitcast.28, f32[4,96,256]{2,1,0:T(8,128)} %ms_ref.5, f32[2,5,256]{2,1,0:T(8,128)} %copy-done.2, f32[2,5,256]{2,1,0:T(8,128)} %copy-done.3, ...), custom_call_target="tpu_custom_call" | custom-call | tf_op jit(solution)/shard_map/pallas_call | solution.py:511
  23.1 0.8 %reduce_sum.9 = f32[32]{0:T(128)S(1)} reduce(f32[32,128]{1,0:T(8,128)} %get-tuple-element.12, f32[]{:T(128)} %constant.2.clone.1), dimensions={1}, to_apply=%region_0.1 | reduce | flops 4064 | bytes 16516 | tf_op jit(solution)/shard_map/reduce_sum | solution.py:522
  23.9 2.5 %collective-permute-start.4 = (f32[32]{0:T(128)S(1)}, f32[32]{0:T(128)S(1)}, u32[]{:S(2)}, u32[]{:S(2)}) collective-permute-start(f32[32]{0:T(128)S(1)} %reduce_sum.9), channel_id=1, source_target_pairs={{0,1},{1,0},{2,3},{3,2},{4,5},{5,4},{6,7},{7,6},{8,9},{9,8},{10,11... | collective-permute-start | bytes 392 | tf_op jit(solution)/shard_map/ppermute | solution.py:42
  26.4 1.5 %collective-permute-done.4 = f32[32]{0:T(128)S(1)} collective-permute-done((f32[32]{0:T(128)S(1)}, f32[32]{0:T(128)S(1)}, u32[]{:S(2)}, u32[]{:S(2)}) %collective-permute-start.4) | collective-permute-done | bytes 160 | tf_op jit(solution)/shard_map/ppermute | solution.py:42
  27.9 1.1 %collective-permute-start.5 = (f32[32]{0:T(128)S(1)}, f32[32]{0:T(128)S(1)}, u32[]{:S(2)}, u32[]{:S(2)}) collective-permute-start(f32[32]{0:T(128)S(1)} %add.8), channel_id=1, source_target_pairs={{0,2},{1,3},{2,0},{3,1},{4,6},{5,7},{6,4},{7,5},{8,10},{9,11},{10,... | collective-permute-start | bytes 392 | tf_op jit(solution)/shard_map/ppermute | solution.py:42
  29.1 3.3 %shard_map.132.ra_ref = f32[5,96,384]{2,1,0:T(8,128)} custom-call(f32[5,5]{1,0:T(8,128)} %ax_ref.5, f32[5,5]{1,0:T(8,128)} %pt_ref.5, f32[5,96,384]{2,1,0:T(8,128)} %get-tuple-element.13.a_ref, f32[4,96,256]{2,1,0:T(8,128)} %ms_ref.5, f32[2,5,256]{2,1,0:T(8,128)} %copy-done.2, f32[2,5,256]{2,1,0:T(8,128)} %copy-done.3, f32[8,896]{1,0:T(8,128)} %select_maximum_fusion.packed_ref), custom_call_target="tpu_custom_call" | custom-call | tf_op jit(solution)/shard_map/pallas_call | solution.py:524
  32.4 0.0 collective-permute-done.5
  32.4 0.5 %add.9.tot_ref = f32[32]{0:T(128)} add(f32[32]{0:T(128)S(1)} %add.8, f32[32]{0:T(128)S(1)} %collective-permute-done.5) | non-fusion elementwise | flops 32 | bytes 384 | tf_op jit(solution)/shard_map/add | solution.py:42
  33.0 3.5 %shard_map.133 = (f32[5,96,256]{2,1,0:T(8,128)}, f32[1,4]{1,0:T(1,128)}, f32[1,4]{1,0:T(1,128)}) custom-call(f32[32]{0:T(128)} %add.9.tot_ref, f32[1,4]{1,0:T(1,128)} %stiff_ref.1, f32[1,4]{1,0:T(1,128)} %disp_ref.1, f32[1,4]{1,0:T(1,128)} %vel_ref.3, f32[5,5]{1,0:T(8,128)} %ax_ref.5, f32[5,5]{1,0:T(8,128)} %pt_ref.5, ...), custom_call_target="tpu_custom_call" | custom-call | tf_op jit(solution)/shard_map/pallas_call | solution.py:533
  (3 shorter events, 0.0 us)
Async XLA Ops:
  0.6 7.1 %copy-start.1 = (f32[1,5,96,256]{3,2,1,0:T(8,128)S(1)}, f32[1,5,96,256]{3,2,1,0:T(8,128)}, u32[]{:S(2)}) copy-start(f32[1,5,96,256]{3,2,1,0:T(8,128)} %param.11) | copy-start | bytes 1474564
  3.1 6.2 %collective-permute-start = (f32[2,5,256]{2,1,0:T(8,128)}, f32[2,5,256]{2,1,0:T(8,128)S(1)}, u32[]{:S(2)}, u32[]{:S(2)}) collective-permute-start(f32[2,5,256]{2,1,0:T(8,128)} %get-tuple-element.10), channel_id=1, source_target_pairs={{0,4},{4,8},{8,12},{12,16},{16,20},{20,24},{24,28},{28,0},{1,5},{5... | collective-permute-start | bytes 30728 | tf_op jit(solution)/shard_map/ppermute | solution.py:23
  3.6 6.7 %collective-permute-start.1 = (f32[2,5,256]{2,1,0:T(8,128)}, f32[2,5,256]{2,1,0:T(8,128)S(1)}, u32[]{:S(2)}, u32[]{:S(2)}) collective-permute-start(f32[2,5,256]{2,1,0:T(8,128)} %get-tuple-element.11), channel_id=1, source_target_pairs={{0,28},{4,0},{8,4},{12,8},{16,12},{20,16},{24,20},{28,24},{1,29},{... | collective-permute-start | bytes 30728 | tf_op jit(solution)/shard_map/ppermute | solution.py:23
  7.7 1.0 %copy-start = (f32[4,96,256]{2,1,0:T(8,128)S(1)}, f32[4,96,256]{2,1,0:T(8,128)}, u32[]{:S(2)}) copy-start(f32[4,96,256]{2,1,0:T(8,128)} %ms_ref.5) | copy-start | bytes 1179652
  9.3 0.6 %copy-start.2 = (f32[2,5,256]{2,1,0:T(8,128)}, f32[2,5,256]{2,1,0:T(8,128)S(1)}, u32[]{:S(2)}) copy-start(f32[2,5,256]{2,1,0:T(8,128)S(1)} %collective-permute-done.glo_ref) | copy-start | bytes 30724
  10.3 0.6 %copy-start.3 = (f32[2,5,256]{2,1,0:T(8,128)}, f32[2,5,256]{2,1,0:T(8,128)S(1)}, u32[]{:S(2)}) copy-start(f32[2,5,256]{2,1,0:T(8,128)S(1)} %collective-permute-done.1.gup_ref) | copy-start | bytes 30724
  11.4 4.7 %collective-permute-start.2 = (f32[3536]{0:T(1024)S(1)}, f32[3536]{0:T(1024)S(1)}, u32[]{:S(2)}, u32[]{:S(2)}) collective-permute-start(f32[3536]{0:T(1024)S(1)} %reshape.48), channel_id=1, source_target_pairs={{0,1},{1,2},{2,3},{3,0},{4,5},{5,6},{6,7},{7,4},{8,9},{9,10},{10,1... | collective-permute-start | bytes 42440 | tf_op jit(solution)/shard_map/ppermute | solution.py:23
  13.6 3.7 %collective-permute-start.3 = (f32[3536]{0:T(1024)S(1)}, f32[3536]{0:T(1024)S(1)}, u32[]{:S(2)}, u32[]{:S(2)}) collective-permute-start(f32[3536]{0:T(1024)S(1)} %reshape.53), channel_id=1, source_target_pairs={{0,3},{1,0},{2,1},{3,2},{4,7},{5,4},{6,5},{7,6},{8,11},{9,8},{10,9... | collective-permute-start | bytes 42440 | tf_op jit(solution)/shard_map/ppermute | solution.py:23
  23.9 4.0 %collective-permute-start.4 = (f32[32]{0:T(128)S(1)}, f32[32]{0:T(128)S(1)}, u32[]{:S(2)}, u32[]{:S(2)}) collective-permute-start(f32[32]{0:T(128)S(1)} %reduce_sum.9), channel_id=1, source_target_pairs={{0,1},{1,0},{2,3},{3,2},{4,5},{5,4},{6,7},{7,6},{8,9},{9,8},{10,11... | collective-permute-start | bytes 392 | tf_op jit(solution)/shard_map/ppermute | solution.py:42
  27.9 4.5 %collective-permute-start.5 = (f32[32]{0:T(128)S(1)}, f32[32]{0:T(128)S(1)}, u32[]{:S(2)}, u32[]{:S(2)}) collective-permute-start(f32[32]{0:T(128)S(1)} %add.8), channel_id=1, source_target_pairs={{0,2},{1,3},{2,0},{3,1},{4,6},{5,7},{6,4},{7,5},{8,10},{9,11},{10,... | collective-permute-start | bytes 392 | tf_op jit(solution)/shard_map/ppermute | solution.py:42

commit v15 on v14

--- a/solution.py
+++ b/solution.py
@@ -209,21 +209,19 @@
 
 
 def pick_kernel(peers, lower_slot_ref, upper_slot_ref, upper_hist_ref, lower_hist_ref, up_ref, down_ref, sems):
-    fields, slots = upper_hist_ref.shape[0], upper_hist_ref.shape[1]
+    slots = upper_hist_ref.shape[1]
     position = lax.axis_index("blk")
     slot_next = lower_slot_ref[(position + 1) % peers]
     slot_prev = upper_slot_ref[(position + peers - 1) % peers]
     copies = []
-    for s in range(up_ref.shape[0]):
-        up_at = (slot_next + s) % slots
-        down_at = (slot_prev + s) % slots
-        for f in range(fields):
-            for hist, at, out in ((upper_hist_ref, up_at, up_ref), (lower_hist_ref, down_at, down_ref)):
-                copy = pltpu.make_async_copy(
-                    hist.at[f, pl.ds(at, 1), :], out.at[s, pl.ds(f, 1), :], sems.at[len(copies)]
-                )
-                copy.start()
-                copies.append(copy)
+    for s in range(up_ref.shape[1]):
+        for hist, first, out in ((upper_hist_ref, slot_next, up_ref), (lower_hist_ref, slot_prev, down_ref)):
+            at = (first + s) % slots
+            copy = pltpu.make_async_copy(
+                hist.at[:, pl.ds(at, 1), :], out.at[:, pl.ds(s, 1), :], sems.at[len(copies)]
+            )
+            copy.start()
+            copies.append(copy)
     for copy in copies:
         copy.wait()
 
@@ -260,15 +258,16 @@
         rows = slice((fields + m) * pitch, (fields + m + 1) * pitch)
         ms.append(widened(ms_ref[m], halo_ref[rows, :]))
     base = (fields + modes) * pitch
-    steps = glo_ref.shape[0]
+    steps = glo_ref.shape[1]
     ghosts = []
     for side, ref in enumerate((glo_ref, gup_ref)):
         per_step = []
         for s in range(steps):
-            start = base + (side * steps + s) * fields
-            rows = slice(start, start + fields)
-            block = widened(ref[s], halo_ref[rows, :])
-            per_step.append([block[j : j + 1, :] for j in range(fields)])
+            per_field = []
+            for j in range(fields):
+                row = base + side * steps * fields + j * steps + s
+                per_field.append(widened(ref[j, pl.ds(s, 1), :], halo_ref[row : row + 1, :]))
+            per_step.append(per_field)
         ghosts.append(per_step)
     return u, ms, ghosts[0], ghosts[1]
 
@@ -474,13 +473,15 @@
     disp0 = displacement[0]
     vel0 = velocity[0]
 
-    row_shape = jax.ShapeDtypeStruct((STEP_COUNT,) + upper_row_history.shape[2:], state0.dtype)
+    row_shape = jax.ShapeDtypeStruct(
+        (upper_row_history.shape[2], STEP_COUNT, upper_row_history.shape[3]), state0.dtype
+    )
     rows_up, rows_down = pl.pallas_call(
         functools.partial(pick_kernel, passages),
         out_shape=(row_shape, row_shape),
         in_specs=[smem_spec(), smem_spec(), any_spec(), any_spec()],
         out_specs=(vmem_spec(), vmem_spec()),
-        scratch_shapes=[pltpu.SemaphoreType.DMA((2 * STEP_COUNT * upper_row_history.shape[2],))],
+        scratch_shapes=[pltpu.SemaphoreType.DMA((2 * STEP_COUNT,))],
     )(
         lower_lag_slot,
         upper_lag_slot,

time: 36.8 us -> 36.2 us (0.984)
    transpose x6 -> x2, local copies, waits for them, and re-layouts: 0.54 us -> 0.16 us  [pack(): flat = [jnp.moveaxis(part, -1, 0).reshape(width, -1) for part in parts]]
    reshape x8 -> x12, local copies, waits for them, and re-layouts: 0.8 us -> 0.87 us  [pack(): flat = [jnp.moveaxis(part, -1, 0).reshape(width, -1) for part in parts]]
  transfers between devices with their start and end apart: 6 -> 6, of which waited for: 3 -> 3; matrix products, arithmetic and copies ran while one was open for 4% -> 3% of each run, Pallas kernels for 9% -> 9%
where the time goes in v15:
time: 36.2 us; the launch traced here: 35.8 us
  Pallas kernels  14.2 us (39%)
  starting transfers between devices  11.1 us (31%)
  waiting for transfers between devices  4.18 us (12%)
  local copies, waits for them, and re-layouts  3.51 us (10%)
  other arithmetic  2.16 us (6%)
  between operations  0.68 us (2%)
    ppermute x4, starting transfers between devices, shifted(): lax.ppermute(value, axis, [(i, (i + by) % peers) for i in range(peers)])  7.54 us
    pallas_call x1, Pallas kernels, on_device(): pl.pallas_call(functools.partial(first_kernel, mesh_peers), out_shape=(ja...  5.12 us
    ppermute x2, starting transfers between devices, mesh_sum(): lax.ppermute(value, 'mesh', [(i, i ^ step) for i in range(peers)])  3.6 us
    pallas_call x1, Pallas kernels, on_device(): pl.pallas_call(functools.partial(second_kernel, mesh_peers, force_scale),...  3.5 us
    pallas_call x1, Pallas kernels, on_device(): pl.pallas_call(functools.partial(step2_rate_kernel, mesh_peers), out_shap...  3.35 us
    ppermute x4, waiting for transfers between devices, shifted(): lax.ppermute(value, axis, [(i, (i + by) % peers) for i in range(peers)])  2.66 us
    pallas_call x1, Pallas kernels, on_device(): pl.pallas_call(functools.partial(pick_kernel, passages), out_shape=(row_s...  2.2 us
    unnamed x8, local copies, waits for them, and re-layouts  1.92 us
  transfers between devices with their start and end apart: 6, of which 3 were waited for; matrix products, arithmetic and copies ran while one was open for 3% of the time, Pallas kernels for 9%

profile of v15, /device:TPU:0, one launch (start us, length us, event | category | flops | bytes accessed | tf_op | source)
XLA Modules:
  0.0 35.8 jit_solution(5808814996466492783)
XLA Ops:
  0.6 0.0 copy-start.1
  0.6 2.2 %shard_map.130 = (f32[5,2,256]{2,1,0:T(2,128)}, f32[5,2,256]{2,1,0:T(2,128)}) custom-call(s32[8]{0:T(128)} %lower_slot_ref.1, s32[8]{0:T(128)} %upper_slot_ref.1, f32[5,64,256]{2,1,0:T(8,128)} %bitcast.42, f32[5,64,256]{2,1,0:T(8,128)} %bitcast.43), custom_call_target="tpu_custom_call" | custom-call | tf_op jit(solution)/shard_map/pallas_call | solution.py:479
  2.9 0.5 %collective-permute-start = (f32[5,2,256]{2,1,0:T(2,128)}, f32[5,2,256]{2,1,0:T(2,128)S(1)}, u32[]{:S(2)}, u32[]{:S(2)}) collective-permute-start(f32[5,2,256]{2,1,0:T(2,128)} %get-tuple-element.10), channel_id=1, source_target_pairs={{0,4},{4,8},{8,12},{12,16},{16,20},{20,24},{24,28},{28,0},{1,5},{5... | collective-permute-start | bytes 30728 | tf_op jit(solution)/shard_map/ppermute | solution.py:23
  3.4 4.1 %collective-permute-start.1 = (f32[5,2,256]{2,1,0:T(2,128)}, f32[5,2,256]{2,1,0:T(2,128)S(1)}, u32[]{:S(2)}, u32[]{:S(2)}) collective-permute-start(f32[5,2,256]{2,1,0:T(2,128)} %get-tuple-element.11), channel_id=1, source_target_pairs={{0,28},{4,0},{8,4},{12,8},{16,12},{20,16},{24,20},{28,24},{1,29},{... | collective-permute-start | bytes 30728 | tf_op jit(solution)/shard_map/ppermute | solution.py:23
  7.5 0.0 copy-done.1
  7.5 0.0 copy-start
  7.5 0.1 fusion
  7.6 0.9 %copy-done = f32[4,96,256]{2,1,0:T(8,128)S(1)} copy-done((f32[4,96,256]{2,1,0:T(8,128)S(1)}, f32[4,96,256]{2,1,0:T(8,128)}, u32[]{:S(2)}) %copy-start) | copy-done | bytes 393240
  8.5 0.1 fusion.1
  8.6 0.1 copy.15
  8.7 0.1 copy.19
  8.8 0.1 copy.14
  8.9 0.1 copy.18
  9.0 0.0 collective-permute-done.glo_ref
  9.0 0.0 copy-start.2
  9.0 0.1 slice_bitcast_fusion.3
  9.1 0.5 %copy-done.2 = f32[5,2,256]{2,1,0:T(2,128)} copy-done((f32[5,2,256]{2,1,0:T(2,128)}, f32[5,2,256]{2,1,0:T(2,128)S(1)}, u32[]{:S(2)}) %copy-start.2) | copy-done | bytes 10264
  9.7 0.1 copy.16
  9.8 0.1 copy.20
  9.9 0.0 collective-permute-done.1.gup_ref
  9.9 0.0 copy-start.3
  9.9 0.1 slice_bitcast_fusion.2
  9.9 0.5 %copy-done.3 = f32[5,2,256]{2,1,0:T(2,128)} copy-done((f32[5,2,256]{2,1,0:T(2,128)}, f32[5,2,256]{2,1,0:T(2,128)S(1)}, u32[]{:S(2)}) %copy-start.3) | copy-done | bytes 10264
  10.5 0.1 copy.17
  10.6 0.1 copy.21
  10.7 0.1 pad_maximum_fusion
  10.7 0.1 reshape.48
  10.8 1.9 %collective-permute-start.2 = (f32[3536]{0:T(1024)S(1)}, f32[3536]{0:T(1024)S(1)}, u32[]{:S(2)}, u32[]{:S(2)}) collective-permute-start(f32[3536]{0:T(1024)S(1)} %reshape.48), channel_id=1, source_target_pairs={{0,1},{1,2},{2,3},{3,0},{4,5},{5,6},{6,7},{7,4},{8,9},{9,10},{10,1... | collective-permute-start | bytes 42440 | tf_op jit(solution)/shard_map/ppermute | solution.py:23
  12.8 0.1 pad_maximum_fusion.1
  12.8 0.1 reshape.53
  12.9 1.0 %collective-permute-start.3 = (f32[3536]{0:T(1024)S(1)}, f32[3536]{0:T(1024)S(1)}, u32[]{:S(2)}, u32[]{:S(2)}) collective-permute-start(f32[3536]{0:T(1024)S(1)} %reshape.53), channel_id=1, source_target_pairs={{0,3},{1,0},{2,1},{3,2},{4,7},{5,4},{6,5},{7,6},{8,11},{9,8},{10,9... | collective-permute-start | bytes 42440 | tf_op jit(solution)/shard_map/ppermute | solution.py:23
  13.9 1.5 %collective-permute-done.2 = f32[3536]{0:T(1024)S(1)} collective-permute-done((f32[3536]{0:T(1024)S(1)}, f32[3536]{0:T(1024)S(1)}, u32[]{:S(2)}, u32[]{:S(2)}) %collective-permute-start.2) | collective-permute-done | bytes 14176 | tf_op jit(solution)/shard_map/ppermute | solution.py:23
  15.5 0.1 select_n.22
  15.6 1.1 %collective-permute-done.3 = f32[3536]{0:T(1024)S(1)} collective-permute-done((f32[3536]{0:T(1024)S(1)}, f32[3536]{0:T(1024)S(1)}, u32[]{:S(2)}, u32[]{:S(2)}) %collective-permute-start.3) | collective-permute-done | bytes 14176 | tf_op jit(solution)/shard_map/ppermute | solution.py:23
  16.7 0.1 select_n.25
  16.7 0.6 %select_maximum_fusion.packed_ref = f32[8,896]{1,0:T(8,128)} fusion(f32[4,884]{1,0:T(4,128)S(1)} %select_n.25, f32[4,884]{1,0:T(4,128)S(1)} %select_n.22), kind=kLoop, calls=%fused_computation | loop fusion | flops 28672 | bytes 56960 | tf_op jit(solution)/shard_map/concatenate | solution.py:506
  17.4 5.1 %shard_map.131 = (f32[5,96,384]{2,1,0:T(8,128)}, f32[32,128]{1,0:T(8,128)}) custom-call(f32[5,5]{1,0:T(8,128)} %ax_ref.5, f32[5,5]{1,0:T(8,128)} %pt_ref.5, f32[1,4]{1,0:T(1,128)} %vel_ref.3, f32[5,96,256]{2,1,0:T(8,128)} %bitcast.36, f32[4,96,256]{2,1,0:T(8,128)} %ms_ref.5, f32[5,2,256]{2,1,0:T(2,128)} %copy-done.2, f32[5,2,256]{2,1,0:T(2,128)} %copy-done.3, ...), custom_call_target="tpu_custom_call" | custom-call | tf_op jit(solution)/shard_map/pallas_call | solution.py:512
  22.5 0.8 %reduce_sum.9 = f32[32]{0:T(128)S(1)} reduce(f32[32,128]{1,0:T(8,128)} %get-tuple-element.12, f32[]{:T(128)} %constant.2.clone.1), dimensions={1}, to_apply=%region_0.1 | reduce | flops 4064 | bytes 16516 | tf_op jit(solution)/shard_map/reduce_sum | solution.py:523
  23.3 2.5 %collective-permute-start.4 = (f32[32]{0:T(128)S(1)}, f32[32]{0:T(128)S(1)}, u32[]{:S(2)}, u32[]{:S(2)}) collective-permute-start(f32[32]{0:T(128)S(1)} %reduce_sum.9), channel_id=1, source_target_pairs={{0,1},{1,0},{2,3},{3,2},{4,5},{5,4},{6,7},{7,6},{8,9},{9,8},{10,11... | collective-permute-start | bytes 392 | tf_op jit(solution)/shard_map/ppermute | solution.py:42
  25.8 1.5 %collective-permute-done.4 = f32[32]{0:T(128)S(1)} collective-permute-done((f32[32]{0:T(128)S(1)}, f32[32]{0:T(128)S(1)}, u32[]{:S(2)}, u32[]{:S(2)}) %collective-permute-start.4) | collective-permute-done | bytes 160 | tf_op jit(solution)/shard_map/ppermute | solution.py:42
  27.3 1.1 %collective-permute-start.5 = (f32[32]{0:T(128)S(1)}, f32[32]{0:T(128)S(1)}, u32[]{:S(2)}, u32[]{:S(2)}) collective-permute-start(f32[32]{0:T(128)S(1)} %add.8), channel_id=1, source_target_pairs={{0,2},{1,3},{2,0},{3,1},{4,6},{5,7},{6,4},{7,5},{8,10},{9,11},{10,... | collective-permute-start | bytes 392 | tf_op jit(solution)/shard_map/ppermute | solution.py:42
  28.4 3.3 %shard_map.132.ra_ref = f32[5,96,384]{2,1,0:T(8,128)} custom-call(f32[5,5]{1,0:T(8,128)} %ax_ref.5, f32[5,5]{1,0:T(8,128)} %pt_ref.5, f32[5,96,384]{2,1,0:T(8,128)} %get-tuple-element.13.a_ref, f32[4,96,256]{2,1,0:T(8,128)} %ms_ref.5, f32[5,2,256]{2,1,0:T(2,128)} %copy-done.2, f32[5,2,256]{2,1,0:T(2,128)} %copy-done.3, f32[8,896]{1,0:T(8,128)} %select_maximum_fusion.packed_ref), custom_call_target="tpu_custom_call" | custom-call | tf_op jit(solution)/shard_map/pallas_call | solution.py:525
  31.8 0.0 collective-permute-done.5
  31.8 0.5 %add.9.tot_ref = f32[32]{0:T(128)} add(f32[32]{0:T(128)S(1)} %add.8, f32[32]{0:T(128)S(1)} %collective-permute-done.5) | non-fusion elementwise | flops 32 | bytes 384 | tf_op jit(solution)/shard_map/add | solution.py:42
  32.3 3.5 %shard_map.133 = (f32[5,96,256]{2,1,0:T(8,128)}, f32[1,4]{1,0:T(1,128)}, f32[1,4]{1,0:T(1,128)}) custom-call(f32[32]{0:T(128)} %add.9.tot_ref, f32[1,4]{1,0:T(1,128)} %stiff_ref.1, f32[1,4]{1,0:T(1,128)} %disp_ref.1, f32[1,4]{1,0:T(1,128)} %vel_ref.3, f32[5,5]{1,0:T(8,128)} %ax_ref.5, f32[5,5]{1,0:T(8,128)} %pt_ref.5, ...), custom_call_target="tpu_custom_call" | custom-call | tf_op jit(solution)/shard_map/pallas_call | solution.py:534
  (7 shorter events, 0.0 us)
Async XLA Ops:
  0.6 6.8 %copy-start.1 = (f32[1,5,96,256]{3,2,1,0:T(8,128)S(1)}, f32[1,5,96,256]{3,2,1,0:T(8,128)}, u32[]{:S(2)}) copy-start(f32[1,5,96,256]{3,2,1,0:T(8,128)} %param.11) | copy-start | bytes 1474564
  2.9 6.2 %collective-permute-start = (f32[5,2,256]{2,1,0:T(2,128)}, f32[5,2,256]{2,1,0:T(2,128)S(1)}, u32[]{:S(2)}, u32[]{:S(2)}) collective-permute-start(f32[5,2,256]{2,1,0:T(2,128)} %get-tuple-element.10), channel_id=1, source_target_pairs={{0,4},{4,8},{8,12},{12,16},{16,20},{20,24},{24,28},{28,0},{1,5},{5... | collective-permute-start | bytes 30728 | tf_op jit(solution)/shard_map/ppermute | solution.py:23
  3.4 6.5 %collective-permute-start.1 = (f32[5,2,256]{2,1,0:T(2,128)}, f32[5,2,256]{2,1,0:T(2,128)S(1)}, u32[]{:S(2)}, u32[]{:S(2)}) collective-permute-start(f32[5,2,256]{2,1,0:T(2,128)} %get-tuple-element.11), channel_id=1, source_target_pairs={{0,28},{4,0},{8,4},{12,8},{16,12},{20,16},{24,20},{28,24},{1,29},{... | collective-permute-start | bytes 30728 | tf_op jit(solution)/shard_map/ppermute | solution.py:23
  7.5 1.0 %copy-start = (f32[4,96,256]{2,1,0:T(8,128)S(1)}, f32[4,96,256]{2,1,0:T(8,128)}, u32[]{:S(2)}) copy-start(f32[4,96,256]{2,1,0:T(8,128)} %ms_ref.5) | copy-start | bytes 1179652
  9.0 0.6 %copy-start.2 = (f32[5,2,256]{2,1,0:T(2,128)}, f32[5,2,256]{2,1,0:T(2,128)S(1)}, u32[]{:S(2)}) copy-start(f32[5,2,256]{2,1,0:T(2,128)S(1)} %collective-permute-done.glo_ref) | copy-start | bytes 30724
  9.9 0.6 %copy-start.3 = (f32[5,2,256]{2,1,0:T(2,128)}, f32[5,2,256]{2,1,0:T(2,128)S(1)}, u32[]{:S(2)}) copy-start(f32[5,2,256]{2,1,0:T(2,128)S(1)} %collective-permute-done.1.gup_ref) | copy-start | bytes 30724
  10.8 4.6 %collective-permute-start.2 = (f32[3536]{0:T(1024)S(1)}, f32[3536]{0:T(1024)S(1)}, u32[]{:S(2)}, u32[]{:S(2)}) collective-permute-start(f32[3536]{0:T(1024)S(1)} %reshape.48), channel_id=1, source_target_pairs={{0,1},{1,2},{2,3},{3,0},{4,5},{5,6},{6,7},{7,4},{8,9},{9,10},{10,1... | collective-permute-start | bytes 42440 | tf_op jit(solution)/shard_map/ppermute | solution.py:23
  12.9 3.7 %collective-permute-start.3 = (f32[3536]{0:T(1024)S(1)}, f32[3536]{0:T(1024)S(1)}, u32[]{:S(2)}, u32[]{:S(2)}) collective-permute-start(f32[3536]{0:T(1024)S(1)} %reshape.53), channel_id=1, source_target_pairs={{0,3},{1,0},{2,1},{3,2},{4,7},{5,4},{6,5},{7,6},{8,11},{9,8},{10,9... | collective-permute-start | bytes 42440 | tf_op jit(solution)/shard_map/ppermute | solution.py:23
  23.3 4.0 %collective-permute-start.4 = (f32[32]{0:T(128)S(1)}, f32[32]{0:T(128)S(1)}, u32[]{:S(2)}, u32[]{:S(2)}) collective-permute-start(f32[32]{0:T(128)S(1)} %reduce_sum.9), channel_id=1, source_target_pairs={{0,1},{1,0},{2,3},{3,2},{4,5},{5,4},{6,7},{7,6},{8,9},{9,8},{10,11... | collective-permute-start | bytes 392 | tf_op jit(solution)/shard_map/ppermute | solution.py:42
  27.3 4.5 %collective-permute-start.5 = (f32[32]{0:T(128)S(1)}, f32[32]{0:T(128)S(1)}, u32[]{:S(2)}, u32[]{:S(2)}) collective-permute-start(f32[32]{0:T(128)S(1)} %add.8), channel_id=1, source_target_pairs={{0,2},{1,3},{2,0},{3,1},{4,6},{5,7},{6,4},{7,5},{8,10},{9,11},{10,... | collective-permute-start | bytes 392 | tf_op jit(solution)/shard_map/ppermute | solution.py:42

commit v16 on v13

--- a/solution.py
+++ b/solution.py
@@ -33,15 +33,15 @@
     return before, after
 
 
-def mesh_sum(value):
+def mesh_sum_pair(value):
     peers = lax.axis_size("mesh")
-    if peers & (peers - 1):
-        return lax.psum(value, "mesh")
+    if peers & (peers - 1) or peers < 2:
+        return lax.psum(value, "mesh"), jnp.zeros_like(value)
     step = 1
-    while step < peers:
+    while 2 * step < peers:
         value = value + lax.ppermute(value, "mesh", [(i, i ^ step) for i in range(peers)])
         step *= 2
-    return value
+    return value, lax.ppermute(value, "mesh", [(i, i ^ step) for i in range(peers)])
 
 
 def pick_rows(table, index, count):
@@ -308,9 +308,9 @@
             part_ref[k + m * modes + n : k + m * modes + n + 1, :] = lane_fold(weighted[m] * t)
 
 
-def modal_steps(force_scale, tot_ref, stiff_ref, disp_ref, vel_ref, modes):
+def modal_steps(force_scale, tot_ref, other_ref, stiff_ref, disp_ref, vel_ref, modes):
     h = TIME_STEP
-    t = [force_scale * tot_ref[k] for k in range(4 * modes + modes * modes)]
+    t = [force_scale * (tot_ref[k] + other_ref[k]) for k in range(4 * modes + modes * modes)]
     force = [t[w * modes : (w + 1) * modes] for w in range(4)]
     couple = [t[4 * modes + m * modes : 4 * modes + (m + 1) * modes] for m in range(modes)]
     stiff = [stiff_ref[0, m] for m in range(modes)]
@@ -365,6 +365,7 @@
     peers,
     force_scale,
     tot_ref,
+    other_ref,
     stiff_ref,
     disp_ref,
     vel_ref,
@@ -387,7 +388,7 @@
     modes = ms_ref.shape[0]
     pitch = ms_ref.shape[1]
     jac = read_jacobians(ax_ref, pt_ref, fields)
-    coef, disp2, vel2 = modal_steps(force_scale, tot_ref, stiff_ref, disp_ref, vel_ref, modes)
+    coef, disp2, vel2 = modal_steps(force_scale, tot_ref, other_ref, stiff_ref, disp_ref, vel_ref, modes)
     for m in range(modes):
         disp_out_ref[0, m] = disp2[m]
         vel_out_ref[0, m] = vel2[m]
@@ -507,7 +508,7 @@
         scratch_shapes=columns,
     )(axial_jacobian, pitch_jacobian, velocity, *ins)
 
-    totals = mesh_sum(jnp.sum(part_lanes, axis=1))
+    totals, totals_other = mesh_sum_pair(jnp.sum(part_lanes, axis=1))
 
     rate_a = pl.pallas_call(
         functools.partial(step2_rate_kernel, mesh_peers),
@@ -521,10 +522,10 @@
     state2, disp2, vel2 = pl.pallas_call(
         functools.partial(second_kernel, mesh_peers, force_scale),
         out_shape=(jax.ShapeDtypeStruct(state0.shape, state0.dtype), small, small),
-        in_specs=[smem_spec()] * 6 + [vmem_spec()] * 6,
+        in_specs=[smem_spec()] * 7 + [vmem_spec()] * 6,
         out_specs=(vmem_spec(), smem_spec(), smem_spec()),
         scratch_shapes=columns,
-    )(totals, stiffness, displacement, velocity, axial_jacobian, pitch_jacobian, base1, rate_a, *ins[1:])
+    )(totals, totals_other, stiffness, displacement, velocity, axial_jacobian, pitch_jacobian, base1, rate_a, *ins[1:])
     return (state2[None], disp2, vel2)
 
 

time: 36 us -> 36 us (level)
  other arithmetic: 2.16 us -> 1.62 us
  local copies, waits for them, and re-layouts: 3.83 us -> 4.36 us
    add x2 -> x1, other arithmetic: 0.55 us -> 0.01 us  [mesh_sum_pair(): value + lax.ppermute(value, 'mesh', [(i, i ^ step) for i in range(peers)])]
    unnamed x8 -> x12, local copies, waits for them, and re-layouts: 1.92 us -> 2.45 us
where the time goes in v16:
time: 36 us; the launch traced here: 35.7 us
  Pallas kernels  13.8 us (38%)
  starting transfers between devices  11.1 us (31%)
  local copies, waits for them, and re-layouts  4.36 us (12%)
  waiting for transfers between devices  4.26 us (12%)
  other arithmetic  1.62 us (4%)
  between operations  0.68 us (2%)
    ppermute x4, starting transfers between devices, shifted(): lax.ppermute(value, axis, [(i, (i + by) % peers) for i in range(peers)])  7.46 us
    pallas_call x1, Pallas kernels, on_device(): pl.pallas_call(functools.partial(first_kernel, mesh_peers), out_shape=(ja...  5.12 us
    ppermute x2, starting transfers between devices, mesh_sum_pair(): lax.ppermute(value, 'mesh', [(i, i ^ step) for i in range(peers)])  3.6 us
    pallas_call x1, Pallas kernels, on_device(): pl.pallas_call(functools.partial(second_kernel, mesh_peers, force_scale),...  3.5 us
    pallas_call x1, Pallas kernels, on_device(): pl.pallas_call(functools.partial(step2_rate_kernel, mesh_peers), out_shap...  3.36 us
    ppermute x4, waiting for transfers between devices, shifted(): lax.ppermute(value, axis, [(i, (i + by) % peers) for i in range(peers)])  2.74 us
    unnamed x12, local copies, waits for them, and re-layouts  2.45 us
    pallas_call x1, Pallas kernels, on_device(): pl.pallas_call(functools.partial(pick_kernel, passages), out_shape=(row_s...  1.78 us
  transfers between devices with their start and end apart: 6, of which 3 were waited for; matrix products, arithmetic and copies ran while one was open for 4% of the time, Pallas kernels for 9%

profile of v16, /device:TPU:0, one launch (start us, length us, event | category | flops | bytes accessed | tf_op | source)
XLA Modules:
  0.0 35.7 jit_solution(11391609031675282459)
XLA Ops:
  0.6 0.0 copy-start.1
  0.6 1.8 %shard_map.130 = (f32[2,5,256]{2,1,0:T(8,128)}, f32[2,5,256]{2,1,0:T(8,128)}) custom-call(s32[8]{0:T(128)} %lower_slot_ref.1, s32[8]{0:T(128)} %upper_slot_ref.1, f32[5,64,256]{2,1,0:T(8,128)} %bitcast.34, f32[5,64,256]{2,1,0:T(8,128)} %bitcast.35), custom_call_target="tpu_custom_call" | custom-call | tf_op jit(solution)/shard_map/pallas_call | solution.py:468
  2.4 0.5 %collective-permute-start = (f32[2,5,256]{2,1,0:T(8,128)}, f32[2,5,256]{2,1,0:T(8,128)S(1)}, u32[]{:S(2)}, u32[]{:S(2)}) collective-permute-start(f32[2,5,256]{2,1,0:T(8,128)} %get-tuple-element.10), channel_id=1, source_target_pairs={{0,4},{4,8},{8,12},{12,16},{16,20},{20,24},{24,28},{28,0},{1,5},{5... | collective-permute-start | bytes 30728 | tf_op jit(solution)/shard_map/ppermute | solution.py:23
  2.9 4.0 %collective-permute-start.1 = (f32[2,5,256]{2,1,0:T(8,128)}, f32[2,5,256]{2,1,0:T(8,128)S(1)}, u32[]{:S(2)}, u32[]{:S(2)}) collective-permute-start(f32[2,5,256]{2,1,0:T(8,128)} %get-tuple-element.11), channel_id=1, source_target_pairs={{0,28},{4,0},{8,4},{12,8},{16,12},{20,16},{24,20},{28,24},{1,29},{... | collective-permute-start | bytes 30728 | tf_op jit(solution)/shard_map/ppermute | solution.py:23
  6.9 0.0 copy-done.1
  6.9 0.0 copy-start
  6.9 0.1 fusion
  7.0 0.9 %copy-done = f32[4,96,256]{2,1,0:T(8,128)S(1)} copy-done((f32[4,96,256]{2,1,0:T(8,128)S(1)}, f32[4,96,256]{2,1,0:T(8,128)}, u32[]{:S(2)}) %copy-start) | copy-done | bytes 393240
  7.9 0.1 fusion.1
  8.0 0.1 copy.25
  8.1 0.1 copy.29
  8.2 0.1 copy.24
  8.4 0.1 copy.28
  8.5 0.0 collective-permute-done.glo_ref
  8.5 0.0 copy-start.2
  8.5 0.1 slice_bitcast_fusion.3
  8.6 0.5 %copy-done.2 = f32[2,5,256]{2,1,0:T(8,128)} copy-done((f32[2,5,256]{2,1,0:T(8,128)}, f32[2,5,256]{2,1,0:T(8,128)S(1)}, u32[]{:S(2)}) %copy-start.2) | copy-done | bytes 10264
  9.1 0.1 copy.22
  9.2 0.1 reshape.46
  9.3 0.1 copy.26
  9.4 0.1 reshape.51
  9.5 0.0 collective-permute-done.1.gup_ref
  9.5 0.0 copy-start.3
  9.5 0.1 slice_bitcast_fusion.2
  9.6 0.5 %copy-done.3 = f32[2,5,256]{2,1,0:T(8,128)} copy-done((f32[2,5,256]{2,1,0:T(8,128)}, f32[2,5,256]{2,1,0:T(8,128)S(1)}, u32[]{:S(2)}) %copy-start.3) | copy-done | bytes 10264
  10.1 0.1 copy.23
  10.2 0.1 reshape.47
  10.3 0.1 copy.27
  10.4 0.1 reshape.52
  10.5 0.1 pad_maximum_fusion
  10.6 0.1 reshape.48
  10.7 2.0 %collective-permute-start.2 = (f32[3536]{0:T(1024)S(1)}, f32[3536]{0:T(1024)S(1)}, u32[]{:S(2)}, u32[]{:S(2)}) collective-permute-start(f32[3536]{0:T(1024)S(1)} %reshape.48), channel_id=1, source_target_pairs={{0,1},{1,2},{2,3},{3,0},{4,5},{5,6},{6,7},{7,4},{8,9},{9,10},{10,1... | collective-permute-start | bytes 42440 | tf_op jit(solution)/shard_map/ppermute | solution.py:23
  12.6 0.1 pad_maximum_fusion.1
  12.7 0.1 reshape.53
  12.8 1.0 %collective-permute-start.3 = (f32[3536]{0:T(1024)S(1)}, f32[3536]{0:T(1024)S(1)}, u32[]{:S(2)}, u32[]{:S(2)}) collective-permute-start(f32[3536]{0:T(1024)S(1)} %reshape.53), channel_id=1, source_target_pairs={{0,3},{1,0},{2,1},{3,2},{4,7},{5,4},{6,5},{7,6},{8,11},{9,8},{10,9... | collective-permute-start | bytes 42440 | tf_op jit(solution)/shard_map/ppermute | solution.py:23
  13.8 1.6 %collective-permute-done.2 = f32[3536]{0:T(1024)S(1)} collective-permute-done((f32[3536]{0:T(1024)S(1)}, f32[3536]{0:T(1024)S(1)}, u32[]{:S(2)}, u32[]{:S(2)}) %collective-permute-start.2) | collective-permute-done | bytes 14176 | tf_op jit(solution)/shard_map/ppermute | solution.py:23
  15.4 0.1 select_n.22
  15.5 1.0 %collective-permute-done.3 = f32[3536]{0:T(1024)S(1)} collective-permute-done((f32[3536]{0:T(1024)S(1)}, f32[3536]{0:T(1024)S(1)}, u32[]{:S(2)}, u32[]{:S(2)}) %collective-permute-start.3) | collective-permute-done | bytes 14176 | tf_op jit(solution)/shard_map/ppermute | solution.py:23
  16.6 0.1 select_n.25
  16.6 0.6 %select_maximum_fusion.packed_ref = f32[8,896]{1,0:T(8,128)} fusion(f32[4,884]{1,0:T(4,128)S(1)} %select_n.25, f32[4,884]{1,0:T(4,128)S(1)} %select_n.22), kind=kLoop, calls=%fused_computation | loop fusion | flops 28672 | bytes 56960 | tf_op jit(solution)/shard_map/concatenate | solution.py:494
  17.3 5.1 %shard_map.131 = (f32[5,96,384]{2,1,0:T(8,128)}, f32[32,128]{1,0:T(8,128)}) custom-call(f32[5,5]{1,0:T(8,128)} %ax_ref.5, f32[5,5]{1,0:T(8,128)} %pt_ref.5, f32[1,4]{1,0:T(1,128)} %vel_ref.3, f32[5,96,256]{2,1,0:T(8,128)} %bitcast.28, f32[4,96,256]{2,1,0:T(8,128)} %ms_ref.5, f32[2,5,256]{2,1,0:T(8,128)} %copy-done.2, f32[2,5,256]{2,1,0:T(8,128)} %copy-done.3, ...), custom_call_target="tpu_custom_call" | custom-call | tf_op jit(solution)/shard_map/pallas_call | solution.py:500
  22.4 0.8 %reduce_sum.9 = f32[32]{0:T(128)S(1)} reduce(f32[32,128]{1,0:T(8,128)} %get-tuple-element.12, f32[]{:T(128)} %constant.2.clone.1), dimensions={1}, to_apply=%region_0.1 | reduce | flops 4064 | bytes 16516 | tf_op jit(solution)/shard_map/reduce_sum | solution.py:511
  23.2 2.5 %collective-permute-start.4 = (f32[32]{0:T(128)S(1)}, f32[32]{0:T(128)S(1)}, u32[]{:S(2)}, u32[]{:S(2)}) collective-permute-start(f32[32]{0:T(128)S(1)} %reduce_sum.9), channel_id=1, source_target_pairs={{0,1},{1,0},{2,3},{3,2},{4,5},{5,4},{6,7},{7,6},{8,9},{9,8},{10,11... | collective-permute-start | bytes 392 | tf_op jit(solution)/shard_map/ppermute | solution.py:42
  25.7 1.5 %collective-permute-done.4 = f32[32]{0:T(128)S(1)} collective-permute-done((f32[32]{0:T(128)S(1)}, f32[32]{0:T(128)S(1)}, u32[]{:S(2)}, u32[]{:S(2)}) %collective-permute-start.4) | collective-permute-done | bytes 160 | tf_op jit(solution)/shard_map/ppermute | solution.py:42
  27.2 0.0 copy-start.4
  27.2 1.1 %collective-permute-start.5 = (f32[32]{0:T(128)S(1)}, f32[32]{0:T(128)S(1)}, u32[]{:S(2)}, u32[]{:S(2)}) collective-permute-start(f32[32]{0:T(128)S(1)} %add.5.tot_ref), channel_id=1, source_target_pairs={{0,2},{1,3},{2,0},{3,1},{4,6},{5,7},{6,4},{7,5},{8,10},{9,11},{10,... | collective-permute-start | bytes 392 | tf_op jit(solution)/shard_map/ppermute | solution.py:44
  28.3 0.0 copy-done.4
  28.3 3.4 %shard_map.132.ra_ref = f32[5,96,384]{2,1,0:T(8,128)} custom-call(f32[5,5]{1,0:T(8,128)} %ax_ref.5, f32[5,5]{1,0:T(8,128)} %pt_ref.5, f32[5,96,384]{2,1,0:T(8,128)} %get-tuple-element.13.a_ref, f32[4,96,256]{2,1,0:T(8,128)} %ms_ref.5, f32[2,5,256]{2,1,0:T(8,128)} %copy-done.2, f32[2,5,256]{2,1,0:T(8,128)} %copy-done.3, f32[8,896]{1,0:T(8,128)} %select_maximum_fusion.packed_ref), custom_call_target="tpu_custom_call" | custom-call | tf_op jit(solution)/shard_map/pallas_call | solution.py:513
  31.7 0.0 collective-permute-done.5.other_ref
  31.7 0.0 copy-start.5
  31.7 0.5 %copy-done.5 = f32[32]{0:T(128)} copy-done((f32[32]{0:T(128)}, f32[32]{0:T(128)S(1)}, u32[]{:S(2)}) %copy-start.5) | copy-done | bytes 152
  32.2 3.5 %shard_map.133 = (f32[5,96,256]{2,1,0:T(8,128)}, f32[1,4]{1,0:T(1,128)}, f32[1,4]{1,0:T(1,128)}) custom-call(f32[32]{0:T(128)} %copy-done.4, f32[32]{0:T(128)} %copy-done.5, f32[1,4]{1,0:T(1,128)} %stiff_ref.1, f32[1,4]{1,0:T(1,128)} %disp_ref.1, f32[1,4]{1,0:T(1,128)} %vel_ref.3, f32[5,5]{1,0:T(8,128)} %ax_ref.5, f32[5,5]{1,0:T(8,128)} %pt_ref.5, ...), custom_call_target="tpu_custom_call" | custom-call | tf_op jit(solution)/shard_map/pallas_call | solution.py:522
  (3 shorter events, 0.0 us)
Async XLA Ops:
  0.6 6.3 %copy-start.1 = (f32[1,5,96,256]{3,2,1,0:T(8,128)S(1)}, f32[1,5,96,256]{3,2,1,0:T(8,128)}, u32[]{:S(2)}) copy-start(f32[1,5,96,256]{3,2,1,0:T(8,128)} %param.11) | copy-start | bytes 1474564
  2.4 6.1 %collective-permute-start = (f32[2,5,256]{2,1,0:T(8,128)}, f32[2,5,256]{2,1,0:T(8,128)S(1)}, u32[]{:S(2)}, u32[]{:S(2)}) collective-permute-start(f32[2,5,256]{2,1,0:T(8,128)} %get-tuple-element.10), channel_id=1, source_target_pairs={{0,4},{4,8},{8,12},{12,16},{16,20},{20,24},{24,28},{28,0},{1,5},{5... | collective-permute-start | bytes 30728 | tf_op jit(solution)/shard_map/ppermute | solution.py:23
  2.9 6.6 %collective-permute-start.1 = (f32[2,5,256]{2,1,0:T(8,128)}, f32[2,5,256]{2,1,0:T(8,128)S(1)}, u32[]{:S(2)}, u32[]{:S(2)}) collective-permute-start(f32[2,5,256]{2,1,0:T(8,128)} %get-tuple-element.11), channel_id=1, source_target_pairs={{0,28},{4,0},{8,4},{12,8},{16,12},{20,16},{24,20},{28,24},{1,29},{... | collective-permute-start | bytes 30728 | tf_op jit(solution)/shard_map/ppermute | solution.py:23
  6.9 1.0 %copy-start = (f32[4,96,256]{2,1,0:T(8,128)S(1)}, f32[4,96,256]{2,1,0:T(8,128)}, u32[]{:S(2)}) copy-start(f32[4,96,256]{2,1,0:T(8,128)} %ms_ref.5) | copy-start | bytes 1179652
  8.5 0.6 %copy-start.2 = (f32[2,5,256]{2,1,0:T(8,128)}, f32[2,5,256]{2,1,0:T(8,128)S(1)}, u32[]{:S(2)}) copy-start(f32[2,5,256]{2,1,0:T(8,128)S(1)} %collective-permute-done.glo_ref) | copy-start | bytes 30724
  9.5 0.6 %copy-start.3 = (f32[2,5,256]{2,1,0:T(8,128)}, f32[2,5,256]{2,1,0:T(8,128)S(1)}, u32[]{:S(2)}) copy-start(f32[2,5,256]{2,1,0:T(8,128)S(1)} %collective-permute-done.1.gup_ref) | copy-start | bytes 30724
  10.7 4.8 %collective-permute-start.2 = (f32[3536]{0:T(1024)S(1)}, f32[3536]{0:T(1024)S(1)}, u32[]{:S(2)}, u32[]{:S(2)}) collective-permute-start(f32[3536]{0:T(1024)S(1)} %reshape.48), channel_id=1, source_target_pairs={{0,1},{1,2},{2,3},{3,0},{4,5},{5,6},{6,7},{7,4},{8,9},{9,10},{10,1... | collective-permute-start | bytes 42440 | tf_op jit(solution)/shard_map/ppermute | solution.py:23
  12.8 3.7 %collective-permute-start.3 = (f32[3536]{0:T(1024)S(1)}, f32[3536]{0:T(1024)S(1)}, u32[]{:S(2)}, u32[]{:S(2)}) collective-permute-start(f32[3536]{0:T(1024)S(1)} %reshape.53), channel_id=1, source_target_pairs={{0,3},{1,0},{2,1},{3,2},{4,7},{5,4},{6,5},{7,6},{8,11},{9,8},{10,9... | collective-permute-start | bytes 42440 | tf_op jit(solution)/shard_map/ppermute | solution.py:23
  23.2 4.0 %collective-permute-start.4 = (f32[32]{0:T(128)S(1)}, f32[32]{0:T(128)S(1)}, u32[]{:S(2)}, u32[]{:S(2)}) collective-permute-start(f32[32]{0:T(128)S(1)} %reduce_sum.9), channel_id=1, source_target_pairs={{0,1},{1,0},{2,3},{3,2},{4,5},{5,4},{6,7},{7,6},{8,9},{9,8},{10,11... | collective-permute-start | bytes 392 | tf_op jit(solution)/shard_map/ppermute | solution.py:42
  27.2 1.2 %copy-start.4 = (f32[32]{0:T(128)}, f32[32]{0:T(128)S(1)}, u32[]{:S(2)}) copy-start(f32[32]{0:T(128)S(1)} %add.5.tot_ref) | copy-start | bytes 388
  27.2 4.5 %collective-permute-start.5 = (f32[32]{0:T(128)S(1)}, f32[32]{0:T(128)S(1)}, u32[]{:S(2)}, u32[]{:S(2)}) collective-permute-start(f32[32]{0:T(128)S(1)} %add.5.tot_ref), channel_id=1, source_target_pairs={{0,2},{1,3},{2,0},{3,1},{4,6},{5,7},{6,4},{7,5},{8,10},{9,11},{10,... | collective-permute-start | bytes 392 | tf_op jit(solution)/shard_map/ppermute | solution.py:44
  31.7 0.5 %copy-start.5 = (f32[32]{0:T(128)}, f32[32]{0:T(128)S(1)}, u32[]{:S(2)}) copy-start(f32[32]{0:T(128)S(1)} %collective-permute-done.5.other_ref) | copy-start | bytes 388

commit v17 on v13

--- a/solution.py
+++ b/solution.py
@@ -249,7 +249,7 @@
         rows = slice(j * pitch, (j + 1) * pitch)
         u.append(widened(u_ref[j], halo_ref[rows, :]))
     ms = []
-    for m in range(modes):
+    for m in range(modes if ms_ref is not None else 0):
         rows = slice((fields + m) * pitch, (fields + m + 1) * pitch)
         ms.append(widened(ms_ref[m], halo_ref[rows, :]))
     base = (fields + modes) * pitch
@@ -346,14 +346,13 @@
     return coef, disp2, vel2
 
 
-def step2_rate_kernel(peers, ax_ref, pt_ref, a_ref, ms_ref, glo_ref, gup_ref, packed_ref, ra_ref, halo_ref):
+def step2_rate_kernel(peers, modes, ax_ref, pt_ref, a_ref, glo_ref, gup_ref, packed_ref, ra_ref, halo_ref):
     unfold_halo(packed_ref, halo_ref)
     fields = a_ref.shape[0]
-    modes = ms_ref.shape[0]
-    pitch = ms_ref.shape[1]
+    pitch = a_ref.shape[1]
     jac = read_jacobians(ax_ref, pt_ref, fields)
-    _, ms, gl, gu = assemble(None, ms_ref, glo_ref, gup_ref, halo_ref, fields, modes, pitch)
-    inside, _ = lane_masks(peers, ms[0].shape, ms_ref.shape[-1])
+    _, _, gl, gu = assemble(None, None, glo_ref, gup_ref, halo_ref, fields, modes, pitch)
+    inside, _ = lane_masks(peers, a_ref.shape[1:], a_ref.shape[-1] - LANES)
     every = list(range(fields))
     a = [a_ref[j] for j in every]
     ra = kernel_rate(a, gl[1], gu[1], jac, None, inside, every)
@@ -510,12 +509,12 @@
     totals = mesh_sum(jnp.sum(part_lanes, axis=1))
 
     rate_a = pl.pallas_call(
-        functools.partial(step2_rate_kernel, mesh_peers),
+        functools.partial(step2_rate_kernel, mesh_peers, modes),
         out_shape=jax.ShapeDtypeStruct(base1.shape, base1.dtype),
-        in_specs=[smem_spec()] * 2 + [vmem_spec()] * 5,
+        in_specs=[smem_spec()] * 2 + [vmem_spec()] * 4,
         out_specs=vmem_spec(),
         scratch_shapes=columns,
-    )(axial_jacobian, pitch_jacobian, base1, *ins[1:])
+    )(axial_jacobian, pitch_jacobian, base1, *ins[2:])
 
     small = jax.ShapeDtypeStruct(displacement.shape, displacement.dtype)
     state2, disp2, vel2 = pl.pallas_call(

time: 36 us -> 35.9 us (level)
  no operation moved by 1% of the time
where the time goes in v17:
time: 35.9 us; the launch traced here: 35.6 us
  Pallas kernels  13.6 us (38%)
  starting transfers between devices  11.1 us (31%)
  waiting for transfers between devices  4.26 us (12%)
  local copies, waits for them, and re-layouts  3.83 us (11%)
  other arithmetic  2.16 us (6%)
  between operations  0.68 us (2%)
    ppermute x4, starting transfers between devices, shifted(): lax.ppermute(value, axis, [(i, (i + by) % peers) for i in range(peers)])  7.46 us
    pallas_call x1, Pallas kernels, on_device(): pl.pallas_call(functools.partial(first_kernel, mesh_peers), out_shape=(ja...  5.11 us
    ppermute x2, starting transfers between devices, mesh_sum(): lax.ppermute(value, 'mesh', [(i, i ^ step) for i in range(peers)])  3.6 us
    pallas_call x1, Pallas kernels, on_device(): pl.pallas_call(functools.partial(second_kernel, mesh_peers, force_scale),...  3.5 us
    pallas_call x1, Pallas kernels, on_device(): pl.pallas_call(functools.partial(step2_rate_kernel, mesh_peers, modes), o...  3.22 us
    ppermute x4, waiting for transfers between devices, shifted(): lax.ppermute(value, axis, [(i, (i + by) % peers) for i in range(peers)])  2.74 us
    unnamed x8, local copies, waits for them, and re-layouts  1.92 us
    pallas_call x1, Pallas kernels, on_device(): pl.pallas_call(functools.partial(pick_kernel, passages), out_shape=(row_s...  1.78 us
  transfers between devices with their start and end apart: 6, of which 3 were waited for; matrix products, arithmetic and copies ran while one was open for 4% of the time, Pallas kernels for 9%

profile of v17, /device:TPU:0, one launch (start us, length us, event | category | flops | bytes accessed | tf_op | source)
XLA Modules:
  0.0 35.6 jit_solution(18265628144253570843)
XLA Ops:
  0.6 0.0 copy-start.1
  0.6 1.8 %shard_map.130 = (f32[2,5,256]{2,1,0:T(8,128)}, f32[2,5,256]{2,1,0:T(8,128)}) custom-call(s32[8]{0:T(128)} %lower_slot_ref.1, s32[8]{0:T(128)} %upper_slot_ref.1, f32[5,64,256]{2,1,0:T(8,128)} %bitcast.34, f32[5,64,256]{2,1,0:T(8,128)} %bitcast.35), custom_call_target="tpu_custom_call" | custom-call | tf_op jit(solution)/shard_map/pallas_call | solution.py:466
  2.4 0.5 %collective-permute-start = (f32[2,5,256]{2,1,0:T(8,128)}, f32[2,5,256]{2,1,0:T(8,128)S(1)}, u32[]{:S(2)}, u32[]{:S(2)}) collective-permute-start(f32[2,5,256]{2,1,0:T(8,128)} %get-tuple-element.10), channel_id=1, source_target_pairs={{0,4},{4,8},{8,12},{12,16},{16,20},{20,24},{24,28},{28,0},{1,5},{5... | collective-permute-start | bytes 30728 | tf_op jit(solution)/shard_map/ppermute | solution.py:23
  2.9 4.0 %collective-permute-start.1 = (f32[2,5,256]{2,1,0:T(8,128)}, f32[2,5,256]{2,1,0:T(8,128)S(1)}, u32[]{:S(2)}, u32[]{:S(2)}) collective-permute-start(f32[2,5,256]{2,1,0:T(8,128)} %get-tuple-element.11), channel_id=1, source_target_pairs={{0,28},{4,0},{8,4},{12,8},{16,12},{20,16},{24,20},{28,24},{1,29},{... | collective-permute-start | bytes 30728 | tf_op jit(solution)/shard_map/ppermute | solution.py:23
  6.9 0.0 copy-done.1
  6.9 0.0 copy-start
  6.9 0.1 fusion
  7.0 0.9 %copy-done = f32[4,96,256]{2,1,0:T(8,128)S(1)} copy-done((f32[4,96,256]{2,1,0:T(8,128)S(1)}, f32[4,96,256]{2,1,0:T(8,128)}, u32[]{:S(2)}) %copy-start) | copy-done | bytes 393240
  7.9 0.1 fusion.1
  8.0 0.1 copy.25
  8.1 0.1 copy.29
  8.2 0.1 copy.24
  8.4 0.1 copy.28
  8.5 0.0 collective-permute-done.glo_ref
  8.5 0.0 copy-start.2
  8.5 0.1 slice_bitcast_fusion.3
  8.6 0.5 %copy-done.2 = f32[2,5,256]{2,1,0:T(8,128)} copy-done((f32[2,5,256]{2,1,0:T(8,128)}, f32[2,5,256]{2,1,0:T(8,128)S(1)}, u32[]{:S(2)}) %copy-start.2) | copy-done | bytes 10264
  9.1 0.1 copy.22
  9.2 0.1 reshape.46
  9.3 0.1 copy.26
  9.4 0.1 reshape.51
  9.5 0.0 collective-permute-done.1.gup_ref
  9.5 0.0 copy-start.3
  9.5 0.1 slice_bitcast_fusion.2
  9.6 0.5 %copy-done.3 = f32[2,5,256]{2,1,0:T(8,128)} copy-done((f32[2,5,256]{2,1,0:T(8,128)}, f32[2,5,256]{2,1,0:T(8,128)S(1)}, u32[]{:S(2)}) %copy-start.3) | copy-done | bytes 10264
  10.1 0.1 copy.23
  10.2 0.1 reshape.47
  10.3 0.1 copy.27
  10.4 0.1 reshape.52
  10.5 0.1 pad_maximum_fusion
  10.6 0.1 reshape.48
  10.6 2.0 %collective-permute-start.2 = (f32[3536]{0:T(1024)S(1)}, f32[3536]{0:T(1024)S(1)}, u32[]{:S(2)}, u32[]{:S(2)}) collective-permute-start(f32[3536]{0:T(1024)S(1)} %reshape.48), channel_id=1, source_target_pairs={{0,1},{1,2},{2,3},{3,0},{4,5},{5,6},{6,7},{7,4},{8,9},{9,10},{10,1... | collective-permute-start | bytes 42440 | tf_op jit(solution)/shard_map/ppermute | solution.py:23
  12.6 0.1 pad_maximum_fusion.1
  12.7 0.1 reshape.53
  12.8 1.0 %collective-permute-start.3 = (f32[3536]{0:T(1024)S(1)}, f32[3536]{0:T(1024)S(1)}, u32[]{:S(2)}, u32[]{:S(2)}) collective-permute-start(f32[3536]{0:T(1024)S(1)} %reshape.53), channel_id=1, source_target_pairs={{0,3},{1,0},{2,1},{3,2},{4,7},{5,4},{6,5},{7,6},{8,11},{9,8},{10,9... | collective-permute-start | bytes 42440 | tf_op jit(solution)/shard_map/ppermute | solution.py:23
  13.8 1.6 %collective-permute-done.2 = f32[3536]{0:T(1024)S(1)} collective-permute-done((f32[3536]{0:T(1024)S(1)}, f32[3536]{0:T(1024)S(1)}, u32[]{:S(2)}, u32[]{:S(2)}) %collective-permute-start.2) | collective-permute-done | bytes 14176 | tf_op jit(solution)/shard_map/ppermute | solution.py:23
  15.4 0.1 select_n.22
  15.5 1.0 %collective-permute-done.3 = f32[3536]{0:T(1024)S(1)} collective-permute-done((f32[3536]{0:T(1024)S(1)}, f32[3536]{0:T(1024)S(1)}, u32[]{:S(2)}, u32[]{:S(2)}) %collective-permute-start.3) | collective-permute-done | bytes 14176 | tf_op jit(solution)/shard_map/ppermute | solution.py:23
  16.5 0.1 select_n.25
  16.6 0.6 %select_maximum_fusion.packed_ref = f32[8,896]{1,0:T(8,128)} fusion(f32[4,884]{1,0:T(4,128)S(1)} %select_n.25, f32[4,884]{1,0:T(4,128)S(1)} %select_n.22), kind=kLoop, calls=%fused_computation | loop fusion | flops 28672 | bytes 56960 | tf_op jit(solution)/shard_map/concatenate | solution.py:492
  17.3 5.1 %shard_map.131 = (f32[5,96,384]{2,1,0:T(8,128)}, f32[32,128]{1,0:T(8,128)}) custom-call(f32[5,5]{1,0:T(8,128)} %ax_ref.5, f32[5,5]{1,0:T(8,128)} %pt_ref.5, f32[1,4]{1,0:T(1,128)} %vel_ref.3, f32[5,96,256]{2,1,0:T(8,128)} %bitcast.28, f32[4,96,256]{2,1,0:T(8,128)} %ms_ref.3, f32[2,5,256]{2,1,0:T(8,128)} %copy-done.2, f32[2,5,256]{2,1,0:T(8,128)} %copy-done.3, ...), custom_call_target="tpu_custom_call" | custom-call | tf_op jit(solution)/shard_map/pallas_call | solution.py:498
  22.4 0.8 %reduce_sum.9 = f32[32]{0:T(128)S(1)} reduce(f32[32,128]{1,0:T(8,128)} %get-tuple-element.12, f32[]{:T(128)} %constant.2.clone.1), dimensions={1}, to_apply=%region_0.1 | reduce | flops 4064 | bytes 16516 | tf_op jit(solution)/shard_map/reduce_sum | solution.py:509
  23.2 2.5 %collective-permute-start.4 = (f32[32]{0:T(128)S(1)}, f32[32]{0:T(128)S(1)}, u32[]{:S(2)}, u32[]{:S(2)}) collective-permute-start(f32[32]{0:T(128)S(1)} %reduce_sum.9), channel_id=1, source_target_pairs={{0,1},{1,0},{2,3},{3,2},{4,5},{5,4},{6,7},{7,6},{8,9},{9,8},{10,11... | collective-permute-start | bytes 392 | tf_op jit(solution)/shard_map/ppermute | solution.py:42
  25.6 1.5 %collective-permute-done.4 = f32[32]{0:T(128)S(1)} collective-permute-done((f32[32]{0:T(128)S(1)}, f32[32]{0:T(128)S(1)}, u32[]{:S(2)}, u32[]{:S(2)}) %collective-permute-start.4) | collective-permute-done | bytes 160 | tf_op jit(solution)/shard_map/ppermute | solution.py:42
  27.2 1.1 %collective-permute-start.5 = (f32[32]{0:T(128)S(1)}, f32[32]{0:T(128)S(1)}, u32[]{:S(2)}, u32[]{:S(2)}) collective-permute-start(f32[32]{0:T(128)S(1)} %add.8), channel_id=1, source_target_pairs={{0,2},{1,3},{2,0},{3,1},{4,6},{5,7},{6,4},{7,5},{8,10},{9,11},{10,... | collective-permute-start | bytes 392 | tf_op jit(solution)/shard_map/ppermute | solution.py:42
  28.3 3.2 %shard_map.132.ra_ref = f32[5,96,384]{2,1,0:T(8,128)} custom-call(f32[5,5]{1,0:T(8,128)} %ax_ref.5, f32[5,5]{1,0:T(8,128)} %pt_ref.5, f32[5,96,384]{2,1,0:T(8,128)} %get-tuple-element.13.a_ref, f32[2,5,256]{2,1,0:T(8,128)} %copy-done.2, f32[2,5,256]{2,1,0:T(8,128)} %copy-done.3, f32[8,896]{1,0:T(8,128)} %select_maximum_fusion.packed_ref), custom_call_target="tpu_custom_call" | custom-call | tf_op jit(solution)/shard_map/pallas_call | solution.py:511
  31.5 0.0 collective-permute-done.5
  31.5 0.5 %add.9.tot_ref = f32[32]{0:T(128)} add(f32[32]{0:T(128)S(1)} %add.8, f32[32]{0:T(128)S(1)} %collective-permute-done.5) | non-fusion elementwise | flops 32 | bytes 384 | tf_op jit(solution)/shard_map/add | solution.py:42
  32.1 3.5 %shard_map.133 = (f32[5,96,256]{2,1,0:T(8,128)}, f32[1,4]{1,0:T(1,128)}, f32[1,4]{1,0:T(1,128)}) custom-call(f32[32]{0:T(128)} %add.9.tot_ref, f32[1,4]{1,0:T(1,128)} %stiff_ref.1, f32[1,4]{1,0:T(1,128)} %disp_ref.1, f32[1,4]{1,0:T(1,128)} %vel_ref.3, f32[5,5]{1,0:T(8,128)} %ax_ref.5, f32[5,5]{1,0:T(8,128)} %pt_ref.5, ...), custom_call_target="tpu_custom_call" | custom-call | tf_op jit(solution)/shard_map/pallas_call | solution.py:520
  (3 shorter events, 0.0 us)
Async XLA Ops:
  0.6 6.3 %copy-start.1 = (f32[1,5,96,256]{3,2,1,0:T(8,128)S(1)}, f32[1,5,96,256]{3,2,1,0:T(8,128)}, u32[]{:S(2)}) copy-start(f32[1,5,96,256]{3,2,1,0:T(8,128)} %param.11) | copy-start | bytes 1474564
  2.4 6.1 %collective-permute-start = (f32[2,5,256]{2,1,0:T(8,128)}, f32[2,5,256]{2,1,0:T(8,128)S(1)}, u32[]{:S(2)}, u32[]{:S(2)}) collective-permute-start(f32[2,5,256]{2,1,0:T(8,128)} %get-tuple-element.10), channel_id=1, source_target_pairs={{0,4},{4,8},{8,12},{12,16},{16,20},{20,24},{24,28},{28,0},{1,5},{5... | collective-permute-start | bytes 30728 | tf_op jit(solution)/shard_map/ppermute | solution.py:23
  2.9 6.6 %collective-permute-start.1 = (f32[2,5,256]{2,1,0:T(8,128)}, f32[2,5,256]{2,1,0:T(8,128)S(1)}, u32[]{:S(2)}, u32[]{:S(2)}) collective-permute-start(f32[2,5,256]{2,1,0:T(8,128)} %get-tuple-element.11), channel_id=1, source_target_pairs={{0,28},{4,0},{8,4},{12,8},{16,12},{20,16},{24,20},{28,24},{1,29},{... | collective-permute-start | bytes 30728 | tf_op jit(solution)/shard_map/ppermute | solution.py:23
  6.9 1.0 %copy-start = (f32[4,96,256]{2,1,0:T(8,128)S(1)}, f32[4,96,256]{2,1,0:T(8,128)}, u32[]{:S(2)}) copy-start(f32[4,96,256]{2,1,0:T(8,128)} %ms_ref.3) | copy-start | bytes 1179652
  8.5 0.6 %copy-start.2 = (f32[2,5,256]{2,1,0:T(8,128)}, f32[2,5,256]{2,1,0:T(8,128)S(1)}, u32[]{:S(2)}) copy-start(f32[2,5,256]{2,1,0:T(8,128)S(1)} %collective-permute-done.glo_ref) | copy-start | bytes 30724
  9.5 0.6 %copy-start.3 = (f32[2,5,256]{2,1,0:T(8,128)}, f32[2,5,256]{2,1,0:T(8,128)S(1)}, u32[]{:S(2)}) copy-start(f32[2,5,256]{2,1,0:T(8,128)S(1)} %collective-permute-done.1.gup_ref) | copy-start | bytes 30724
  10.6 4.8 %collective-permute-start.2 = (f32[3536]{0:T(1024)S(1)}, f32[3536]{0:T(1024)S(1)}, u32[]{:S(2)}, u32[]{:S(2)}) collective-permute-start(f32[3536]{0:T(1024)S(1)} %reshape.48), channel_id=1, source_target_pairs={{0,1},{1,2},{2,3},{3,0},{4,5},{5,6},{6,7},{7,4},{8,9},{9,10},{10,1... | collective-permute-start | bytes 42440 | tf_op jit(solution)/shard_map/ppermute | solution.py:23
  12.8 3.7 %collective-permute-start.3 = (f32[3536]{0:T(1024)S(1)}, f32[3536]{0:T(1024)S(1)}, u32[]{:S(2)}, u32[]{:S(2)}) collective-permute-start(f32[3536]{0:T(1024)S(1)} %reshape.53), channel_id=1, source_target_pairs={{0,3},{1,0},{2,1},{3,2},{4,7},{5,4},{6,5},{7,6},{8,11},{9,8},{10,9... | collective-permute-start | bytes 42440 | tf_op jit(solution)/shard_map/ppermute | solution.py:23
  23.2 4.0 %collective-permute-start.4 = (f32[32]{0:T(128)S(1)}, f32[32]{0:T(128)S(1)}, u32[]{:S(2)}, u32[]{:S(2)}) collective-permute-start(f32[32]{0:T(128)S(1)} %reduce_sum.9), channel_id=1, source_target_pairs={{0,1},{1,0},{2,3},{3,2},{4,5},{5,4},{6,7},{7,6},{8,9},{9,8},{10,11... | collective-permute-start | bytes 392 | tf_op jit(solution)/shard_map/ppermute | solution.py:42
  27.2 4.4 %collective-permute-start.5 = (f32[32]{0:T(128)S(1)}, f32[32]{0:T(128)S(1)}, u32[]{:S(2)}, u32[]{:S(2)}) collective-permute-start(f32[32]{0:T(128)S(1)} %add.8), channel_id=1, source_target_pairs={{0,2},{1,3},{2,0},{3,1},{4,6},{5,7},{6,4},{7,5},{8,10},{9,11},{10,... | collective-permute-start | bytes 392 | tf_op jit(solution)/shard_map/ppermute | solution.py:42

commit v18 on v17

--- a/solution.py
+++ b/solution.py
@@ -31,6 +31,17 @@
     before = jnp.where(me > 0, before, jnp.zeros_like(before))
     after = jnp.where(me < peers - 1, after, jnp.zeros_like(after))
     return before, after
+
+
+def mesh_sum_pair(value):
+    peers = lax.axis_size("mesh")
+    if peers & (peers - 1) or peers < 2:
+        return lax.psum(value, "mesh"), jnp.zeros_like(value)
+    step = 1
+    while 2 * step < peers:
+        value = value + lax.ppermute(value, "mesh", [(i, i ^ step) for i in range(peers)])
+        step *= 2
+    return value, lax.ppermute(value, "mesh", [(i, i ^ step) for i in range(peers)])
 
 
 def mesh_sum(value):
@@ -308,9 +319,9 @@
             part_ref[k + m * modes + n : k + m * modes + n + 1, :] = lane_fold(weighted[m] * t)
 
 
-def modal_steps(force_scale, tot_ref, stiff_ref, disp_ref, vel_ref, modes):
+def modal_steps(force_scale, sums, stiff_ref, disp_ref, vel_ref, modes):
     h = TIME_STEP
-    t = [force_scale * tot_ref[k] for k in range(4 * modes + modes * modes)]
+    t = [force_scale * value for value in sums]
     force = [t[w * modes : (w + 1) * modes] for w in range(4)]
     couple = [t[4 * modes + m * modes : 4 * modes + (m + 1) * modes] for m in range(modes)]
     stiff = [stiff_ref[0, m] for m in range(modes)]
@@ -363,12 +374,13 @@
 def second_kernel(
     peers,
     force_scale,
-    tot_ref,
     stiff_ref,
     disp_ref,
     vel_ref,
     ax_ref,
     pt_ref,
+    tot_ref,
+    other_ref,
     a_ref,
     ra_ref,
     ms_ref,
@@ -386,7 +398,14 @@
     modes = ms_ref.shape[0]
     pitch = ms_ref.shape[1]
     jac = read_jacobians(ax_ref, pt_ref, fields)
-    coef, disp2, vel2 = modal_steps(force_scale, tot_ref, stiff_ref, disp_ref, vel_ref, modes)
+    coef, disp2, vel2 = modal_steps(
+        force_scale,
+        [jnp.sum(tot_ref[k : k + 1, :] + other_ref[k : k + 1, :]) for k in range(tot_ref.shape[0])],
+        stiff_ref,
+        disp_ref,
+        vel_ref,
+        modes,
+    )
     for m in range(modes):
         disp_out_ref[0, m] = disp2[m]
         vel_out_ref[0, m] = vel2[m]
@@ -506,7 +525,7 @@
         scratch_shapes=columns,
     )(axial_jacobian, pitch_jacobian, velocity, *ins)
 
-    totals = mesh_sum(jnp.sum(part_lanes, axis=1))
+    totals, totals_other = mesh_sum_pair(part_lanes)
 
     rate_a = pl.pallas_call(
         functools.partial(step2_rate_kernel, mesh_peers, modes),
@@ -520,10 +539,21 @@
     state2, disp2, vel2 = pl.pallas_call(
         functools.partial(second_kernel, mesh_peers, force_scale),
         out_shape=(jax.ShapeDtypeStruct(state0.shape, state0.dtype), small, small),
-        in_specs=[smem_spec()] * 6 + [vmem_spec()] * 6,
+        in_specs=[smem_spec()] * 5 + [vmem_spec()] * 8,
         out_specs=(vmem_spec(), smem_spec(), smem_spec()),
         scratch_shapes=columns,
-    )(totals, stiffness, displacement, velocity, axial_jacobian, pitch_jacobian, base1, rate_a, *ins[1:])
+    )(
+        stiffness,
+        displacement,
+        velocity,
+        axial_jacobian,
+        pitch_jacobian,
+        totals,
+        totals_other,
+        base1,
+        rate_a,
+        *ins[1:],
+    )
     return (state2[None], disp2, vel2)
 
 

time: 35.9 us -> 36.3 us (1.011)
  other arithmetic: 2.16 us -> 1.51 us
  local copies, waits for them, and re-layouts: 3.83 us -> 4.43 us
  waiting for transfers between devices: 4.26 us -> 4.67 us
    reduce_sum x1 -> x0, other arithmetic: 0.83 us -> none  [on_device(): totals = mesh_sum(jnp.sum(part_lanes, axis=1))]
    unnamed x8 -> x12, local copies, waits for them, and re-layouts: 1.92 us -> 2.52 us
    ppermute x2, waiting for transfers between devices: 1.52 us -> 1.93 us  [mesh_sum_pair(): lax.ppermute(value, 'mesh', [(i, i ^ step) for i in range(peers)])]
where the time goes in v18:
time: 36.3 us; the launch traced here: 36 us
  Pallas kernels  13.7 us (38%)
  starting transfers between devices  11 us (30%)
  waiting for transfers between devices  4.67 us (13%)
  local copies, waits for them, and re-layouts  4.43 us (12%)
  other arithmetic  1.51 us (4%)
  between operations  0.69 us (2%)
    ppermute x4, starting transfers between devices, shifted(): lax.ppermute(value, axis, [(i, (i + by) % peers) for i in range(peers)])  7.46 us
    pallas_call x1, Pallas kernels, on_device(): pl.pallas_call(functools.partial(first_kernel, mesh_peers), out_shape=(ja...  5.13 us
    pallas_call x1, Pallas kernels, on_device(): pl.pallas_call(functools.partial(second_kernel, mesh_peers, force_scale),...  3.58 us
    ppermute x2, starting transfers between devices, mesh_sum_pair(): lax.ppermute(value, 'mesh', [(i, i ^ step) for i in range(peers)])  3.54 us
    pallas_call x1, Pallas kernels, on_device(): pl.pallas_call(functools.partial(step2_rate_kernel, mesh_peers, modes), o...  3.23 us
    ppermute x4, waiting for transfers between devices, shifted(): lax.ppermute(value, axis, [(i, (i + by) % peers) for i in range(peers)])  2.74 us
    unnamed x12, local copies, waits for them, and re-layouts  2.52 us
    ppermute x2, waiting for transfers between devices, mesh_sum_pair(): lax.ppermute(value, 'mesh', [(i, i ^ step) for i in range(peers)])  1.93 us
  transfers between devices with their start and end apart: 6, of which 3 were waited for; matrix products, arithmetic and copies ran while one was open for 4% of the time, Pallas kernels for 9%

profile of v18, /device:TPU:0, one launch (start us, length us, event | category | flops | bytes accessed | tf_op | source)
XLA Modules:
  0.0 36.0 jit_solution(9326831068036239483)
XLA Ops:
  0.6 0.0 copy-start.1
  0.6 1.8 %shard_map.130 = (f32[2,5,256]{2,1,0:T(8,128)}, f32[2,5,256]{2,1,0:T(8,128)}) custom-call(s32[8]{0:T(128)} %lower_slot_ref.1, s32[8]{0:T(128)} %upper_slot_ref.1, f32[5,64,256]{2,1,0:T(8,128)} %bitcast.34, f32[5,64,256]{2,1,0:T(8,128)} %bitcast.35), custom_call_target="tpu_custom_call" | custom-call | tf_op jit(solution)/shard_map/pallas_call | solution.py:485
  2.4 0.5 %collective-permute-start = (f32[2,5,256]{2,1,0:T(8,128)}, f32[2,5,256]{2,1,0:T(8,128)S(1)}, u32[]{:S(2)}, u32[]{:S(2)}) collective-permute-start(f32[2,5,256]{2,1,0:T(8,128)} %get-tuple-element.10), channel_id=1, source_target_pairs={{0,4},{4,8},{8,12},{12,16},{16,20},{20,24},{24,28},{28,0},{1,5},{5... | collective-permute-start | bytes 30728 | tf_op jit(solution)/shard_map/ppermute | solution.py:23
  2.9 4.0 %collective-permute-start.1 = (f32[2,5,256]{2,1,0:T(8,128)}, f32[2,5,256]{2,1,0:T(8,128)S(1)}, u32[]{:S(2)}, u32[]{:S(2)}) collective-permute-start(f32[2,5,256]{2,1,0:T(8,128)} %get-tuple-element.11), channel_id=1, source_target_pairs={{0,28},{4,0},{8,4},{12,8},{16,12},{20,16},{24,20},{28,24},{1,29},{... | collective-permute-start | bytes 30728 | tf_op jit(solution)/shard_map/ppermute | solution.py:23
  6.9 0.0 copy-done.1
  6.9 0.0 copy-start
  6.9 0.1 fusion
  7.1 0.9 %copy-done = f32[4,96,256]{2,1,0:T(8,128)S(1)} copy-done((f32[4,96,256]{2,1,0:T(8,128)S(1)}, f32[4,96,256]{2,1,0:T(8,128)}, u32[]{:S(2)}) %copy-start) | copy-done | bytes 393240
  7.9 0.1 fusion.1
  8.0 0.1 copy.25
  8.1 0.1 copy.29
  8.2 0.1 copy.24
  8.4 0.1 copy.28
  8.5 0.0 collective-permute-done.glo_ref
  8.5 0.0 copy-start.2
  8.5 0.1 slice_bitcast_fusion.3
  8.6 0.5 %copy-done.2 = f32[2,5,256]{2,1,0:T(8,128)} copy-done((f32[2,5,256]{2,1,0:T(8,128)}, f32[2,5,256]{2,1,0:T(8,128)S(1)}, u32[]{:S(2)}) %copy-start.2) | copy-done | bytes 10264
  9.1 0.1 copy.22
  9.2 0.1 reshape.46
  9.3 0.1 copy.26
  9.4 0.1 reshape.51
  9.5 0.0 collective-permute-done.1.gup_ref
  9.5 0.0 copy-start.3
  9.5 0.1 slice_bitcast_fusion.2
  9.6 0.5 %copy-done.3 = f32[2,5,256]{2,1,0:T(8,128)} copy-done((f32[2,5,256]{2,1,0:T(8,128)}, f32[2,5,256]{2,1,0:T(8,128)S(1)}, u32[]{:S(2)}) %copy-start.3) | copy-done | bytes 10264
  10.1 0.1 copy.23
  10.2 0.1 reshape.47
  10.3 0.1 copy.27
  10.4 0.1 reshape.52
  10.5 0.1 pad_maximum_fusion
  10.6 0.1 reshape.48
  10.6 2.0 %collective-permute-start.2 = (f32[3536]{0:T(1024)S(1)}, f32[3536]{0:T(1024)S(1)}, u32[]{:S(2)}, u32[]{:S(2)}) collective-permute-start(f32[3536]{0:T(1024)S(1)} %reshape.48), channel_id=1, source_target_pairs={{0,1},{1,2},{2,3},{3,0},{4,5},{5,6},{6,7},{7,4},{8,9},{9,10},{10,1... | collective-permute-start | bytes 42440 | tf_op jit(solution)/shard_map/ppermute | solution.py:23
  12.6 0.1 pad_maximum_fusion.1
  12.7 0.1 reshape.53
  12.8 1.0 %collective-permute-start.3 = (f32[3536]{0:T(1024)S(1)}, f32[3536]{0:T(1024)S(1)}, u32[]{:S(2)}, u32[]{:S(2)}) collective-permute-start(f32[3536]{0:T(1024)S(1)} %reshape.53), channel_id=1, source_target_pairs={{0,3},{1,0},{2,1},{3,2},{4,7},{5,4},{6,5},{7,6},{8,11},{9,8},{10,9... | collective-permute-start | bytes 42440 | tf_op jit(solution)/shard_map/ppermute | solution.py:23
  13.8 1.6 %collective-permute-done.2 = f32[3536]{0:T(1024)S(1)} collective-permute-done((f32[3536]{0:T(1024)S(1)}, f32[3536]{0:T(1024)S(1)}, u32[]{:S(2)}, u32[]{:S(2)}) %collective-permute-start.2) | collective-permute-done | bytes 14176 | tf_op jit(solution)/shard_map/ppermute | solution.py:23
  15.4 0.1 select_n.22
  15.5 1.0 %collective-permute-done.3 = f32[3536]{0:T(1024)S(1)} collective-permute-done((f32[3536]{0:T(1024)S(1)}, f32[3536]{0:T(1024)S(1)}, u32[]{:S(2)}, u32[]{:S(2)}) %collective-permute-start.3) | collective-permute-done | bytes 14176 | tf_op jit(solution)/shard_map/ppermute | solution.py:23
  16.6 0.1 select_n.25
  16.6 0.6 %select_maximum_fusion.packed_ref = f32[8,896]{1,0:T(8,128)} fusion(f32[4,884]{1,0:T(4,128)S(1)} %select_n.25, f32[4,884]{1,0:T(4,128)S(1)} %select_n.22), kind=kLoop, calls=%fused_computation | loop fusion | flops 28672 | bytes 56960 | tf_op jit(solution)/shard_map/concatenate | solution.py:511
  17.3 5.1 %shard_map.131 = (f32[5,96,384]{2,1,0:T(8,128)}, f32[32,128]{1,0:T(8,128)}) custom-call(f32[5,5]{1,0:T(8,128)} %ax_ref.5, f32[5,5]{1,0:T(8,128)} %pt_ref.5, f32[1,4]{1,0:T(1,128)} %vel_ref.3, f32[5,96,256]{2,1,0:T(8,128)} %bitcast.28, f32[4,96,256]{2,1,0:T(8,128)} %ms_ref.3, f32[2,5,256]{2,1,0:T(8,128)} %copy-done.2, f32[2,5,256]{2,1,0:T(8,128)} %copy-done.3, ...), custom_call_target="tpu_custom_call" | custom-call | tf_op jit(solution)/shard_map/pallas_call | solution.py:517
  22.4 2.4 %collective-permute-start.4 = (f32[32,128]{1,0:T(8,128)}, f32[32,128]{1,0:T(8,128)S(1)}, u32[]{:S(2)}, u32[]{:S(2)}) collective-permute-start(f32[32,128]{1,0:T(8,128)} %get-tuple-element.12), channel_id=1, source_target_pairs={{0,1},{1,0},{2,3},{3,2},{4,5},{5,4},{6,7},{7,6},{8,9},{9,8},{10,11... | collective-permute-start | bytes 49160 | tf_op jit(solution)/shard_map/ppermute | solution.py:42
  24.8 1.9 %collective-permute-done.4 = f32[32,128]{1,0:T(8,128)S(1)} collective-permute-done((f32[32,128]{1,0:T(8,128)}, f32[32,128]{1,0:T(8,128)S(1)}, u32[]{:S(2)}, u32[]{:S(2)}) %collective-permute-start.4) | collective-permute-done | bytes 16416 | tf_op jit(solution)/shard_map/ppermute | solution.py:42
  26.7 0.7 %add.5.tot_ref = f32[32,128]{1,0:T(8,128)S(1)} add(f32[32,128]{1,0:T(8,128)} %get-tuple-element.12, f32[32,128]{1,0:T(8,128)S(1)} %collective-permute-done.4) | non-fusion elementwise | flops 4096 | bytes 49152 | tf_op jit(solution)/shard_map/add | solution.py:42
  27.4 0.0 copy-start.4
  27.4 1.2 %collective-permute-start.5 = (f32[32,128]{1,0:T(8,128)S(1)}, f32[32,128]{1,0:T(8,128)S(1)}, u32[]{:S(2)}, u32[]{:S(2)}) collective-permute-start(f32[32,128]{1,0:T(8,128)S(1)} %add.5.tot_ref), channel_id=1, source_target_pairs={{0,2},{1,3},{2,0},{3,1},{4,6},{5,7},{6,4},{7,5},{8,10},{9,11},{10,... | collective-permute-start | bytes 49160 | tf_op jit(solution)/shard_map/ppermute | solution.py:44
  28.6 3.2 %shard_map.132.ra_ref = f32[5,96,384]{2,1,0:T(8,128)} custom-call(f32[5,5]{1,0:T(8,128)} %ax_ref.5, f32[5,5]{1,0:T(8,128)} %pt_ref.5, f32[5,96,384]{2,1,0:T(8,128)} %get-tuple-element.13.a_ref, f32[2,5,256]{2,1,0:T(8,128)} %copy-done.2, f32[2,5,256]{2,1,0:T(8,128)} %copy-done.3, f32[8,896]{1,0:T(8,128)} %select_maximum_fusion.packed_ref), custom_call_target="tpu_custom_call" | custom-call | tf_op jit(solution)/shard_map/pallas_call | solution.py:530
  31.8 0.0 copy-done.4
  31.8 0.0 collective-permute-done.5.other_ref
  31.8 0.0 copy-start.5
  31.8 0.6 %copy-done.5 = f32[32,128]{1,0:T(8,128)} copy-done((f32[32,128]{1,0:T(8,128)}, f32[32,128]{1,0:T(8,128)S(1)}, u32[]{:S(2)}) %copy-start.5) | copy-done | bytes 16408
  32.4 3.6 %shard_map.133 = (f32[5,96,256]{2,1,0:T(8,128)}, f32[1,4]{1,0:T(1,128)}, f32[1,4]{1,0:T(1,128)}) custom-call(f32[1,4]{1,0:T(1,128)} %stiff_ref.1, f32[1,4]{1,0:T(1,128)} %disp_ref.1, f32[1,4]{1,0:T(1,128)} %vel_ref.3, f32[5,5]{1,0:T(8,128)} %ax_ref.5, f32[5,5]{1,0:T(8,128)} %pt_ref.5, f32[32,128]{1,0:T(8,128)} %copy-done.4, f32[32,128]{1,0:T(8,128)} %copy-done.5, ...), custom_call_target="tpu_custom_call" | custom-call | tf_op jit(solution)/shard_map/pallas_call | solution.py:539
  (2 shorter events, 0.0 us)
Async XLA Ops:
  0.6 6.3 %copy-start.1 = (f32[1,5,96,256]{3,2,1,0:T(8,128)S(1)}, f32[1,5,96,256]{3,2,1,0:T(8,128)}, u32[]{:S(2)}) copy-start(f32[1,5,96,256]{3,2,1,0:T(8,128)} %param.11) | copy-start | bytes 1474564
  2.4 6.1 %collective-permute-start = (f32[2,5,256]{2,1,0:T(8,128)}, f32[2,5,256]{2,1,0:T(8,128)S(1)}, u32[]{:S(2)}, u32[]{:S(2)}) collective-permute-start(f32[2,5,256]{2,1,0:T(8,128)} %get-tuple-element.10), channel_id=1, source_target_pairs={{0,4},{4,8},{8,12},{12,16},{16,20},{20,24},{24,28},{28,0},{1,5},{5... | collective-permute-start | bytes 30728 | tf_op jit(solution)/shard_map/ppermute | solution.py:23
  2.9 6.6 %collective-permute-start.1 = (f32[2,5,256]{2,1,0:T(8,128)}, f32[2,5,256]{2,1,0:T(8,128)S(1)}, u32[]{:S(2)}, u32[]{:S(2)}) collective-permute-start(f32[2,5,256]{2,1,0:T(8,128)} %get-tuple-element.11), channel_id=1, source_target_pairs={{0,28},{4,0},{8,4},{12,8},{16,12},{20,16},{24,20},{28,24},{1,29},{... | collective-permute-start | bytes 30728 | tf_op jit(solution)/shard_map/ppermute | solution.py:23
  6.9 1.0 %copy-start = (f32[4,96,256]{2,1,0:T(8,128)S(1)}, f32[4,96,256]{2,1,0:T(8,128)}, u32[]{:S(2)}) copy-start(f32[4,96,256]{2,1,0:T(8,128)} %ms_ref.3) | copy-start | bytes 1179652
  8.5 0.6 %copy-start.2 = (f32[2,5,256]{2,1,0:T(8,128)}, f32[2,5,256]{2,1,0:T(8,128)S(1)}, u32[]{:S(2)}) copy-start(f32[2,5,256]{2,1,0:T(8,128)S(1)} %collective-permute-done.glo_ref) | copy-start | bytes 30724
  9.5 0.6 %copy-start.3 = (f32[2,5,256]{2,1,0:T(8,128)}, f32[2,5,256]{2,1,0:T(8,128)S(1)}, u32[]{:S(2)}) copy-start(f32[2,5,256]{2,1,0:T(8,128)S(1)} %collective-permute-done.1.gup_ref) | copy-start | bytes 30724
  10.6 4.8 %collective-permute-start.2 = (f32[3536]{0:T(1024)S(1)}, f32[3536]{0:T(1024)S(1)}, u32[]{:S(2)}, u32[]{:S(2)}) collective-permute-start(f32[3536]{0:T(1024)S(1)} %reshape.48), channel_id=1, source_target_pairs={{0,1},{1,2},{2,3},{3,0},{4,5},{5,6},{6,7},{7,4},{8,9},{9,10},{10,1... | collective-permute-start | bytes 42440 | tf_op jit(solution)/shard_map/ppermute | solution.py:23
  12.8 3.7 %collective-permute-start.3 = (f32[3536]{0:T(1024)S(1)}, f32[3536]{0:T(1024)S(1)}, u32[]{:S(2)}, u32[]{:S(2)}) collective-permute-start(f32[3536]{0:T(1024)S(1)} %reshape.53), channel_id=1, source_target_pairs={{0,3},{1,0},{2,1},{3,2},{4,7},{5,4},{6,5},{7,6},{8,11},{9,8},{10,9... | collective-permute-start | bytes 42440 | tf_op jit(solution)/shard_map/ppermute | solution.py:23
  22.4 4.3 %collective-permute-start.4 = (f32[32,128]{1,0:T(8,128)}, f32[32,128]{1,0:T(8,128)S(1)}, u32[]{:S(2)}, u32[]{:S(2)}) collective-permute-start(f32[32,128]{1,0:T(8,128)} %get-tuple-element.12), channel_id=1, source_target_pairs={{0,1},{1,0},{2,3},{3,2},{4,5},{5,4},{6,7},{7,6},{8,9},{9,8},{10,11... | collective-permute-start | bytes 49160 | tf_op jit(solution)/shard_map/ppermute | solution.py:42
  27.4 4.4 %copy-start.4 = (f32[32,128]{1,0:T(8,128)}, f32[32,128]{1,0:T(8,128)S(1)}, u32[]{:S(2)}) copy-start(f32[32,128]{1,0:T(8,128)S(1)} %add.5.tot_ref) | copy-start | bytes 49156
  27.4 4.4 %collective-permute-start.5 = (f32[32,128]{1,0:T(8,128)S(1)}, f32[32,128]{1,0:T(8,128)S(1)}, u32[]{:S(2)}, u32[]{:S(2)}) collective-permute-start(f32[32,128]{1,0:T(8,128)S(1)} %add.5.tot_ref), channel_id=1, source_target_pairs={{0,2},{1,3},{2,0},{3,1},{4,6},{5,7},{6,4},{7,5},{8,10},{9,11},{10,... | collective-permute-start | bytes 49160 | tf_op jit(solution)/shard_map/ppermute | solution.py:44
  31.8 0.6 %copy-start.5 = (f32[32,128]{1,0:T(8,128)}, f32[32,128]{1,0:T(8,128)S(1)}, u32[]{:S(2)}) copy-start(f32[32,128]{1,0:T(8,128)S(1)} %collective-permute-done.5.other_ref) | copy-start | bytes 49156
